TPU v7x, 32 devices: a whole 2x2x4 slice. The times are simulated.
32 devices in a mesh: blk: 8 (over z, core), tp: 4 (over y, x).
Axes of the slice: x: 2, y: 2, z: 4, core: 2. Of those that a mesh axis runs over, the one named last changes fastest.
Arguments:
- tokens: bfloat16 [2048, 5120], P('blk', 'tp'), may hold values from -31 to 31
- norm_gain: bfloat16 [5120], P('tp'), may hold values from 0.15 to 2
- w_query: bfloat16 [5120, 5120], P(None, 'tp'), may hold values from -0.078125 to 0.078125
- w_key: bfloat16 [5120, 1024], P(None, 'tp'), may hold values from -0.078125 to 0.078125
- w_value: bfloat16 [5120, 1024], P(None, 'tp'), may hold values from -0.078125 to 0.078125
- query_bias: bfloat16 [5120], P('tp'), may hold values from -45 to 45
- key_bias: bfloat16 [1024], P('tp'), may hold values from -45 to 45
- value_bias: bfloat16 [1024], P('tp'), may hold values from -4 to 4
- lengths: int32 [8], replicated, may hold values from 1 to 1024, 2048 in all
- page_table: int32 [16], replicated, may hold values from 0 to 15, as said below
Outputs:
- attended: bfloat16 [2048, 5120], P('blk', 'tp')
- kv_cache: bfloat16 [16, 2, 128, 1024], P('blk', None, None, 'tp')
Inputs may be any that keep to these rules, and one draw needn't show every extreme that they name: `lengths`: the last piece is padding; the others are prompts. `page_table`: A permutation of the 16 slots; slot s belongs to index s // 2 of blk.
All inputs are finite; a program needn't handle non-finite values.
Results may differ from a plain program's by a relative error of at most 0.012.
The roundings to bfloat16 on the way count: a program that leaves them out, or rounds other values in their place, can miss the bound.
Values may be sent and summed in bfloat16 or wider, within the bound.
No kernel may reach another device: no remote copies, remote signals or barrier semaphores. Data moves between devices by JAX's collectives and lax.ppermute only.
A program may use at most 128 MiB of HBM per device.

v0:
```python
import jax
import jax.numpy as jnp
from jax import lax
from jax.sharding import PartitionSpec as P

D = 5120
HEADS = 40
KV_HEADS = 8
HEAD = 128
PAGE = 128


rope_base = 1000000.0
norm_eps = 1e-06
neg_large = -1e30


def token_meta(positions, lengths):
    ends = jnp.cumsum(lengths)
    past = (positions[:, None] >= ends[None, :]).astype(jnp.int32)
    segment = jnp.sum(past, axis=1)
    start = jnp.sum(past * lengths[None, :], axis=1)
    return (segment, positions - start)


def rotate(values, offsets):
    half = HEAD // 2
    freq = rope_base ** (-2.0 * jnp.arange(half, dtype=jnp.float32) / HEAD)
    angle = offsets.astype(jnp.float32)[:, None] * freq[None, :]
    cosine = jnp.cos(angle)[:, None, :]
    sine = jnp.sin(angle)[:, None, :]
    first = values[..., :half]
    second = values[..., half:]
    return jnp.concatenate(
        [first * cosine - second * sine, second * cosine + first * sine], axis=-1
    )


def on_device(
    tokens,
    norm_gain,
    w_query,
    w_key,
    w_value,
    query_bias,
    key_bias,
    value_bias,
    lengths,
    page_table,
):
    rows = tokens.shape[0]
    blocks = lax.axis_size("blk")
    me = lax.axis_index("blk")
    q_width = w_query.shape[1]
    kv_width = w_key.shape[1]
    kv_dev = kv_width // HEAD
    group = HEADS // KV_HEADS
    slots = rows // PAGE
    docs = lengths.shape[0]
    scale = 1.0 / float(HEAD) ** 0.5
    wide = tokens.astype(jnp.float32)
    scaled = (wide * norm_gain.astype(jnp.float32)).astype(jnp.bfloat16)
    empty = (
        jnp.zeros((rows, q_width), jnp.float32),
        jnp.zeros((rows, kv_width), jnp.float32),
        jnp.zeros((rows, kv_width), jnp.float32),
    )
    piece = lax.all_gather(scaled, "tp", axis=1, tiled=True)
    count = piece.shape[1]
    totals = []
    for total, weight in zip(empty, (w_query, w_key, w_value)):
        totals.append(jnp.dot(piece, weight, preferred_element_type=jnp.float32))
    proj_query, proj_key, proj_value = tuple(totals)
    squares = lax.psum(jnp.sum(wide * wide, axis=1), "tp")
    rstd = lax.rsqrt(squares / D + norm_eps)
    own_pos = me * rows + jnp.arange(rows, dtype=jnp.int32)
    own_seg, own_off = token_meta(own_pos, lengths)
    own_live = own_seg < docs - 1
    query = rstd[:, None] * proj_query + query_bias.astype(jnp.float32)
    key = rstd[:, None] * proj_key + key_bias.astype(jnp.float32)
    value = rstd[:, None] * proj_value + value_bias.astype(jnp.float32)
    query = (
        rotate(query.reshape(rows, q_width // HEAD, HEAD), own_off)
        .reshape(rows, q_width)
        .astype(jnp.bfloat16)
    )
    key = (
        jnp.where(own_live[:, None, None], rotate(key.reshape(rows, kv_dev, HEAD), own_off), 0.0)
        .reshape(rows, kv_width)
        .astype(jnp.bfloat16)
    )
    value = jnp.where(own_live[:, None], value, 0.0).astype(jnp.bfloat16)
    q_seg, q_off = token_meta(own_pos, lengths)
    q_live = q_seg < docs - 1
    q_grouped = query.reshape(rows, kv_dev, group, HEAD)

    both = lax.all_gather(jnp.concatenate([key, value], axis=1), "blk", axis=0, tiled=True)
    count = both.shape[0]
    longest = count // 2
    span = min(count, longest + rows)
    first = jnp.clip(me * rows - longest, 0, count - span)
    window = lax.dynamic_slice_in_dim(both, first, span, 0)
    k_pos = first + jnp.arange(span, dtype=jnp.int32)
    k_seg, k_off = token_meta(k_pos, lengths)
    allowed = (
        (k_seg[None, :] == q_seg[:, None])
        & (k_pos[None, :] <= own_pos[:, None])
        & q_live[:, None]
    )
    scores = (
        jnp.einsum(
            "qcgh,tch->cgqt",
            q_grouped,
            window[:, :kv_width].reshape(span, kv_dev, HEAD),
            preferred_element_type=jnp.float32,
        )
        * scale
    )
    scores = jnp.where(allowed, scores, neg_large)
    top = jnp.max(scores, axis=3, keepdims=True)
    expo = jnp.where(allowed, jnp.exp(scores - top), 0.0)
    denom = jnp.sum(expo, axis=3)
    acc = jnp.einsum(
        "cgqt,tch->cgqh",
        expo.astype(jnp.bfloat16),
        window[:, kv_width:].reshape(span, kv_dev, HEAD),
        preferred_element_type=jnp.float32,
    )
    attention = (None, denom, acc)
    numbers = jnp.arange(page_table.shape[0], dtype=jnp.int32)
    cache = []
    for j in range(slots):
        page = jnp.sum(jnp.where(page_table == me * slots + j, numbers, 0))
        held = lax.dynamic_slice_in_dim(both, page * PAGE, PAGE, 0)
        cache.append(jnp.stack([held[:, :kv_width], held[:, kv_width:]], axis=0))
    kv_cache = jnp.stack(cache, axis=0)
    mixed = attention[2] / jnp.where(q_live, attention[1], 1.0)[..., None]
    mixed = jnp.transpose(mixed, (2, 0, 1, 3)).reshape(rows, q_width)
    mixed = jnp.where(q_live[:, None], mixed, 0.0).astype(jnp.bfloat16)
    return (mixed, kv_cache)


def solution(mesh):
    in_specs = (
        P("blk", "tp"),
        P("tp"),
        P(None, "tp"),
        P(None, "tp"),
        P(None, "tp"),
        P("tp"),
        P("tp"),
        P("tp"),
        P(),
        P(),
    )
    out_specs = (P("blk", "tp"), P("blk", None, None, "tp"))
    return jax.shard_map(
        on_device, mesh=mesh, in_specs=in_specs, out_specs=out_specs, check_vma=False
    )
```

profile of v0, /device:TPU:9, one launch (start us, length us, event | category | flops | bytes accessed | tf_op | source)
XLA Modules:
  0.0 118.3 jit_solution(8796197390272474836)
XLA Ops:
  7.2 0.8 convert_element_type.53
  8.1 2.1 %fusion.13 = (f32[256]{0:T(256)S(1)}, bf16[256,1280]{1,0:T(8,128)(2,1)}) fusion(bf16[256,1280]{1,0:T(8,128)(2,1)} %param.10, f32[1280]{0:T(1024)S(1)} %convert_element_type.53), kind=kLoop, calls=%fused_computation.15 | loop fusion | flops 1638144 | bytes 1316864 | tf_op jit(solution)/shard_map/reduce_sum | solution.py:74
  10.3 0.7 convert_element_type.55
  10.9 0.7 convert_element_type.58
  11.6 0.8 reduce-window.8
  12.4 7.9 %psum.7 = f32[256]{0:T(256)S(1)} all-reduce(f32[256]{0:T(256)S(1)} %get-tuple-element.20), channel_id=1, replica_groups=mesh['blk'=8,'tp'=4] {'tp'}, use_global_device_ids=true, to_apply=%region_4.5 | all-reduce | flops 256 | bytes 2048 | tf_op jit(solution)/shard_map/psum | solution.py:74
  20.3 0.7 fusion.24
  21.4 29.9 %all-gather.3.cloned.1.call-done = bf16[256,5120]{1,0:T(8,128)(2,1)} async-done(((bf16[256,1280]{1,0:T(8,128)(2,1)}), bf16[256,5120]{1,0:T(8,128)(2,1)}) %all-gather.3.cloned.1.call-update) | async-done | bytes 2621456 | tf_op jit(solution)/shard_map/all_gather | solution.py:68
  51.3 3.1 %fusion.18 = f32[256,256]{0,1:T(8,128)S(1)} fusion(bf16[256,5120]{1,0:T(8,128)(2,1)} %all-gather.3.cloned.1.call-done, bf16[5120,256]{1,0:T(8,128)(2,1)S(1)} %copy-done, f32[256]{0:T(256)S(1)} %convert_element_type.55, f32[256]{0:T(256)S(1)} %add_rsqrt_fusion), kind=kOutput, calls=%fused_computation.22 | convolution fusion | flops 671219712 | bytes 5507072 | tf_op jit(solution)/shard_map/dot_general | solution.py:72
  54.6 1.2 fusion.21
  55.8 0.7 pad_maximum_fusion.2
  56.5 0.6 fusion.25
  58.9 1.2 copy.27
  60.1 10.4 %fusion.7 = f32[256,1280]{1,0:T(8,128)} fusion(bf16[256,5120]{1,0:T(8,128)(2,1)} %all-gather.3.cloned.1.call-done, bf16[5120,1280]{1,0:T(8,128)(2,1)} %param.12, f32[1280]{0:T(1024)S(1)} %convert_element_type.60, f32[256]{0:T(256)S(1)} %add_rsqrt_fusion), kind=kOutput, calls=%fused_computation.10 | convolution fusion | flops 3356098560 | bytes 17045504 | tf_op jit(solution)/shard_map/dot_general | solution.py:72
  70.4 2.8 %copy.28 = f32[256,1280]{0,1:T(8,128)} copy(f32[256,1280]{1,0:T(8,128)} %fusion.7) | data formatting | bytes 2621440 | tf_op jit(solution)/shard_map/add | solution.py:79
  73.2 1.5 %subtract_convert_fusion = (bf16[256,10,64]{0,2,1:T(8,128)(2,1)S(1)}, bf16[256,10,64]{0,2,1:T(8,128)(2,1)S(1)}) fusion(f32[256,10,128]{0,2,1:T(8,128)} %bitcast.56, f32[256,64]{0,1:T(8,128)S(1)} %get-tuple-element.25, f32[256,64]{0,1:T(8,128)S(1)} %get-tuple-element.24), kind=kLoop, calls=%fused_computation.28 | loop fusion | flops 1310720 | bytes 2097152 | tf_op jit(solution)/shard_map/convert
  74.7 15.0 %all-gather.5.cloned.1.call-done = bf16[2048,512]{0,1:T(8,128)(2,1)} async-done(((bf16[256,512]{0,1:T(8,128)(2,1)}), bf16[2048,512]{0,1:T(8,128)(2,1)}) %all-gather.5.cloned.1.call-update) | async-done | bytes 2097168 | tf_op jit(solution)/shard_map/all_gather | solution.py:97
  89.7 1.0 dynamic-slice_bitcast_fusion.3
  90.8 0.9 copy.33
  91.6 3.0 %constant_dynamic-slice_fusion = (bf16[1280,256]{0,1:T(8,128)(2,1)}, bf16[1280,256]{0,1:T(8,128)(2,1)}) fusion(bf16[2048,512]{0,1:T(8,128)(2,1)} %all-gather.5.cloned.1.call-done, s32[]{:T(128)S(6)} %min.4, s32[]{:T(128)S(6)} %add.93), kind=kLoop, calls=%fused_computation.56 | loop fusion | bytes 2621448 | tf_op jit(solution)/shard_map/slice | solution.py:114
  94.7 9.5 %fusion.29 = (f32[2,5,256]{2,1,0:T(8,128)S(1)}, bf16[2,5,256,1280]{2,3,1,0:T(8,128)(2,1)}) fusion(pred[256,1280]{0,1:T(8,128)(4,1)} %copy.27, bf16[1280,2,128,1]{0,2,3,1:T(8,128)(2,1)} %bitcast.61, bf16[256,2,5,128]{0,3,2,1:T(8,128)(2,1)S(1)} %bitcast.58), kind=kOutput, calls=%fused_computation.63 | convolution fusion | flops 858522880 | bytes 8202240 | tf_op jit(solution)/shard_map/sub | solution.py:121
  104.1 4.9 %fusion.15 = bf16[256,2,5,128]{0,3,2,1:T(8,128)(2,1)} fusion(bf16[1280,2,128,1]{0,2,3,1:T(8,128)(2,1)} %bitcast.60, bf16[2,5,256,1280]{2,3,1,0:T(8,128)(2,1)} %get-tuple-element.27, f32[256,2,5]{0,2,1:T(8,128)S(1)} %select_bitcast_fusion), kind=kOutput, calls=%fused_computation.19 | convolution fusion | flops 839516160 | bytes 7874560 | tf_op jit(solution)/shard_map/cgqt,tch->cgqh/dot_general | solution.py:123
  109.1 1.3 %copy.32 = bf16[256,1280]{1,0:T(8,128)(2,1)S(1)} copy(bf16[256,1280]{0,1:T(8,128)(2,1)} %bitcast.59) | data formatting | bytes 1310720 | tf_op jit(solution)/shard_map/reshape | solution.py:138
  110.4 1.0 select_convert_fusion
  (31 shorter events, 1.3 us)
Async XLA Ops:
  7.2 44.1 %copy-start = (bf16[5120,256]{1,0:T(8,128)(2,1)S(1)}, bf16[5120,256]{1,0:T(8,128)(2,1)}, u32[]{:S(2)}) copy-start(bf16[5120,256]{1,0:T(8,128)(2,1)} %param.13) | copy-start | bytes 7864324
  7.2 44.1 %all-gather.3.cloned.1.call-start = ((), (), s32[]{:S(2)}) async-start(), calls=%async_computation | async-start | bytes 3276800 | tf_op jit(solution)/shard_map/all_gather | solution.py:68
  10.2 79.5 %all-gather.5.cloned.1.call-start = ((), (), s32[]{:S(2)}) async-start(), calls=%async_computation.1 | async-start | bytes 2359296 | tf_op jit(solution)/shard_map/all_gather | solution.py:97
  51.3 3.2 %copy-start.1 = (bf16[256,5120]{1,0:T(8,128)(2,1)S(1)}, bf16[256,5120]{1,0:T(8,128)(2,1)}, u32[]{:S(2)}) copy-start(bf16[256,5120]{1,0:T(8,128)(2,1)} %all-gather.3.cloned.1.call-done) | copy-start | bytes 7864324
  51.3 3.3 %copy-start.2 = (bf16[5120,256]{1,0:T(8,128)(2,1)S(1)}, bf16[5120,256]{1,0:T(8,128)(2,1)}, u32[]{:S(2)}) copy-start(bf16[5120,256]{1,0:T(8,128)(2,1)} %param.14) | copy-start | bytes 7864324
  54.6 1.9 %copy-start.4 = (s32[16]{0:T(128)S(1)}, s32[16]{0:T(128)}, u32[]{:S(2)}) copy-start(s32[16]{0:T(128)} %param.19) | copy-start | bytes 196
  54.6 3.8 %copy-start.3 = (bf16[1280]{0:T(1024)(128)(2,1)S(1)}, bf16[1280]{0:T(1024)(128)(2,1)}, u32[]{:S(2)}) copy-start(bf16[1280]{0:T(1024)(128)(2,1)} %param.15) | copy-start | bytes 7684
Sparse Core Ops, SparseCore 0:
  10.4 40.8 all-gather.2
  56.6 33.0 all-gather.4
where the time goes:
time: 119 us; the launch traced here: 118 us
  waiting for transfers between devices  45 us (38%)
  matrix products  29 us (24%)
  between operations  15.4 us (13%)
  other arithmetic  10.7 us (9%)
  local copies, waits for them, and re-layouts  10.3 us (9%)
  blocking collectives  7.86 us (7%)
    all_gather x1, waiting for transfers between devices, on_device(): piece = lax.all_gather(scaled, 'tp', axis=1, tiled=True)  29.9 us
    all_gather x1, waiting for transfers between devices, on_device(): lax.all_gather(jnp.concatenate([key, value], axis=1), 'blk', axis=0, tile...  15 us
    dot_general x3, matrix products, on_device(): totals.append(jnp.dot(piece, weight, preferred_element_type=jnp.float32))  14.6 us
    sub x1, matrix products, on_device(): expo = jnp.where(allowed, jnp.exp(scores - top), 0.0)  9.49 us
    psum x1, blocking collectives, on_device(): squares = lax.psum(jnp.sum(wide * wide, axis=1), 'tp')  7.86 us
    dot_general x1, matrix products, on_device(): jnp.einsum('cgqt,tch->cgqh', expo.astype(jnp.bfloat16), window[:, kv_widt...  4.95 us
    slice x1, local copies, waits for them, and re-layouts, on_device(): window[:, :kv_width].reshape(span, kv_dev, HEAD)  3.02 us
    add x1, local copies, waits for them, and re-layouts, on_device(): query = rstd[:, None] * proj_query + query_bias.astype(jnp.float32)  2.78 us
  transfers between devices with their start and end apart: 2, of which 2 were waited for; matrix products, arithmetic and copies ran while one was open for 17% of the time, Pallas kernels for 0%

commit v1 on v0

--- a/solution.py
+++ b/solution.py
@@ -1,6 +1,8 @@
 import jax
 import jax.numpy as jnp
 from jax import lax
+from jax.experimental import pallas as pl
+from jax.experimental.pallas import tpu as pltpu
 from jax.sharding import PartitionSpec as P
 
 D = 5120
@@ -35,6 +37,64 @@
         [first * cosine - second * sine, second * cosine + first * sine], axis=-1
     )
 
+
+def window_attention(first, query, both, q_seg, q_pos, k_seg, k_pos, docs, interpret=False):
+    rows, q_width = query.shape
+    count, both_width = both.shape
+    span = k_seg.shape[0]
+    kv_dev = both_width // (2 * HEAD)
+    group = q_width // (kv_dev * HEAD)
+    scale = 1.0 / float(HEAD) ** 0.5
+
+    def kernel(first_ref, q_ref, k_ref, v_ref, qs_ref, qp_ref, ks_ref, kp_ref, o_ref):
+        start = pl.multiple_of(first_ref[0], PAGE)
+        keys = k_ref[pl.ds(start, span), :]
+        values = v_ref[pl.ds(start, span), :]
+        qs = qs_ref[...]
+        live = qs < docs - 1
+        allowed = (ks_ref[...] == qs) & (kp_ref[...] <= qp_ref[...]) & live
+        for g in range(group):
+            q = q_ref[:, g * HEAD:(g + 1) * HEAD]
+            scores = lax.dot_general(
+                q, keys, (((1,), (1,)), ((), ())), preferred_element_type=jnp.float32
+            ) * scale
+            scores = jnp.where(allowed, scores, neg_large)
+            top = jnp.max(scores, axis=1, keepdims=True)
+            expo = jnp.where(allowed, jnp.exp(scores - top), 0.0)
+            denom = jnp.sum(expo, axis=1, keepdims=True)
+            acc = jnp.dot(expo.astype(jnp.bfloat16), values, preferred_element_type=jnp.float32)
+            out = jnp.where(live, acc / jnp.where(live, denom, 1.0), 0.0)
+            o_ref[:, g * HEAD:(g + 1) * HEAD] = out.astype(o_ref.dtype)
+
+    spec = pltpu.PrefetchScalarGridSpec(
+        num_scalar_prefetch=1,
+        grid=(kv_dev,),
+        in_specs=[
+            pl.BlockSpec((rows, group * HEAD), lambda c, f: (0, c)),
+            pl.BlockSpec((count, HEAD), lambda c, f: (0, c)),
+            pl.BlockSpec((count, HEAD), lambda c, f: (0, kv_dev + c)),
+            pl.BlockSpec((rows, 1), lambda c, f: (0, 0)),
+            pl.BlockSpec((rows, 1), lambda c, f: (0, 0)),
+            pl.BlockSpec((1, span), lambda c, f: (0, 0)),
+            pl.BlockSpec((1, span), lambda c, f: (0, 0)),
+        ],
+        out_specs=pl.BlockSpec((rows, group * HEAD), lambda c, f: (0, c)),
+    )
+    return pl.pallas_call(
+        kernel,
+        grid_spec=spec,
+        out_shape=jax.ShapeDtypeStruct((rows, q_width), jnp.bfloat16),
+        interpret=interpret,
+    )(
+        first.reshape(1).astype(jnp.int32),
+        query,
+        both,
+        both,
+        q_seg.reshape(rows, 1),
+        q_pos.reshape(rows, 1),
+        k_seg.reshape(1, span),
+        k_pos.reshape(1, span),
+    )
 
 def on_device(
     tokens,
@@ -99,34 +159,9 @@
     longest = count // 2
     span = min(count, longest + rows)
     first = jnp.clip(me * rows - longest, 0, count - span)
-    window = lax.dynamic_slice_in_dim(both, first, span, 0)
     k_pos = first + jnp.arange(span, dtype=jnp.int32)
     k_seg, k_off = token_meta(k_pos, lengths)
-    allowed = (
-        (k_seg[None, :] == q_seg[:, None])
-        & (k_pos[None, :] <= own_pos[:, None])
-        & q_live[:, None]
-    )
-    scores = (
-        jnp.einsum(
-            "qcgh,tch->cgqt",
-            q_grouped,
-            window[:, :kv_width].reshape(span, kv_dev, HEAD),
-            preferred_element_type=jnp.float32,
-        )
-        * scale
-    )
-    scores = jnp.where(allowed, scores, neg_large)
-    top = jnp.max(scores, axis=3, keepdims=True)
-    expo = jnp.where(allowed, jnp.exp(scores - top), 0.0)
-    denom = jnp.sum(expo, axis=3)
-    acc = jnp.einsum(
-        "cgqt,tch->cgqh",
-        expo.astype(jnp.bfloat16),
-        window[:, kv_width:].reshape(span, kv_dev, HEAD),
-        preferred_element_type=jnp.float32,
-    )
-    attention = (None, denom, acc)
+    mixed = window_attention(first, query, both, q_seg, own_pos, k_seg, k_pos, docs)
     numbers = jnp.arange(page_table.shape[0], dtype=jnp.int32)
     cache = []
     for j in range(slots):
@@ -134,9 +169,6 @@
         held = lax.dynamic_slice_in_dim(both, page * PAGE, PAGE, 0)
         cache.append(jnp.stack([held[:, :kv_width], held[:, kv_width:]], axis=0))
     kv_cache = jnp.stack(cache, axis=0)
-    mixed = attention[2] / jnp.where(q_live, attention[1], 1.0)[..., None]
-    mixed = jnp.transpose(mixed, (2, 0, 1, 3)).reshape(rows, q_width)
-    mixed = jnp.where(q_live[:, None], mixed, 0.0).astype(jnp.bfloat16)
     return (mixed, kv_cache)
 
 

time: 119 us -> 109 us (0.916)
  matrix products: 29 us -> 16.5 us
  Pallas kernels: 0 us -> 10.4 us
  waiting for transfers between devices: 45 us -> 38.2 us
  local copies, waits for them, and re-layouts: 10.3 us -> 6.59 us
  other arithmetic: 10.7 us -> 12.7 us
    pallas_call x0 -> x1, Pallas kernels: none -> 10.4 us  [window_attention(): pl.pallas_call(kernel, grid_spec=spec, out_shape=jax.ShapeDtypeStruct((ro...]
    sub x1 -> x0, matrix products: 9.49 us -> none  [on_device(): expo = jnp.where(allowed, jnp.exp(scores - top), 0.0)]
    all_gather x1, waiting for transfers between devices: 15 us -> 9.01 us  [on_device(): lax.all_gather(jnp.concatenate([key, value], axis=1), 'blk', axis=0, tile...]
    dot_general x1 -> x0, matrix products: 4.95 us -> none  [on_device(): jnp.einsum('cgqt,tch->cgqh', expo.astype(jnp.bfloat16), window[:, kv_widt...]
    slice x1 -> x0, local copies, waits for them, and re-layouts: 3.02 us -> none  [on_device(): window[:, :kv_width].reshape(span, kv_dev, HEAD)]
    dot_general x3, matrix products: 14.6 us -> 16.5 us  [on_device(): totals.append(jnp.dot(piece, weight, preferred_element_type=jnp.float32))]
  transfers between devices with their start and end apart: 2 -> 2, of which waited for: 2 -> 2; matrix products, arithmetic and copies ran while one was open for 17% -> 22% of each run, Pallas kernels for 0% -> 0%
where the time goes in v1:
time: 109 us; the launch traced here: 108 us
  waiting for transfers between devices  38.2 us (35%)
  matrix products  16.5 us (15%)
  between operations  15.4 us (14%)
  other arithmetic  12.7 us (12%)
  Pallas kernels  10.4 us (10%)
  blocking collectives  7.89 us (7%)
  local copies, waits for them, and re-layouts  6.59 us (6%)
    all_gather x1, waiting for transfers between devices, on_device(): piece = lax.all_gather(scaled, 'tp', axis=1, tiled=True)  29.1 us
    dot_general x3, matrix products, on_device(): totals.append(jnp.dot(piece, weight, preferred_element_type=jnp.float32))  16.5 us
    pallas_call x1, Pallas kernels, window_attention(): pl.pallas_call(kernel, grid_spec=spec, out_shape=jax.ShapeDtypeStruct((ro...  10.4 us
    all_gather x1, waiting for transfers between devices, on_device(): lax.all_gather(jnp.concatenate([key, value], axis=1), 'blk', axis=0, tile...  9.01 us
    psum x1, blocking collectives, on_device(): squares = lax.psum(jnp.sum(wide * wide, axis=1), 'tp')  7.89 us
    add x1, local copies, waits for them, and re-layouts, on_device(): query = rstd[:, None] * proj_query + query_bias.astype(jnp.float32)  2.83 us
    another operation x2, other arithmetic  2.34 us
  transfers between devices with their start and end apart: 2, of which 2 were waited for; matrix products, arithmetic and copies ran while one was open for 22% of the time, Pallas kernels for 0%

profile of v1, /device:TPU:9, one launch (start us, length us, event | category | flops | bytes accessed | tf_op | source)
XLA Modules:
  0.0 107.8 jit_solution(12687904830957787269)
XLA Ops:
  7.2 0.8 convert_element_type.43
  8.1 2.1 %fusion.1 = (f32[256]{0:T(256)S(1)}, bf16[256,1280]{1,0:T(8,128)(2,1)}) fusion(bf16[256,1280]{1,0:T(8,128)(2,1)} %param.10, f32[1280]{0:T(1024)S(1)} %convert_element_type.43), kind=kLoop, calls=%fused_computation.4 | loop fusion | flops 1638144 | bytes 1316864 | tf_op jit(solution)/shard_map/reduce_sum | solution.py:134
  10.3 0.7 convert_element_type.49
  10.9 1.2 %convert_element_type.51 = f32[256]{0:T(256)} convert(bf16[256]{0:T(256)(128)(2,1)} %param.17) | non-fusion elementwise | flops 256 | bytes 1536 | tf_op jit(solution)/shard_map/convert_element_type | solution.py:141
  12.1 0.8 reduce-window.8
  13.0 0.7 fusion.9
  14.2 7.9 %psum.7 = f32[256]{0:T(256)S(1)} all-reduce(f32[256]{0:T(256)S(1)} %get-tuple-element.12), channel_id=1, replica_groups=mesh['blk'=8,'tp'=4] {'tp'}, use_global_device_ids=true, to_apply=%region_1.0 | all-reduce | flops 256 | bytes 2048 | tf_op jit(solution)/shard_map/psum | solution.py:134
  22.2 29.1 %all-gather.3.cloned.1.call-done = bf16[256,5120]{1,0:T(8,128)(2,1)} async-done(((bf16[256,1280]{1,0:T(8,128)(2,1)}), bf16[256,5120]{1,0:T(8,128)(2,1)}) %all-gather.3.cloned.1.call-update) | async-done | bytes 2621456 | tf_op jit(solution)/shard_map/all_gather | solution.py:128
  51.3 2.6 %fusion.3 = f32[256,256]{1,0:T(8,128)S(1)} fusion(bf16[256,5120]{1,0:T(8,128)(2,1)} %all-gather.3.cloned.1.call-done, bf16[5120,256]{1,0:T(8,128)(2,1)S(1)} %copy-done, f32[256]{0:T(256)S(1)} %convert_element_type.49, f32[256]{0:T(256)S(1)} %add_rsqrt_fusion), kind=kOutput, calls=%fused_computation.8 | convolution fusion | flops 671219712 | bytes 5507072 | tf_op jit(solution)/shard_map/dot_general | solution.py:132
  55.0 3.4 %fusion.6 = bf16[256,256]{1,0:T(8,128)(2,1)S(1)} fusion(bf16[256,5120]{1,0:T(8,128)(2,1)} %all-gather.3.cloned.1.call-done, bf16[5120,256]{1,0:T(8,128)(2,1)} %param.14, f32[256]{0:T(256)} %convert_element_type.51, f32[256]{0:T(256)S(1)} %add_rsqrt_fusion, pred[256]{0:T(512)(128)(4,1)S(1)} %broadcast_compare_fusion), kind=kOutput, calls=%fused_computation.11 | convolution fusion | flops 671350784 | bytes 5376256 | tf_op jit(solution)/shard_map/dot_general | solution.py:132
  58.4 0.7 pad_maximum_fusion.2
  59.2 0.6 fusion.10
  61.1 0.6 reshape.141.ks_ref
  61.7 0.8 copy.27.qs_ref
  62.5 0.7 iota_add_fusion.qp_ref
  63.2 0.6 iota_add_fusion.2.kp_ref
  63.8 10.5 %fusion = f32[256,1280]{1,0:T(8,128)} fusion(bf16[256,5120]{1,0:T(8,128)(2,1)} %all-gather.3.cloned.1.call-done, bf16[5120,1280]{1,0:T(8,128)(2,1)} %param.12, f32[1280]{0:T(1024)S(1)} %convert_element_type.45, f32[256]{0:T(256)S(1)} %add_rsqrt_fusion), kind=kOutput, calls=%fused_computation.1 | convolution fusion | flops 3356098560 | bytes 17045504 | tf_op jit(solution)/shard_map/dot_general | solution.py:132
  74.3 2.8 %copy.21 = f32[256,1280]{0,1:T(8,128)} copy(f32[256,1280]{1,0:T(8,128)} %fusion) | data formatting | bytes 2621440 | tf_op jit(solution)/shard_map/add | solution.py:139
  77.1 1.5 %subtract_convert_fusion = (bf16[256,10,64]{0,2,1:T(8,128)(2,1)S(1)}, bf16[256,10,64]{0,2,1:T(8,128)(2,1)S(1)}) fusion(f32[256,10,128]{0,2,1:T(8,128)} %bitcast.29, f32[256,64]{0,1:T(8,128)S(1)} %get-tuple-element.17, f32[256,64]{0,1:T(8,128)S(1)} %get-tuple-element.16), kind=kLoop, calls=%fused_computation.14 | loop fusion | flops 1310720 | bytes 2097152 | tf_op jit(solution)/shard_map/convert
  78.7 1.1 copy.26.q_ref
  79.8 9.0 %all-gather.5.cloned.1.call-done.k_ref.v_ref = bf16[2048,512]{1,0:T(8,128)(2,1)} async-done(((bf16[256,512]{1,0:T(8,128)(2,1)}), bf16[2048,512]{1,0:T(8,128)(2,1)}) %all-gather.5.cloned.1.call-update) | async-done | bytes 2097168 | tf_op jit(solution)/shard_map/all_gather | solution.py:157
  88.8 1.0 dynamic-slice_bitcast_fusion.3
  89.8 0.7 pad_maximum_fusion.3
  90.5 10.4 %shard_map.113 = bf16[256,1280]{1,0:T(8,128)(2,1)} custom-call(s32[1]{0:T(128)} %bitcast.first_ref, bf16[256,1280]{1,0:T(8,128)(2,1)} %copy.26.q_ref, bf16[2048,512]{1,0:T(8,128)(2,1)} %all-gather.5.cloned.1.call-done.k_ref.v_ref, bf16[2048,512]{1,0:T(8,128)(2,1)} %all-gather.5.cloned.1.call-done.k_ref.v_ref, s32[256,1]{1,0:T(8,128)} %copy.27.qs_ref, ...), custom_call_target="tpu_custom_call" | custom-call | tf_op jit(solution)/shard_map/pallas_call | solution.py:83
  (27 shorter events, 1.9 us)
Async XLA Ops:
  7.2 44.1 %copy-start = (bf16[5120,256]{1,0:T(8,128)(2,1)S(1)}, bf16[5120,256]{1,0:T(8,128)(2,1)}, u32[]{:S(2)}) copy-start(bf16[5120,256]{1,0:T(8,128)(2,1)} %param.13) | copy-start | bytes 7864324
  7.2 44.1 %all-gather.3.cloned.1.call-start = ((), (), s32[]{:S(2)}) async-start(), calls=%async_computation | async-start | bytes 3276800 | tf_op jit(solution)/shard_map/all_gather | solution.py:128
  10.2 78.6 %all-gather.5.cloned.1.call-start = ((), (), s32[]{:S(2)}) async-start(), calls=%async_computation.1 | async-start | bytes 2359296 | tf_op jit(solution)/shard_map/all_gather | solution.py:157
  55.0 4.2 %copy-start.2 = (s32[16]{0:T(128)S(1)}, s32[16]{0:T(128)}, u32[]{:S(2)}) copy-start(s32[16]{0:T(128)} %param.19) | copy-start | bytes 196
  55.0 6.0 %copy-start.1 = (bf16[1280]{0:T(1024)(128)(2,1)S(1)}, bf16[1280]{0:T(1024)(128)(2,1)}, u32[]{:S(2)}) copy-start(bf16[1280]{0:T(1024)(128)(2,1)} %param.15) | copy-start | bytes 7684
Sparse Core Ops, SparseCore 0:
  10.4 40.8 all-gather.2
  59.3 29.4 all-gather.4

commit v2 on v1

--- a/solution.py
+++ b/solution.py
@@ -125,13 +125,37 @@
         jnp.zeros((rows, kv_width), jnp.float32),
         jnp.zeros((rows, kv_width), jnp.float32),
     )
-    piece = lax.all_gather(scaled, "tp", axis=1, tiled=True)
-    count = piece.shape[1]
-    totals = []
-    for total, weight in zip(empty, (w_query, w_key, w_value)):
-        totals.append(jnp.dot(piece, weight, preferred_element_type=jnp.float32))
-    proj_query, proj_key, proj_value = tuple(totals)
-    squares = lax.psum(jnp.sum(wide * wide, axis=1), "tp")
+    part_sq = jnp.sum(wide * wide, axis=1)
+    width = tokens.shape[1]
+    parts = lax.axis_size("tp")
+    mine = lax.axis_index("tp")
+    weights = (w_query, w_key, w_value)
+    half = rows // 2
+    piece = lax.all_gather(scaled[:half], "tp", axis=1, tiled=True)
+    upper = [jnp.dot(piece, weight, preferred_element_type=jnp.float32) for weight in weights]
+    lower_rows = scaled[half:]
+
+    def project(chunk, source):
+        return [
+            jnp.dot(
+                chunk,
+                lax.dynamic_slice_in_dim(weight, source * width, width, 0),
+                preferred_element_type=jnp.float32,
+            )
+            for weight in weights
+        ]
+
+    lower = project(lower_rows, mine)
+    squares = part_sq
+    for shift in range(1, parts):
+        perm = [(j, (j + shift) % parts) for j in range(parts)]
+        got = lax.ppermute(lower_rows, "tp", perm)
+        squares = squares + lax.ppermute(part_sq, "tp", perm)
+        more = project(got, (mine + parts - shift) % parts)
+        lower = [a + b for a, b in zip(lower, more)]
+    proj_query, proj_key, proj_value = tuple(
+        jnp.concatenate([a, b], axis=0) for a, b in zip(upper, lower)
+    )
     rstd = lax.rsqrt(squares / D + norm_eps)
     own_pos = me * rows + jnp.arange(rows, dtype=jnp.int32)
     own_seg, own_off = token_meta(own_pos, lengths)

time: 109 us -> 110 us (level)
  waiting for transfers between devices: 38.2 us -> 18.7 us
  matrix products: 16.5 us -> 33.8 us
  blocking collectives: 7.89 us -> 0 us
  starting transfers between devices: 0.08 us -> 5.38 us
  local copies, waits for them, and re-layouts: 6.59 us -> 9.97 us
  other arithmetic: 12.7 us -> 14.6 us
    all_gather x1, waiting for transfers between devices: 29.1 us -> 8.39 us  [on_device(): piece = lax.all_gather(scaled[:half], 'tp', axis=1, tiled=True)]
    dot_general x3 -> x15, matrix products: 16.5 us -> 33.8 us  [the longest x12 20 us: project(): jnp.dot(chunk, lax.dynamic_slice_in_dim(weight, source * width, width, 0)...]
    ppermute x0 -> x6, waiting for transfers between devices: none -> 8.82 us  [the longest x3 8.81 us: on_device(): got = lax.ppermute(lower_rows, 'tp', perm)]
    psum x1 -> x0, blocking collectives: 7.89 us -> none  [on_device(): squares = lax.psum(jnp.sum(wide * wide, axis=1), 'tp')]
    all_gather x1, waiting for transfers between devices: 9.01 us -> 1.47 us  [on_device(): lax.all_gather(jnp.concatenate([key, value], axis=1), 'blk', axis=0, tile...]
    ppermute x0 -> x6, starting transfers between devices: none -> 5.3 us  [the longest x3 2.71 us: on_device(): squares = squares + lax.ppermute(part_sq, 'tp', perm)]
    add x0 -> x4, other arithmetic: none -> 2.78 us  [the longest x2 2.54 us: on_device(): key = rstd[:, None] * proj_key + key_bias.astype(jnp.float32)]
    concatenate x0 -> x2, local copies, waits for them, and re-layouts: none -> 2.33 us  [on_device(): jnp.concatenate([a, b], axis=0)]
  transfers between devices with their start and end apart: 2 -> 8, of which waited for: 2 -> 3; matrix products, arithmetic and copies ran while one was open for 22% -> 39% of each run, Pallas kernels for 0% -> 0%
where the time goes in v2:
time: 110 us; the launch traced here: 109 us
  matrix products  33.8 us (31%)
  waiting for transfers between devices  18.7 us (17%)
  between operations  15.7 us (14%)
  other arithmetic  14.6 us (13%)
  Pallas kernels  10.4 us (9%)
  local copies, waits for them, and re-layouts  9.97 us (9%)
  starting transfers between devices  5.38 us (5%)
    dot_general x12, matrix products, project(): jnp.dot(chunk, lax.dynamic_slice_in_dim(weight, source * width, width, 0)...  20 us
    dot_general x3, matrix products, on_device(): jnp.dot(piece, weight, preferred_element_type=jnp.float32)  13.8 us
    pallas_call x1, Pallas kernels, window_attention(): pl.pallas_call(kernel, grid_spec=spec, out_shape=jax.ShapeDtypeStruct((ro...  10.4 us
    ppermute x3, waiting for transfers between devices, on_device(): got = lax.ppermute(lower_rows, 'tp', perm)  8.81 us
    all_gather x1, waiting for transfers between devices, on_device(): piece = lax.all_gather(scaled[:half], 'tp', axis=1, tiled=True)  8.39 us
    ppermute x3, starting transfers between devices, on_device(): squares = squares + lax.ppermute(part_sq, 'tp', perm)  2.71 us
    ppermute x3, starting transfers between devices, on_device(): got = lax.ppermute(lower_rows, 'tp', perm)  2.59 us
    add x2, other arithmetic, on_device(): key = rstd[:, None] * proj_key + key_bias.astype(jnp.float32)  2.54 us
  transfers between devices with their start and end apart: 8, of which 3 were waited for; matrix products, arithmetic and copies ran while one was open for 39% of the time, Pallas kernels for 0%

profile of v2, /device:TPU:9, one launch (start us, length us, event | category | flops | bytes accessed | tf_op | source)
XLA Modules:
  0.0 108.6 jit_solution(13826136004424093500)
XLA Ops:
  8.1 1.4 %fusion.17 = (f32[256]{0:T(256)S(1)}, bf16[256,1280]{1,0:T(8,128)(2,1)S(1)}) fusion(bf16[256,1280]{1,0:T(8,128)(2,1)} %param.10, f32[1280]{0:T(1024)S(1)} %convert_element_type.39), kind=kLoop, calls=%fused_computation.13 | loop fusion | flops 1638144 | bytes 1316864 | tf_op jit(solution)/shard_map/reduce_sum | solution.py:128
  10.3 2.2 %collective-permute-start.5 = (bf16[128,1280]{1,0:T(8,128)(2,1)}, bf16[128,1280]{1,0:T(8,128)(2,1)}, u32[]{:S(2)}, u32[]{:S(2)}) collective-permute-start(bf16[128,1280]{1,0:T(8,128)(2,1)} %get-tuple-element.15), channel_id=1, source_target_pairs={{0,3},{1,0},{2,1},{3,2},{4,7},{5,4},{6,5},{7,6},{8,11},{9,8},{10,9... | collective-permute-start | bytes 983048 | tf_op jit(solution)/shard_map/ppermute | solution.py:152
  13.0 1.2 %collective-permute-start.1 = (f32[256]{0:T(256)S(1)}, f32[256]{0:T(256)}, u32[]{:S(2)}, u32[]{:S(2)}) collective-permute-start(f32[256]{0:T(256)S(1)} %get-tuple-element.12), channel_id=1, source_target_pairs={{0,2},{1,3},{2,0},{3,1},{4,6},{5,7},{6,4},{7,5},{8,10},{9,11},{10,... | collective-permute-start | bytes 3080 | tf_op jit(solution)/shard_map/ppermute | solution.py:153
  15.8 2.0 %fusion.26 = f32[128,256]{1,0:T(8,128)} fusion(bf16[5120,256]{1,0:T(8,128)(2,1)} %param.14, s32[]{:T(128)S(6)} %select_n.57, bf16[256,1280]{1,0:T(8,128)(2,1)S(1)} %get-tuple-element.13), kind=kOutput, calls=%fused_computation.28 | convolution fusion | flops 83886080 | bytes 1114116 | tf_op jit(solution)/shard_map/dot_general | solution.py:140
  18.4 1.2 %bitcast_convert_fusion.1 = f32[2,128]{1,0:T(2,128)} fusion(bf16[256]{0:T(256)(128)(2,1)} %param.16), kind=kLoop, calls=%fused_computation.87 | loop fusion | flops 256 | bytes 1536 | tf_op jit(solution)/shard_map/add | solution.py:164
  23.3 1.2 %fusion.28 = f32[128,256]{1,0:T(8,128)S(1)} fusion(bf16[128,1280]{1,0:T(8,128)(2,1)} %collective-permute-done.5, bf16[5120,256]{1,0:T(8,128)(2,1)S(1)} %copy-done, s32[]{:T(128)S(6)} %select_n.63), kind=kOutput, calls=%fused_computation.30 | convolution fusion | flops 83886080 | bytes 1114116 | tf_op jit(solution)/shard_map/dot_general | solution.py:140
  24.5 8.8 %collective-permute-done.3 = bf16[128,1280]{1,0:T(8,128)(2,1)S(1)} collective-permute-done((bf16[128,1280]{1,0:T(8,128)(2,1)}, bf16[128,1280]{1,0:T(8,128)(2,1)S(1)}, u32[]{:S(2)}, u32[]{:S(2)}) %collective-permute-start.3) | collective-permute-done | bytes 327712 | tf_op jit(solution)/shard_map/ppermute | solution.py:152
  36.3 1.4 %fusion.22 = f32[128,256]{1,0:T(8,128)S(1)} fusion(bf16[128,1280]{1,0:T(8,128)(2,1)} %collective-permute-done.5, bf16[5120,256]{1,0:T(8,128)(2,1)} %param.14, s32[]{:T(128)S(6)} %select_n.63), kind=kOutput, calls=%fused_computation.24 | convolution fusion | flops 83886080 | bytes 1114116 | tf_op jit(solution)/shard_map/dot_general | solution.py:140
  37.7 1.5 %convolution_add_fusion.1 = f32[128,256]{1,0:T(8,128)S(1)} fusion(f32[128,256]{1,0:T(8,128)} %fusion.26, bf16[128,1280]{1,0:T(8,128)(2,1)} %copy-done.1, bf16[5120,256]{1,0:T(8,128)(2,1)} %param.14, s32[]{:T(128)S(6)} %select_n.59), kind=kOutput, calls=%fused_computation.18 | convolution fusion | flops 83918848 | bytes 1245188 | tf_op jit(solution)/shard_map/dot_general | solution.py:140
  39.2 1.5 %fusion.21 = f32[128,256]{1,0:T(8,128)S(1)} fusion(f32[128,256]{1,0:T(8,128)S(1)} %fusion.22, f32[128,256]{1,0:T(8,128)S(1)} %convolution_add_fusion.1, bf16[128,1280]{1,0:T(8,128)(2,1)} %collective-permute-done.4, bf16[5120,256]{1,0:T(8,128)(2,1)} %param.14, s32[]{:T(128)S(6)} %select_n.61), kind=kOutput, calls=%fused_computation.22 | convolution fusion | flops 83951616 | bytes 1376260 | tf_op jit(solution)/shard_map/dot_general | solution.py:140
  40.7 8.4 %all-gather.3.cloned.1.call-done = bf16[128,5120]{1,0:T(8,128)(2,1)} async-done(((bf16[128,1280]{1,0:T(8,128)(2,1)}), bf16[128,5120]{1,0:T(8,128)(2,1)}) %all-gather.3.cloned.1.call-update) | async-done | bytes 1310736 | tf_op jit(solution)/shard_map/all_gather | solution.py:134
  49.1 2.5 %fusion.60 = f32[128,256]{1,0:T(8,128)} fusion(bf16[128,5120]{1,0:T(8,128)(2,1)} %all-gather.3.cloned.1.call-done, bf16[5120,256]{1,0:T(8,128)(2,1)S(1)} %copy-done), kind=kOutput, calls=%fused_computation.95 | convolution fusion | flops 335544320 | bytes 4063232 | tf_op jit(solution)/shard_map/dot_general | solution.py:135
  51.6 1.6 %concatenate.35 = f32[128,2,128]{2,1,0:T(2,128)} reshape(f32[128,256]{1,0:T(8,128)} %fusion.60) | data formatting | bytes 262144 | tf_op jit(solution)/shard_map/concatenate | solution.py:157
  53.2 1.3 %fusion.35 = f32[256,2,128]{2,1,0:T(2,128)S(1)} fusion(f32[128,2,128]{2,1,0:T(2,128)} %concatenate.36, f32[128,2,128]{2,1,0:T(2,128)} %concatenate.35, f32[256]{0:T(256)S(1)} %add_rsqrt_fusion, f32[2,128]{1,0:T(2,128)S(1)} %copy-done.6), kind=kLoop, calls=%fused_computation.41 | loop fusion | flops 196608 | bytes 526336 | tf_op jit(solution)/shard_map/add | solution.py:164
  54.5 1.4 %multiply_subtract_fusion = (bf16[256,2,64]{2,1,0:T(2,128)(2,1)S(1)}, bf16[256,2,64]{2,1,0:T(2,128)(2,1)S(1)}) fusion(f32[256,2,128]{2,1,0:T(2,128)S(1)} %fusion.35, f32[256,64]{1,0:T(8,128)} %copy.21, f32[256,64]{1,0:T(8,128)} %copy.20), kind=kLoop, calls=%fused_computation.50 | loop fusion | flops 262144 | bytes 524288 | tf_op jit(solution)/shard_map/sub | solution.py:37
  56.4 2.7 %fusion.61 = f32[128,256]{1,0:T(8,128)S(1)} fusion(bf16[128,5120]{1,0:T(8,128)(2,1)} %all-gather.3.cloned.1.call-done, bf16[5120,256]{1,0:T(8,128)(2,1)} %param.14), kind=kOutput, calls=%fused_computation.96 | convolution fusion | flops 335544320 | bytes 4063232 | tf_op jit(solution)/shard_map/dot_general | solution.py:135
  60.0 1.4 %fusion.53 = (s32[]{:T(128)}, s32[]{:T(128)}) fusion(s32[16]{0:T(128)} %param.19, s32[]{:T(128)S(6)} %mul.196, s32[]{:T(128)S(6)} %add.218), kind=kLoop, calls=%fused_computation.85 | loop fusion | flops 94 | bytes 80 | tf_op jit(solution)/shard_map/reduce_sum | solution.py:192
  66.1 2.6 %fusion.6 = f32[128,1280]{1,0:T(8,128)S(1)} fusion(bf16[5120,1280]{1,0:T(8,128)(2,1)} %param.12, s32[]{:T(128)S(6)} %select_n.57, bf16[256,1280]{1,0:T(8,128)(2,1)S(1)} %get-tuple-element.13), kind=kOutput, calls=%fused_computation.6 | convolution fusion | flops 419430400 | bytes 4259844 | tf_op jit(solution)/shard_map/dot_general | solution.py:140
  68.8 2.7 %fusion = f32[128,1280]{1,0:T(8,128)S(1)} fusion(bf16[128,1280]{1,0:T(8,128)(2,1)} %collective-permute-done.5, bf16[5120,1280]{1,0:T(8,128)(2,1)} %param.12, s32[]{:T(128)S(6)} %select_n.63), kind=kOutput, calls=%fused_computation | convolution fusion | flops 419430400 | bytes 4259844 | tf_op jit(solution)/shard_map/dot_general | solution.py:140
  71.4 2.7 %fusion.2 = f32[128,1280]{1,0:T(8,128)S(1)} fusion(bf16[128,1280]{1,0:T(8,128)(2,1)} %collective-permute-done.4, bf16[5120,1280]{1,0:T(8,128)(2,1)} %param.12, s32[]{:T(128)S(6)} %select_n.61), kind=kOutput, calls=%fused_computation.2 | convolution fusion | flops 419430400 | bytes 4259844 | tf_op jit(solution)/shard_map/dot_general | solution.py:140
  74.2 2.6 %fusion.14 = f32[128,1280]{1,0:T(8,128)S(1)} fusion(f32[128,1280]{1,0:T(8,128)S(1)} %fusion, f32[128,1280]{1,0:T(8,128)S(1)} %fusion.2, f32[128,1280]{1,0:T(8,128)S(1)} %fusion.6, bf16[128,1280]{1,0:T(8,128)(2,1)S(1)} %copy-done.2, bf16[5120,1280]{1,0:T(8,128)(2,1)} %param.12, s32[]{:T(128)S(6)} %select_n.59), kind=kOutput, calls=%fused_computation.10 | convolution fusion | flops 419921920 | bytes 6225924 | tf_op jit(solution)/shard_map/dot_general | solution.py:140
  77.9 8.7 %fusion.59 = f32[128,1280]{0,1:T(8,128)S(1)} fusion(bf16[128,5120]{1,0:T(8,128)(2,1)} %all-gather.3.cloned.1.call-done, bf16[5120,1280]{1,0:T(8,128)(2,1)} %param.12), kind=kOutput, calls=%fused_computation.94 | convolution fusion | flops 1677721600 | bytes 15073280 | tf_op jit(solution)/shard_map/dot_general | solution.py:135
  88.2 1.5 %all-gather.5.cloned.1.call-done.k_ref.v_ref = bf16[2048,512]{1,0:T(8,128)(2,1)} async-done(((bf16[256,512]{1,0:T(8,128)(2,1)}), bf16[2048,512]{1,0:T(8,128)(2,1)}) %all-gather.5.cloned.1.call-update) | async-done | bytes 2097168 | tf_op jit(solution)/shard_map/all_gather | solution.py:181
  91.4 10.4 %shard_map.113 = bf16[256,1280]{1,0:T(8,128)(2,1)} custom-call(s32[1]{0:T(128)} %bitcast.first_ref, bf16[256,1280]{1,0:T(8,128)(2,1)} %copy.22.q_ref, bf16[2048,512]{1,0:T(8,128)(2,1)} %all-gather.5.cloned.1.call-done.k_ref.v_ref, bf16[2048,512]{1,0:T(8,128)(2,1)} %all-gather.5.cloned.1.call-done.k_ref.v_ref, s32[256,1]{1,0:T(8,128)} %copy.23.qs_ref, ...), custom_call_target="tpu_custom_call" | custom-call | tf_op jit(solution)/shard_map/pallas_call | solution.py:83
  (67 shorter events, 20.0 us)
Async XLA Ops:
  7.2 10.7 %copy-start = (bf16[5120,256]{1,0:T(8,128)(2,1)S(1)}, bf16[5120,256]{1,0:T(8,128)(2,1)}, u32[]{:S(2)}) copy-start(bf16[5120,256]{1,0:T(8,128)(2,1)} %param.13) | copy-start | bytes 7864324
  7.2 8.3 %copy-start.8 = (s32[8]{0:T(128)S(1)}, s32[8]{0:T(128)}, u32[]{:S(2)}) copy-start(s32[8]{0:T(128)} %param.18) | copy-start | bytes 100
  7.2 41.9 %all-gather.3.cloned.1.call-start = ((), (), s32[]{:S(2)}) async-start(), calls=%async_computation | async-start | bytes 1638400 | tf_op jit(solution)/shard_map/all_gather | solution.py:134
  10.3 13.0 %collective-permute-start.5 = (bf16[128,1280]{1,0:T(8,128)(2,1)}, bf16[128,1280]{1,0:T(8,128)(2,1)}, u32[]{:S(2)}, u32[]{:S(2)}) collective-permute-start(bf16[128,1280]{1,0:T(8,128)(2,1)} %get-tuple-element.15), channel_id=1, source_target_pairs={{0,3},{1,0},{2,1},{3,2},{4,7},{5,4},{6,5},{7,6},{8,11},{9,8},{10,9... | collective-permute-start | bytes 983048 | tf_op jit(solution)/shard_map/ppermute | solution.py:152
  12.5 21.9 %collective-permute-start.4 = (bf16[128,1280]{1,0:T(8,128)(2,1)}, bf16[128,1280]{1,0:T(8,128)(2,1)}, u32[]{:S(2)}, u32[]{:S(2)}) collective-permute-start(bf16[128,1280]{1,0:T(8,128)(2,1)} %get-tuple-element.15), channel_id=1, source_target_pairs={{0,2},{1,3},{2,0},{3,1},{4,6},{5,7},{6,4},{7,5},{8,10},{9,11},{10,... | collective-permute-start | bytes 983048 | tf_op jit(solution)/shard_map/ppermute | solution.py:152
  12.7 9.7 %collective-permute-start.2 = (f32[256]{0:T(256)S(1)}, f32[256]{0:T(256)}, u32[]{:S(2)}, u32[]{:S(2)}) collective-permute-start(f32[256]{0:T(256)S(1)} %get-tuple-element.12), channel_id=1, source_target_pairs={{0,3},{1,0},{2,1},{3,2},{4,7},{5,4},{6,5},{7,6},{8,11},{9,8},{10,9... | collective-permute-start | bytes 3080 | tf_op jit(solution)/shard_map/ppermute | solution.py:153
  13.0 9.6 %collective-permute-start.1 = (f32[256]{0:T(256)S(1)}, f32[256]{0:T(256)}, u32[]{:S(2)}, u32[]{:S(2)}) collective-permute-start(f32[256]{0:T(256)S(1)} %get-tuple-element.12), channel_id=1, source_target_pairs={{0,2},{1,3},{2,0},{3,1},{4,6},{5,7},{6,4},{7,5},{8,10},{9,11},{10,... | collective-permute-start | bytes 3080 | tf_op jit(solution)/shard_map/ppermute | solution.py:153
  14.2 8.4 %collective-permute-start = (f32[256]{0:T(256)S(1)}, f32[256]{0:T(256)}, u32[]{:S(2)}, u32[]{:S(2)}) collective-permute-start(f32[256]{0:T(256)S(1)} %get-tuple-element.12), channel_id=1, source_target_pairs={{0,1},{1,2},{2,3},{3,0},{4,5},{5,6},{6,7},{7,4},{8,9},{9,10},{10,1... | collective-permute-start | bytes 3080 | tf_op jit(solution)/shard_map/ppermute | solution.py:153
  15.4 74.2 %all-gather.5.cloned.1.call-start = ((), (), s32[]{:S(2)}) async-start(), calls=%async_computation.1 | async-start | bytes 2359296 | tf_op jit(solution)/shard_map/all_gather | solution.py:181
  15.7 2.1 %copy-start.5 = (s32[8,1]{0,1:T(1,128)}, s32[8,1]{0,1:T(1,128)S(1)}, u32[]{:S(2)}) copy-start(s32[8,1]{0,1:T(1,128)S(1)} %reduce-window.8) | copy-start | bytes 100
  22.4 11.0 %collective-permute-start.3 = (bf16[128,1280]{1,0:T(8,128)(2,1)}, bf16[128,1280]{1,0:T(8,128)(2,1)S(1)}, u32[]{:S(2)}, u32[]{:S(2)}) collective-permute-start(bf16[128,1280]{1,0:T(8,128)(2,1)} %get-tuple-element.15), channel_id=1, source_target_pairs={{0,1},{1,2},{2,3},{3,0},{4,5},{5,6},{6,7},{7,4},{8,9},{9,10},{10,1... | collective-permute-start | bytes 983048 | tf_op jit(solution)/shard_map/ppermute | solution.py:152
  33.3 0.7 copy-start.1
  39.2 14.0 %copy-start.6 = (f32[2,128]{1,0:T(2,128)S(1)}, f32[2,128]{1,0:T(2,128)}, u32[]{:S(2)}) copy-start(f32[2,128]{1,0:T(2,128)} %bitcast_convert_fusion.1) | copy-start | bytes 3076
  55.9 3.2 %copy-start.7 = (f32[256]{0:T(256)S(1)}, f32[256]{0:T(256)}, u32[]{:S(2)}) copy-start(f32[256]{0:T(256)} %convert_element_type.45) | copy-start | bytes 3076
  56.4 9.7 %copy-start.4 = (bf16[1280]{0:T(1024)(128)(2,1)S(1)}, bf16[1280]{0:T(1024)(128)(2,1)}, u32[]{:S(2)}) copy-start(bf16[1280]{0:T(1024)(128)(2,1)} %param.15) | copy-start | bytes 7684
  71.4 2.8 %copy-start.2 = (bf16[128,1280]{1,0:T(8,128)(2,1)S(1)}, bf16[128,1280]{1,0:T(8,128)(2,1)}, u32[]{:S(2)}) copy-start(bf16[128,1280]{1,0:T(8,128)(2,1)} %copy-done.1) | copy-start | bytes 983044
  77.9 8.7 %copy-start.3 = (f32[128,1280]{0,1:T(8,128)S(1)}, f32[128,1280]{0,1:T(8,128)}, u32[]{:S(2)}) copy-start(f32[128,1280]{0,1:T(8,128)} %copy.19) | copy-start | bytes 1966084
Sparse Core Ops, SparseCore 0:
  15.5 33.4 all-gather.2
  60.1 29.4 all-gather.4

commit v3 on v2

--- a/solution.py
+++ b/solution.py
@@ -153,32 +153,50 @@
         squares = squares + lax.ppermute(part_sq, "tp", perm)
         more = project(got, (mine + parts - shift) % parts)
         lower = [a + b for a, b in zip(lower, more)]
-    proj_query, proj_key, proj_value = tuple(
-        jnp.concatenate([a, b], axis=0) for a, b in zip(upper, lower)
-    )
     rstd = lax.rsqrt(squares / D + norm_eps)
     own_pos = me * rows + jnp.arange(rows, dtype=jnp.int32)
     own_seg, own_off = token_meta(own_pos, lengths)
     own_live = own_seg < docs - 1
-    query = rstd[:, None] * proj_query + query_bias.astype(jnp.float32)
-    key = rstd[:, None] * proj_key + key_bias.astype(jnp.float32)
-    value = rstd[:, None] * proj_value + value_bias.astype(jnp.float32)
-    query = (
-        rotate(query.reshape(rows, q_width // HEAD, HEAD), own_off)
-        .reshape(rows, q_width)
-        .astype(jnp.bfloat16)
-    )
-    key = (
-        jnp.where(own_live[:, None, None], rotate(key.reshape(rows, kv_dev, HEAD), own_off), 0.0)
-        .reshape(rows, kv_width)
-        .astype(jnp.bfloat16)
-    )
-    value = jnp.where(own_live[:, None], value, 0.0).astype(jnp.bfloat16)
-    q_seg, q_off = token_meta(own_pos, lengths)
-    q_live = q_seg < docs - 1
-    q_grouped = query.reshape(rows, kv_dev, group, HEAD)
-
-    both = lax.all_gather(jnp.concatenate([key, value], axis=1), "blk", axis=0, tiled=True)
+
+    def finish(totals, part):
+        count_here = totals[0].shape[0]
+        lo = part * half
+        norm = rstd[lo:lo + count_here, None]
+        off = own_off[lo:lo + count_here]
+        live = own_live[lo:lo + count_here]
+        query = norm * totals[0] + query_bias.astype(jnp.float32)
+        key = norm * totals[1] + key_bias.astype(jnp.float32)
+        value = norm * totals[2] + value_bias.astype(jnp.float32)
+        query = (
+            rotate(query.reshape(count_here, q_width // HEAD, HEAD), off)
+            .reshape(count_here, q_width)
+            .astype(jnp.bfloat16)
+        )
+        key = (
+            jnp.where(live[:, None, None], rotate(key.reshape(count_here, kv_dev, HEAD), off), 0.0)
+            .reshape(count_here, kv_width)
+            .astype(jnp.bfloat16)
+        )
+        value = jnp.where(live[:, None], value, 0.0).astype(jnp.bfloat16)
+        return query, jnp.concatenate([key, value], axis=1)
+
+    query_up, kv_up = finish(upper, 0)
+    query_low, kv_low = finish(lower, 1)
+    query = jnp.concatenate([query_up, query_low], axis=0)
+    key = jnp.concatenate([kv_up[:, :kv_width], kv_low[:, :kv_width]], axis=0)
+    q_seg = own_seg
+    q_live = own_live
+
+    low_all = jnp.zeros((blocks,) + kv_low.shape, kv_low.dtype)
+    low_all = lax.dynamic_update_slice_in_dim(low_all, kv_low[None], me, 0)
+    for shift in range(1, blocks):
+        perm = [(j, (j + shift) % blocks) for j in range(blocks)]
+        got = lax.ppermute(kv_low, "blk", perm)
+        low_all = lax.dynamic_update_slice_in_dim(
+            low_all, got[None], (me + blocks - shift) % blocks, 0
+        )
+    up_all = lax.all_gather(kv_up, "blk", axis=0, tiled=False)
+    both = jnp.stack([up_all, low_all], axis=1).reshape(blocks * rows, 2 * kv_width)
     count = both.shape[0]
     longest = count // 2
     span = min(count, longest + rows)

time: 110 us -> 134 us (1.22)
  starting transfers between devices: 5.38 us -> 21 us
  local copies, waits for them, and re-layouts: 9.97 us -> 20.8 us
  waiting for transfers between devices: 18.7 us -> 11.5 us
  other arithmetic: 14.6 us -> 20 us
  matrix products: 33.8 us -> 32.4 us
    ppermute x0 -> x7, starting transfers between devices: none -> 15.6 us  [on_device(): got = lax.ppermute(kv_low, 'blk', perm)]
    all_gather x1, waiting for transfers between devices: 8.39 us -> 0.01 us  [on_device(): piece = lax.all_gather(scaled[:half], 'tp', axis=1, tiled=True)]
    dynamic_update_slice x0 -> x7, local copies, waits for them, and re-layouts: none -> 7.38 us  [on_device(): lax.dynamic_update_slice_in_dim(low_all, got[None], (me + blocks - shift)...]
    all_gather x1, waiting for transfers between devices: 1.47 us -> 5.22 us  [on_device(): up_all = lax.all_gather(kv_up, 'blk', axis=0, tiled=False)]
    another operation x2 -> x3, other arithmetic: 0.37 us -> 4.1 us
    add x4 -> x0, other arithmetic: 2.78 us -> none  [the longest x2 2.54 us: on_device(): key = rstd[:, None] * proj_key + key_bias.astype(jnp.float32)]
    ppermute x3, waiting for transfers between devices: 8.81 us -> 6.2 us  [on_device(): got = lax.ppermute(lower_rows, 'tp', perm)]
    concatenate x2 -> x0, local copies, waits for them, and re-layouts: 2.33 us -> none  [on_device(): jnp.concatenate([a, b], axis=0)]
  transfers between devices with their start and end apart: 8 -> 15, of which waited for: 3 -> 2; matrix products, arithmetic and copies ran while one was open for 39% -> 49% of each run, Pallas kernels for 0% -> 0%
where the time goes in v3:
time: 134 us; the launch traced here: 132 us
  matrix products  32.4 us (24%)
  starting transfers between devices  21 us (16%)
  local copies, waits for them, and re-layouts  20.8 us (16%)
  other arithmetic  20 us (15%)
  between operations  15.8 us (12%)
  waiting for transfers between devices  11.5 us (9%)
  Pallas kernels  10.4 us (8%)
    dot_general x12, matrix products, project(): jnp.dot(chunk, lax.dynamic_slice_in_dim(weight, source * width, width, 0)...  20.9 us
    ppermute x7, starting transfers between devices, on_device(): got = lax.ppermute(kv_low, 'blk', perm)  15.6 us
    dot_general x3, matrix products, on_device(): jnp.dot(piece, weight, preferred_element_type=jnp.float32)  11.6 us
    pallas_call x1, Pallas kernels, window_attention(): pl.pallas_call(kernel, grid_spec=spec, out_shape=jax.ShapeDtypeStruct((ro...  10.4 us
    dynamic_update_slice x7, local copies, waits for them, and re-layouts, on_device(): lax.dynamic_update_slice_in_dim(low_all, got[None], (me + blocks - shift)...  7.38 us
    ppermute x3, waiting for transfers between devices, on_device(): got = lax.ppermute(lower_rows, 'tp', perm)  6.2 us
    all_gather x1, waiting for transfers between devices, on_device(): up_all = lax.all_gather(kv_up, 'blk', axis=0, tiled=False)  5.22 us
    add x2, local copies, waits for them, and re-layouts, finish(): query = norm * totals[0] + query_bias.astype(jnp.float32)  3.23 us
  transfers between devices with their start and end apart: 15, of which 2 were waited for; matrix products, arithmetic and copies ran while one was open for 49% of the time, Pallas kernels for 0%

profile of v3, /device:TPU:9, one launch (start us, length us, event | category | flops | bytes accessed | tf_op | source)
XLA Modules:
  0.0 131.9 jit_solution(9231400747211668850)
XLA Ops:
  8.1 1.9 %fusion.24 = (f32[256]{0:T(256)}, bf16[256,1280]{1,0:T(8,128)(2,1)S(1)}) fusion(bf16[256,1280]{1,0:T(8,128)(2,1)} %param.10, f32[1280]{0:T(1024)S(1)} %convert_element_type.56), kind=kLoop, calls=%fused_computation.18 | loop fusion | flops 1638144 | bytes 1316864 | tf_op jit(solution)/shard_map/reduce_sum | solution.py:128
  10.9 2.2 %collective-permute-start.5 = (bf16[128,1280]{1,0:T(8,128)(2,1)}, bf16[128,1280]{1,0:T(8,128)(2,1)}, u32[]{:S(2)}, u32[]{:S(2)}) collective-permute-start(bf16[128,1280]{1,0:T(8,128)(2,1)} %get-tuple-element.15), channel_id=1, source_target_pairs={{0,3},{1,0},{2,1},{3,2},{4,7},{5,4},{6,5},{7,6},{8,11},{9,8},{10,9... | collective-permute-start | bytes 983048 | tf_op jit(solution)/shard_map/ppermute | solution.py:152
  21.2 3.4 %fusion.6 = f32[128,1280]{1,0:T(8,128)} fusion(bf16[5120,1280]{1,0:T(8,128)(2,1)} %param.12, s32[]{:T(128)S(6)} %select_n.116, bf16[256,1280]{1,0:T(8,128)(2,1)S(1)} %get-tuple-element.17), kind=kOutput, calls=%fused_computation.6 | convolution fusion | flops 419430400 | bytes 4259844 | tf_op jit(solution)/shard_map/dot_general | solution.py:140
  35.6 6.2 %collective-permute-done.3 = bf16[128,1280]{1,0:T(8,128)(2,1)S(1)} collective-permute-done((bf16[128,1280]{1,0:T(8,128)(2,1)}, bf16[128,1280]{1,0:T(8,128)(2,1)S(1)}, u32[]{:S(2)}, u32[]{:S(2)}) %collective-permute-start.3) | collective-permute-done | bytes 327712 | tf_op jit(solution)/shard_map/ppermute | solution.py:152
  45.4 1.5 %fusion.38 = f32[128,256]{1,0:T(8,128)S(1)} fusion(bf16[128,1280]{1,0:T(8,128)(2,1)} %collective-permute-done.5, bf16[5120,256]{1,0:T(8,128)(2,1)} %param.14, s32[]{:T(128)S(6)} %select_n.122), kind=kOutput, calls=%fused_computation.39 | convolution fusion | flops 83886080 | bytes 1114116 | tf_op jit(solution)/shard_map/dot_general | solution.py:140
  48.2 1.5 %fusion.37 = bf16[128,256]{1,0:T(8,128)(2,1)S(1)} fusion(f32[128,256]{1,0:T(8,128)S(1)} %fusion.38, f32[128,256]{1,0:T(8,128)S(1)} %convolution_add_fusion.1, bf16[128,1280]{1,0:T(8,128)(2,1)} %collective-permute-done.4, bf16[5120,256]{1,0:T(8,128)(2,1)} %param.14, s32[]{:T(128)S(6)} %select_n.120, f32[128]{0:T(128)S(1)} %get-tuple-element.27, ...), kind=kOutput, calls=%fused_computation.37 | convolution fusion | flops 84082688 | bytes 1312388 | tf_op jit(solution)/shard_map/dot_general | solution.py:140
  49.7 9.6 %collective-permute-start.6 = (bf16[128,512]{1,0:T(8,128)(2,1)S(1)}, bf16[128,512]{1,0:T(8,128)(2,1)S(1)}, u32[]{:S(2)}, u32[]{:S(2)}) collective-permute-start(bf16[128,512]{1,0:T(8,128)(2,1)S(1)} %pad_maximum_fusion.8), channel_id=1, source_target_pairs={{0,4},{4,8},{8,12},{12,16},{16,20},{20,24},{24,28},{28,0},{1,5},{5... | collective-permute-start | bytes 393224 | tf_op jit(solution)/shard_map/ppermute | solution.py:194
  59.3 1.4 %collective-permute-start.7 = (bf16[128,512]{1,0:T(8,128)(2,1)S(1)}, bf16[128,512]{1,0:T(8,128)(2,1)}, u32[]{:S(2)}, u32[]{:S(2)}) collective-permute-start(bf16[128,512]{1,0:T(8,128)(2,1)S(1)} %pad_maximum_fusion.8), channel_id=1, source_target_pairs={{0,8},{4,12},{8,16},{12,20},{16,24},{20,28},{24,0},{28,4},{1,9},{5... | collective-permute-start | bytes 393224 | tf_op jit(solution)/shard_map/ppermute | solution.py:194
  62.0 1.5 %collective-permute-start.10 = (bf16[128,512]{1,0:T(8,128)(2,1)S(1)}, bf16[128,512]{1,0:T(8,128)(2,1)S(1)}, u32[]{:S(2)}, u32[]{:S(2)}) collective-permute-start(bf16[128,512]{1,0:T(8,128)(2,1)S(1)} %pad_maximum_fusion.8), channel_id=1, source_target_pairs={{0,20},{4,24},{8,28},{12,0},{16,4},{20,8},{24,12},{28,16},{1,21},{... | collective-permute-start | bytes 393224 | tf_op jit(solution)/shard_map/ppermute | solution.py:194
  63.5 2.6 %fusion = f32[128,1280]{1,0:T(8,128)S(1)} fusion(bf16[128,1280]{1,0:T(8,128)(2,1)} %collective-permute-done.5, bf16[5120,1280]{1,0:T(8,128)(2,1)} %param.12, s32[]{:T(128)S(6)} %select_n.122), kind=kOutput, calls=%fused_computation | convolution fusion | flops 419430400 | bytes 4259844 | tf_op jit(solution)/shard_map/dot_general | solution.py:140
  66.1 2.7 %fusion.2 = f32[128,1280]{1,0:T(8,128)S(1)} fusion(bf16[128,1280]{1,0:T(8,128)(2,1)} %collective-permute-done.4, bf16[5120,1280]{1,0:T(8,128)(2,1)} %param.12, s32[]{:T(128)S(6)} %select_n.120), kind=kOutput, calls=%fused_computation.2 | convolution fusion | flops 419430400 | bytes 4259844 | tf_op jit(solution)/shard_map/dot_general | solution.py:140
  68.8 3.5 %fusion.20 = f32[128,1280]{1,0:T(8,128)} fusion(f32[128,1280]{1,0:T(8,128)S(1)} %fusion, f32[128,1280]{1,0:T(8,128)S(1)} %fusion.2, f32[128,1280]{1,0:T(8,128)S(1)} %copy-done.2, bf16[128,1280]{1,0:T(8,128)(2,1)S(1)} %collective-permute-done.3, bf16[5120,1280]{1,0:T(8,128)(2,1)} %param.12, s32[]{:T(128)S(6)} %select_n.118, f32[128]{0:T(128)S(1)} %get-tuple-element.27, ...), kind=kOutput, calls=%fused_computation.12 | convolution fusion | flops 420249600 | bytes 6231556 | tf_op jit(solution)/shard_map/dot_general | solution.py:140
  72.3 2.2 %copy.24 = f32[128,1280]{0,1:T(8,128)} copy(f32[128,1280]{1,0:T(8,128)} %fusion.20) | data formatting | bytes 1310720 | tf_op jit(solution)/shard_map/add | solution.py:167
  78.7 1.6 %bitcast_dynamic-update-slice_fusion.5 = bf16[8,1,128,512]{3,2,1,0:T(8,128)(2,1)} fusion(bf16[8,1,128,512]{3,2,1,0:T(8,128)(2,1)} %bitcast_dynamic-update-slice_fusion.6, s32[]{:T(128)S(6)} %select_n.131, bf16[128,512]{1,0:T(8,128)(2,1)} %collective-permute-done.7), kind=kLoop, calls=%fused_computation.73 | loop fusion | bytes 262148 | tf_op jit(solution)/shard_map/dynamic_update_slice | solution.py:195
  80.3 1.6 %bitcast_dynamic-update-slice_fusion.4 = bf16[8,1,128,512]{3,2,1,0:T(8,128)(2,1)} fusion(bf16[8,1,128,512]{3,2,1,0:T(8,128)(2,1)} %bitcast_dynamic-update-slice_fusion.5, s32[]{:T(128)S(6)} %select_n.133, bf16[128,512]{1,0:T(8,128)(2,1)} %collective-permute-done.8), kind=kLoop, calls=%fused_computation.72 | loop fusion | bytes 262148 | tf_op jit(solution)/shard_map/dynamic_update_slice | solution.py:195
  81.9 1.6 %bitcast_dynamic-update-slice_fusion.3 = bf16[8,1,128,512]{3,2,1,0:T(8,128)(2,1)} fusion(bf16[8,1,128,512]{3,2,1,0:T(8,128)(2,1)} %bitcast_dynamic-update-slice_fusion.4, s32[]{:T(128)S(6)} %select_n.135, bf16[128,512]{1,0:T(8,128)(2,1)} %collective-permute-done.9), kind=kLoop, calls=%fused_computation.71 | loop fusion | bytes 262148 | tf_op jit(solution)/shard_map/dynamic_update_slice | solution.py:195
  84.1 1.8 %fusion.34 = f32[128,256]{1,0:T(8,128)S(1)} fusion(bf16[128,5120]{1,0:T(8,128)(2,1)} %all-gather.4.cloned.1.call-done, bf16[5120,256]{1,0:T(8,128)(2,1)S(1)} %copy-done, f32[256]{0:T(256)S(1)} %copy-done.16, f32[128]{0:T(128)S(1)} %get-tuple-element.26), kind=kOutput, calls=%fused_computation.34 | convolution fusion | flops 335609856 | bytes 4064768 | tf_op jit(solution)/shard_map/dot_general | solution.py:135
  86.5 2.6 %fusion.36 = bf16[128,256]{1,0:T(8,128)(2,1)S(1)} fusion(bf16[128,5120]{1,0:T(8,128)(2,1)} %all-gather.4.cloned.1.call-done, bf16[5120,256]{1,0:T(8,128)(2,1)} %param.14, f32[256]{0:T(256)} %convert_element_type.66, f32[128]{0:T(128)S(1)} %get-tuple-element.26, pred[128]{0:T(512)(128)(4,1)S(1)} %copy-done.11), kind=kOutput, calls=%fused_computation.36 | convolution fusion | flops 335675392 | bytes 3999360 | tf_op jit(solution)/shard_map/dot_general | solution.py:135
  91.3 7.1 %fusion.23 = f32[128,1280]{1,0:T(8,128)S(1)} fusion(bf16[128,5120]{1,0:T(8,128)(2,1)} %all-gather.4.cloned.1.call-done, bf16[5120,1280]{1,0:T(8,128)(2,1)} %param.12, f32[1280]{0:T(1024)S(1)} %convert_element_type.58, f32[128]{0:T(128)S(1)} %get-tuple-element.26), kind=kOutput, calls=%fused_computation.14 | convolution fusion | flops 1678049280 | bytes 15078912 | tf_op jit(solution)/shard_map/dot_general | solution.py:135
  99.5 2.2 %subtract_convert_fusion = (bf16[128,10,64]{0,2,1:T(8,128)(2,1)S(1)}, bf16[128,10,64]{0,2,1:T(8,128)(2,1)S(1)}, bf16[128,10,64]{0,2,1:T(8,128)(2,1)S(1)}, bf16[128,10,64]{0,2,1:T(8,128)(2,1)}) fusion(f32[128,10,128]{0,2,1:T(8,128)} %bitcast.68, f32[128,64]{0,1:T(8,128)S(1)} %copy-done.8, f32[128,64]{0,1:T(8,128)} %copy-done.9, f32[128,64]{0,1:T(8,128)S(1)} %copy-done.6, ...), kind=kLoop, calls=%fused_computation.54 | loop fusion | flops 1310720 | bytes 2097152 | tf_op jit(solution)/shard_map/convert
  101.9 1.7 %pad_maximum_fusion.2 = bf16[128,10,128]{0,2,1:T(8,128)(2,1)} fusion(bf16[128,10,64]{0,2,1:T(8,128)(2,1)S(1)} %get-tuple-element.34, bf16[128,10,64]{0,2,1:T(8,128)(2,1)} %get-tuple-element.35), kind=kLoop, calls=%fused_computation.51 | loop fusion | flops 655360 | bytes 655360 | tf_op jit(solution)/shard_map/concatenate | solution.py:36
  105.6 5.2 %all-gather.6.cloned.1.call-done = bf16[1024,512]{1,0:T(8,128)(2,1)} async-done(((bf16[128,512]{1,0:T(8,128)(2,1)}), bf16[1024,512]{1,0:T(8,128)(2,1)}) %all-gather.6.cloned.1.call-update) | async-done | bytes 1048592 | tf_op jit(solution)/shard_map/all_gather | solution.py:198
  110.8 1.7 %pad_maximum_fusion = bf16[8,2,128,512]{3,2,1,0:T(8,128)(2,1)S(1)} fusion(bf16[8,1,128,512]{3,2,1,0:T(8,128)(2,1)} %bitcast_dynamic-update-slice_fusion, bf16[8,1,128,512]{3,2,1,0:T(8,128)(2,1)} %bitcast.72), kind=kLoop, calls=%fused_computation.15 | loop fusion | flops 1048576 | bytes 4194304 | tf_op jit(solution)/shard_map/stack | solution.py:199
  114.6 10.4 %shard_map.113 = bf16[256,1280]{1,0:T(8,128)(2,1)} custom-call(s32[1]{0:T(128)} %bitcast.first_ref, bf16[256,1280]{1,0:T(8,128)(2,1)} %pad_maximum_fusion.1.q_ref, bf16[2048,512]{1,0:T(8,128)(2,1)} %bitcast.66, bf16[2048,512]{1,0:T(8,128)(2,1)} %bitcast.67, s32[256,1]{1,0:T(8,128)} %copy.32.qs_ref, s32[256,1]{1,0:T(8,128)} %iota_add_fusion.qp_ref, ...), custom_call_target="tpu_custom_call" | custom-call | tf_op jit(solution)/shard_map/pallas_call | solution.py:83
  (133 shorter events, 38.5 us)
Async XLA Ops:
  7.2 20.0 %copy-start = (bf16[5120,256]{1,0:T(8,128)(2,1)S(1)}, bf16[5120,256]{1,0:T(8,128)(2,1)}, u32[]{:S(2)}) copy-start(bf16[5120,256]{1,0:T(8,128)(2,1)} %param.13) | copy-start | bytes 7864324
  7.2 10.8 %copy-start.21 = (s32[16]{0:T(128)S(1)}, s32[16]{0:T(128)}, u32[]{:S(2)}) copy-start(s32[16]{0:T(128)} %param.19) | copy-start | bytes 196
  7.2 12.7 %copy-start.15 = (bf16[1280]{0:T(1024)(128)(2,1)S(1)}, bf16[1280]{0:T(1024)(128)(2,1)}, u32[]{:S(2)}) copy-start(bf16[1280]{0:T(1024)(128)(2,1)} %param.15) | copy-start | bytes 7684
  7.2 12.7 %copy-start.22 = (s32[8]{0:T(128)S(1)}, s32[8]{0:T(128)}, u32[]{:S(2)}) copy-start(s32[8]{0:T(128)} %param.18) | copy-start | bytes 100
  7.2 76.9 %all-gather.4.cloned.1.call-start = ((), (), s32[]{:S(2)}) async-start(), calls=%async_computation | async-start | bytes 1638400 | tf_op jit(solution)/shard_map/all_gather | solution.py:134
  10.9 23.4 %collective-permute-start.5 = (bf16[128,1280]{1,0:T(8,128)(2,1)}, bf16[128,1280]{1,0:T(8,128)(2,1)}, u32[]{:S(2)}, u32[]{:S(2)}) collective-permute-start(bf16[128,1280]{1,0:T(8,128)(2,1)} %get-tuple-element.15), channel_id=1, source_target_pairs={{0,3},{1,0},{2,1},{3,2},{4,7},{5,4},{6,5},{7,6},{8,11},{9,8},{10,9... | collective-permute-start | bytes 983048 | tf_op jit(solution)/shard_map/ppermute | solution.py:152
  13.1 29.0 %collective-permute-start.4 = (bf16[128,1280]{1,0:T(8,128)(2,1)}, bf16[128,1280]{1,0:T(8,128)(2,1)}, u32[]{:S(2)}, u32[]{:S(2)}) collective-permute-start(bf16[128,1280]{1,0:T(8,128)(2,1)} %get-tuple-element.15), channel_id=1, source_target_pairs={{0,2},{1,3},{2,0},{3,1},{4,6},{5,7},{6,4},{7,5},{8,10},{9,11},{10,... | collective-permute-start | bytes 983048 | tf_op jit(solution)/shard_map/ppermute | solution.py:152
  13.3 20.1 %collective-permute-start.2 = (f32[256]{0:T(256)}, f32[256]{0:T(256)}, u32[]{:S(2)}, u32[]{:S(2)}) collective-permute-start(f32[256]{0:T(256)} %get-tuple-element.16), channel_id=1, source_target_pairs={{0,3},{1,0},{2,1},{3,2},{4,7},{5,4},{6,5},{7,6},{8,11},{9,8},{10,9... | collective-permute-start | bytes 3080 | tf_op jit(solution)/shard_map/ppermute | solution.py:153
  13.6 20.0 %collective-permute-start.1 = (f32[256]{0:T(256)}, f32[256]{0:T(256)}, u32[]{:S(2)}, u32[]{:S(2)}) collective-permute-start(f32[256]{0:T(256)} %get-tuple-element.16), channel_id=1, source_target_pairs={{0,2},{1,3},{2,0},{3,1},{4,6},{5,7},{6,4},{7,5},{8,10},{9,11},{10,... | collective-permute-start | bytes 3080 | tf_op jit(solution)/shard_map/ppermute | solution.py:153
  14.8 18.8 %collective-permute-start = (f32[256]{0:T(256)}, f32[256]{0:T(256)}, u32[]{:S(2)}, u32[]{:S(2)}) collective-permute-start(f32[256]{0:T(256)} %get-tuple-element.16), channel_id=1, source_target_pairs={{0,1},{1,2},{2,3},{3,0},{4,5},{5,6},{6,7},{7,4},{8,9},{9,10},{10,1... | collective-permute-start | bytes 3080 | tf_op jit(solution)/shard_map/ppermute | solution.py:153
  16.1 94.7 %all-gather.6.cloned.1.call-start = ((), (), s32[]{:S(2)}) async-start(), calls=%async_computation.1 | async-start | bytes 1179648 | tf_op jit(solution)/shard_map/all_gather | solution.py:198
  21.2 6.8 %copy-start.18 = (f32[128]{0:T(128)S(1)}, f32[128]{0:T(128)}, u32[]{:S(2)}) copy-start(f32[128]{0:T(128)} %get-tuple-element.25) | copy-start | bytes 1540
  33.4 8.4 %collective-permute-start.3 = (bf16[128,1280]{1,0:T(8,128)(2,1)}, bf16[128,1280]{1,0:T(8,128)(2,1)S(1)}, u32[]{:S(2)}, u32[]{:S(2)}) collective-permute-start(bf16[128,1280]{1,0:T(8,128)(2,1)} %get-tuple-element.15), channel_id=1, source_target_pairs={{0,1},{1,2},{2,3},{3,0},{4,5},{5,6},{6,7},{7,4},{8,9},{9,10},{10,1... | collective-permute-start | bytes 983048 | tf_op jit(solution)/shard_map/ppermute | solution.py:152
  49.7 26.5 %collective-permute-start.6 = (bf16[128,512]{1,0:T(8,128)(2,1)S(1)}, bf16[128,512]{1,0:T(8,128)(2,1)S(1)}, u32[]{:S(2)}, u32[]{:S(2)}) collective-permute-start(bf16[128,512]{1,0:T(8,128)(2,1)S(1)} %pad_maximum_fusion.8), channel_id=1, source_target_pairs={{0,4},{4,8},{8,12},{12,16},{16,20},{20,24},{24,28},{28,0},{1,5},{5... | collective-permute-start | bytes 393224 | tf_op jit(solution)/shard_map/ppermute | solution.py:194
  59.3 19.0 %collective-permute-start.7 = (bf16[128,512]{1,0:T(8,128)(2,1)S(1)}, bf16[128,512]{1,0:T(8,128)(2,1)}, u32[]{:S(2)}, u32[]{:S(2)}) collective-permute-start(bf16[128,512]{1,0:T(8,128)(2,1)S(1)} %pad_maximum_fusion.8), channel_id=1, source_target_pairs={{0,8},{4,12},{8,16},{12,20},{16,24},{20,28},{24,0},{28,4},{1,9},{5... | collective-permute-start | bytes 393224 | tf_op jit(solution)/shard_map/ppermute | solution.py:194
  60.7 19.6 %collective-permute-start.8 = (bf16[128,512]{1,0:T(8,128)(2,1)S(1)}, bf16[128,512]{1,0:T(8,128)(2,1)}, u32[]{:S(2)}, u32[]{:S(2)}) collective-permute-start(bf16[128,512]{1,0:T(8,128)(2,1)S(1)} %pad_maximum_fusion.8), channel_id=1, source_target_pairs={{0,12},{4,16},{8,20},{12,24},{16,28},{20,0},{24,4},{28,8},{1,13},{... | collective-permute-start | bytes 393224 | tf_op jit(solution)/shard_map/ppermute | solution.py:194
  60.7 21.2 %collective-permute-start.9 = (bf16[128,512]{1,0:T(8,128)(2,1)S(1)}, bf16[128,512]{1,0:T(8,128)(2,1)}, u32[]{:S(2)}, u32[]{:S(2)}) collective-permute-start(bf16[128,512]{1,0:T(8,128)(2,1)S(1)} %pad_maximum_fusion.8), channel_id=1, source_target_pairs={{0,16},{4,20},{8,24},{12,28},{16,0},{20,4},{24,8},{28,12},{1,17},{... | collective-permute-start | bytes 393224 | tf_op jit(solution)/shard_map/ppermute | solution.py:194
  62.0 21.4 %collective-permute-start.10 = (bf16[128,512]{1,0:T(8,128)(2,1)S(1)}, bf16[128,512]{1,0:T(8,128)(2,1)S(1)}, u32[]{:S(2)}, u32[]{:S(2)}) collective-permute-start(bf16[128,512]{1,0:T(8,128)(2,1)S(1)} %pad_maximum_fusion.8), channel_id=1, source_target_pairs={{0,20},{4,24},{8,28},{12,0},{16,4},{20,8},{24,12},{28,16},{1,21},{... | collective-permute-start | bytes 393224 | tf_op jit(solution)/shard_map/ppermute | solution.py:194
  72.3 11.8 %copy-start.16 = (f32[256]{0:T(256)S(1)}, f32[256]{0:T(256)}, u32[]{:S(2)}) copy-start(f32[256]{0:T(256)} %convert_element_type.64) | copy-start | bytes 3076
  76.2 13.8 %collective-permute-start.11 = (bf16[128,512]{1,0:T(8,128)(2,1)S(1)}, bf16[128,512]{1,0:T(8,128)(2,1)S(1)}, u32[]{:S(2)}, u32[]{:S(2)}) collective-permute-start(bf16[128,512]{1,0:T(8,128)(2,1)S(1)} %pad_maximum_fusion.8), channel_id=1, source_target_pairs={{0,24},{4,28},{8,0},{12,4},{16,8},{20,12},{24,16},{28,20},{1,25},{... | collective-permute-start | bytes 393224 | tf_op jit(solution)/shard_map/ppermute | solution.py:194
  78.3 12.4 %collective-permute-start.12 = (bf16[128,512]{1,0:T(8,128)(2,1)S(1)}, bf16[128,512]{1,0:T(8,128)(2,1)S(1)}, u32[]{:S(2)}, u32[]{:S(2)}) collective-permute-start(bf16[128,512]{1,0:T(8,128)(2,1)S(1)} %pad_maximum_fusion.8), channel_id=1, source_target_pairs={{0,28},{4,0},{8,4},{12,8},{16,12},{20,16},{24,20},{28,24},{1,29},{... | collective-permute-start | bytes 393224 | tf_op jit(solution)/shard_map/ppermute | solution.py:194
  91.3 8.2 %copy-start.4 = (f32[128,64]{0,1:T(8,128)S(1)}, f32[128,64]{0,1:T(8,128)}, u32[]{:S(2)}) copy-start(f32[128,64]{0,1:T(8,128)} %copy-done.3) | copy-start | bytes 98308
  91.3 8.2 %copy-start.6 = (f32[128,64]{0,1:T(8,128)S(1)}, f32[128,64]{0,1:T(8,128)}, u32[]{:S(2)}) copy-start(f32[128,64]{0,1:T(8,128)} %copy-done.5) | copy-start | bytes 98308
  91.3 8.2 %copy-start.8 = (f32[128,64]{0,1:T(8,128)S(1)}, f32[128,64]{0,1:T(8,128)}, u32[]{:S(2)}) copy-start(f32[128,64]{0,1:T(8,128)} %copy-done.7) | copy-start | bytes 98308
  (16 other events, 76.4 us)
Sparse Core Ops, SparseCore 0:
  16.2 35.3 all-gather.3
  90.1 20.6 all-gather.5

commit v4 on v1

--- a/solution.py
+++ b/solution.py
@@ -60,7 +60,7 @@
             ) * scale
             scores = jnp.where(allowed, scores, neg_large)
             top = jnp.max(scores, axis=1, keepdims=True)
-            expo = jnp.where(allowed, jnp.exp(scores - top), 0.0)
+            expo = jnp.exp(scores - top)
             denom = jnp.sum(expo, axis=1, keepdims=True)
             acc = jnp.dot(expo.astype(jnp.bfloat16), values, preferred_element_type=jnp.float32)
             out = jnp.where(live, acc / jnp.where(live, denom, 1.0), 0.0)
@@ -120,18 +120,18 @@
     scale = 1.0 / float(HEAD) ** 0.5
     wide = tokens.astype(jnp.float32)
     scaled = (wide * norm_gain.astype(jnp.float32)).astype(jnp.bfloat16)
-    empty = (
-        jnp.zeros((rows, q_width), jnp.float32),
-        jnp.zeros((rows, kv_width), jnp.float32),
-        jnp.zeros((rows, kv_width), jnp.float32),
-    )
+    part_sq = jnp.sum(wide * wide, axis=1)
+    parts = lax.axis_size("tp")
+    squares = part_sq
+    for shift in range(1, parts):
+        perm = [(j, (j + shift) % parts) for j in range(parts)]
+        squares = squares + lax.ppermute(part_sq, "tp", perm)
     piece = lax.all_gather(scaled, "tp", axis=1, tiled=True)
-    count = piece.shape[1]
-    totals = []
-    for total, weight in zip(empty, (w_query, w_key, w_value)):
-        totals.append(jnp.dot(piece, weight, preferred_element_type=jnp.float32))
-    proj_query, proj_key, proj_value = tuple(totals)
-    squares = lax.psum(jnp.sum(wide * wide, axis=1), "tp")
+    w_kv = jnp.concatenate([w_key, w_value], axis=1)
+    proj_kv = jnp.dot(piece, w_kv, preferred_element_type=jnp.float32)
+    proj_query = jnp.dot(piece, w_query, preferred_element_type=jnp.float32)
+    proj_key = proj_kv[:, :kv_width]
+    proj_value = proj_kv[:, kv_width:]
     rstd = lax.rsqrt(squares / D + norm_eps)
     own_pos = me * rows + jnp.arange(rows, dtype=jnp.int32)
     own_seg, own_off = token_meta(own_pos, lengths)

time: 109 us -> 108 us (level)
  waiting for transfers between devices: 38.2 us -> 50.1 us
  blocking collectives: 7.89 us -> 0 us
  matrix products: 16.5 us -> 13 us
  starting transfers between devices: 0.08 us -> 2.84 us
  local copies, waits for them, and re-layouts: 6.59 us -> 4.15 us
  other arithmetic: 12.7 us -> 10.8 us
    psum x1 -> x0, blocking collectives: 7.89 us -> none  [on_device(): squares = lax.psum(jnp.sum(wide * wide, axis=1), 'tp')]
    all_gather x1, waiting for transfers between devices: 9.01 us -> 15.1 us  [on_device(): lax.all_gather(jnp.concatenate([key, value], axis=1), 'blk', axis=0, tile...]
    all_gather x1, waiting for transfers between devices: 29.1 us -> 34.9 us  [on_device(): piece = lax.all_gather(scaled, 'tp', axis=1, tiled=True)]
    dot_general x3 -> x2, matrix products: 16.5 us -> 13 us  [the longest x1 8.19 us: on_device(): proj_query = jnp.dot(piece, w_query, preferred_element_type=jnp.float32)]
    ppermute x0 -> x3, starting transfers between devices: none -> 2.76 us  [on_device(): squares = squares + lax.ppermute(part_sq, 'tp', perm)]
    add x1, local copies, waits for them, and re-layouts: 2.83 us -> 0.4 us  [on_device(): query = rstd[:, None] * proj_query + query_bias.astype(jnp.float32)]
    another operation x2, other arithmetic: 2.34 us -> 1.01 us
  transfers between devices with their start and end apart: 2 -> 5, of which waited for: 2 -> 2; matrix products, arithmetic and copies ran while one was open for 22% -> 16% of each run, Pallas kernels for 0% -> 0%
where the time goes in v4:
time: 108 us; the launch traced here: 106 us
  waiting for transfers between devices  50.1 us (46%)
  between operations  15.5 us (14%)
  matrix products  13 us (12%)
  other arithmetic  10.8 us (10%)
  Pallas kernels  9.79 us (9%)
  local copies, waits for them, and re-layouts  4.15 us (4%)
  starting transfers between devices  2.84 us (3%)
    all_gather x1, waiting for transfers between devices, on_device(): piece = lax.all_gather(scaled, 'tp', axis=1, tiled=True)  34.9 us
    all_gather x1, waiting for transfers between devices, on_device(): lax.all_gather(jnp.concatenate([key, value], axis=1), 'blk', axis=0, tile...  15.1 us
    pallas_call x1, Pallas kernels, window_attention(): pl.pallas_call(kernel, grid_spec=spec, out_shape=jax.ShapeDtypeStruct((ro...  9.79 us
    dot_general x1, matrix products, on_device(): proj_query = jnp.dot(piece, w_query, preferred_element_type=jnp.float32)  8.19 us
    dot_general x1, matrix products, on_device(): proj_kv = jnp.dot(piece, w_kv, preferred_element_type=jnp.float32)  4.82 us
    ppermute x3, starting transfers between devices, on_device(): squares = squares + lax.ppermute(part_sq, 'tp', perm)  2.76 us
  transfers between devices with their start and end apart: 5, of which 2 were waited for; matrix products, arithmetic and copies ran while one was open for 16% of the time, Pallas kernels for 0%

profile of v4, /device:TPU:9, one launch (start us, length us, event | category | flops | bytes accessed | tf_op | source)
XLA Modules:
  0.0 106.1 jit_solution(16744310124178811488)
XLA Ops:
  7.2 0.7 convert_element_type.43
  7.9 2.1 %fusion.4 = (f32[256]{0:T(256)S(1)}, bf16[256,1280]{1,0:T(8,128)(2,1)}) fusion(bf16[256,1280]{1,0:T(8,128)(2,1)} %param.10, f32[1280]{0:T(1024)S(1)} %convert_element_type.43), kind=kLoop, calls=%fused_computation.6 | loop fusion | flops 1638144 | bytes 1316864 | tf_op jit(solution)/shard_map/reduce_sum | solution.py:123
  10.1 2.2 %collective-permute-start.2 = (f32[256]{0:T(256)S(1)}, f32[256]{0:T(256)S(1)}, u32[]{:S(2)}, u32[]{:S(2)}) collective-permute-start(f32[256]{0:T(256)S(1)} %get-tuple-element.12), channel_id=1, source_target_pairs={{0,3},{1,0},{2,1},{3,2},{4,7},{5,4},{6,5},{7,6},{8,11},{9,8},{10,9... | collective-permute-start | bytes 3080 | tf_op jit(solution)/shard_map/ppermute | solution.py:128
  12.8 0.8 reduce-window.8
  13.7 0.7 fusion.12
  14.8 0.7 convert_element_type.49
  15.4 0.7 convert_element_type.51
  16.3 34.9 %all-gather.3.cloned.1.call-done = bf16[256,5120]{1,0:T(8,128)(2,1)} async-done(((bf16[256,1280]{1,0:T(8,128)(2,1)}), bf16[256,5120]{1,0:T(8,128)(2,1)}) %all-gather.3.cloned.1.call-update) | async-done | bytes 2621456 | tf_op jit(solution)/shard_map/all_gather | solution.py:129
  51.3 4.8 %fusion = f32[256,512]{1,0:T(8,128)S(1)} fusion(bf16[256,5120]{1,0:T(8,128)(2,1)} %all-gather.3.cloned.1.call-done, bf16[5120,256]{1,0:T(8,128)(2,1)} %param.14, bf16[5120,256]{1,0:T(8,128)(2,1)} %param.13), kind=kOutput, calls=%fused_computation | convolution fusion | flops 1352663040 | bytes 8388608 | tf_op jit(solution)/shard_map/dot_general | solution.py:131
  56.4 0.5 multiply_subtract_fusion
  56.9 0.4 pad_maximum_fusion.1
  57.4 0.7 pad_maximum_fusion.2
  58.2 0.6 fusion.13
  60.1 0.6 reshape.141.ks_ref
  60.7 0.8 copy.21.qs_ref
  61.5 0.7 iota_add_fusion.qp_ref
  62.2 0.6 iota_add_fusion.2.kp_ref
  62.8 8.2 %multiply_add_fusion = f32[256,1280]{1,0:T(8,128)S(1)} fusion(f32[1280]{0:T(1024)S(1)} %convert_element_type.45, f32[256]{0:T(256)S(1)} %add_rsqrt_fusion, bf16[256,5120]{1,0:T(8,128)(2,1)} %all-gather.3.cloned.1.call-done, bf16[5120,1280]{1,0:T(8,128)(2,1)} %param.12), kind=kOutput, calls=%fused_computation.8 | convolution fusion | flops 3356098560 | bytes 17045504 | tf_op jit(solution)/shard_map/dot_general | solution.py:132
  71.0 0.4 copy.17
  71.6 1.1 %copy.20.q_ref = bf16[256,1280]{1,0:T(8,128)(2,1)} copy(bf16[256,1280]{0,1:T(8,128)(2,1)S(1)} %bitcast.27) | data formatting | bytes 1310720 | tf_op jit(solution)/shard_map/convert_element_type | solution.py:145
  72.7 15.1 %all-gather.5.cloned.1.call-done.k_ref.v_ref = bf16[2048,512]{1,0:T(8,128)(2,1)} async-done(((bf16[256,512]{1,0:T(8,128)(2,1)}), bf16[2048,512]{1,0:T(8,128)(2,1)}) %all-gather.5.cloned.1.call-update) | async-done | bytes 2097168 | tf_op jit(solution)/shard_map/all_gather | solution.py:157
  87.8 1.0 dynamic-slice_bitcast_fusion.3
  88.8 0.7 pad_maximum_fusion.3
  89.5 9.8 %shard_map.113 = bf16[256,1280]{1,0:T(8,128)(2,1)} custom-call(s32[1]{0:T(128)} %bitcast.first_ref, bf16[256,1280]{1,0:T(8,128)(2,1)} %copy.20.q_ref, bf16[2048,512]{1,0:T(8,128)(2,1)} %all-gather.5.cloned.1.call-done.k_ref.v_ref, bf16[2048,512]{1,0:T(8,128)(2,1)} %all-gather.5.cloned.1.call-done.k_ref.v_ref, s32[256,1]{1,0:T(8,128)} %copy.21.qs_ref, ...), custom_call_target="tpu_custom_call" | custom-call | tf_op jit(solution)/shard_map/pallas_call | solution.py:83
  (30 shorter events, 1.9 us)
Async XLA Ops:
  7.2 44.1 %all-gather.3.cloned.1.call-start = ((), (), s32[]{:S(2)}) async-start(), calls=%async_computation | async-start | bytes 3276800 | tf_op jit(solution)/shard_map/all_gather | solution.py:129
  10.0 77.8 %all-gather.5.cloned.1.call-start = ((), (), s32[]{:S(2)}) async-start(), calls=%async_computation.1 | async-start | bytes 2359296 | tf_op jit(solution)/shard_map/all_gather | solution.py:157
  10.1 6.2 %collective-permute-start.2 = (f32[256]{0:T(256)S(1)}, f32[256]{0:T(256)S(1)}, u32[]{:S(2)}, u32[]{:S(2)}) collective-permute-start(f32[256]{0:T(256)S(1)} %get-tuple-element.12), channel_id=1, source_target_pairs={{0,3},{1,0},{2,1},{3,2},{4,7},{5,4},{6,5},{7,6},{8,11},{9,8},{10,9... | collective-permute-start | bytes 3080 | tf_op jit(solution)/shard_map/ppermute | solution.py:128
  12.3 4.0 %collective-permute-start.1 = (f32[256]{0:T(256)S(1)}, f32[256]{0:T(256)S(1)}, u32[]{:S(2)}, u32[]{:S(2)}) collective-permute-start(f32[256]{0:T(256)S(1)} %get-tuple-element.12), channel_id=1, source_target_pairs={{0,2},{1,3},{2,0},{3,1},{4,6},{5,7},{6,4},{7,5},{8,10},{9,11},{10,... | collective-permute-start | bytes 3080 | tf_op jit(solution)/shard_map/ppermute | solution.py:128
  12.5 3.8 %collective-permute-start = (f32[256]{0:T(256)S(1)}, f32[256]{0:T(256)S(1)}, u32[]{:S(2)}, u32[]{:S(2)}) collective-permute-start(f32[256]{0:T(256)S(1)} %get-tuple-element.12), channel_id=1, source_target_pairs={{0,1},{1,2},{2,3},{3,0},{4,5},{5,6},{6,7},{7,4},{8,9},{9,10},{10,1... | collective-permute-start | bytes 3080 | tf_op jit(solution)/shard_map/ppermute | solution.py:128
  56.1 2.1 %copy-start.1 = (s32[16]{0:T(128)S(1)}, s32[16]{0:T(128)}, u32[]{:S(2)}) copy-start(s32[16]{0:T(128)} %param.19) | copy-start | bytes 196
  56.1 3.9 %copy-start = (bf16[1280]{0:T(1024)(128)(2,1)S(1)}, bf16[1280]{0:T(1024)(128)(2,1)}, u32[]{:S(2)}) copy-start(bf16[1280]{0:T(1024)(128)(2,1)} %param.15) | copy-start | bytes 7684
Sparse Core Ops, SparseCore 0:
  10.4 40.8 all-gather.2
  58.3 29.4 all-gather.4

commit v5 on v4

--- a/solution.py
+++ b/solution.py
@@ -37,6 +37,17 @@
         [first * cosine - second * sine, second * cosine + first * sine], axis=-1
     )
 
+
+def partners(size):
+    if size & (size - 1) == 0:
+        return [
+            ((lambda i, s=s: jnp.bitwise_xor(i, s)), [(j, j ^ s) for j in range(size)])
+            for s in range(1, size)
+        ]
+    return [
+        ((lambda i, s=s: (i + size - s) % size), [(j, (j + s) % size) for j in range(size)])
+        for s in range(1, size)
+    ]
 
 def window_attention(first, query, both, q_seg, q_pos, k_seg, k_pos, docs, interpret=False):
     rows, q_width = query.shape
@@ -123,13 +134,28 @@
     part_sq = jnp.sum(wide * wide, axis=1)
     parts = lax.axis_size("tp")
     squares = part_sq
-    for shift in range(1, parts):
-        perm = [(j, (j + shift) % parts) for j in range(parts)]
+    for flip, perm in partners(parts):
         squares = squares + lax.ppermute(part_sq, "tp", perm)
-    piece = lax.all_gather(scaled, "tp", axis=1, tiled=True)
     w_kv = jnp.concatenate([w_key, w_value], axis=1)
-    proj_kv = jnp.dot(piece, w_kv, preferred_element_type=jnp.float32)
-    proj_query = jnp.dot(piece, w_query, preferred_element_type=jnp.float32)
+    width = tokens.shape[1]
+    mine = lax.axis_index("tp")
+
+    def project(chunk, source):
+        return [
+            jnp.dot(
+                chunk,
+                lax.dynamic_slice_in_dim(weight, source * width, width, 0),
+                preferred_element_type=jnp.float32,
+            )
+            for weight in (w_kv, w_query)
+        ]
+
+    proj_kv, proj_query = project(scaled, mine)
+    for flip, perm in partners(parts):
+        got = lax.ppermute(scaled, "tp", perm)
+        more = project(got, flip(mine))
+        proj_kv = proj_kv + more[0]
+        proj_query = proj_query + more[1]
     proj_key = proj_kv[:, :kv_width]
     proj_value = proj_kv[:, kv_width:]
     rstd = lax.rsqrt(squares / D + norm_eps)
@@ -154,7 +180,13 @@
     q_live = q_seg < docs - 1
     q_grouped = query.reshape(rows, kv_dev, group, HEAD)
 
-    both = lax.all_gather(jnp.concatenate([key, value], axis=1), "blk", axis=0, tiled=True)
+    own_kv = jnp.concatenate([key, value], axis=1)
+    both = jnp.zeros((blocks,) + own_kv.shape, own_kv.dtype)
+    both = lax.dynamic_update_slice_in_dim(both, own_kv[None], me, 0)
+    for flip, perm in partners(blocks):
+        got = lax.ppermute(own_kv, "blk", perm)
+        both = lax.dynamic_update_slice_in_dim(both, got[None], flip(me), 0)
+    both = both.reshape(blocks * rows, 2 * kv_width)
     count = both.shape[0]
     longest = count // 2
     span = min(count, longest + rows)

time: 108 us -> 110 us (1.019)
  waiting for transfers between devices: 50.1 us -> 36.7 us
  between operations: 15.5 us -> 2.27 us
  starting transfers between devices: 2.84 us -> 14.5 us
  local copies, waits for them, and re-layouts: 4.15 us -> 13.8 us
  matrix products: 13 us -> 21.2 us
    all_gather x2 -> x0, waiting for transfers between devices: 50 us -> none  [the longest x1 34.9 us: on_device(): piece = lax.all_gather(scaled, 'tp', axis=1, tiled=True)]
    ppermute x0 -> x10, waiting for transfers between devices: none -> 29.4 us  [the longest x7 27.6 us: on_device(): got = lax.ppermute(own_kv, 'blk', perm)]
    ppermute x0 -> x10, starting transfers between devices: none -> 11.9 us  [the longest x7 9.16 us: on_device(): got = lax.ppermute(own_kv, 'blk', perm)]
    dot_general x2 -> x8, matrix products: 13 us -> 21.2 us  [project(): jnp.dot(chunk, lax.dynamic_slice_in_dim(weight, source * width, width, 0)...]
    ppermute x3, waiting for transfers between devices: 0.01 us -> 7.32 us  [on_device(): squares = squares + lax.ppermute(part_sq, 'tp', perm)]
    unnamed x4 -> x21, local copies, waits for them, and re-layouts: 0.01 us -> 4.13 us
    dynamic_update_slice x0 -> x7, local copies, waits for them, and re-layouts: none -> 3.94 us  [on_device(): both = lax.dynamic_update_slice_in_dim(both, got[None], flip(me), 0)]
    reduce_sum x1 -> x0, other arithmetic: 2.11 us -> none  [on_device(): part_sq = jnp.sum(wide * wide, axis=1)]
  transfers between devices with their start and end apart: 5 -> 13, of which waited for: 2 -> 6; matrix products, arithmetic and copies ran while one was open for 16% -> 35% of each run, Pallas kernels for 0% -> 0%
where the time goes in v5:
time: 110 us; the launch traced here: 108 us
  waiting for transfers between devices  36.7 us (33%)
  matrix products  21.2 us (19%)
  starting transfers between devices  14.5 us (13%)
  local copies, waits for them, and re-layouts  13.8 us (13%)
  other arithmetic  10 us (9%)
  Pallas kernels  9.79 us (9%)
  between operations  2.27 us (2%)
    ppermute x7, waiting for transfers between devices, on_device(): got = lax.ppermute(own_kv, 'blk', perm)  27.6 us
    dot_general x8, matrix products, project(): jnp.dot(chunk, lax.dynamic_slice_in_dim(weight, source * width, width, 0)...  21.2 us
    pallas_call x1, Pallas kernels, window_attention(): pl.pallas_call(kernel, grid_spec=spec, out_shape=jax.ShapeDtypeStruct((ro...  9.79 us
    ppermute x7, starting transfers between devices, on_device(): got = lax.ppermute(own_kv, 'blk', perm)  9.16 us
    ppermute x3, waiting for transfers between devices, on_device(): squares = squares + lax.ppermute(part_sq, 'tp', perm)  7.32 us
    unnamed x21, local copies, waits for them, and re-layouts  4.13 us
    dynamic_update_slice x7, local copies, waits for them, and re-layouts, on_device(): both = lax.dynamic_update_slice_in_dim(both, got[None], flip(me), 0)  3.94 us
    ppermute x3, starting transfers between devices, on_device(): got = lax.ppermute(scaled, 'tp', perm)  2.71 us
  transfers between devices with their start and end apart: 13, of which 6 were waited for; matrix products, arithmetic and copies ran while one was open for 35% of the time, Pallas kernels for 0%

profile of v5, /device:TPU:9, one launch (start us, length us, event | category | flops | bytes accessed | tf_op | source)
XLA Modules:
  0.0 108.3 jit_solution(12273831943122497731)
XLA Ops:
  1.3 1.4 %fusion.18 = (bf16[256,1280]{1,0:T(8,128)(2,1)S(1)}, f32[256]{0:T(256)S(1)}) fusion(bf16[256,1280]{1,0:T(8,128)(2,1)} %param.10, f32[1280]{0:T(1024)S(1)} %convert_element_type.43), kind=kLoop, calls=%fused_computation.14 | loop fusion | flops 1638144 | bytes 1316864 | tf_op jit(solution)/shard_map/convert_element_type | solution.py:133
  2.7 2.2 %collective-permute-start.5 = (bf16[256,1280]{1,0:T(8,128)(2,1)S(1)}, bf16[256,1280]{1,0:T(8,128)(2,1)}, u32[]{:S(2)}, u32[]{:S(2)}) collective-permute-start(bf16[256,1280]{1,0:T(8,128)(2,1)S(1)} %get-tuple-element.12), channel_id=1, source_target_pairs={{0,3},{1,2},{2,1},{3,0},{4,7},{5,6},{6,5},{7,4},{8,11},{9,10},{10,... | collective-permute-start | bytes 1966088 | tf_op jit(solution)/shard_map/ppermute | solution.py:155
  7.8 1.3 %fusion.53 = (s32[]{:T(128)}, s32[]{:T(128)}) fusion(s32[16]{0:T(128)} %param.19, s32[]{:T(128)S(6)} %mul.187, s32[]{:T(128)S(6)} %add.195), kind=kLoop, calls=%fused_computation.82 | loop fusion | flops 94 | bytes 80 | tf_op jit(solution)/shard_map/reduce_sum | solution.py:200
  11.1 3.6 %constant_dynamic-update-slice_fusion.1 = bf16[5120,512]{1,0:T(8,128)(2,1)} fusion(bf16[5120,256]{1,0:T(8,128)(2,1)} %param.13), kind=kLoop, calls=%fused_computation.67 | loop fusion | bytes 5242880
  17.2 1.7 %constant_dynamic-update-slice_fusion = bf16[5120,512]{1,0:T(8,128)(2,1)} fusion(bf16[5120,512]{1,0:T(8,128)(2,1)} %constant_dynamic-update-slice_fusion.1, bf16[5120,256]{1,0:T(8,128)(2,1)S(1)} %copy-done.1), kind=kLoop, calls=%fused_computation.66 | loop fusion | bytes 5242880 | tf_op jit(solution)/shard_map/concatenate | solution.py:139
  18.9 1.8 %fusion.25 = f32[256,512]{1,0:T(8,128)S(1)} fusion(bf16[256,1280]{1,0:T(8,128)(2,1)S(1)} %get-tuple-element.12, bf16[5120,512]{1,0:T(8,128)(2,1)} %constant_dynamic-update-slice_fusion, s32[]{:T(128)S(6)} %select_n.62), kind=kOutput, calls=%fused_computation.21 | convolution fusion | flops 335544320 | bytes 2490372 | tf_op jit(solution)/shard_map/dot_general | solution.py:145
  20.8 4.1 %fusion.6 = f32[256,1280]{1,0:T(8,128)} fusion(bf16[256,1280]{1,0:T(8,128)(2,1)S(1)} %get-tuple-element.12, bf16[5120,1280]{1,0:T(8,128)(2,1)} %param.12, s32[]{:T(128)S(6)} %select_n.62), kind=kOutput, calls=%fused_computation.6 | convolution fusion | flops 838860800 | bytes 5242884 | tf_op jit(solution)/shard_map/dot_general | solution.py:145
  27.2 7.3 %collective-permute-done.1 = f32[256]{0:T(256)} collective-permute-done((f32[256]{0:T(256)S(1)}, f32[256]{0:T(256)}, u32[]{:S(2)}, u32[]{:S(2)}) %collective-permute-start.1) | collective-permute-done | bytes 1056 | tf_op jit(solution)/shard_map/ppermute | solution.py:138
  35.2 2.0 %fusion.19 = f32[256,512]{1,0:T(8,128)S(1)} fusion(bf16[256,1280]{1,0:T(8,128)(2,1)} %collective-permute-done.5, bf16[5120,512]{1,0:T(8,128)(2,1)} %constant_dynamic-update-slice_fusion, s32[]{:T(128)S(6)} %select_n.65), kind=kOutput, calls=%fused_computation.15 | convolution fusion | flops 335544320 | bytes 2490372 | tf_op jit(solution)/shard_map/dot_general | solution.py:145
  37.2 2.0 %fusion.21 = f32[256,512]{1,0:T(8,128)S(1)} fusion(bf16[256,1280]{1,0:T(8,128)(2,1)} %collective-permute-done.4, bf16[5120,512]{1,0:T(8,128)(2,1)} %constant_dynamic-update-slice_fusion, s32[]{:T(128)S(6)} %select_n.64), kind=kOutput, calls=%fused_computation.17 | convolution fusion | flops 335544320 | bytes 2490372 | tf_op jit(solution)/shard_map/dot_general | solution.py:145
  39.3 1.8 %collective-permute-done.3 = bf16[256,1280]{1,0:T(8,128)(2,1)S(1)} collective-permute-done((bf16[256,1280]{1,0:T(8,128)(2,1)S(1)}, bf16[256,1280]{1,0:T(8,128)(2,1)S(1)}, u32[]{:S(2)}, u32[]{:S(2)}) %collective-permute-start.3) | collective-permute-done | bytes 655392 | tf_op jit(solution)/shard_map/ppermute | solution.py:155
  41.1 1.8 %fusion.33 = f32[256,512]{1,0:T(8,128)S(1)} fusion(f32[256,512]{1,0:T(8,128)S(1)} %fusion.19, f32[256,512]{1,0:T(8,128)S(1)} %fusion.21, f32[256,512]{1,0:T(8,128)S(1)} %fusion.25, bf16[256,1280]{1,0:T(8,128)(2,1)S(1)} %collective-permute-done.3, bf16[5120,512]{1,0:T(8,128)(2,1)} %constant_dynamic-update-slice_fusion, s32[]{:T(128)S(6)} %select_n.63), kind=kOutput, calls=%fused_computation.26 | convolution fusion | flops 335937536 | bytes 4063236 | tf_op jit(solution)/shard_map/dot_general | solution.py:145
  44.9 3.0 %collective-permute-start.6 = (bf16[256,512]{1,0:T(8,128)(2,1)}, bf16[256,512]{1,0:T(8,128)(2,1)}, u32[]{:S(2)}, u32[]{:S(2)}) collective-permute-start(bf16[256,512]{1,0:T(8,128)(2,1)} %pad_maximum_fusion.2), channel_id=1, source_target_pairs={{0,4},{4,0},{8,12},{12,8},{16,20},{20,16},{24,28},{28,24},{1,5},{5... | collective-permute-start | bytes 786440 | tf_op jit(solution)/shard_map/ppermute | solution.py:187
  48.1 1.5 %collective-permute-start.8 = (bf16[256,512]{1,0:T(8,128)(2,1)}, bf16[256,512]{1,0:T(8,128)(2,1)}, u32[]{:S(2)}, u32[]{:S(2)}) collective-permute-start(bf16[256,512]{1,0:T(8,128)(2,1)} %pad_maximum_fusion.2), channel_id=1, source_target_pairs={{0,12},{4,8},{8,4},{12,0},{16,28},{20,24},{24,20},{28,16},{1,13},{... | collective-permute-start | bytes 786440 | tf_op jit(solution)/shard_map/ppermute | solution.py:187
  49.5 2.3 %collective-permute-start.9 = (bf16[256,512]{1,0:T(8,128)(2,1)}, bf16[256,512]{1,0:T(8,128)(2,1)}, u32[]{:S(2)}, u32[]{:S(2)}) collective-permute-start(bf16[256,512]{1,0:T(8,128)(2,1)} %pad_maximum_fusion.2), channel_id=1, source_target_pairs={{0,16},{4,20},{8,24},{12,28},{16,0},{20,4},{24,8},{28,12},{1,17},{... | collective-permute-start | bytes 786440 | tf_op jit(solution)/shard_map/ppermute | solution.py:187
  52.3 3.1 %fusion = f32[256,1280]{1,0:T(8,128)S(1)} fusion(bf16[256,1280]{1,0:T(8,128)(2,1)} %collective-permute-done.5, bf16[5120,1280]{1,0:T(8,128)(2,1)} %param.12, s32[]{:T(128)S(6)} %select_n.65), kind=kOutput, calls=%fused_computation | convolution fusion | flops 838860800 | bytes 5242884 | tf_op jit(solution)/shard_map/dot_general | solution.py:145
  55.4 3.2 %fusion.2 = f32[256,1280]{1,0:T(8,128)S(1)} fusion(bf16[256,1280]{1,0:T(8,128)(2,1)} %collective-permute-done.4, bf16[5120,1280]{1,0:T(8,128)(2,1)} %param.12, s32[]{:T(128)S(6)} %select_n.64), kind=kOutput, calls=%fused_computation.2 | convolution fusion | flops 838860800 | bytes 5242884 | tf_op jit(solution)/shard_map/dot_general | solution.py:145
  58.7 3.1 %multiply_add_fusion = f32[256,1280]{1,0:T(8,128)S(1)} fusion(f32[1280]{0:T(1024)S(1)} %convert_element_type.45, f32[256]{0:T(256)S(1)} %add_rsqrt_fusion, f32[256,1280]{1,0:T(8,128)S(1)} %fusion, f32[256,1280]{1,0:T(8,128)S(1)} %fusion.2, f32[256,1280]{1,0:T(8,128)S(1)} %copy-done.2, bf16[256,1280]{1,0:T(8,128)(2,1)S(1)} %collective-permute-done.3, ...), kind=kOutput, calls=%fused_computation.23 | convolution fusion | flops 840499200 | bytes 9181188 | tf_op jit(solution)/shard_map/dot_general | solution.py:145
  63.7 1.3 %collective-permute-start.11 = (bf16[256,512]{1,0:T(8,128)(2,1)}, bf16[256,512]{1,0:T(8,128)(2,1)S(1)}, u32[]{:S(2)}, u32[]{:S(2)}) collective-permute-start(bf16[256,512]{1,0:T(8,128)(2,1)} %pad_maximum_fusion.2), channel_id=1, source_target_pairs={{0,24},{4,28},{8,16},{12,20},{16,8},{20,12},{24,0},{28,4},{1,25},{... | collective-permute-start | bytes 786440 | tf_op jit(solution)/shard_map/ppermute | solution.py:187
  67.4 3.0 %collective-permute-done.8 = bf16[256,512]{1,0:T(8,128)(2,1)} collective-permute-done((bf16[256,512]{1,0:T(8,128)(2,1)}, bf16[256,512]{1,0:T(8,128)(2,1)}, u32[]{:S(2)}, u32[]{:S(2)}) %collective-permute-start.8) | collective-permute-done | bytes 262176 | tf_op jit(solution)/shard_map/ppermute | solution.py:187
  72.5 13.3 %collective-permute-done.10 = bf16[256,512]{1,0:T(8,128)(2,1)S(1)} collective-permute-done((bf16[256,512]{1,0:T(8,128)(2,1)}, bf16[256,512]{1,0:T(8,128)(2,1)S(1)}, u32[]{:S(2)}, u32[]{:S(2)}) %collective-permute-start.10) | collective-permute-done | bytes 262176 | tf_op jit(solution)/shard_map/ppermute | solution.py:187
  85.8 5.6 %collective-permute-done.11 = bf16[256,512]{1,0:T(8,128)(2,1)S(1)} collective-permute-done((bf16[256,512]{1,0:T(8,128)(2,1)}, bf16[256,512]{1,0:T(8,128)(2,1)S(1)}, u32[]{:S(2)}, u32[]{:S(2)}) %collective-permute-start.11) | collective-permute-done | bytes 262176 | tf_op jit(solution)/shard_map/ppermute | solution.py:187
  91.4 5.6 %collective-permute-done.12 = bf16[256,512]{1,0:T(8,128)(2,1)S(1)} collective-permute-done((bf16[256,512]{1,0:T(8,128)(2,1)}, bf16[256,512]{1,0:T(8,128)(2,1)S(1)}, u32[]{:S(2)}, u32[]{:S(2)}) %collective-permute-start.12) | collective-permute-done | bytes 262176 | tf_op jit(solution)/shard_map/ppermute | solution.py:187
  98.5 9.8 %shard_map.113 = bf16[256,1280]{1,0:T(8,128)(2,1)} custom-call(s32[1]{0:T(128)} %bitcast.first_ref, bf16[256,1280]{1,0:T(8,128)(2,1)} %copy.20.q_ref, bf16[2048,512]{1,0:T(8,128)(2,1)} %bitcast.49, bf16[2048,512]{1,0:T(8,128)(2,1)} %bitcast.50, s32[256,1]{1,0:T(8,128)} %copy.21.qs_ref, s32[256,1]{1,0:T(8,128)} %iota_add_fusion.qp_ref, ...), custom_call_target="tpu_custom_call" | custom-call | tf_op jit(solution)/shard_map/pallas_call | solution.py:94
  (77 shorter events, 20.1 us)
Async XLA Ops:
  2.7 32.5 %collective-permute-start.5 = (bf16[256,1280]{1,0:T(8,128)(2,1)S(1)}, bf16[256,1280]{1,0:T(8,128)(2,1)}, u32[]{:S(2)}, u32[]{:S(2)}) collective-permute-start(bf16[256,1280]{1,0:T(8,128)(2,1)S(1)} %get-tuple-element.12), channel_id=1, source_target_pairs={{0,3},{1,2},{2,1},{3,0},{4,7},{5,6},{6,5},{7,4},{8,11},{9,10},{10,... | collective-permute-start | bytes 1966088 | tf_op jit(solution)/shard_map/ppermute | solution.py:155
  4.9 32.3 %collective-permute-start.4 = (bf16[256,1280]{1,0:T(8,128)(2,1)S(1)}, bf16[256,1280]{1,0:T(8,128)(2,1)}, u32[]{:S(2)}, u32[]{:S(2)}) collective-permute-start(bf16[256,1280]{1,0:T(8,128)(2,1)S(1)} %get-tuple-element.12), channel_id=1, source_target_pairs={{0,2},{1,3},{2,0},{3,1},{4,6},{5,7},{6,4},{7,5},{8,10},{9,11},{10,... | collective-permute-start | bytes 1966088 | tf_op jit(solution)/shard_map/ppermute | solution.py:155
  5.1 21.8 %collective-permute-start = (f32[256]{0:T(256)S(1)}, f32[256]{0:T(256)}, u32[]{:S(2)}, u32[]{:S(2)}) collective-permute-start(f32[256]{0:T(256)S(1)} %get-tuple-element.13), channel_id=1, source_target_pairs={{0,1},{1,0},{2,3},{3,2},{4,5},{5,4},{6,7},{7,6},{8,9},{9,8},{10,11... | collective-permute-start | bytes 3080 | tf_op jit(solution)/shard_map/ppermute | solution.py:138
  5.4 29.1 %collective-permute-start.1 = (f32[256]{0:T(256)S(1)}, f32[256]{0:T(256)}, u32[]{:S(2)}, u32[]{:S(2)}) collective-permute-start(f32[256]{0:T(256)S(1)} %get-tuple-element.13), channel_id=1, source_target_pairs={{0,2},{1,3},{2,0},{3,1},{4,6},{5,7},{6,4},{7,5},{8,10},{9,11},{10,... | collective-permute-start | bytes 3080 | tf_op jit(solution)/shard_map/ppermute | solution.py:138
  6.6 27.9 %collective-permute-start.2 = (f32[256]{0:T(256)S(1)}, f32[256]{0:T(256)}, u32[]{:S(2)}, u32[]{:S(2)}) collective-permute-start(f32[256]{0:T(256)S(1)} %get-tuple-element.13), channel_id=1, source_target_pairs={{0,3},{1,2},{2,1},{3,0},{4,7},{5,6},{6,5},{7,4},{8,11},{9,10},{10,... | collective-permute-start | bytes 3080 | tf_op jit(solution)/shard_map/ppermute | solution.py:138
  11.1 3.6 %copy-start.7 = (s32[8]{0:T(128)S(1)}, s32[8]{0:T(128)}, u32[]{:S(2)}) copy-start(s32[8]{0:T(128)} %param.18) | copy-start | bytes 100
  11.1 3.8 %copy-start.8 = (bf16[256]{0:T(256)(128)(2,1)S(1)}, bf16[256]{0:T(256)(128)(2,1)}, u32[]{:S(2)}) copy-start(bf16[256]{0:T(256)(128)(2,1)} %param.16) | copy-start | bytes 1540
  11.1 4.4 %copy-start.9 = (bf16[256]{0:T(256)(128)(2,1)S(1)}, bf16[256]{0:T(256)(128)(2,1)}, u32[]{:S(2)}) copy-start(bf16[256]{0:T(256)(128)(2,1)} %param.17) | copy-start | bytes 1540
  11.1 6.2 %copy-start.1 = (bf16[5120,256]{1,0:T(8,128)(2,1)S(1)}, bf16[5120,256]{1,0:T(8,128)(2,1)}, u32[]{:S(2)}) copy-start(bf16[5120,256]{1,0:T(8,128)(2,1)} %param.14) | copy-start | bytes 7864324
  20.7 4.8 %copy-start.4 = (bf16[1280]{0:T(1024)(128)(2,1)S(1)}, bf16[1280]{0:T(1024)(128)(2,1)}, u32[]{:S(2)}) copy-start(bf16[1280]{0:T(1024)(128)(2,1)} %param.15) | copy-start | bytes 7684
  26.9 14.1 %collective-permute-start.3 = (bf16[256,1280]{1,0:T(8,128)(2,1)S(1)}, bf16[256,1280]{1,0:T(8,128)(2,1)S(1)}, u32[]{:S(2)}, u32[]{:S(2)}) collective-permute-start(bf16[256,1280]{1,0:T(8,128)(2,1)S(1)} %get-tuple-element.12), channel_id=1, source_target_pairs={{0,1},{1,0},{2,3},{3,2},{4,5},{5,4},{6,7},{7,6},{8,9},{9,8},{10,11... | collective-permute-start | bytes 1966088 | tf_op jit(solution)/shard_map/ppermute | solution.py:155
  39.3 3.6 %copy-start.5 = (f32[256]{0:T(256)S(1)}, f32[256]{0:T(256)}, u32[]{:S(2)}) copy-start(f32[256]{0:T(256)} %convert_element_type.49) | copy-start | bytes 3076
  39.3 3.6 %copy-start.6 = (f32[256]{0:T(256)S(1)}, f32[256]{0:T(256)}, u32[]{:S(2)}) copy-start(f32[256]{0:T(256)} %convert_element_type.51) | copy-start | bytes 3076
  39.3 3.9 %copy-start.3 = (f32[256,64]{1,0:T(8,128)S(1)}, f32[256,64]{1,0:T(8,128)}, u32[]{:S(2)}) copy-start(f32[256,64]{1,0:T(8,128)} %copy.19) | copy-start | bytes 196612
  44.9 18.8 %collective-permute-start.6 = (bf16[256,512]{1,0:T(8,128)(2,1)}, bf16[256,512]{1,0:T(8,128)(2,1)}, u32[]{:S(2)}, u32[]{:S(2)}) collective-permute-start(bf16[256,512]{1,0:T(8,128)(2,1)} %pad_maximum_fusion.2), channel_id=1, source_target_pairs={{0,4},{4,0},{8,12},{12,8},{16,20},{20,16},{24,28},{28,24},{1,5},{5... | collective-permute-start | bytes 786440 | tf_op jit(solution)/shard_map/ppermute | solution.py:187
  47.9 18.1 %collective-permute-start.7 = (bf16[256,512]{1,0:T(8,128)(2,1)}, bf16[256,512]{1,0:T(8,128)(2,1)}, u32[]{:S(2)}, u32[]{:S(2)}) collective-permute-start(bf16[256,512]{1,0:T(8,128)(2,1)} %pad_maximum_fusion.2), channel_id=1, source_target_pairs={{0,8},{4,12},{8,0},{12,4},{16,24},{20,28},{24,16},{28,20},{1,9},{5... | collective-permute-start | bytes 786440 | tf_op jit(solution)/shard_map/ppermute | solution.py:187
  48.1 22.4 %collective-permute-start.8 = (bf16[256,512]{1,0:T(8,128)(2,1)}, bf16[256,512]{1,0:T(8,128)(2,1)}, u32[]{:S(2)}, u32[]{:S(2)}) collective-permute-start(bf16[256,512]{1,0:T(8,128)(2,1)} %pad_maximum_fusion.2), channel_id=1, source_target_pairs={{0,12},{4,8},{8,4},{12,0},{16,28},{20,24},{24,20},{28,16},{1,13},{... | collective-permute-start | bytes 786440 | tf_op jit(solution)/shard_map/ppermute | solution.py:187
  49.5 21.9 %collective-permute-start.9 = (bf16[256,512]{1,0:T(8,128)(2,1)}, bf16[256,512]{1,0:T(8,128)(2,1)}, u32[]{:S(2)}, u32[]{:S(2)}) collective-permute-start(bf16[256,512]{1,0:T(8,128)(2,1)} %pad_maximum_fusion.2), channel_id=1, source_target_pairs={{0,16},{4,20},{8,24},{12,28},{16,0},{20,4},{24,8},{28,12},{1,17},{... | collective-permute-start | bytes 786440 | tf_op jit(solution)/shard_map/ppermute | solution.py:187
  51.8 33.9 %collective-permute-start.10 = (bf16[256,512]{1,0:T(8,128)(2,1)}, bf16[256,512]{1,0:T(8,128)(2,1)S(1)}, u32[]{:S(2)}, u32[]{:S(2)}) collective-permute-start(bf16[256,512]{1,0:T(8,128)(2,1)} %pad_maximum_fusion.2), channel_id=1, source_target_pairs={{0,20},{4,16},{8,28},{12,24},{16,4},{20,0},{24,12},{28,8},{1,21},{... | collective-permute-start | bytes 786440 | tf_op jit(solution)/shard_map/ppermute | solution.py:187
  55.4 3.3 %copy-start.2 = (f32[256,1280]{1,0:T(8,128)S(1)}, f32[256,1280]{1,0:T(8,128)}, u32[]{:S(2)}) copy-start(f32[256,1280]{1,0:T(8,128)} %fusion.6) | copy-start | bytes 3932164
  63.7 27.6 %collective-permute-start.11 = (bf16[256,512]{1,0:T(8,128)(2,1)}, bf16[256,512]{1,0:T(8,128)(2,1)S(1)}, u32[]{:S(2)}, u32[]{:S(2)}) collective-permute-start(bf16[256,512]{1,0:T(8,128)(2,1)} %pad_maximum_fusion.2), channel_id=1, source_target_pairs={{0,24},{4,28},{8,16},{12,20},{16,8},{20,12},{24,0},{28,4},{1,25},{... | collective-permute-start | bytes 786440 | tf_op jit(solution)/shard_map/ppermute | solution.py:187
  66.0 31.0 %collective-permute-start.12 = (bf16[256,512]{1,0:T(8,128)(2,1)}, bf16[256,512]{1,0:T(8,128)(2,1)S(1)}, u32[]{:S(2)}, u32[]{:S(2)}) collective-permute-start(bf16[256,512]{1,0:T(8,128)(2,1)} %pad_maximum_fusion.2), channel_id=1, source_target_pairs={{0,28},{4,24},{8,20},{12,16},{16,12},{20,8},{24,4},{28,0},{1,29},{... | collective-permute-start | bytes 786440 | tf_op jit(solution)/shard_map/ppermute | solution.py:187
  97.1 1.4 %copy-start = (bf16[8,256,512]{2,1,0:T(8,128)(2,1)}, bf16[8,256,512]{2,1,0:T(8,128)(2,1)S(1)}, u32[]{:S(2)}) copy-start(bf16[8,256,512]{2,1,0:T(8,128)(2,1)S(1)} %bitcast_dynamic-update-slice_fusion) | copy-start | bytes 6291460

commit v6 on v5

--- a/solution.py
+++ b/solution.py
@@ -180,13 +180,7 @@
     q_live = q_seg < docs - 1
     q_grouped = query.reshape(rows, kv_dev, group, HEAD)
 
-    own_kv = jnp.concatenate([key, value], axis=1)
-    both = jnp.zeros((blocks,) + own_kv.shape, own_kv.dtype)
-    both = lax.dynamic_update_slice_in_dim(both, own_kv[None], me, 0)
-    for flip, perm in partners(blocks):
-        got = lax.ppermute(own_kv, "blk", perm)
-        both = lax.dynamic_update_slice_in_dim(both, got[None], flip(me), 0)
-    both = both.reshape(blocks * rows, 2 * kv_width)
+    both = lax.all_gather(jnp.concatenate([key, value], axis=1), "blk", axis=0, tiled=True)
     count = both.shape[0]
     longest = count // 2
     span = min(count, longest + rows)

time: 110 us -> 98.9 us (0.90)
  between operations: 2.27 us -> 15.6 us
  waiting for transfers between devices: 36.7 us -> 28.2 us
  starting transfers between devices: 14.5 us -> 6.4 us
  local copies, waits for them, and re-layouts: 13.8 us -> 9.5 us
  other arithmetic: 10 us -> 7.49 us
    ppermute x7 -> x0, waiting for transfers between devices: 27.6 us -> none  [on_device(): got = lax.ppermute(own_kv, 'blk', perm)]
    all_gather x0 -> x1, waiting for transfers between devices: none -> 10.9 us  [on_device(): lax.all_gather(jnp.concatenate([key, value], axis=1), 'blk', axis=0, tile...]
    ppermute x3, waiting for transfers between devices: 7.32 us -> 17.4 us  [on_device(): squares = squares + lax.ppermute(part_sq, 'tp', perm)]
    ppermute x7 -> x0, starting transfers between devices: 9.16 us -> none  [on_device(): got = lax.ppermute(own_kv, 'blk', perm)]
    dynamic_update_slice x7 -> x0, local copies, waits for them, and re-layouts: 3.94 us -> none  [on_device(): both = lax.dynamic_update_slice_in_dim(both, got[None], flip(me), 0)]
    ppermute x3, waiting for transfers between devices: 1.77 us -> 0.01 us  [on_device(): got = lax.ppermute(scaled, 'tp', perm)]
    unnamed x21 -> x13, local copies, waits for them, and re-layouts: 4.13 us -> 3.65 us
  transfers between devices with their start and end apart: 13 -> 7, of which waited for: 6 -> 3; matrix products, arithmetic and copies ran while one was open for 35% -> 31% of each run, Pallas kernels for 0% -> 0%
where the time goes in v6:
time: 98.9 us; the launch traced here: 97.3 us
  waiting for transfers between devices  28.2 us (29%)
  matrix products  20.3 us (21%)
  between operations  15.6 us (16%)
  Pallas kernels  9.79 us (10%)
  local copies, waits for them, and re-layouts  9.5 us (10%)
  other arithmetic  7.49 us (8%)
  starting transfers between devices  6.4 us (6%)
    dot_general x8, matrix products, project(): jnp.dot(chunk, lax.dynamic_slice_in_dim(weight, source * width, width, 0)...  20.3 us
    ppermute x3, waiting for transfers between devices, on_device(): squares = squares + lax.ppermute(part_sq, 'tp', perm)  17.4 us
    all_gather x1, waiting for transfers between devices, on_device(): lax.all_gather(jnp.concatenate([key, value], axis=1), 'blk', axis=0, tile...  10.9 us
    pallas_call x1, Pallas kernels, window_attention(): pl.pallas_call(kernel, grid_spec=spec, out_shape=jax.ShapeDtypeStruct((ro...  9.79 us
    ppermute x3, starting transfers between devices, on_device(): got = lax.ppermute(scaled, 'tp', perm)  3.71 us
    unnamed x13, local copies, waits for them, and re-layouts  3.65 us
    ppermute x3, starting transfers between devices, on_device(): squares = squares + lax.ppermute(part_sq, 'tp', perm)  2.65 us
    convert_element_type x2, other arithmetic, on_device(): scaled = (wide * norm_gain.astype(jnp.float32)).astype(jnp.bfloat16)  2.05 us
  transfers between devices with their start and end apart: 7, of which 3 were waited for; matrix products, arithmetic and copies ran while one was open for 31% of the time, Pallas kernels for 0%

profile of v6, /device:TPU:9, one launch (start us, length us, event | category | flops | bytes accessed | tf_op | source)
XLA Modules:
  0.0 97.3 jit_solution(10193459787421361475)
XLA Ops:
  7.9 1.4 %fusion.18 = (bf16[256,1280]{1,0:T(8,128)(2,1)S(1)}, f32[256]{0:T(256)S(1)}) fusion(bf16[256,1280]{1,0:T(8,128)(2,1)} %param.10, f32[1280]{0:T(1024)S(1)} %convert_element_type.43), kind=kLoop, calls=%fused_computation.14 | loop fusion | flops 1638144 | bytes 1316864 | tf_op jit(solution)/shard_map/convert_element_type | solution.py:133
  9.3 2.2 %collective-permute-start.5 = (bf16[256,1280]{1,0:T(8,128)(2,1)S(1)}, bf16[256,1280]{1,0:T(8,128)(2,1)}, u32[]{:S(2)}, u32[]{:S(2)}) collective-permute-start(bf16[256,1280]{1,0:T(8,128)(2,1)S(1)} %get-tuple-element.12), channel_id=1, source_target_pairs={{0,3},{1,2},{2,1},{3,0},{4,7},{5,6},{6,5},{7,4},{8,11},{9,10},{10,... | collective-permute-start | bytes 1966088 | tf_op jit(solution)/shard_map/ppermute | solution.py:155
  12.0 1.2 %collective-permute-start.1 = (f32[256]{0:T(256)S(1)}, f32[256]{0:T(256)S(1)}, u32[]{:S(2)}, u32[]{:S(2)}) collective-permute-start(f32[256]{0:T(256)S(1)} %get-tuple-element.13), channel_id=1, source_target_pairs={{0,2},{1,3},{2,0},{3,1},{4,6},{5,7},{6,4},{7,5},{8,10},{9,11},{10,... | collective-permute-start | bytes 3080 | tf_op jit(solution)/shard_map/ppermute | solution.py:138
  13.2 1.2 %collective-permute-start.2 = (f32[256]{0:T(256)S(1)}, f32[256]{0:T(256)S(1)}, u32[]{:S(2)}, u32[]{:S(2)}) collective-permute-start(f32[256]{0:T(256)S(1)} %get-tuple-element.13), channel_id=1, source_target_pairs={{0,3},{1,2},{2,1},{3,0},{4,7},{5,6},{6,5},{7,4},{8,11},{9,10},{10,... | collective-permute-start | bytes 3080 | tf_op jit(solution)/shard_map/ppermute | solution.py:138
  14.4 3.6 %constant_dynamic-update-slice_fusion.1 = bf16[5120,512]{1,0:T(8,128)(2,1)} fusion(bf16[5120,256]{1,0:T(8,128)(2,1)} %param.13), kind=kLoop, calls=%fused_computation.59 | loop fusion | bytes 5242880
  18.3 1.7 %constant_dynamic-update-slice_fusion = bf16[5120,512]{1,0:T(8,128)(2,1)} fusion(bf16[5120,512]{1,0:T(8,128)(2,1)} %constant_dynamic-update-slice_fusion.1, bf16[5120,256]{1,0:T(8,128)(2,1)S(1)} %copy-done), kind=kLoop, calls=%fused_computation.58 | loop fusion | bytes 5242880 | tf_op jit(solution)/shard_map/concatenate | solution.py:139
  20.0 1.8 %fusion.25 = f32[256,512]{1,0:T(8,128)S(1)} fusion(bf16[256,1280]{1,0:T(8,128)(2,1)S(1)} %get-tuple-element.12, bf16[5120,512]{1,0:T(8,128)(2,1)} %constant_dynamic-update-slice_fusion, s32[]{:T(128)S(6)} %select_n.38), kind=kOutput, calls=%fused_computation.21 | convolution fusion | flops 335544320 | bytes 2490372 | tf_op jit(solution)/shard_map/dot_general | solution.py:145
  22.4 3.6 %collective-permute-done = f32[256]{0:T(256)S(1)} collective-permute-done((f32[256]{0:T(256)S(1)}, f32[256]{0:T(256)S(1)}, u32[]{:S(2)}, u32[]{:S(2)}) %collective-permute-start) | collective-permute-done | bytes 1056 | tf_op jit(solution)/shard_map/ppermute | solution.py:138
  26.0 1.3 %collective-permute-start.3 = (bf16[256,1280]{1,0:T(8,128)(2,1)S(1)}, bf16[256,1280]{1,0:T(8,128)(2,1)S(1)}, u32[]{:S(2)}, u32[]{:S(2)}) collective-permute-start(bf16[256,1280]{1,0:T(8,128)(2,1)S(1)} %get-tuple-element.12), channel_id=1, source_target_pairs={{0,1},{1,0},{2,3},{3,2},{4,5},{5,4},{6,7},{7,6},{8,9},{9,8},{10,11... | collective-permute-start | bytes 1966088 | tf_op jit(solution)/shard_map/ppermute | solution.py:155
  27.3 13.8 %collective-permute-done.1 = f32[256]{0:T(256)S(1)} collective-permute-done((f32[256]{0:T(256)S(1)}, f32[256]{0:T(256)S(1)}, u32[]{:S(2)}, u32[]{:S(2)}) %collective-permute-start.1) | collective-permute-done | bytes 1056 | tf_op jit(solution)/shard_map/ppermute | solution.py:138
  41.1 2.0 %fusion.19 = f32[256,512]{1,0:T(8,128)S(1)} fusion(bf16[256,1280]{1,0:T(8,128)(2,1)} %collective-permute-done.5, bf16[5120,512]{1,0:T(8,128)(2,1)} %constant_dynamic-update-slice_fusion, s32[]{:T(128)S(6)} %select_n.41), kind=kOutput, calls=%fused_computation.15 | convolution fusion | flops 335544320 | bytes 2490372 | tf_op jit(solution)/shard_map/dot_general | solution.py:145
  43.1 2.0 %fusion.21 = f32[256,512]{1,0:T(8,128)S(1)} fusion(bf16[256,1280]{1,0:T(8,128)(2,1)} %collective-permute-done.4, bf16[5120,512]{1,0:T(8,128)(2,1)} %constant_dynamic-update-slice_fusion, s32[]{:T(128)S(6)} %select_n.40), kind=kOutput, calls=%fused_computation.17 | convolution fusion | flops 335544320 | bytes 2490372 | tf_op jit(solution)/shard_map/dot_general | solution.py:145
  45.2 1.8 %fusion.33 = f32[256,512]{1,0:T(8,128)S(1)} fusion(f32[256,512]{1,0:T(8,128)S(1)} %fusion.19, f32[256,512]{1,0:T(8,128)S(1)} %fusion.21, f32[256,512]{1,0:T(8,128)S(1)} %fusion.25, bf16[256,1280]{1,0:T(8,128)(2,1)S(1)} %collective-permute-done.3, bf16[5120,512]{1,0:T(8,128)(2,1)} %constant_dynamic-update-slice_fusion, s32[]{:T(128)S(6)} %select_n.39), kind=kOutput, calls=%fused_computation.26 | convolution fusion | flops 335937536 | bytes 4063236 | tf_op jit(solution)/shard_map/dot_general | solution.py:145
  48.3 0.7 pad_maximum_fusion.2
  51.0 0.8 copy.21.qs_ref
  53.8 2.9 %fusion.6 = f32[256,1280]{1,0:T(8,128)S(1)} fusion(bf16[256,1280]{1,0:T(8,128)(2,1)S(1)} %get-tuple-element.12, bf16[5120,1280]{1,0:T(8,128)(2,1)} %param.12, s32[]{:T(128)S(6)} %select_n.38), kind=kOutput, calls=%fused_computation.6 | convolution fusion | flops 838860800 | bytes 5242884 | tf_op jit(solution)/shard_map/dot_general | solution.py:145
  56.7 3.4 %fusion = f32[256,1280]{1,0:T(8,128)S(1)} fusion(bf16[256,1280]{1,0:T(8,128)(2,1)} %collective-permute-done.5, bf16[5120,1280]{1,0:T(8,128)(2,1)} %param.12, s32[]{:T(128)S(6)} %select_n.41), kind=kOutput, calls=%fused_computation | convolution fusion | flops 838860800 | bytes 5242884 | tf_op jit(solution)/shard_map/dot_general | solution.py:145
  60.1 3.2 %fusion.2 = f32[256,1280]{1,0:T(8,128)S(1)} fusion(bf16[256,1280]{1,0:T(8,128)(2,1)} %collective-permute-done.4, bf16[5120,1280]{1,0:T(8,128)(2,1)} %param.12, s32[]{:T(128)S(6)} %select_n.40), kind=kOutput, calls=%fused_computation.2 | convolution fusion | flops 838860800 | bytes 5242884 | tf_op jit(solution)/shard_map/dot_general | solution.py:145
  63.3 3.1 %multiply_add_fusion = f32[256,1280]{1,0:T(8,128)S(1)} fusion(f32[1280]{0:T(1024)S(1)} %convert_element_type.45, f32[256]{0:T(256)S(1)} %add_rsqrt_fusion, f32[256,1280]{1,0:T(8,128)S(1)} %fusion, f32[256,1280]{1,0:T(8,128)S(1)} %fusion.2, f32[256,1280]{1,0:T(8,128)S(1)} %fusion.6, bf16[256,1280]{1,0:T(8,128)(2,1)S(1)} %collective-permute-done.3, ...), kind=kOutput, calls=%fused_computation.23 | convolution fusion | flops 840499200 | bytes 9181188 | tf_op jit(solution)/shard_map/dot_general | solution.py:145
  67.0 1.1 %copy.20.q_ref = bf16[256,1280]{1,0:T(8,128)(2,1)} copy(bf16[256,1280]{0,1:T(8,128)(2,1)S(1)} %bitcast.32) | data formatting | bytes 1310720 | tf_op jit(solution)/shard_map/convert_element_type | solution.py:171
  68.1 10.9 %all-gather.2.cloned.1.call-done.k_ref.v_ref = bf16[2048,512]{1,0:T(8,128)(2,1)} async-done(((bf16[256,512]{1,0:T(8,128)(2,1)}), bf16[2048,512]{1,0:T(8,128)(2,1)}) %all-gather.2.cloned.1.call-update) | async-done | bytes 2097168 | tf_op jit(solution)/shard_map/all_gather | solution.py:183
  79.0 1.0 dynamic-slice_bitcast_fusion.3
  79.9 0.7 pad_maximum_fusion.3
  80.7 9.8 %shard_map.113 = bf16[256,1280]{1,0:T(8,128)(2,1)} custom-call(s32[1]{0:T(128)} %bitcast.first_ref, bf16[256,1280]{1,0:T(8,128)(2,1)} %copy.20.q_ref, bf16[2048,512]{1,0:T(8,128)(2,1)} %all-gather.2.cloned.1.call-done.k_ref.v_ref, bf16[2048,512]{1,0:T(8,128)(2,1)} %all-gather.2.cloned.1.call-done.k_ref.v_ref, s32[256,1]{1,0:T(8,128)} %copy.21.qs_ref, ...), custom_call_target="tpu_custom_call" | custom-call | tf_op jit(solution)/shard_map/pallas_call | solution.py:94
  (49 shorter events, 6.6 us)
Async XLA Ops:
  7.2 71.8 %all-gather.2.cloned.1.call-start = ((), (), s32[]{:S(2)}) async-start(), calls=%async_computation | async-start | bytes 2359296 | tf_op jit(solution)/shard_map/all_gather | solution.py:183
  9.3 31.8 %collective-permute-start.5 = (bf16[256,1280]{1,0:T(8,128)(2,1)S(1)}, bf16[256,1280]{1,0:T(8,128)(2,1)}, u32[]{:S(2)}, u32[]{:S(2)}) collective-permute-start(bf16[256,1280]{1,0:T(8,128)(2,1)S(1)} %get-tuple-element.12), channel_id=1, source_target_pairs={{0,3},{1,2},{2,1},{3,0},{4,7},{5,6},{6,5},{7,4},{8,11},{9,10},{10,... | collective-permute-start | bytes 1966088 | tf_op jit(solution)/shard_map/ppermute | solution.py:155
  11.5 31.6 %collective-permute-start.4 = (bf16[256,1280]{1,0:T(8,128)(2,1)S(1)}, bf16[256,1280]{1,0:T(8,128)(2,1)}, u32[]{:S(2)}, u32[]{:S(2)}) collective-permute-start(bf16[256,1280]{1,0:T(8,128)(2,1)S(1)} %get-tuple-element.12), channel_id=1, source_target_pairs={{0,2},{1,3},{2,0},{3,1},{4,6},{5,7},{6,4},{7,5},{8,10},{9,11},{10,... | collective-permute-start | bytes 1966088 | tf_op jit(solution)/shard_map/ppermute | solution.py:155
  11.7 14.3 %collective-permute-start = (f32[256]{0:T(256)S(1)}, f32[256]{0:T(256)S(1)}, u32[]{:S(2)}, u32[]{:S(2)}) collective-permute-start(f32[256]{0:T(256)S(1)} %get-tuple-element.13), channel_id=1, source_target_pairs={{0,1},{1,0},{2,3},{3,2},{4,5},{5,4},{6,7},{7,6},{8,9},{9,8},{10,11... | collective-permute-start | bytes 3080 | tf_op jit(solution)/shard_map/ppermute | solution.py:138
  12.0 29.1 %collective-permute-start.1 = (f32[256]{0:T(256)S(1)}, f32[256]{0:T(256)S(1)}, u32[]{:S(2)}, u32[]{:S(2)}) collective-permute-start(f32[256]{0:T(256)S(1)} %get-tuple-element.13), channel_id=1, source_target_pairs={{0,2},{1,3},{2,0},{3,1},{4,6},{5,7},{6,4},{7,5},{8,10},{9,11},{10,... | collective-permute-start | bytes 3080 | tf_op jit(solution)/shard_map/ppermute | solution.py:138
  13.2 27.9 %collective-permute-start.2 = (f32[256]{0:T(256)S(1)}, f32[256]{0:T(256)S(1)}, u32[]{:S(2)}, u32[]{:S(2)}) collective-permute-start(f32[256]{0:T(256)S(1)} %get-tuple-element.13), channel_id=1, source_target_pairs={{0,3},{1,2},{2,1},{3,0},{4,7},{5,6},{6,5},{7,4},{8,11},{9,10},{10,... | collective-permute-start | bytes 3080 | tf_op jit(solution)/shard_map/ppermute | solution.py:138
  14.4 3.6 %copy-start.3 = (s32[8]{0:T(128)S(1)}, s32[8]{0:T(128)}, u32[]{:S(2)}) copy-start(s32[8]{0:T(128)} %param.18) | copy-start | bytes 100
  14.4 3.9 %copy-start = (bf16[5120,256]{1,0:T(8,128)(2,1)S(1)}, bf16[5120,256]{1,0:T(8,128)(2,1)}, u32[]{:S(2)}) copy-start(bf16[5120,256]{1,0:T(8,128)(2,1)} %param.14) | copy-start | bytes 7864324
  20.0 2.2 %copy-start.4 = (bf16[256]{0:T(256)(128)(2,1)S(1)}, bf16[256]{0:T(256)(128)(2,1)}, u32[]{:S(2)}) copy-start(bf16[256]{0:T(256)(128)(2,1)} %param.16) | copy-start | bytes 1540
  20.0 2.2 %copy-start.5 = (bf16[256]{0:T(256)(128)(2,1)S(1)}, bf16[256]{0:T(256)(128)(2,1)}, u32[]{:S(2)}) copy-start(bf16[256]{0:T(256)(128)(2,1)} %param.17) | copy-start | bytes 1540
  26.0 19.1 %collective-permute-start.3 = (bf16[256,1280]{1,0:T(8,128)(2,1)S(1)}, bf16[256,1280]{1,0:T(8,128)(2,1)S(1)}, u32[]{:S(2)}, u32[]{:S(2)}) collective-permute-start(bf16[256,1280]{1,0:T(8,128)(2,1)S(1)} %get-tuple-element.12), channel_id=1, source_target_pairs={{0,1},{1,0},{2,3},{3,2},{4,5},{5,4},{6,7},{7,6},{8,9},{9,8},{10,11... | collective-permute-start | bytes 1966088 | tf_op jit(solution)/shard_map/ppermute | solution.py:155
  47.0 2.0 %copy-start.2 = (s32[16]{0:T(128)S(1)}, s32[16]{0:T(128)}, u32[]{:S(2)}) copy-start(s32[16]{0:T(128)} %param.19) | copy-start | bytes 196
  47.0 4.0 %copy-start.1 = (bf16[1280]{0:T(1024)(128)(2,1)S(1)}, bf16[1280]{0:T(1024)(128)(2,1)}, u32[]{:S(2)}) copy-start(bf16[1280]{0:T(1024)(128)(2,1)} %param.15) | copy-start | bytes 7684
Sparse Core Ops, SparseCore 0:
  49.1 29.7 all-gather.1

commit v7 on v6

--- a/solution.py
+++ b/solution.py
@@ -180,7 +180,29 @@
     q_live = q_seg < docs - 1
     q_grouped = query.reshape(rows, kv_dev, group, HEAD)
 
-    both = lax.all_gather(jnp.concatenate([key, value], axis=1), "blk", axis=0, tiled=True)
+    own_kv = jnp.concatenate([key, value], axis=1)
+    chips = blocks // 2
+    chip = me // 2
+    core = me % 2
+    rightward = [(i, i + 2) for i in range(blocks - 2)]
+    leftward = [(i, i - 2) for i in range(2, blocks)]
+    near = [own_kv] * (2 * chips - 1)
+    from_left = own_kv
+    from_right = own_kv
+    for step in range(1, chips):
+        from_left = lax.ppermute(from_left, "blk", rightward)
+        from_right = lax.ppermute(from_right, "blk", leftward)
+        near[chips - 1 - step] = from_left
+        near[chips - 1 + step] = from_right
+    same_core = lax.dynamic_slice_in_dim(jnp.stack(near, axis=0), chips - 1 - chip, chips, 0)
+    other_core = lax.ppermute(same_core, "blk", [(i, i ^ 1) for i in range(blocks)])
+    both = jnp.stack(
+        [
+            jnp.where(core == 0, same_core, other_core),
+            jnp.where(core == 0, other_core, same_core),
+        ],
+        axis=1,
+    ).reshape(blocks * rows, 2 * kv_width)
     count = both.shape[0]
     longest = count // 2
     span = min(count, longest + rows)

time: 98.9 us -> 102 us (1.031)
  starting transfers between devices: 6.4 us -> 25.5 us
  between operations: 15.6 us -> 2.46 us
  waiting for transfers between devices: 28.2 us -> 22.4 us
  local copies, waits for them, and re-layouts: 9.5 us -> 12.2 us
    ppermute x0 -> x7, starting transfers between devices: none -> 19.2 us  [the longest x3 9.59 us: on_device(): from_left = lax.ppermute(from_left, 'blk', rightward)]
    all_gather x1 -> x0, waiting for transfers between devices: 10.9 us -> none  [on_device(): lax.all_gather(jnp.concatenate([key, value], axis=1), 'blk', axis=0, tile...]
    ppermute x0 -> x7, waiting for transfers between devices: none -> 5.74 us  [the longest x3 5.72 us: on_device(): from_right = lax.ppermute(from_right, 'blk', leftward)]
    unnamed x13 -> x24, local copies, waits for them, and re-layouts: 3.65 us -> 6.05 us
    another operation x2 -> x4, other arithmetic: 0.36 us -> 1.92 us  [the longest x2 1.56 us: on_device(): jnp.stack([jnp.where(core == 0, same_core, other_core), jnp.where(core ==...]
    dynamic_slice x0 -> x1, local copies, waits for them, and re-layouts: none -> 1.04 us  [on_device(): lax.dynamic_slice_in_dim(jnp.stack(near, axis=0), chips - 1 - chip, chips...]
  transfers between devices with their start and end apart: 7 -> 13, of which waited for: 3 -> 4; matrix products, arithmetic and copies ran while one was open for 31% -> 29% of each run, Pallas kernels for 0% -> 0%
where the time goes in v7:
time: 102 us; the launch traced here: 101 us
  starting transfers between devices  25.5 us (25%)
  waiting for transfers between devices  22.4 us (22%)
  matrix products  20 us (20%)
  local copies, waits for them, and re-layouts  12.2 us (12%)
  Pallas kernels  9.78 us (10%)
  other arithmetic  8.43 us (8%)
  between operations  2.46 us (2%)
    dot_general x8, matrix products, project(): jnp.dot(chunk, lax.dynamic_slice_in_dim(weight, source * width, width, 0)...  20 us
    ppermute x3, waiting for transfers between devices, on_device(): squares = squares + lax.ppermute(part_sq, 'tp', perm)  16.6 us
    pallas_call x1, Pallas kernels, window_attention(): pl.pallas_call(kernel, grid_spec=spec, out_shape=jax.ShapeDtypeStruct((ro...  9.78 us
    ppermute x3, starting transfers between devices, on_device(): from_left = lax.ppermute(from_left, 'blk', rightward)  9.59 us
    ppermute x3, starting transfers between devices, on_device(): from_right = lax.ppermute(from_right, 'blk', leftward)  6.44 us
    unnamed x24, local copies, waits for them, and re-layouts  6.05 us
    ppermute x3, waiting for transfers between devices, on_device(): from_right = lax.ppermute(from_right, 'blk', leftward)  5.72 us
    ppermute x3, starting transfers between devices, on_device(): got = lax.ppermute(scaled, 'tp', perm)  3.71 us
  transfers between devices with their start and end apart: 13, of which 4 were waited for; matrix products, arithmetic and copies ran while one was open for 29% of the time, Pallas kernels for 0%

profile of v7, /device:TPU:9, one launch (start us, length us, event | category | flops | bytes accessed | tf_op | source)
XLA Modules:
  0.0 100.8 jit_solution(1711539969567718792)
XLA Ops:
  1.3 1.4 %fusion.18 = (bf16[256,1280]{1,0:T(8,128)(2,1)S(1)}, f32[256]{0:T(256)S(1)}) fusion(bf16[256,1280]{1,0:T(8,128)(2,1)} %param.10, f32[1280]{0:T(1024)S(1)} %convert_element_type.43), kind=kLoop, calls=%fused_computation.15 | loop fusion | flops 1638144 | bytes 1316864 | tf_op jit(solution)/shard_map/convert_element_type | solution.py:133
  2.7 2.2 %collective-permute-start.5 = (bf16[256,1280]{1,0:T(8,128)(2,1)S(1)}, bf16[256,1280]{1,0:T(8,128)(2,1)}, u32[]{:S(2)}, u32[]{:S(2)}) collective-permute-start(bf16[256,1280]{1,0:T(8,128)(2,1)S(1)} %get-tuple-element.14), channel_id=1, source_target_pairs={{0,3},{1,2},{2,1},{3,0},{4,7},{5,6},{6,5},{7,4},{8,11},{9,10},{10,... | collective-permute-start | bytes 1966088 | tf_op jit(solution)/shard_map/ppermute | solution.py:155
  8.5 3.6 %constant_dynamic-update-slice_fusion.1 = bf16[5120,512]{1,0:T(8,128)(2,1)} fusion(bf16[5120,256]{1,0:T(8,128)(2,1)} %param.13), kind=kLoop, calls=%fused_computation.64 | loop fusion | bytes 5242880
  12.5 1.7 %constant_dynamic-update-slice_fusion = bf16[5120,512]{1,0:T(8,128)(2,1)} fusion(bf16[5120,512]{1,0:T(8,128)(2,1)} %constant_dynamic-update-slice_fusion.1, bf16[5120,256]{1,0:T(8,128)(2,1)S(1)} %copy-done.3), kind=kLoop, calls=%fused_computation.63 | loop fusion | bytes 5242880 | tf_op jit(solution)/shard_map/concatenate | solution.py:139
  14.1 1.8 %fusion.25 = f32[256,512]{1,0:T(8,128)S(1)} fusion(bf16[256,1280]{1,0:T(8,128)(2,1)S(1)} %get-tuple-element.14, bf16[5120,512]{1,0:T(8,128)(2,1)} %constant_dynamic-update-slice_fusion, s32[]{:T(128)S(6)} %select_n.64), kind=kOutput, calls=%fused_computation.22 | convolution fusion | flops 335544320 | bytes 2490372 | tf_op jit(solution)/shard_map/dot_general | solution.py:145
  16.6 2.9 %collective-permute-done = f32[256]{0:T(256)S(1)} collective-permute-done((f32[256]{0:T(256)S(1)}, f32[256]{0:T(256)S(1)}, u32[]{:S(2)}, u32[]{:S(2)}) %collective-permute-start) | collective-permute-done | bytes 1056 | tf_op jit(solution)/shard_map/ppermute | solution.py:138
  20.7 13.8 %collective-permute-done.1 = f32[256]{0:T(256)S(1)} collective-permute-done((f32[256]{0:T(256)S(1)}, f32[256]{0:T(256)S(1)}, u32[]{:S(2)}, u32[]{:S(2)}) %collective-permute-start.1) | collective-permute-done | bytes 1056 | tf_op jit(solution)/shard_map/ppermute | solution.py:138
  34.5 2.0 %fusion.19 = f32[256,512]{1,0:T(8,128)S(1)} fusion(bf16[256,1280]{1,0:T(8,128)(2,1)} %collective-permute-done.5, bf16[5120,512]{1,0:T(8,128)(2,1)} %constant_dynamic-update-slice_fusion, s32[]{:T(128)S(6)} %select_n.67), kind=kOutput, calls=%fused_computation.16 | convolution fusion | flops 335544320 | bytes 2490372 | tf_op jit(solution)/shard_map/dot_general | solution.py:145
  36.5 2.0 %fusion.21 = f32[256,512]{1,0:T(8,128)S(1)} fusion(bf16[256,1280]{1,0:T(8,128)(2,1)} %collective-permute-done.4, bf16[5120,512]{1,0:T(8,128)(2,1)} %constant_dynamic-update-slice_fusion, s32[]{:T(128)S(6)} %select_n.66), kind=kOutput, calls=%fused_computation.18 | convolution fusion | flops 335544320 | bytes 2490372 | tf_op jit(solution)/shard_map/dot_general | solution.py:145
  38.6 1.8 %fusion.33 = f32[256,512]{1,0:T(8,128)S(1)} fusion(f32[256,512]{1,0:T(8,128)S(1)} %fusion.19, f32[256,512]{1,0:T(8,128)S(1)} %fusion.21, f32[256,512]{1,0:T(8,128)S(1)} %fusion.25, bf16[256,1280]{1,0:T(8,128)(2,1)S(1)} %collective-permute-done.3, bf16[5120,512]{1,0:T(8,128)(2,1)} %constant_dynamic-update-slice_fusion, s32[]{:T(128)S(6)} %select_n.65), kind=kOutput, calls=%fused_computation.27 | convolution fusion | flops 335937536 | bytes 4063236 | tf_op jit(solution)/shard_map/dot_general | solution.py:145
  41.7 3.2 %collective-permute-start.6 = (bf16[256,512]{1,0:T(8,128)(2,1)S(1)}, bf16[256,512]{1,0:T(8,128)(2,1)S(1)}, u32[]{:S(2)}, u32[]{:S(2)}) collective-permute-start(bf16[256,512]{1,0:T(8,128)(2,1)S(1)} %pad_maximum_fusion.3), channel_id=1, source_target_pairs={{0,8},{4,12},{8,16},{12,20},{16,24},{20,28},{1,9},{5,13},{9,17},{1... | collective-permute-start | bytes 786440 | tf_op jit(solution)/shard_map/ppermute | solution.py:193
  48.9 2.1 %collective-permute-start.9 = (bf16[256,512]{1,0:T(8,128)(2,1)S(1)}, bf16[256,512]{1,0:T(8,128)(2,1)S(1)}, u32[]{:S(2)}, u32[]{:S(2)}) collective-permute-start(bf16[256,512]{1,0:T(8,128)(2,1)S(1)} %pad_maximum_fusion.3), channel_id=1, source_target_pairs={{8,0},{12,4},{16,8},{20,12},{24,16},{28,20},{9,1},{13,5},{17,9},{2... | collective-permute-start | bytes 786440 | tf_op jit(solution)/shard_map/ppermute | solution.py:194
  51.0 3.2 %collective-permute-start.7 = (bf16[256,512]{1,0:T(8,128)(2,1)S(1)}, bf16[256,512]{1,0:T(8,128)(2,1)S(1)}, u32[]{:S(2)}, u32[]{:S(2)}) collective-permute-start(bf16[256,512]{1,0:T(8,128)(2,1)S(1)} %collective-permute-done.6), channel_id=1, source_target_pairs={{0,8},{4,12},{8,16},{12,20},{16,24},{20,28},{1,9},{5,13},{9,17},{1... | collective-permute-start | bytes 786440 | tf_op jit(solution)/shard_map/ppermute | solution.py:193
  54.2 2.9 %fusion.6 = f32[256,1280]{1,0:T(8,128)S(1)} fusion(bf16[256,1280]{1,0:T(8,128)(2,1)S(1)} %get-tuple-element.14, bf16[5120,1280]{1,0:T(8,128)(2,1)} %param.12, s32[]{:T(128)S(6)} %select_n.64), kind=kOutput, calls=%fused_computation.6 | convolution fusion | flops 838860800 | bytes 5242884 | tf_op jit(solution)/shard_map/dot_general | solution.py:145
  57.9 2.1 %collective-permute-start.10 = (bf16[256,512]{1,0:T(8,128)(2,1)S(1)}, bf16[256,512]{1,0:T(8,128)(2,1)S(1)}, u32[]{:S(2)}, u32[]{:S(2)}) collective-permute-start(bf16[256,512]{1,0:T(8,128)(2,1)S(1)} %collective-permute-done.9), channel_id=1, source_target_pairs={{8,0},{12,4},{16,8},{20,12},{24,16},{28,20},{9,1},{13,5},{17,9},{2... | collective-permute-start | bytes 786440 | tf_op jit(solution)/shard_map/ppermute | solution.py:194
  60.0 3.2 %collective-permute-start.8 = (bf16[256,512]{1,0:T(8,128)(2,1)S(1)}, bf16[256,512]{1,0:T(8,128)(2,1)S(1)}, u32[]{:S(2)}, u32[]{:S(2)}) collective-permute-start(bf16[256,512]{1,0:T(8,128)(2,1)S(1)} %collective-permute-done.7), channel_id=1, source_target_pairs={{0,8},{4,12},{8,16},{12,20},{16,24},{20,28},{1,9},{5,13},{9,17},{1... | collective-permute-start | bytes 786440 | tf_op jit(solution)/shard_map/ppermute | solution.py:193
  63.2 3.2 %fusion = f32[256,1280]{1,0:T(8,128)S(1)} fusion(bf16[256,1280]{1,0:T(8,128)(2,1)} %collective-permute-done.5, bf16[5120,1280]{1,0:T(8,128)(2,1)} %param.12, s32[]{:T(128)S(6)} %select_n.67), kind=kOutput, calls=%fused_computation | convolution fusion | flops 838860800 | bytes 5242884 | tf_op jit(solution)/shard_map/dot_general | solution.py:145
  66.3 2.3 %collective-permute-start.11 = (bf16[256,512]{1,0:T(8,128)(2,1)S(1)}, bf16[256,512]{1,0:T(8,128)(2,1)S(1)}, u32[]{:S(2)}, u32[]{:S(2)}) collective-permute-start(bf16[256,512]{1,0:T(8,128)(2,1)S(1)} %collective-permute-done.10), channel_id=1, source_target_pairs={{8,0},{12,4},{16,8},{20,12},{24,16},{28,20},{9,1},{13,5},{17,9},{2... | collective-permute-start | bytes 786440 | tf_op jit(solution)/shard_map/ppermute | solution.py:194
  68.8 5.0 %collective-permute-done.11 = bf16[256,512]{1,0:T(8,128)(2,1)S(1)} collective-permute-done((bf16[256,512]{1,0:T(8,128)(2,1)S(1)}, bf16[256,512]{1,0:T(8,128)(2,1)S(1)}, u32[]{:S(2)}, u32[]{:S(2)}) %collective-permute-start.11) | collective-permute-done | bytes 262176 | tf_op jit(solution)/shard_map/ppermute | solution.py:194
  76.1 3.1 %collective-permute-start.12 = (bf16[4,256,512]{2,1,0:T(8,128)(2,1)}, bf16[4,256,512]{2,1,0:T(8,128)(2,1)}, u32[]{:S(2)}, u32[]{:S(2)}) collective-permute-start(bf16[4,256,512]{2,1,0:T(8,128)(2,1)} %constant_dynamic-slice_fusion), channel_id=1, source_target_pairs={{0,4},{4,0},{8,12},{12,8},{16,20},{20,16},{24,28},{28,24},{1,5},{5... | collective-permute-start | bytes 3145736 | tf_op jit(solution)/shard_map/ppermute | solution.py:198
  79.3 3.2 %fusion.2 = f32[256,1280]{1,0:T(8,128)S(1)} fusion(bf16[256,1280]{1,0:T(8,128)(2,1)} %collective-permute-done.4, bf16[5120,1280]{1,0:T(8,128)(2,1)} %param.12, s32[]{:T(128)S(6)} %select_n.66), kind=kOutput, calls=%fused_computation.2 | convolution fusion | flops 838860800 | bytes 5242884 | tf_op jit(solution)/shard_map/dot_general | solution.py:145
  82.4 3.1 %multiply_add_fusion = f32[256,1280]{1,0:T(8,128)S(1)} fusion(f32[1280]{0:T(1024)S(1)} %convert_element_type.45, f32[256]{0:T(256)S(1)} %add_rsqrt_fusion, f32[256,1280]{1,0:T(8,128)S(1)} %fusion, f32[256,1280]{1,0:T(8,128)S(1)} %fusion.2, f32[256,1280]{1,0:T(8,128)S(1)} %fusion.6, bf16[256,1280]{1,0:T(8,128)(2,1)S(1)} %collective-permute-done.3, ...), kind=kOutput, calls=%fused_computation.24 | convolution fusion | flops 840499200 | bytes 9181188 | tf_op jit(solution)/shard_map/dot_general | solution.py:145
  87.8 1.4 %select_bitcast_fusion.1 = (bf16[4,1,256,512]{3,2,0,1:T(8,128)(2,1)S(1)}, bf16[4,1,256,512]{3,2,0,1:T(8,128)(2,1)S(1)}) fusion(bf16[4,256,512]{2,1,0:T(8,128)(2,1)} %collective-permute-done.12, pred[]{:T(512)S(6)} %eq.18, bf16[7,256,512]{2,1,0:T(8,128)(2,1)S(1)} %copy-done.2, s32[]{:T(128)S(6)} %select_n.73), kind=kLoop, calls=%fused_computation.29 | loop fusion | flops 1048576 | bytes 4194309 | tf_op jit(solution)/shard_map/stack | solution.py:199
  91.0 9.8 %shard_map.113 = bf16[256,1280]{1,0:T(8,128)(2,1)} custom-call(s32[1]{0:T(128)} %bitcast.first_ref, bf16[256,1280]{1,0:T(8,128)(2,1)} %copy.23.q_ref, bf16[2048,512]{1,0:T(8,128)(2,1)} %bitcast.51, bf16[2048,512]{1,0:T(8,128)(2,1)} %bitcast.52, s32[256,1]{1,0:T(8,128)} %copy.24.qs_ref, s32[256,1]{1,0:T(8,128)} %iota_add_fusion.qp_ref, ...), custom_call_target="tpu_custom_call" | custom-call | tf_op jit(solution)/shard_map/pallas_call | solution.py:94
  (77 shorter events, 17.5 us)
Async XLA Ops:
  2.7 31.8 %collective-permute-start.5 = (bf16[256,1280]{1,0:T(8,128)(2,1)S(1)}, bf16[256,1280]{1,0:T(8,128)(2,1)}, u32[]{:S(2)}, u32[]{:S(2)}) collective-permute-start(bf16[256,1280]{1,0:T(8,128)(2,1)S(1)} %get-tuple-element.14), channel_id=1, source_target_pairs={{0,3},{1,2},{2,1},{3,0},{4,7},{5,6},{6,5},{7,4},{8,11},{9,10},{10,... | collective-permute-start | bytes 1966088 | tf_op jit(solution)/shard_map/ppermute | solution.py:155
  4.9 31.6 %collective-permute-start.4 = (bf16[256,1280]{1,0:T(8,128)(2,1)S(1)}, bf16[256,1280]{1,0:T(8,128)(2,1)}, u32[]{:S(2)}, u32[]{:S(2)}) collective-permute-start(bf16[256,1280]{1,0:T(8,128)(2,1)S(1)} %get-tuple-element.14), channel_id=1, source_target_pairs={{0,2},{1,3},{2,0},{3,1},{4,6},{5,7},{6,4},{7,5},{8,10},{9,11},{10,... | collective-permute-start | bytes 1966088 | tf_op jit(solution)/shard_map/ppermute | solution.py:155
  5.1 14.3 %collective-permute-start = (f32[256]{0:T(256)S(1)}, f32[256]{0:T(256)S(1)}, u32[]{:S(2)}, u32[]{:S(2)}) collective-permute-start(f32[256]{0:T(256)S(1)} %get-tuple-element.15), channel_id=1, source_target_pairs={{0,1},{1,0},{2,3},{3,2},{4,5},{5,4},{6,7},{7,6},{8,9},{9,8},{10,11... | collective-permute-start | bytes 3080 | tf_op jit(solution)/shard_map/ppermute | solution.py:138
  5.4 29.1 %collective-permute-start.1 = (f32[256]{0:T(256)S(1)}, f32[256]{0:T(256)S(1)}, u32[]{:S(2)}, u32[]{:S(2)}) collective-permute-start(f32[256]{0:T(256)S(1)} %get-tuple-element.15), channel_id=1, source_target_pairs={{0,2},{1,3},{2,0},{3,1},{4,6},{5,7},{6,4},{7,5},{8,10},{9,11},{10,... | collective-permute-start | bytes 3080 | tf_op jit(solution)/shard_map/ppermute | solution.py:138
  6.6 27.9 %collective-permute-start.2 = (f32[256]{0:T(256)S(1)}, f32[256]{0:T(256)S(1)}, u32[]{:S(2)}, u32[]{:S(2)}) collective-permute-start(f32[256]{0:T(256)S(1)} %get-tuple-element.15), channel_id=1, source_target_pairs={{0,3},{1,2},{2,1},{3,0},{4,7},{5,6},{6,5},{7,4},{8,11},{9,10},{10,... | collective-permute-start | bytes 3080 | tf_op jit(solution)/shard_map/ppermute | solution.py:138
  8.5 3.6 %copy-start.6 = (s32[8]{0:T(128)S(1)}, s32[8]{0:T(128)}, u32[]{:S(2)}) copy-start(s32[8]{0:T(128)} %param.18) | copy-start | bytes 100
  8.5 4.0 %copy-start.3 = (bf16[5120,256]{1,0:T(8,128)(2,1)S(1)}, bf16[5120,256]{1,0:T(8,128)(2,1)}, u32[]{:S(2)}) copy-start(bf16[5120,256]{1,0:T(8,128)(2,1)} %param.14) | copy-start | bytes 7864324
  14.1 2.2 %copy-start.7 = (bf16[256]{0:T(256)(128)(2,1)S(1)}, bf16[256]{0:T(256)(128)(2,1)}, u32[]{:S(2)}) copy-start(bf16[256]{0:T(256)(128)(2,1)} %param.16) | copy-start | bytes 1540
  14.1 2.2 %copy-start.8 = (bf16[256]{0:T(256)(128)(2,1)S(1)}, bf16[256]{0:T(256)(128)(2,1)}, u32[]{:S(2)}) copy-start(bf16[256]{0:T(256)(128)(2,1)} %param.17) | copy-start | bytes 1540
  19.5 19.1 %collective-permute-start.3 = (bf16[256,1280]{1,0:T(8,128)(2,1)S(1)}, bf16[256,1280]{1,0:T(8,128)(2,1)S(1)}, u32[]{:S(2)}, u32[]{:S(2)}) collective-permute-start(bf16[256,1280]{1,0:T(8,128)(2,1)S(1)} %get-tuple-element.14), channel_id=1, source_target_pairs={{0,1},{1,0},{2,3},{3,2},{4,5},{5,4},{6,7},{7,6},{8,9},{9,8},{10,11... | collective-permute-start | bytes 1966088 | tf_op jit(solution)/shard_map/ppermute | solution.py:155
  40.4 4.5 %copy-start.5 = (s32[16]{0:T(128)S(1)}, s32[16]{0:T(128)}, u32[]{:S(2)}) copy-start(s32[16]{0:T(128)} %param.19) | copy-start | bytes 196
  40.4 6.5 %copy-start.4 = (bf16[1280]{0:T(1024)(128)(2,1)S(1)}, bf16[1280]{0:T(1024)(128)(2,1)}, u32[]{:S(2)}) copy-start(bf16[1280]{0:T(1024)(128)(2,1)} %param.15) | copy-start | bytes 7684
  41.7 9.3 %collective-permute-start.6 = (bf16[256,512]{1,0:T(8,128)(2,1)S(1)}, bf16[256,512]{1,0:T(8,128)(2,1)S(1)}, u32[]{:S(2)}, u32[]{:S(2)}) collective-permute-start(bf16[256,512]{1,0:T(8,128)(2,1)S(1)} %pad_maximum_fusion.3), channel_id=1, source_target_pairs={{0,8},{4,12},{8,16},{12,20},{16,24},{20,28},{1,9},{5,13},{9,17},{1... | collective-permute-start | bytes 786440 | tf_op jit(solution)/shard_map/ppermute | solution.py:193
  48.9 9.0 %collective-permute-start.9 = (bf16[256,512]{1,0:T(8,128)(2,1)S(1)}, bf16[256,512]{1,0:T(8,128)(2,1)S(1)}, u32[]{:S(2)}, u32[]{:S(2)}) collective-permute-start(bf16[256,512]{1,0:T(8,128)(2,1)S(1)} %pad_maximum_fusion.3), channel_id=1, source_target_pairs={{8,0},{12,4},{16,8},{20,12},{24,16},{28,20},{9,1},{13,5},{17,9},{2... | collective-permute-start | bytes 786440 | tf_op jit(solution)/shard_map/ppermute | solution.py:194
  51.0 8.9 %collective-permute-start.7 = (bf16[256,512]{1,0:T(8,128)(2,1)S(1)}, bf16[256,512]{1,0:T(8,128)(2,1)S(1)}, u32[]{:S(2)}, u32[]{:S(2)}) collective-permute-start(bf16[256,512]{1,0:T(8,128)(2,1)S(1)} %collective-permute-done.6), channel_id=1, source_target_pairs={{0,8},{4,12},{8,16},{12,20},{16,24},{20,28},{1,9},{5,13},{9,17},{1... | collective-permute-start | bytes 786440 | tf_op jit(solution)/shard_map/ppermute | solution.py:193
  57.9 8.5 %collective-permute-start.10 = (bf16[256,512]{1,0:T(8,128)(2,1)S(1)}, bf16[256,512]{1,0:T(8,128)(2,1)S(1)}, u32[]{:S(2)}, u32[]{:S(2)}) collective-permute-start(bf16[256,512]{1,0:T(8,128)(2,1)S(1)} %collective-permute-done.9), channel_id=1, source_target_pairs={{8,0},{12,4},{16,8},{20,12},{24,16},{28,20},{9,1},{13,5},{17,9},{2... | collective-permute-start | bytes 786440 | tf_op jit(solution)/shard_map/ppermute | solution.py:194
  60.0 8.7 %collective-permute-start.8 = (bf16[256,512]{1,0:T(8,128)(2,1)S(1)}, bf16[256,512]{1,0:T(8,128)(2,1)S(1)}, u32[]{:S(2)}, u32[]{:S(2)}) collective-permute-start(bf16[256,512]{1,0:T(8,128)(2,1)S(1)} %collective-permute-done.7), channel_id=1, source_target_pairs={{0,8},{4,12},{8,16},{12,20},{16,24},{20,28},{1,9},{5,13},{9,17},{1... | collective-permute-start | bytes 786440 | tf_op jit(solution)/shard_map/ppermute | solution.py:193
  66.3 7.5 %collective-permute-start.11 = (bf16[256,512]{1,0:T(8,128)(2,1)S(1)}, bf16[256,512]{1,0:T(8,128)(2,1)S(1)}, u32[]{:S(2)}, u32[]{:S(2)}) collective-permute-start(bf16[256,512]{1,0:T(8,128)(2,1)S(1)} %collective-permute-done.10), channel_id=1, source_target_pairs={{8,0},{12,4},{16,8},{20,12},{24,16},{28,20},{9,1},{13,5},{17,9},{2... | collective-permute-start | bytes 786440 | tf_op jit(solution)/shard_map/ppermute | solution.py:194
  73.8 1.3 %copy-start.1 = (bf16[7,256,512]{2,1,0:T(8,128)(2,1)}, bf16[7,256,512]{2,1,0:T(8,128)(2,1)S(1)}, u32[]{:S(2)}) copy-start(bf16[7,256,512]{2,1,0:T(8,128)(2,1)S(1)} %bitcast_dynamic-update-slice_fusion) | copy-start | bytes 5505028
  76.1 11.1 %collective-permute-start.12 = (bf16[4,256,512]{2,1,0:T(8,128)(2,1)}, bf16[4,256,512]{2,1,0:T(8,128)(2,1)}, u32[]{:S(2)}, u32[]{:S(2)}) collective-permute-start(bf16[4,256,512]{2,1,0:T(8,128)(2,1)} %constant_dynamic-slice_fusion), channel_id=1, source_target_pairs={{0,4},{4,0},{8,12},{12,8},{16,20},{20,16},{24,28},{28,24},{1,5},{5... | collective-permute-start | bytes 3145736 | tf_op jit(solution)/shard_map/ppermute | solution.py:198
  86.1 1.7 %copy-start.2 = (bf16[7,256,512]{2,1,0:T(8,128)(2,1)S(1)}, bf16[7,256,512]{2,1,0:T(8,128)(2,1)}, u32[]{:S(2)}) copy-start(bf16[7,256,512]{2,1,0:T(8,128)(2,1)} %copy-done.1) | copy-start | bytes 5505028
  89.6 1.4 %copy-start = (bf16[4,2,256,512]{3,2,1,0:T(8,128)(2,1)}, bf16[4,2,256,512]{3,2,1,0:T(8,128)(2,1)S(1)}, u32[]{:S(2)}) copy-start(bf16[4,2,256,512]{3,2,1,0:T(8,128)(2,1)S(1)} %copy.22) | copy-start | bytes 6291460

commit v8 on v6

--- a/solution.py
+++ b/solution.py
@@ -134,8 +134,6 @@
     part_sq = jnp.sum(wide * wide, axis=1)
     parts = lax.axis_size("tp")
     squares = part_sq
-    for flip, perm in partners(parts):
-        squares = squares + lax.ppermute(part_sq, "tp", perm)
     w_kv = jnp.concatenate([w_key, w_value], axis=1)
     width = tokens.shape[1]
     mine = lax.axis_index("tp")
@@ -151,9 +149,15 @@
         ]
 
     proj_kv, proj_query = project(scaled, mine)
+    extended = jnp.concatenate(
+        [tokens, norm_gain[None, :], jnp.zeros((15, width), tokens.dtype)], axis=0
+    )
     for flip, perm in partners(parts):
-        got = lax.ppermute(scaled, "tp", perm)
-        more = project(got, flip(mine))
+        got = lax.ppermute(extended, "tp", perm)
+        got_wide = got[:rows].astype(jnp.float32)
+        squares = squares + jnp.sum(got_wide * got_wide, axis=1)
+        got_scaled = (got_wide * got[rows].astype(jnp.float32)[None, :]).astype(jnp.bfloat16)
+        more = project(got_scaled, flip(mine))
         proj_kv = proj_kv + more[0]
         proj_query = proj_query + more[1]
     proj_key = proj_kv[:, :kv_width]

time: 98.9 us -> 105 us (1.062)
  other arithmetic: 7.49 us -> 13.2 us
  waiting for transfers between devices: 28.2 us -> 32 us
  starting transfers between devices: 6.4 us -> 2.69 us
  matrix products: 20.3 us -> 18.8 us
    reduce_sum x0 -> x4, other arithmetic: none -> 4.09 us  [the longest x3 2.8 us: on_device(): squares = squares + jnp.sum(got_wide * got_wide, axis=1)]
    ppermute x6 -> x3, starting transfers between devices: 6.36 us -> 2.65 us  [on_device(): got = lax.ppermute(extended, 'tp', perm)]
    ppermute x6 -> x3, waiting for transfers between devices: 17.4 us -> 21.1 us  [on_device(): got = lax.ppermute(extended, 'tp', perm)]
    concatenate x0 -> x1, other arithmetic: none -> 2.14 us  [on_device(): jnp.concatenate([tokens, norm_gain[None, :], jnp.zeros((15, width), token...]
    convert_element_type x2 -> x1, other arithmetic: 2.05 us -> 0.01 us  [on_device(): scaled = (wide * norm_gain.astype(jnp.float32)).astype(jnp.bfloat16)]
    mul x0 -> x3, other arithmetic: none -> 1.52 us  [on_device(): got_wide * got[rows].astype(jnp.float32)[None, :]]
    dot_general x8, matrix products: 20.3 us -> 18.8 us  [project(): jnp.dot(chunk, lax.dynamic_slice_in_dim(weight, source * width, width, 0)...]
    unnamed x13 -> x19, local copies, waits for them, and re-layouts: 3.65 us -> 3.64 us
  transfers between devices with their start and end apart: 7 -> 4, of which waited for: 3 -> 3; matrix products, arithmetic and copies ran while one was open for 31% -> 28% of each run, Pallas kernels for 0% -> 0%
where the time goes in v8:
time: 105 us; the launch traced here: 103 us
  waiting for transfers between devices  32 us (30%)
  matrix products  18.8 us (18%)
  between operations  15.7 us (15%)
  other arithmetic  13.2 us (13%)
  local copies, waits for them, and re-layouts  10.2 us (10%)
  Pallas kernels  10 us (10%)
  starting transfers between devices  2.69 us (3%)
    ppermute x3, waiting for transfers between devices, on_device(): got = lax.ppermute(extended, 'tp', perm)  21.1 us
    dot_general x8, matrix products, project(): jnp.dot(chunk, lax.dynamic_slice_in_dim(weight, source * width, width, 0)...  18.8 us
    all_gather x1, waiting for transfers between devices, on_device(): lax.all_gather(jnp.concatenate([key, value], axis=1), 'blk', axis=0, tile...  11 us
    pallas_call x1, Pallas kernels, window_attention(): pl.pallas_call(kernel, grid_spec=spec, out_shape=jax.ShapeDtypeStruct((ro...  10 us
    unnamed x19, local copies, waits for them, and re-layouts  3.64 us
    reduce_sum x3, other arithmetic, on_device(): squares = squares + jnp.sum(got_wide * got_wide, axis=1)  2.8 us
    ppermute x3, starting transfers between devices, on_device(): got = lax.ppermute(extended, 'tp', perm)  2.65 us
    concatenate x1, other arithmetic, on_device(): jnp.concatenate([tokens, norm_gain[None, :], jnp.zeros((15, width), token...  2.14 us
  transfers between devices with their start and end apart: 4, of which 3 were waited for; matrix products, arithmetic and copies ran while one was open for 28% of the time, Pallas kernels for 0%

profile of v8, /device:TPU:9, one launch (start us, length us, event | category | flops | bytes accessed | tf_op | source)
XLA Modules:
  0.0 102.7 jit_solution(1348963043716152832)
XLA Ops:
  8.0 2.1 %maximum_maximum_fusion = bf16[272,1280]{1,0:T(8,128)(2,1)} fusion(bf16[1,1280]{1,0:T(2,128)(2,1)S(1)} %broadcast_in_dim.20, bf16[256,1280]{1,0:T(8,128)(2,1)} %param.10, bf16[272]{0:T(512)(128)(2,1)S(1)} %pad.14.clone), kind=kLoop, calls=%fused_computation.40 | loop fusion | flops 2088960 | bytes 1354784 | tf_op jit(solution)/shard_map/concatenate | solution.py:152
  10.1 2.2 %collective-permute-start.2 = (bf16[272,1280]{1,0:T(8,128)(2,1)}, bf16[272,1280]{1,0:T(8,128)(2,1)}, u32[]{:S(2)}, u32[]{:S(2)}) collective-permute-start(bf16[272,1280]{1,0:T(8,128)(2,1)} %maximum_maximum_fusion), channel_id=1, source_target_pairs={{0,3},{1,2},{2,1},{3,0},{4,7},{5,6},{6,5},{7,4},{8,11},{9,10},{10,... | collective-permute-start | bytes 2088968 | tf_op jit(solution)/shard_map/ppermute | solution.py:156
  12.8 3.6 %constant_dynamic-update-slice_fusion.1 = bf16[5120,512]{1,0:T(8,128)(2,1)} fusion(bf16[5120,256]{1,0:T(8,128)(2,1)} %param.13), kind=kLoop, calls=%fused_computation.73 | loop fusion | bytes 5242880
  16.7 1.7 %constant_dynamic-update-slice_fusion = bf16[5120,512]{1,0:T(8,128)(2,1)} fusion(bf16[5120,512]{1,0:T(8,128)(2,1)} %constant_dynamic-update-slice_fusion.1, bf16[5120,256]{1,0:T(8,128)(2,1)S(1)} %copy-done.1), kind=kLoop, calls=%fused_computation.72 | loop fusion | bytes 5242880 | tf_op jit(solution)/shard_map/concatenate | solution.py:137
  19.0 1.3 %fusion.23 = f32[256]{0:T(256)S(1)} fusion(bf16[256,1280]{1,0:T(8,128)(2,1)} %param.10), kind=kLoop, calls=%fused_computation.21 | loop fusion | flops 982784 | bytes 656384 | tf_op jit(solution)/shard_map/reduce_sum | solution.py:134
  20.3 2.2 %fusion.37 = f32[256,512]{1,0:T(8,128)S(1)} fusion(bf16[5120,512]{1,0:T(8,128)(2,1)} %constant_dynamic-update-slice_fusion, s32[]{:T(128)S(6)} %select_n.38, bf16[256,1280]{1,0:T(8,128)(2,1)} %param.10, f32[1280]{0:T(1024)S(1)} %convert_element_type.70), kind=kOutput, calls=%fused_computation.35 | convolution fusion | flops 336527360 | bytes 2495492 | tf_op jit(solution)/shard_map/dot_general | solution.py:143
  22.5 20.3 %collective-permute-done = bf16[272,1280]{1,0:T(8,128)(2,1)S(1)} collective-permute-done((bf16[272,1280]{1,0:T(8,128)(2,1)}, bf16[272,1280]{1,0:T(8,128)(2,1)S(1)}, u32[]{:S(2)}, u32[]{:S(2)}) %collective-permute-start) | collective-permute-done | bytes 696352 | tf_op jit(solution)/shard_map/ppermute | solution.py:156
  43.1 0.7 collective-permute-done.1
  43.8 1.3 %fusion.27 = f32[256]{0:T(256)S(1)} fusion(bf16[272,1280]{1,0:T(8,128)(2,1)} %collective-permute-done.1), kind=kLoop, calls=%fused_computation.25 | loop fusion | flops 982784 | bytes 656384 | tf_op jit(solution)/shard_map/reduce_sum | solution.py:158
  45.1 1.3 %fusion.29 = f32[256]{0:T(256)S(1)} fusion(bf16[272,1280]{1,0:T(8,128)(2,1)} %collective-permute-done.2), kind=kLoop, calls=%fused_computation.27 | loop fusion | flops 982784 | bytes 656384 | tf_op jit(solution)/shard_map/reduce_sum | solution.py:158
  46.4 0.8 fusion.63
  47.2 0.7 fusion.64
  47.9 2.0 %fusion.31 = f32[256,512]{1,0:T(8,128)S(1)} fusion(bf16[5120,512]{1,0:T(8,128)(2,1)} %constant_dynamic-update-slice_fusion, s32[]{:T(128)S(6)} %select_n.41, f32[1280]{0:T(1024)S(1)} %fusion.63, bf16[272,1280]{1,0:T(8,128)(2,1)} %collective-permute-done.2), kind=kOutput, calls=%fused_computation.29 | convolution fusion | flops 336527360 | bytes 2495492 | tf_op jit(solution)/shard_map/dot_general | solution.py:143
  50.0 1.6 %fusion.33 = f32[256,512]{1,0:T(8,128)S(1)} fusion(bf16[5120,512]{1,0:T(8,128)(2,1)S(1)} %copy-done, s32[]{:T(128)S(6)} %select_n.40, f32[1280]{0:T(1024)S(1)} %fusion.64, bf16[272,1280]{1,0:T(8,128)(2,1)} %collective-permute-done.1), kind=kOutput, calls=%fused_computation.31 | convolution fusion | flops 336527360 | bytes 2498564 | tf_op jit(solution)/shard_map/dot_general | solution.py:143
  56.2 0.8 copy.21.qs_ref
  58.9 3.0 %fusion.6 = f32[256,1280]{1,0:T(8,128)S(1)} fusion(bf16[5120,1280]{1,0:T(8,128)(2,1)} %param.12, s32[]{:T(128)S(6)} %select_n.38, bf16[256,1280]{1,0:T(8,128)(2,1)S(1)} %copy-done.2, f32[1280]{0:T(1024)S(1)} %convert_element_type.70), kind=kOutput, calls=%fused_computation.6 | convolution fusion | flops 839843840 | bytes 5248004 | tf_op jit(solution)/shard_map/dot_general | solution.py:143
  61.9 3.4 %fusion.2 = f32[256,1280]{1,0:T(8,128)S(1)} fusion(bf16[5120,1280]{1,0:T(8,128)(2,1)} %param.12, s32[]{:T(128)S(6)} %select_n.40, f32[1280]{0:T(1024)S(1)} %fusion.64, bf16[272,1280]{1,0:T(8,128)(2,1)} %collective-permute-done.1), kind=kOutput, calls=%fused_computation.2 | convolution fusion | flops 839843840 | bytes 5248004 | tf_op jit(solution)/shard_map/dot_general | solution.py:143
  65.3 3.0 %fusion.17 = f32[256,1280]{1,0:T(8,128)S(1)} fusion(f32[256,1280]{1,0:T(8,128)S(1)} %fusion.2, f32[256,1280]{1,0:T(8,128)S(1)} %fusion.6, bf16[5120,1280]{1,0:T(8,128)(2,1)} %param.12, s32[]{:T(128)S(6)} %select_n.39, f32[1280]{0:T(1024)S(1)} %fusion.65, bf16[272,1280]{1,0:T(8,128)(2,1)S(1)} %collective-permute-done), kind=kOutput, calls=%fused_computation.11 | convolution fusion | flops 840499200 | bytes 7872516 | tf_op jit(solution)/shard_map/dot_general | solution.py:143
  68.2 3.2 %fusion.20 = f32[256,1280]{1,0:T(8,128)S(1)} fusion(f32[256,1280]{1,0:T(8,128)S(1)} %fusion.17, bf16[5120,1280]{1,0:T(8,128)(2,1)} %param.12, s32[]{:T(128)S(6)} %select_n.41, f32[1280]{0:T(1024)S(1)} %convert_element_type.75, f32[256]{0:T(256)S(1)} %add_rsqrt_fusion, f32[1280]{0:T(1024)S(1)} %fusion.63, bf16[272,1280]{1,0:T(8,128)(2,1)} %collective-permute-done.2), kind=kOutput, calls=%fused_computation.12 | convolution fusion | flops 840826880 | bytes 6564868 | tf_op jit(solution)/shard_map/dot_general | solution.py:143
  72.1 1.1 %copy.20.q_ref = bf16[256,1280]{1,0:T(8,128)(2,1)} copy(bf16[256,1280]{0,1:T(8,128)(2,1)S(1)} %bitcast.24) | data formatting | bytes 1310720 | tf_op jit(solution)/shard_map/convert_element_type | solution.py:175
  73.2 11.0 %all-gather.2.cloned.1.call-done.k_ref.v_ref = bf16[2048,512]{1,0:T(8,128)(2,1)} async-done(((bf16[256,512]{1,0:T(8,128)(2,1)}), bf16[2048,512]{1,0:T(8,128)(2,1)}) %all-gather.2.cloned.1.call-update) | async-done | bytes 2097168 | tf_op jit(solution)/shard_map/all_gather | solution.py:187
  84.1 1.0 dynamic-slice_bitcast_fusion.3
  85.1 0.7 pad_maximum_fusion.3
  85.9 10.0 %shard_map.113 = bf16[256,1280]{1,0:T(8,128)(2,1)} custom-call(s32[1]{0:T(128)} %bitcast.first_ref, bf16[256,1280]{1,0:T(8,128)(2,1)} %copy.20.q_ref, bf16[2048,512]{1,0:T(8,128)(2,1)} %all-gather.2.cloned.1.call-done.k_ref.v_ref, bf16[2048,512]{1,0:T(8,128)(2,1)} %all-gather.2.cloned.1.call-done.k_ref.v_ref, s32[256,1]{1,0:T(8,128)} %copy.21.qs_ref, ...), custom_call_target="tpu_custom_call" | custom-call | tf_op jit(solution)/shard_map/pallas_call | solution.py:94
  (59 shorter events, 8.2 us)
Async XLA Ops:
  7.2 77.0 %all-gather.2.cloned.1.call-start = ((), (), s32[]{:S(2)}) async-start(), calls=%async_computation | async-start | bytes 2359296 | tf_op jit(solution)/shard_map/all_gather | solution.py:187
  10.1 35.0 %collective-permute-start.2 = (bf16[272,1280]{1,0:T(8,128)(2,1)}, bf16[272,1280]{1,0:T(8,128)(2,1)}, u32[]{:S(2)}, u32[]{:S(2)}) collective-permute-start(bf16[272,1280]{1,0:T(8,128)(2,1)} %maximum_maximum_fusion), channel_id=1, source_target_pairs={{0,3},{1,2},{2,1},{3,0},{4,7},{5,6},{6,5},{7,4},{8,11},{9,10},{10,... | collective-permute-start | bytes 2088968 | tf_op jit(solution)/shard_map/ppermute | solution.py:156
  12.3 31.5 %collective-permute-start.1 = (bf16[272,1280]{1,0:T(8,128)(2,1)}, bf16[272,1280]{1,0:T(8,128)(2,1)}, u32[]{:S(2)}, u32[]{:S(2)}) collective-permute-start(bf16[272,1280]{1,0:T(8,128)(2,1)} %maximum_maximum_fusion), channel_id=1, source_target_pairs={{0,2},{1,3},{2,0},{3,1},{4,6},{5,7},{6,4},{7,5},{8,10},{9,11},{10,... | collective-permute-start | bytes 2088968 | tf_op jit(solution)/shard_map/ppermute | solution.py:156
  12.5 30.3 %collective-permute-start = (bf16[272,1280]{1,0:T(8,128)(2,1)}, bf16[272,1280]{1,0:T(8,128)(2,1)S(1)}, u32[]{:S(2)}, u32[]{:S(2)}) collective-permute-start(bf16[272,1280]{1,0:T(8,128)(2,1)} %maximum_maximum_fusion), channel_id=1, source_target_pairs={{0,1},{1,0},{2,3},{3,2},{4,5},{5,4},{6,7},{7,6},{8,9},{9,8},{10,11... | collective-permute-start | bytes 2088968 | tf_op jit(solution)/shard_map/ppermute | solution.py:156
  12.8 3.6 %copy-start.6 = (s32[8]{0:T(128)S(1)}, s32[8]{0:T(128)}, u32[]{:S(2)}) copy-start(s32[8]{0:T(128)} %param.18) | copy-start | bytes 100
  12.8 3.9 %copy-start.1 = (bf16[5120,256]{1,0:T(8,128)(2,1)S(1)}, bf16[5120,256]{1,0:T(8,128)(2,1)}, u32[]{:S(2)}) copy-start(bf16[5120,256]{1,0:T(8,128)(2,1)} %param.14) | copy-start | bytes 7864324
  16.7 2.1 %copy-start.3 = (bf16[1280]{0:T(1024)(128)(2,1)S(1)}, bf16[1280]{0:T(1024)(128)(2,1)}, u32[]{:S(2)}) copy-start(bf16[1280]{0:T(1024)(128)(2,1)} %param.11) | copy-start | bytes 7684
  16.7 2.1 %copy-start.7 = (bf16[256]{0:T(256)(128)(2,1)S(1)}, bf16[256]{0:T(256)(128)(2,1)}, u32[]{:S(2)}) copy-start(bf16[256]{0:T(256)(128)(2,1)} %param.16) | copy-start | bytes 1540
  16.7 2.1 %copy-start.8 = (bf16[256]{0:T(256)(128)(2,1)S(1)}, bf16[256]{0:T(256)(128)(2,1)}, u32[]{:S(2)}) copy-start(bf16[256]{0:T(256)(128)(2,1)} %param.17) | copy-start | bytes 1540
  20.3 29.6 %copy-start = (bf16[5120,512]{1,0:T(8,128)(2,1)S(1)}, bf16[5120,512]{1,0:T(8,128)(2,1)}, u32[]{:S(2)}) copy-start(bf16[5120,512]{1,0:T(8,128)(2,1)} %constant_dynamic-update-slice_fusion) | copy-start | bytes 15728644
  52.4 1.8 %copy-start.5 = (s32[16]{0:T(128)S(1)}, s32[16]{0:T(128)}, u32[]{:S(2)}) copy-start(s32[16]{0:T(128)} %param.19) | copy-start | bytes 196
  52.4 3.7 %copy-start.4 = (bf16[1280]{0:T(1024)(128)(2,1)S(1)}, bf16[1280]{0:T(1024)(128)(2,1)}, u32[]{:S(2)}) copy-start(bf16[1280]{0:T(1024)(128)(2,1)} %param.15) | copy-start | bytes 7684
  52.4 6.5 %copy-start.2 = (bf16[256,1280]{1,0:T(8,128)(2,1)S(1)}, bf16[256,1280]{1,0:T(8,128)(2,1)}, u32[]{:S(2)}) copy-start(bf16[256,1280]{1,0:T(8,128)(2,1)} %param.10) | copy-start | bytes 1966084
Sparse Core Ops, SparseCore 0:
  54.3 29.7 all-gather.1

commit v9 on v6

--- a/solution.py
+++ b/solution.py
@@ -150,37 +150,46 @@
             for weight in (w_kv, w_query)
         ]
 
-    proj_kv, proj_query = project(scaled, mine)
-    for flip, perm in partners(parts):
-        got = lax.ppermute(scaled, "tp", perm)
-        more = project(got, flip(mine))
-        proj_kv = proj_kv + more[0]
-        proj_query = proj_query + more[1]
-    proj_key = proj_kv[:, :kv_width]
-    proj_value = proj_kv[:, kv_width:]
     rstd = lax.rsqrt(squares / D + norm_eps)
     own_pos = me * rows + jnp.arange(rows, dtype=jnp.int32)
     own_seg, own_off = token_meta(own_pos, lengths)
     own_live = own_seg < docs - 1
-    query = rstd[:, None] * proj_query + query_bias.astype(jnp.float32)
-    key = rstd[:, None] * proj_key + key_bias.astype(jnp.float32)
-    value = rstd[:, None] * proj_value + value_bias.astype(jnp.float32)
-    query = (
-        rotate(query.reshape(rows, q_width // HEAD, HEAD), own_off)
-        .reshape(rows, q_width)
-        .astype(jnp.bfloat16)
-    )
-    key = (
-        jnp.where(own_live[:, None, None], rotate(key.reshape(rows, kv_dev, HEAD), own_off), 0.0)
-        .reshape(rows, kv_width)
-        .astype(jnp.bfloat16)
-    )
-    value = jnp.where(own_live[:, None], value, 0.0).astype(jnp.bfloat16)
-    q_seg, q_off = token_meta(own_pos, lengths)
-    q_live = q_seg < docs - 1
-    q_grouped = query.reshape(rows, kv_dev, group, HEAD)
-
-    both = lax.all_gather(jnp.concatenate([key, value], axis=1), "blk", axis=0, tiled=True)
+    q_seg = own_seg
+    q_live = own_live
+    half = rows // 2
+
+    def finish(lo):
+        chunk = scaled[lo:lo + half]
+        proj_kv, proj_query = project(chunk, mine)
+        for flip, perm in partners(parts):
+            got = lax.ppermute(chunk, "tp", perm)
+            more = project(got, flip(mine))
+            proj_kv = proj_kv + more[0]
+            proj_query = proj_query + more[1]
+        norm = rstd[lo:lo + half, None]
+        off = own_off[lo:lo + half]
+        live = own_live[lo:lo + half]
+        query = norm * proj_query + query_bias.astype(jnp.float32)
+        key = norm * proj_kv[:, :kv_width] + key_bias.astype(jnp.float32)
+        value = norm * proj_kv[:, kv_width:] + value_bias.astype(jnp.float32)
+        query = (
+            rotate(query.reshape(half, q_width // HEAD, HEAD), off)
+            .reshape(half, q_width)
+            .astype(jnp.bfloat16)
+        )
+        key = (
+            jnp.where(live[:, None, None], rotate(key.reshape(half, kv_dev, HEAD), off), 0.0)
+            .reshape(half, kv_width)
+            .astype(jnp.bfloat16)
+        )
+        value = jnp.where(live[:, None], value, 0.0).astype(jnp.bfloat16)
+        gathered = lax.all_gather(jnp.concatenate([key, value], axis=1), "blk", axis=0, tiled=False)
+        return query, gathered
+
+    query_up, kv_up = finish(0)
+    query_low, kv_low = finish(half)
+    query = jnp.concatenate([query_up, query_low], axis=0)
+    both = jnp.stack([kv_up, kv_low], axis=1).reshape(blocks * rows, 2 * kv_width)
     count = both.shape[0]
     longest = count // 2
     span = min(count, longest + rows)

time: 98.9 us -> 122 us (1.23)
  matrix products: 20.3 us -> 30.4 us
  other arithmetic: 7.49 us -> 13.4 us
  starting transfers between devices: 6.4 us -> 9.28 us
  waiting for transfers between devices: 28.2 us -> 30.8 us
    ppermute x3, waiting for transfers between devices: 17.4 us -> 1.36 us  [on_device(): squares = squares + lax.ppermute(part_sq, 'tp', perm)]
    ppermute x3 -> x6, waiting for transfers between devices: 0.01 us -> 12.1 us  [finish(): got = lax.ppermute(chunk, 'tp', perm)]
    dot_general x8 -> x16, matrix products: 20.3 us -> 30.4 us  [project(): jnp.dot(chunk, lax.dynamic_slice_in_dim(weight, source * width, width, 0)...]
    all_gather x1 -> x2, waiting for transfers between devices: 10.9 us -> 17.4 us  [finish(): lax.all_gather(jnp.concatenate([key, value], axis=1), 'blk', axis=0, tile...]
    ppermute x3 -> x6, starting transfers between devices: 3.71 us -> 6.38 us  [finish(): got = lax.ppermute(chunk, 'tp', perm)]
    concatenate x1 -> x3, other arithmetic: 0.72 us -> 3.05 us  [the longest x2 2.17 us: finish(): jnp.concatenate([key, value], axis=1)]
    another operation x2 -> x3, other arithmetic: 0.36 us -> 2.12 us  [the longest x1 1.74 us: on_device(): jnp.stack([kv_up, kv_low], axis=1).reshape(blocks * rows, 2 * kv_width)]
    concatenate x1, local copies, waits for them, and re-layouts: 1.7 us -> 3.43 us  [on_device(): w_kv = jnp.concatenate([w_key, w_value], axis=1)]
  transfers between devices with their start and end apart: 7 -> 11, of which waited for: 3 -> 5; matrix products, arithmetic and copies ran while one was open for 31% -> 38% of each run, Pallas kernels for 0% -> 0%
where the time goes in v9:
time: 122 us; the launch traced here: 120 us
  waiting for transfers between devices  30.8 us (25%)
  matrix products  30.4 us (25%)
  between operations  15.8 us (13%)
  other arithmetic  13.4 us (11%)
  local copies, waits for them, and re-layouts  10.6 us (9%)
  Pallas kernels  9.77 us (8%)
  starting transfers between devices  9.28 us (8%)
    dot_general x16, matrix products, project(): jnp.dot(chunk, lax.dynamic_slice_in_dim(weight, source * width, width, 0)...  30.4 us
    all_gather x2, waiting for transfers between devices, finish(): lax.all_gather(jnp.concatenate([key, value], axis=1), 'blk', axis=0, tile...  17.4 us
    ppermute x6, waiting for transfers between devices, finish(): got = lax.ppermute(chunk, 'tp', perm)  12.1 us
    pallas_call x1, Pallas kernels, window_attention(): pl.pallas_call(kernel, grid_spec=spec, out_shape=jax.ShapeDtypeStruct((ro...  9.77 us
    ppermute x6, starting transfers between devices, finish(): got = lax.ppermute(chunk, 'tp', perm)  6.38 us
    concatenate x1, local copies, waits for them, and re-layouts, on_device(): w_kv = jnp.concatenate([w_key, w_value], axis=1)  3.43 us
    ppermute x3, starting transfers between devices, on_device(): squares = squares + lax.ppermute(part_sq, 'tp', perm)  2.65 us
  transfers between devices with their start and end apart: 11, of which 5 were waited for; matrix products, arithmetic and copies ran while one was open for 38% of the time, Pallas kernels for 0%

profile of v9, /device:TPU:9, one launch (start us, length us, event | category | flops | bytes accessed | tf_op | source)
XLA Modules:
  0.0 120.1 jit_solution(15974052641436109777)
XLA Ops:
  8.1 1.4 %fusion.46 = (f32[256]{0:T(256)S(1)}, bf16[256,1280]{1,0:T(8,128)(2,1)S(1)}) fusion(bf16[256,1280]{1,0:T(8,128)(2,1)} %param.10, f32[1280]{0:T(1024)S(1)} %convert_element_type.56), kind=kLoop, calls=%fused_computation.29 | loop fusion | flops 1638144 | bytes 1316864 | tf_op jit(solution)/shard_map/reduce_sum | solution.py:134
  15.4 1.7 %constant_dynamic-update-slice_fusion.1 = bf16[5120,512]{1,0:T(8,128)(2,1)} fusion(bf16[5120,256]{1,0:T(8,128)(2,1)S(1)} %copy-done.2), kind=kLoop, calls=%fused_computation.99 | loop fusion | bytes 5242880
  17.1 3.4 %constant_dynamic-update-slice_fusion = bf16[5120,512]{1,0:T(8,128)(2,1)} fusion(bf16[5120,512]{1,0:T(8,128)(2,1)} %constant_dynamic-update-slice_fusion.1, bf16[5120,256]{1,0:T(8,128)(2,1)} %param.14), kind=kLoop, calls=%fused_computation.98 | loop fusion | bytes 5242880 | tf_op jit(solution)/shard_map/concatenate | solution.py:139
  20.5 1.7 %fusion.60 = f32[128,512]{1,0:T(8,128)S(1)} fusion(bf16[5120,512]{1,0:T(8,128)(2,1)} %constant_dynamic-update-slice_fusion, s32[]{:T(128)S(6)} %select_n.53, bf16[256,1280]{1,0:T(8,128)(2,1)S(1)} %get-tuple-element.17), kind=kOutput, calls=%fused_computation.47 | convolution fusion | flops 167772160 | bytes 1900548 | tf_op jit(solution)/shard_map/dot_general | solution.py:145
  22.2 1.7 %fusion.58 = f32[128,512]{1,0:T(8,128)S(1)} fusion(bf16[5120,512]{1,0:T(8,128)(2,1)} %constant_dynamic-update-slice_fusion, s32[]{:T(128)S(6)} %select_n.53, bf16[256,1280]{1,0:T(8,128)(2,1)S(1)} %get-tuple-element.17), kind=kOutput, calls=%fused_computation.45 | convolution fusion | flops 167772160 | bytes 1900548 | tf_op jit(solution)/shard_map/dot_general | solution.py:145
  24.9 1.4 %collective-permute-done = f32[256]{0:T(256)S(1)} collective-permute-done((f32[256]{0:T(256)S(1)}, f32[256]{0:T(256)S(1)}, u32[]{:S(2)}, u32[]{:S(2)}) %collective-permute-start) | collective-permute-done | bytes 1056 | tf_op jit(solution)/shard_map/ppermute | solution.py:138
  30.2 1.8 %convolution_add_fusion.3 = f32[128,512]{1,0:T(8,128)S(1)} fusion(f32[128,512]{1,0:T(8,128)S(1)} %fusion.60, bf16[128,1280]{1,0:T(8,128)(2,1)} %collective-permute-done.3, bf16[5120,512]{1,0:T(8,128)(2,1)} %constant_dynamic-update-slice_fusion, s32[]{:T(128)S(6)} %select_n.54), kind=kOutput, calls=%fused_computation.36 | convolution fusion | flops 167837696 | bytes 2162692 | tf_op jit(solution)/shard_map/dot_general | solution.py:145
  32.0 2.9 %collective-permute-done.6 = bf16[128,1280]{1,0:T(8,128)(2,1)S(1)} collective-permute-done((bf16[128,1280]{1,0:T(8,128)(2,1)S(1)}, bf16[128,1280]{1,0:T(8,128)(2,1)S(1)}, u32[]{:S(2)}, u32[]{:S(2)}) %collective-permute-start.6) | collective-permute-done | bytes 327712 | tf_op jit(solution)/shard_map/ppermute | solution.py:165
  34.9 1.7 %convolution_add_fusion.1 = f32[128,512]{1,0:T(8,128)S(1)} fusion(f32[128,512]{1,0:T(8,128)S(1)} %fusion.58, bf16[128,1280]{1,0:T(8,128)(2,1)S(1)} %collective-permute-done.6, bf16[5120,512]{1,0:T(8,128)(2,1)} %constant_dynamic-update-slice_fusion, s32[]{:T(128)S(6)} %select_n.54), kind=kOutput, calls=%fused_computation.33 | convolution fusion | flops 167837696 | bytes 2162692 | tf_op jit(solution)/shard_map/dot_general | solution.py:145
  36.6 1.8 %fusion.52 = f32[128,512]{1,0:T(8,128)S(1)} fusion(bf16[128,1280]{1,0:T(8,128)(2,1)} %collective-permute-done.5, bf16[5120,512]{1,0:T(8,128)(2,1)} %constant_dynamic-update-slice_fusion, s32[]{:T(128)S(6)} %select_n.56), kind=kOutput, calls=%fused_computation.39 | convolution fusion | flops 167772160 | bytes 1900548 | tf_op jit(solution)/shard_map/dot_general | solution.py:145
  38.4 3.6 %collective-permute-done.8 = bf16[128,1280]{1,0:T(8,128)(2,1)S(1)} collective-permute-done((bf16[128,1280]{1,0:T(8,128)(2,1)S(1)}, bf16[128,1280]{1,0:T(8,128)(2,1)S(1)}, u32[]{:S(2)}, u32[]{:S(2)}) %collective-permute-start.8) | collective-permute-done | bytes 327712 | tf_op jit(solution)/shard_map/ppermute | solution.py:165
  42.7 5.5 %collective-permute-done.7 = bf16[128,1280]{1,0:T(8,128)(2,1)S(1)} collective-permute-done((bf16[128,1280]{1,0:T(8,128)(2,1)S(1)}, bf16[128,1280]{1,0:T(8,128)(2,1)S(1)}, u32[]{:S(2)}, u32[]{:S(2)}) %collective-permute-start.7) | collective-permute-done | bytes 327712 | tf_op jit(solution)/shard_map/ppermute | solution.py:165
  57.1 2.5 %fusion.14 = f32[128,1280]{1,0:T(8,128)S(1)} fusion(bf16[5120,1280]{1,0:T(8,128)(2,1)} %param.12, s32[]{:T(128)S(6)} %select_n.53, bf16[256,1280]{1,0:T(8,128)(2,1)S(1)} %get-tuple-element.17), kind=kOutput, calls=%fused_computation.14 | convolution fusion | flops 419430400 | bytes 4259844 | tf_op jit(solution)/shard_map/dot_general | solution.py:145
  59.6 2.6 %fusion.12 = f32[128,1280]{1,0:T(8,128)S(1)} fusion(bf16[5120,1280]{1,0:T(8,128)(2,1)} %param.12, s32[]{:T(128)S(6)} %select_n.53, bf16[256,1280]{1,0:T(8,128)(2,1)S(1)} %get-tuple-element.17), kind=kOutput, calls=%fused_computation.12 | convolution fusion | flops 419430400 | bytes 4259844 | tf_op jit(solution)/shard_map/dot_general | solution.py:145
  63.7 1.5 %pad_maximum_fusion.8 = bf16[128,512]{1,0:T(8,128)(2,1)} fusion(bf16[128,256]{1,0:T(8,128)(2,1)} %get-tuple-element.21, bf16[128,256]{1,0:T(8,128)(2,1)S(1)} %fusion.62), kind=kLoop, calls=%fused_computation.76 | loop fusion | flops 262144 | bytes 262144 | tf_op jit(solution)/shard_map/concatenate | solution.py:186
  65.2 2.7 %fusion.2 = f32[128,1280]{1,0:T(8,128)S(1)} fusion(bf16[128,1280]{1,0:T(8,128)(2,1)} %collective-permute-done.5, bf16[5120,1280]{1,0:T(8,128)(2,1)} %param.12, s32[]{:T(128)S(6)} %select_n.56), kind=kOutput, calls=%fused_computation.2 | convolution fusion | flops 419430400 | bytes 4259844 | tf_op jit(solution)/shard_map/dot_general | solution.py:145
  67.9 2.6 %fusion.6 = f32[128,1280]{1,0:T(8,128)S(1)} fusion(bf16[128,1280]{1,0:T(8,128)(2,1)S(1)} %collective-permute-done.4, bf16[5120,1280]{1,0:T(8,128)(2,1)} %param.12, s32[]{:T(128)S(6)} %select_n.55), kind=kOutput, calls=%fused_computation.6 | convolution fusion | flops 419430400 | bytes 4259844 | tf_op jit(solution)/shard_map/dot_general | solution.py:145
  70.5 2.8 %fusion.43 = f32[128,1280]{1,0:T(8,128)S(1)} fusion(f32[128,1280]{1,0:T(8,128)S(1)} %fusion.2, f32[128,1280]{1,0:T(8,128)S(1)} %fusion.6, f32[128,1280]{1,0:T(8,128)S(1)} %fusion.14, bf16[128,1280]{1,0:T(8,128)(2,1)} %collective-permute-done.3, bf16[5120,1280]{1,0:T(8,128)(2,1)} %param.12, s32[]{:T(128)S(6)} %select_n.54, ...), kind=kOutput, calls=%fused_computation.25 | convolution fusion | flops 420249600 | bytes 6231556 | tf_op jit(solution)/shard_map/dot_general | solution.py:145
  73.5 2.5 %fusion.4 = f32[128,1280]{1,0:T(8,128)S(1)} fusion(bf16[128,1280]{1,0:T(8,128)(2,1)S(1)} %collective-permute-done.7, bf16[5120,1280]{1,0:T(8,128)(2,1)} %param.12, s32[]{:T(128)S(6)} %select_n.55), kind=kOutput, calls=%fused_computation.4 | convolution fusion | flops 419430400 | bytes 4259844 | tf_op jit(solution)/shard_map/dot_general | solution.py:145
  76.1 2.5 %fusion = f32[128,1280]{1,0:T(8,128)S(1)} fusion(bf16[128,1280]{1,0:T(8,128)(2,1)S(1)} %collective-permute-done.8, bf16[5120,1280]{1,0:T(8,128)(2,1)} %param.12, s32[]{:T(128)S(6)} %select_n.56), kind=kOutput, calls=%fused_computation | convolution fusion | flops 419430400 | bytes 4259844 | tf_op jit(solution)/shard_map/dot_general | solution.py:145
  78.6 2.6 %fusion.34 = f32[128,1280]{1,0:T(8,128)S(1)} fusion(f32[128,1280]{1,0:T(8,128)S(1)} %fusion, f32[128,1280]{1,0:T(8,128)S(1)} %fusion.4, f32[128,1280]{1,0:T(8,128)S(1)} %fusion.12, bf16[128,1280]{1,0:T(8,128)(2,1)S(1)} %collective-permute-done.6, bf16[5120,1280]{1,0:T(8,128)(2,1)} %param.12, s32[]{:T(128)S(6)} %select_n.54, f32[128]{0:T(128)S(1)} %get-tuple-element.33, ...), kind=kOutput, calls=%fused_computation.22 | convolution fusion | flops 420249600 | bytes 6231556 | tf_op jit(solution)/shard_map/dot_general | solution.py:145
  83.0 17.4 %all-gather.7.cloned.1.call-done = bf16[1024,512]{1,0:T(8,128)(2,1)} async-done(((bf16[128,512]{1,0:T(8,128)(2,1)}), bf16[1024,512]{1,0:T(8,128)(2,1)}) %all-gather.7.cloned.1.call-update) | async-done | bytes 1048592 | tf_op jit(solution)/shard_map/all_gather | solution.py:186
  100.4 1.7 %pad_maximum_fusion = bf16[8,2,128,512]{3,2,1,0:T(8,128)(2,1)S(1)} fusion(bf16[8,1,128,512]{3,2,1,0:T(8,128)(2,1)} %bitcast.57, bf16[8,1,128,512]{3,2,1,0:T(8,128)(2,1)} %bitcast.56), kind=kLoop, calls=%fused_computation.26 | loop fusion | flops 1048576 | bytes 4194304 | tf_op jit(solution)/shard_map/stack | solution.py:192
  103.5 9.8 %shard_map.113 = bf16[256,1280]{1,0:T(8,128)(2,1)} custom-call(s32[1]{0:T(128)} %bitcast.first_ref, bf16[256,1280]{1,0:T(8,128)(2,1)} %pad_maximum_fusion.1.q_ref, bf16[2048,512]{1,0:T(8,128)(2,1)} %bitcast.50, bf16[2048,512]{1,0:T(8,128)(2,1)} %bitcast.51, s32[256,1]{1,0:T(8,128)} %copy.35.qs_ref, s32[256,1]{1,0:T(8,128)} %iota_add_fusion.qp_ref, ...), custom_call_target="tpu_custom_call" | custom-call | tf_op jit(solution)/shard_map/pallas_call | solution.py:94
  (92 shorter events, 24.6 us)
Async XLA Ops:
  7.2 8.2 %copy-start.2 = (bf16[5120,256]{1,0:T(8,128)(2,1)S(1)}, bf16[5120,256]{1,0:T(8,128)(2,1)}, u32[]{:S(2)}) copy-start(bf16[5120,256]{1,0:T(8,128)(2,1)} %param.13) | copy-start | bytes 7864324
  7.2 75.8 %all-gather.5.cloned.1.call-start = ((), (), s32[]{:S(2)}) async-start(), calls=%async_computation | async-start | bytes 1179648 | tf_op jit(solution)/shard_map/all_gather | solution.py:186
  10.3 18.6 %collective-permute-start.3 = (bf16[128,1280]{1,0:T(8,128)(2,1)}, bf16[128,1280]{1,0:T(8,128)(2,1)}, u32[]{:S(2)}, u32[]{:S(2)}) collective-permute-start(bf16[128,1280]{1,0:T(8,128)(2,1)} %get-tuple-element.14), channel_id=1, source_target_pairs={{0,1},{1,0},{2,3},{3,2},{4,5},{5,4},{6,7},{7,6},{8,9},{9,8},{10,11... | collective-permute-start | bytes 983048 | tf_op jit(solution)/shard_map/ppermute | solution.py:165
  11.5 25.1 %collective-permute-start.5 = (bf16[128,1280]{1,0:T(8,128)(2,1)}, bf16[128,1280]{1,0:T(8,128)(2,1)}, u32[]{:S(2)}, u32[]{:S(2)}) collective-permute-start(bf16[128,1280]{1,0:T(8,128)(2,1)} %get-tuple-element.14), channel_id=1, source_target_pairs={{0,3},{1,2},{2,1},{3,0},{4,7},{5,6},{6,5},{7,4},{8,11},{9,10},{10,... | collective-permute-start | bytes 983048 | tf_op jit(solution)/shard_map/ppermute | solution.py:165
  12.7 13.5 %collective-permute-start = (f32[256]{0:T(256)S(1)}, f32[256]{0:T(256)S(1)}, u32[]{:S(2)}, u32[]{:S(2)}) collective-permute-start(f32[256]{0:T(256)S(1)} %get-tuple-element.16), channel_id=1, source_target_pairs={{0,1},{1,0},{2,3},{3,2},{4,5},{5,4},{6,7},{7,6},{8,9},{9,8},{10,11... | collective-permute-start | bytes 3080 | tf_op jit(solution)/shard_map/ppermute | solution.py:138
  13.9 13.5 %collective-permute-start.1 = (f32[256]{0:T(256)S(1)}, f32[256]{0:T(256)S(1)}, u32[]{:S(2)}, u32[]{:S(2)}) collective-permute-start(f32[256]{0:T(256)S(1)} %get-tuple-element.16), channel_id=1, source_target_pairs={{0,2},{1,3},{2,0},{3,1},{4,6},{5,7},{6,4},{7,5},{8,10},{9,11},{10,... | collective-permute-start | bytes 3080 | tf_op jit(solution)/shard_map/ppermute | solution.py:138
  14.2 14.5 %collective-permute-start.2 = (f32[256]{0:T(256)S(1)}, f32[256]{0:T(256)S(1)}, u32[]{:S(2)}, u32[]{:S(2)}) collective-permute-start(f32[256]{0:T(256)S(1)} %get-tuple-element.16), channel_id=1, source_target_pairs={{0,3},{1,2},{2,1},{3,0},{4,7},{5,6},{6,5},{7,4},{8,11},{9,10},{10,... | collective-permute-start | bytes 3080 | tf_op jit(solution)/shard_map/ppermute | solution.py:138
  17.1 6.8 %copy-start.8 = (s32[8]{0:T(128)S(1)}, s32[8]{0:T(128)}, u32[]{:S(2)}) copy-start(s32[8]{0:T(128)} %param.18) | copy-start | bytes 100
  20.5 4.1 %copy-start.9 = (bf16[256]{0:T(256)(128)(2,1)S(1)}, bf16[256]{0:T(256)(128)(2,1)}, u32[]{:S(2)}) copy-start(bf16[256]{0:T(256)(128)(2,1)} %param.16) | copy-start | bytes 1540
  20.5 4.1 %copy-start.10 = (bf16[256]{0:T(256)(128)(2,1)S(1)}, bf16[256]{0:T(256)(128)(2,1)}, u32[]{:S(2)}) copy-start(bf16[256]{0:T(256)(128)(2,1)} %param.17) | copy-start | bytes 1540
  20.5 6.9 %copy-start.3 = (bf16[128,1280]{1,0:T(8,128)(2,1)S(1)}, bf16[128,1280]{1,0:T(8,128)(2,1)}, u32[]{:S(2)}) copy-start(bf16[128,1280]{1,0:T(8,128)(2,1)} %get-tuple-element.15) | copy-start | bytes 983044
  24.9 17.1 %copy-start = (bf16[5120,512]{1,0:T(8,128)(2,1)S(1)}, bf16[5120,512]{1,0:T(8,128)(2,1)}, u32[]{:S(2)}) copy-start(bf16[5120,512]{1,0:T(8,128)(2,1)} %constant_dynamic-update-slice_fusion) | copy-start | bytes 15728644
  26.2 16.1 %collective-permute-start.4 = (bf16[128,1280]{1,0:T(8,128)(2,1)}, bf16[128,1280]{1,0:T(8,128)(2,1)S(1)}, u32[]{:S(2)}, u32[]{:S(2)}) collective-permute-start(bf16[128,1280]{1,0:T(8,128)(2,1)} %get-tuple-element.14), channel_id=1, source_target_pairs={{0,2},{1,3},{2,0},{3,1},{4,6},{5,7},{6,4},{7,5},{8,10},{9,11},{10,... | collective-permute-start | bytes 983048 | tf_op jit(solution)/shard_map/ppermute | solution.py:165
  27.5 7.5 %collective-permute-start.6 = (bf16[128,1280]{1,0:T(8,128)(2,1)S(1)}, bf16[128,1280]{1,0:T(8,128)(2,1)S(1)}, u32[]{:S(2)}, u32[]{:S(2)}) collective-permute-start(bf16[128,1280]{1,0:T(8,128)(2,1)S(1)} %copy-done.3), channel_id=1, source_target_pairs={{0,1},{1,0},{2,3},{3,2},{4,5},{5,4},{6,7},{7,6},{8,9},{9,8},{10,11... | collective-permute-start | bytes 983048 | tf_op jit(solution)/shard_map/ppermute | solution.py:165
  28.7 13.3 %collective-permute-start.8 = (bf16[128,1280]{1,0:T(8,128)(2,1)S(1)}, bf16[128,1280]{1,0:T(8,128)(2,1)S(1)}, u32[]{:S(2)}, u32[]{:S(2)}) collective-permute-start(bf16[128,1280]{1,0:T(8,128)(2,1)S(1)} %copy-done.3), channel_id=1, source_target_pairs={{0,3},{1,2},{2,1},{3,0},{4,7},{5,6},{6,5},{7,4},{8,11},{9,10},{10,... | collective-permute-start | bytes 983048 | tf_op jit(solution)/shard_map/ppermute | solution.py:165
  28.9 19.7 %copy-start.4 = (f32[128]{0:T(128)}, f32[128]{0:T(128)S(1)}, u32[]{:S(2)}) copy-start(f32[128]{0:T(128)S(1)} %get-tuple-element.32) | copy-start | bytes 1540
  28.9 19.3 %collective-permute-start.7 = (bf16[128,1280]{1,0:T(8,128)(2,1)S(1)}, bf16[128,1280]{1,0:T(8,128)(2,1)S(1)}, u32[]{:S(2)}, u32[]{:S(2)}) collective-permute-start(bf16[128,1280]{1,0:T(8,128)(2,1)S(1)} %copy-done.3), channel_id=1, source_target_pairs={{0,2},{1,3},{2,0},{3,1},{4,6},{5,7},{6,4},{7,5},{8,10},{9,11},{10,... | collective-permute-start | bytes 983048 | tf_op jit(solution)/shard_map/ppermute | solution.py:165
  42.3 8.6 %copy-start.7 = (s32[16]{0:T(128)S(1)}, s32[16]{0:T(128)}, u32[]{:S(2)}) copy-start(s32[16]{0:T(128)} %param.19) | copy-start | bytes 196
  42.3 12.0 %copy-start.6 = (bf16[1280]{0:T(1024)(128)(2,1)S(1)}, bf16[1280]{0:T(1024)(128)(2,1)}, u32[]{:S(2)}) copy-start(bf16[1280]{0:T(1024)(128)(2,1)} %param.15) | copy-start | bytes 7684
  50.7 49.7 %all-gather.7.cloned.1.call-start = ((), (), s32[]{:S(2)}) async-start(), calls=%async_computation.1 | async-start | bytes 1179648 | tf_op jit(solution)/shard_map/all_gather | solution.py:186
  65.2 5.3 %copy-start.5 = (f32[128]{0:T(128)S(1)}, f32[128]{0:T(128)}, u32[]{:S(2)}) copy-start(f32[128]{0:T(128)} %copy-done.4) | copy-start | bytes 1540
  102.1 1.4 %copy-start.1 = (bf16[8,2,128,512]{3,2,1,0:T(8,128)(2,1)}, bf16[8,2,128,512]{3,2,1,0:T(8,128)(2,1)S(1)}, u32[]{:S(2)}) copy-start(bf16[8,2,128,512]{3,2,1,0:T(8,128)(2,1)S(1)} %pad_maximum_fusion) | copy-start | bytes 6291460
Sparse Core Ops, SparseCore 0:
  50.8 25.5 all-gather.4
  78.6 21.7 all-gather.6

commit v10 on v6

--- a/solution.py
+++ b/solution.py
@@ -105,6 +105,122 @@
         q_pos.reshape(rows, 1),
         k_seg.reshape(1, span),
         k_pos.reshape(1, span),
+    )
+
+
+def local_attention(query, own_kv, q_seg, q_pos, docs, interpret=False):
+    rows, q_width = query.shape
+    kv_dev = own_kv.shape[1] // (2 * HEAD)
+    group = q_width // (kv_dev * HEAD)
+    scale = 1.0 / float(HEAD) ** 0.5
+
+    def kernel(q_ref, k_ref, v_ref, qs_ref, qp_ref, ks_ref, kp_ref, acc_ref, top_ref, sum_ref):
+        keys = k_ref[...]
+        values = v_ref[...]
+        qs = qs_ref[...]
+        allowed = (ks_ref[...] == qs) & (kp_ref[...] <= qp_ref[...]) & (qs < docs - 1)
+        for g in range(group):
+            cols = slice(g * HEAD, (g + 1) * HEAD)
+            scores = lax.dot_general(
+                q_ref[:, cols], keys, (((1,), (1,)), ((), ())), preferred_element_type=jnp.float32
+            ) * scale
+            scores = jnp.where(allowed, scores, neg_large)
+            top = jnp.max(scores, axis=1, keepdims=True)
+            expo = jnp.exp(scores - top)
+            acc_ref[:, cols] = jnp.dot(
+                expo.astype(jnp.bfloat16), values, preferred_element_type=jnp.float32
+            )
+            top_ref[:, cols] = jnp.broadcast_to(top, (rows, HEAD))
+            sum_ref[:, cols] = jnp.broadcast_to(jnp.sum(expo, axis=1, keepdims=True), (rows, HEAD))
+
+    block = pl.BlockSpec((rows, group * HEAD), lambda c: (0, c))
+    return pl.pallas_call(
+        kernel,
+        grid=(kv_dev,),
+        in_specs=[
+            block,
+            pl.BlockSpec((rows, HEAD), lambda c: (0, c)),
+            pl.BlockSpec((rows, HEAD), lambda c: (0, kv_dev + c)),
+            pl.BlockSpec((rows, 1), lambda c: (0, 0)),
+            pl.BlockSpec((rows, 1), lambda c: (0, 0)),
+            pl.BlockSpec((1, rows), lambda c: (0, 0)),
+            pl.BlockSpec((1, rows), lambda c: (0, 0)),
+        ],
+        out_specs=[block, block, block],
+        out_shape=[jax.ShapeDtypeStruct((rows, q_width), jnp.float32)] * 3,
+        interpret=interpret,
+    )(
+        query,
+        own_kv,
+        own_kv,
+        q_seg.reshape(rows, 1),
+        q_pos.reshape(rows, 1),
+        q_seg.reshape(1, rows),
+        q_pos.reshape(1, rows),
+    )
+
+
+def remote_attention(first, query, both, q_seg, k_seg, partial, docs, interpret=False):
+    rows, q_width = query.shape
+    count, both_width = both.shape
+    span = k_seg.shape[0]
+    kv_dev = both_width // (2 * HEAD)
+    group = q_width // (kv_dev * HEAD)
+    scale = 1.0 / float(HEAD) ** 0.5
+
+    def kernel(first_ref, q_ref, k_ref, v_ref, qs_ref, ks_ref, acc_ref, top_ref, sum_ref, o_ref):
+        start = pl.multiple_of(first_ref[0], PAGE)
+        keys = k_ref[pl.ds(start, span), :]
+        values = v_ref[pl.ds(start, span), :]
+        qs = qs_ref[...]
+        live = qs < docs - 1
+        allowed = (ks_ref[...] == qs) & live
+        for g in range(group):
+            cols = slice(g * HEAD, (g + 1) * HEAD)
+            scores = lax.dot_general(
+                q_ref[:, cols], keys, (((1,), (1,)), ((), ())), preferred_element_type=jnp.float32
+            ) * scale
+            scores = jnp.where(allowed, scores, neg_large)
+            old = top_ref[:, g * HEAD:g * HEAD + 1]
+            top = jnp.maximum(old, jnp.max(scores, axis=1, keepdims=True))
+            expo = jnp.where(allowed, jnp.exp(scores - top), 0.0)
+            shrink = jnp.exp(old - top)
+            denom = sum_ref[:, g * HEAD:g * HEAD + 1] * shrink + jnp.sum(expo, axis=1, keepdims=True)
+            acc = acc_ref[:, cols] * shrink + jnp.dot(
+                expo.astype(jnp.bfloat16), values, preferred_element_type=jnp.float32
+            )
+            out = jnp.where(live, acc / jnp.where(live, denom, 1.0), 0.0)
+            o_ref[:, cols] = out.astype(o_ref.dtype)
+
+    block = pl.BlockSpec((rows, group * HEAD), lambda c, f: (0, c))
+    spec = pltpu.PrefetchScalarGridSpec(
+        num_scalar_prefetch=1,
+        grid=(kv_dev,),
+        in_specs=[
+            block,
+            pl.BlockSpec((count, HEAD), lambda c, f: (0, c)),
+            pl.BlockSpec((count, HEAD), lambda c, f: (0, kv_dev + c)),
+            pl.BlockSpec((rows, 1), lambda c, f: (0, 0)),
+            pl.BlockSpec((1, span), lambda c, f: (0, 0)),
+            block,
+            block,
+            block,
+        ],
+        out_specs=block,
+    )
+    return pl.pallas_call(
+        kernel,
+        grid_spec=spec,
+        out_shape=jax.ShapeDtypeStruct((rows, q_width), jnp.bfloat16),
+        interpret=interpret,
+    )(
+        first.reshape(1).astype(jnp.int32),
+        query,
+        both,
+        both,
+        q_seg.reshape(rows, 1),
+        k_seg.reshape(1, span),
+        *partial,
     )
 
 def on_device(
@@ -180,14 +296,17 @@
     q_live = q_seg < docs - 1
     q_grouped = query.reshape(rows, kv_dev, group, HEAD)
 
-    both = lax.all_gather(jnp.concatenate([key, value], axis=1), "blk", axis=0, tiled=True)
+    own_kv = jnp.concatenate([key, value], axis=1)
+    partial = local_attention(query, own_kv, q_seg, own_pos, docs)
+    both = lax.all_gather(own_kv, "blk", axis=0, tiled=True)
     count = both.shape[0]
     longest = count // 2
-    span = min(count, longest + rows)
+    span = longest
     first = jnp.clip(me * rows - longest, 0, count - span)
     k_pos = first + jnp.arange(span, dtype=jnp.int32)
     k_seg, k_off = token_meta(k_pos, lengths)
-    mixed = window_attention(first, query, both, q_seg, own_pos, k_seg, k_pos, docs)
+    k_seg = jnp.where(k_pos < me * rows, k_seg, -1)
+    mixed = remote_attention(first, query, both, q_seg, k_seg, partial, docs)
     numbers = jnp.arange(page_table.shape[0], dtype=jnp.int32)
     cache = []
     for j in range(slots):

time: 98.9 us -> 99.7 us (level)
  Pallas kernels: 9.79 us -> 15 us
  waiting for transfers between devices: 28.2 us -> 23.9 us
    pallas_call x1 -> x2, Pallas kernels: 9.79 us -> 15 us  [the longest x1 10.6 us: remote_attention(): pl.pallas_call(kernel, grid_spec=spec, out_shape=jax.ShapeDtypeStruct((ro...]
    all_gather x1, waiting for transfers between devices: 10.9 us -> 6.48 us  [on_device(): both = lax.all_gather(own_kv, 'blk', axis=0, tiled=True)]
    unnamed x13 -> x15, local copies, waits for them, and re-layouts: 3.65 us -> 3.65 us
  transfers between devices with their start and end apart: 7 -> 7, of which waited for: 3 -> 3; matrix products, arithmetic and copies ran while one was open for 31% -> 30% of each run, Pallas kernels for 0% -> 5%
where the time goes in v10:
time: 99.7 us; the launch traced here: 98.1 us
  waiting for transfers between devices  23.9 us (24%)
  matrix products  20.3 us (20%)
  between operations  15.6 us (16%)
  Pallas kernels  15 us (15%)
  local copies, waits for them, and re-layouts  8.9 us (9%)
  other arithmetic  7.97 us (8%)
  starting transfers between devices  6.4 us (6%)
    dot_general x8, matrix products, project(): jnp.dot(chunk, lax.dynamic_slice_in_dim(weight, source * width, width, 0)...  20.3 us
    ppermute x3, waiting for transfers between devices, on_device(): squares = squares + lax.ppermute(part_sq, 'tp', perm)  17.4 us
    pallas_call x1, Pallas kernels, remote_attention(): pl.pallas_call(kernel, grid_spec=spec, out_shape=jax.ShapeDtypeStruct((ro...  10.6 us
    all_gather x1, waiting for transfers between devices, on_device(): both = lax.all_gather(own_kv, 'blk', axis=0, tiled=True)  6.48 us
    pallas_call x1, Pallas kernels, local_attention(): pl.pallas_call(kernel, grid=(kv_dev,), in_specs=[block, pl.BlockSpec((row...  4.48 us
    ppermute x3, starting transfers between devices, on_device(): got = lax.ppermute(scaled, 'tp', perm)  3.71 us
    unnamed x15, local copies, waits for them, and re-layouts  3.65 us
    ppermute x3, starting transfers between devices, on_device(): squares = squares + lax.ppermute(part_sq, 'tp', perm)  2.65 us
  transfers between devices with their start and end apart: 7, of which 3 were waited for; matrix products, arithmetic and copies ran while one was open for 30% of the time, Pallas kernels for 5%

profile of v10, /device:TPU:9, one launch (start us, length us, event | category | flops | bytes accessed | tf_op | source)
XLA Modules:
  0.0 98.1 jit_solution(2843599898367521290)
XLA Ops:
  7.9 1.4 %fusion.18 = (bf16[256,1280]{1,0:T(8,128)(2,1)S(1)}, f32[256]{0:T(256)S(1)}) fusion(bf16[256,1280]{1,0:T(8,128)(2,1)} %param.10, f32[1280]{0:T(1024)S(1)} %convert_element_type.43), kind=kLoop, calls=%fused_computation.14 | loop fusion | flops 1638144 | bytes 1316864 | tf_op jit(solution)/shard_map/convert_element_type | solution.py:249
  9.3 2.2 %collective-permute-start.5 = (bf16[256,1280]{1,0:T(8,128)(2,1)S(1)}, bf16[256,1280]{1,0:T(8,128)(2,1)}, u32[]{:S(2)}, u32[]{:S(2)}) collective-permute-start(bf16[256,1280]{1,0:T(8,128)(2,1)S(1)} %get-tuple-element.18), channel_id=1, source_target_pairs={{0,3},{1,2},{2,1},{3,0},{4,7},{5,6},{6,5},{7,4},{8,11},{9,10},{10,... | collective-permute-start | bytes 1966088 | tf_op jit(solution)/shard_map/ppermute | solution.py:271
  12.0 1.2 %collective-permute-start.1 = (f32[256]{0:T(256)S(1)}, f32[256]{0:T(256)S(1)}, u32[]{:S(2)}, u32[]{:S(2)}) collective-permute-start(f32[256]{0:T(256)S(1)} %get-tuple-element.19), channel_id=1, source_target_pairs={{0,2},{1,3},{2,0},{3,1},{4,6},{5,7},{6,4},{7,5},{8,10},{9,11},{10,... | collective-permute-start | bytes 3080 | tf_op jit(solution)/shard_map/ppermute | solution.py:254
  13.2 1.2 %collective-permute-start.2 = (f32[256]{0:T(256)S(1)}, f32[256]{0:T(256)S(1)}, u32[]{:S(2)}, u32[]{:S(2)}) collective-permute-start(f32[256]{0:T(256)S(1)} %get-tuple-element.19), channel_id=1, source_target_pairs={{0,3},{1,2},{2,1},{3,0},{4,7},{5,6},{6,5},{7,4},{8,11},{9,10},{10,... | collective-permute-start | bytes 3080 | tf_op jit(solution)/shard_map/ppermute | solution.py:254
  14.4 3.6 %constant_dynamic-update-slice_fusion.1 = bf16[5120,512]{1,0:T(8,128)(2,1)} fusion(bf16[5120,256]{1,0:T(8,128)(2,1)} %param.13), kind=kLoop, calls=%fused_computation.59 | loop fusion | bytes 5242880
  18.3 1.7 %constant_dynamic-update-slice_fusion = bf16[5120,512]{1,0:T(8,128)(2,1)} fusion(bf16[5120,512]{1,0:T(8,128)(2,1)} %constant_dynamic-update-slice_fusion.1, bf16[5120,256]{1,0:T(8,128)(2,1)S(1)} %copy-done), kind=kLoop, calls=%fused_computation.58 | loop fusion | bytes 5242880 | tf_op jit(solution)/shard_map/concatenate | solution.py:255
  20.0 1.8 %fusion.25 = f32[256,512]{1,0:T(8,128)S(1)} fusion(bf16[256,1280]{1,0:T(8,128)(2,1)S(1)} %get-tuple-element.18, bf16[5120,512]{1,0:T(8,128)(2,1)} %constant_dynamic-update-slice_fusion, s32[]{:T(128)S(6)} %select_n.49), kind=kOutput, calls=%fused_computation.21 | convolution fusion | flops 335544320 | bytes 2490372 | tf_op jit(solution)/shard_map/dot_general | solution.py:261
  22.4 3.6 %collective-permute-done = f32[256]{0:T(256)S(1)} collective-permute-done((f32[256]{0:T(256)S(1)}, f32[256]{0:T(256)S(1)}, u32[]{:S(2)}, u32[]{:S(2)}) %collective-permute-start) | collective-permute-done | bytes 1056 | tf_op jit(solution)/shard_map/ppermute | solution.py:254
  26.0 1.3 %collective-permute-start.3 = (bf16[256,1280]{1,0:T(8,128)(2,1)S(1)}, bf16[256,1280]{1,0:T(8,128)(2,1)S(1)}, u32[]{:S(2)}, u32[]{:S(2)}) collective-permute-start(bf16[256,1280]{1,0:T(8,128)(2,1)S(1)} %get-tuple-element.18), channel_id=1, source_target_pairs={{0,1},{1,0},{2,3},{3,2},{4,5},{5,4},{6,7},{7,6},{8,9},{9,8},{10,11... | collective-permute-start | bytes 1966088 | tf_op jit(solution)/shard_map/ppermute | solution.py:271
  27.3 13.8 %collective-permute-done.1 = f32[256]{0:T(256)S(1)} collective-permute-done((f32[256]{0:T(256)S(1)}, f32[256]{0:T(256)S(1)}, u32[]{:S(2)}, u32[]{:S(2)}) %collective-permute-start.1) | collective-permute-done | bytes 1056 | tf_op jit(solution)/shard_map/ppermute | solution.py:254
  41.1 2.0 %fusion.19 = f32[256,512]{1,0:T(8,128)S(1)} fusion(bf16[256,1280]{1,0:T(8,128)(2,1)} %collective-permute-done.5, bf16[5120,512]{1,0:T(8,128)(2,1)} %constant_dynamic-update-slice_fusion, s32[]{:T(128)S(6)} %select_n.52), kind=kOutput, calls=%fused_computation.15 | convolution fusion | flops 335544320 | bytes 2490372 | tf_op jit(solution)/shard_map/dot_general | solution.py:261
  43.1 2.0 %fusion.21 = f32[256,512]{1,0:T(8,128)S(1)} fusion(bf16[256,1280]{1,0:T(8,128)(2,1)} %collective-permute-done.4, bf16[5120,512]{1,0:T(8,128)(2,1)} %constant_dynamic-update-slice_fusion, s32[]{:T(128)S(6)} %select_n.51), kind=kOutput, calls=%fused_computation.17 | convolution fusion | flops 335544320 | bytes 2490372 | tf_op jit(solution)/shard_map/dot_general | solution.py:261
  45.2 1.8 %fusion.33 = f32[256,512]{1,0:T(8,128)S(1)} fusion(f32[256,512]{1,0:T(8,128)S(1)} %fusion.19, f32[256,512]{1,0:T(8,128)S(1)} %fusion.21, f32[256,512]{1,0:T(8,128)S(1)} %fusion.25, bf16[256,1280]{1,0:T(8,128)(2,1)S(1)} %collective-permute-done.3, bf16[5120,512]{1,0:T(8,128)(2,1)} %constant_dynamic-update-slice_fusion, s32[]{:T(128)S(6)} %select_n.50), kind=kOutput, calls=%fused_computation.26 | convolution fusion | flops 335937536 | bytes 4063236 | tf_op jit(solution)/shard_map/dot_general | solution.py:261
  50.9 0.8 copy.25.qs_ref
  53.6 2.9 %fusion.6 = f32[256,1280]{1,0:T(8,128)S(1)} fusion(bf16[256,1280]{1,0:T(8,128)(2,1)S(1)} %get-tuple-element.18, bf16[5120,1280]{1,0:T(8,128)(2,1)} %param.12, s32[]{:T(128)S(6)} %select_n.49), kind=kOutput, calls=%fused_computation.6 | convolution fusion | flops 838860800 | bytes 5242884 | tf_op jit(solution)/shard_map/dot_general | solution.py:261
  56.6 3.4 %fusion = f32[256,1280]{1,0:T(8,128)S(1)} fusion(bf16[256,1280]{1,0:T(8,128)(2,1)} %collective-permute-done.5, bf16[5120,1280]{1,0:T(8,128)(2,1)} %param.12, s32[]{:T(128)S(6)} %select_n.52), kind=kOutput, calls=%fused_computation | convolution fusion | flops 838860800 | bytes 5242884 | tf_op jit(solution)/shard_map/dot_general | solution.py:261
  60.0 3.2 %fusion.2 = f32[256,1280]{1,0:T(8,128)S(1)} fusion(bf16[256,1280]{1,0:T(8,128)(2,1)} %collective-permute-done.4, bf16[5120,1280]{1,0:T(8,128)(2,1)} %param.12, s32[]{:T(128)S(6)} %select_n.51), kind=kOutput, calls=%fused_computation.2 | convolution fusion | flops 838860800 | bytes 5242884 | tf_op jit(solution)/shard_map/dot_general | solution.py:261
  63.2 3.1 %multiply_add_fusion = f32[256,1280]{1,0:T(8,128)S(1)} fusion(f32[1280]{0:T(1024)S(1)} %convert_element_type.45, f32[256]{0:T(256)S(1)} %add_rsqrt_fusion, f32[256,1280]{1,0:T(8,128)S(1)} %fusion, f32[256,1280]{1,0:T(8,128)S(1)} %fusion.2, f32[256,1280]{1,0:T(8,128)S(1)} %fusion.6, bf16[256,1280]{1,0:T(8,128)(2,1)S(1)} %collective-permute-done.3, ...), kind=kOutput, calls=%fused_computation.23 | convolution fusion | flops 840499200 | bytes 9181188 | tf_op jit(solution)/shard_map/dot_general | solution.py:261
  66.9 1.1 %copy.24.q_ref = bf16[256,1280]{1,0:T(8,128)(2,1)} copy(bf16[256,1280]{0,1:T(8,128)(2,1)S(1)} %bitcast.34) | data formatting | bytes 1310720 | tf_op jit(solution)/shard_map/convert_element_type | solution.py:287
  68.0 4.5 %shard_map.113 = (f32[256,1280]{1,0:T(8,128)}, f32[256,1280]{1,0:T(8,128)}, f32[256,1280]{1,0:T(8,128)}) custom-call(bf16[256,1280]{1,0:T(8,128)(2,1)} %copy.24.q_ref, bf16[256,512]{1,0:T(8,128)(2,1)} %pad_maximum_fusion.2.k_ref.v_ref, bf16[256,512]{1,0:T(8,128)(2,1)} %pad_maximum_fusion.2.k_ref.v_ref, s32[256,1]{1,0:T(8,128)} %copy.25.qs_ref, ...), custom_call_target="tpu_custom_call" | custom-call | tf_op jit(solution)/shard_map/pallas_call | solution.py:137
  72.5 6.5 %all-gather.2.cloned.1.call-done.k_ref.v_ref = bf16[2048,512]{1,0:T(8,128)(2,1)} async-done(((bf16[256,512]{1,0:T(8,128)(2,1)}), bf16[2048,512]{1,0:T(8,128)(2,1)}) %all-gather.2.cloned.1.call-update) | async-done | bytes 2097168 | tf_op jit(solution)/shard_map/all_gather | solution.py:301
  79.0 1.0 dynamic-slice_bitcast_fusion.3
  79.9 0.7 pad_maximum_fusion.3
  80.7 10.6 %shard_map.114 = bf16[256,1280]{1,0:T(8,128)(2,1)} custom-call(s32[1]{0:T(128)} %bitcast.first_ref, bf16[256,1280]{1,0:T(8,128)(2,1)} %copy.24.q_ref, bf16[2048,512]{1,0:T(8,128)(2,1)} %all-gather.2.cloned.1.call-done.k_ref.v_ref, bf16[2048,512]{1,0:T(8,128)(2,1)} %all-gather.2.cloned.1.call-done.k_ref.v_ref, s32[256,1]{1,0:T(8,128)} %copy.25.qs_ref, ...), custom_call_target="tpu_custom_call" | custom-call | tf_op jit(solution)/shard_map/pallas_call | solution.py:211
  (52 shorter events, 7.2 us)
Async XLA Ops:
  7.2 71.8 %all-gather.2.cloned.1.call-start = ((), (), s32[]{:S(2)}) async-start(), calls=%async_computation | async-start | bytes 2359296 | tf_op jit(solution)/shard_map/all_gather | solution.py:301
  9.3 31.8 %collective-permute-start.5 = (bf16[256,1280]{1,0:T(8,128)(2,1)S(1)}, bf16[256,1280]{1,0:T(8,128)(2,1)}, u32[]{:S(2)}, u32[]{:S(2)}) collective-permute-start(bf16[256,1280]{1,0:T(8,128)(2,1)S(1)} %get-tuple-element.18), channel_id=1, source_target_pairs={{0,3},{1,2},{2,1},{3,0},{4,7},{5,6},{6,5},{7,4},{8,11},{9,10},{10,... | collective-permute-start | bytes 1966088 | tf_op jit(solution)/shard_map/ppermute | solution.py:271
  11.5 31.6 %collective-permute-start.4 = (bf16[256,1280]{1,0:T(8,128)(2,1)S(1)}, bf16[256,1280]{1,0:T(8,128)(2,1)}, u32[]{:S(2)}, u32[]{:S(2)}) collective-permute-start(bf16[256,1280]{1,0:T(8,128)(2,1)S(1)} %get-tuple-element.18), channel_id=1, source_target_pairs={{0,2},{1,3},{2,0},{3,1},{4,6},{5,7},{6,4},{7,5},{8,10},{9,11},{10,... | collective-permute-start | bytes 1966088 | tf_op jit(solution)/shard_map/ppermute | solution.py:271
  11.7 14.3 %collective-permute-start = (f32[256]{0:T(256)S(1)}, f32[256]{0:T(256)S(1)}, u32[]{:S(2)}, u32[]{:S(2)}) collective-permute-start(f32[256]{0:T(256)S(1)} %get-tuple-element.19), channel_id=1, source_target_pairs={{0,1},{1,0},{2,3},{3,2},{4,5},{5,4},{6,7},{7,6},{8,9},{9,8},{10,11... | collective-permute-start | bytes 3080 | tf_op jit(solution)/shard_map/ppermute | solution.py:254
  12.0 29.1 %collective-permute-start.1 = (f32[256]{0:T(256)S(1)}, f32[256]{0:T(256)S(1)}, u32[]{:S(2)}, u32[]{:S(2)}) collective-permute-start(f32[256]{0:T(256)S(1)} %get-tuple-element.19), channel_id=1, source_target_pairs={{0,2},{1,3},{2,0},{3,1},{4,6},{5,7},{6,4},{7,5},{8,10},{9,11},{10,... | collective-permute-start | bytes 3080 | tf_op jit(solution)/shard_map/ppermute | solution.py:254
  13.2 27.9 %collective-permute-start.2 = (f32[256]{0:T(256)S(1)}, f32[256]{0:T(256)S(1)}, u32[]{:S(2)}, u32[]{:S(2)}) collective-permute-start(f32[256]{0:T(256)S(1)} %get-tuple-element.19), channel_id=1, source_target_pairs={{0,3},{1,2},{2,1},{3,0},{4,7},{5,6},{6,5},{7,4},{8,11},{9,10},{10,... | collective-permute-start | bytes 3080 | tf_op jit(solution)/shard_map/ppermute | solution.py:254
  14.4 3.6 %copy-start.4 = (s32[8]{0:T(128)S(1)}, s32[8]{0:T(128)}, u32[]{:S(2)}) copy-start(s32[8]{0:T(128)} %param.18) | copy-start | bytes 100
  14.4 3.9 %copy-start = (bf16[5120,256]{1,0:T(8,128)(2,1)S(1)}, bf16[5120,256]{1,0:T(8,128)(2,1)}, u32[]{:S(2)}) copy-start(bf16[5120,256]{1,0:T(8,128)(2,1)} %param.14) | copy-start | bytes 7864324
  18.3 32.6 %copy-start.1 = (s32[256]{0:T(256)}, s32[256]{0:T(256)S(1)}, u32[]{:S(2)}) copy-start(s32[256]{0:T(256)S(1)} %get-tuple-element.8) | copy-start | bytes 3076
  20.0 2.2 %copy-start.5 = (bf16[256]{0:T(256)(128)(2,1)S(1)}, bf16[256]{0:T(256)(128)(2,1)}, u32[]{:S(2)}) copy-start(bf16[256]{0:T(256)(128)(2,1)} %param.16) | copy-start | bytes 1540
  20.0 2.2 %copy-start.6 = (bf16[256]{0:T(256)(128)(2,1)S(1)}, bf16[256]{0:T(256)(128)(2,1)}, u32[]{:S(2)}) copy-start(bf16[256]{0:T(256)(128)(2,1)} %param.17) | copy-start | bytes 1540
  26.0 19.1 %collective-permute-start.3 = (bf16[256,1280]{1,0:T(8,128)(2,1)S(1)}, bf16[256,1280]{1,0:T(8,128)(2,1)S(1)}, u32[]{:S(2)}, u32[]{:S(2)}) collective-permute-start(bf16[256,1280]{1,0:T(8,128)(2,1)S(1)} %get-tuple-element.18), channel_id=1, source_target_pairs={{0,1},{1,0},{2,3},{3,2},{4,5},{5,4},{6,7},{7,6},{8,9},{9,8},{10,11... | collective-permute-start | bytes 1966088 | tf_op jit(solution)/shard_map/ppermute | solution.py:271
  47.3 1.7 %copy-start.3 = (s32[16]{0:T(128)S(1)}, s32[16]{0:T(128)}, u32[]{:S(2)}) copy-start(s32[16]{0:T(128)} %param.19) | copy-start | bytes 196
  47.3 3.6 %copy-start.2 = (bf16[1280]{0:T(1024)(128)(2,1)S(1)}, bf16[1280]{0:T(1024)(128)(2,1)}, u32[]{:S(2)}) copy-start(bf16[1280]{0:T(1024)(128)(2,1)} %param.15) | copy-start | bytes 7684
Sparse Core Ops, SparseCore 0:
  49.1 29.7 all-gather.1

commit v11 on v6

--- a/solution.py
+++ b/solution.py
@@ -68,10 +68,10 @@
             q = q_ref[:, g * HEAD:(g + 1) * HEAD]
             scores = lax.dot_general(
                 q, keys, (((1,), (1,)), ((), ())), preferred_element_type=jnp.float32
-            ) * scale
+            )
             scores = jnp.where(allowed, scores, neg_large)
             top = jnp.max(scores, axis=1, keepdims=True)
-            expo = jnp.exp(scores - top)
+            expo = jnp.exp((scores - top) * scale)
             denom = jnp.sum(expo, axis=1, keepdims=True)
             acc = jnp.dot(expo.astype(jnp.bfloat16), values, preferred_element_type=jnp.float32)
             out = jnp.where(live, acc / jnp.where(live, denom, 1.0), 0.0)

time: 98.9 us -> 99.3 us (level)
  transfers between devices with their start and end apart: 7 -> 7, of which waited for: 3 -> 3; matrix products, arithmetic and copies ran while one was open for 31% -> 30% of each run, Pallas kernels for 0% -> 0%
where the time goes in v11:
time: 99.3 us; the launch traced here: 97.6 us
  waiting for transfers between devices  28.2 us (28%)
  matrix products  20.3 us (20%)
  between operations  15.6 us (16%)
  Pallas kernels  10.1 us (10%)
  local copies, waits for them, and re-layouts  9.5 us (10%)
  other arithmetic  7.49 us (8%)
  starting transfers between devices  6.4 us (6%)
    dot_general x8, matrix products, project(): jnp.dot(chunk, lax.dynamic_slice_in_dim(weight, source * width, width, 0)...  20.3 us
    ppermute x3, waiting for transfers between devices, on_device(): squares = squares + lax.ppermute(part_sq, 'tp', perm)  17.4 us
    all_gather x1, waiting for transfers between devices, on_device(): lax.all_gather(jnp.concatenate([key, value], axis=1), 'blk', axis=0, tile...  10.8 us
    pallas_call x1, Pallas kernels, window_attention(): pl.pallas_call(kernel, grid_spec=spec, out_shape=jax.ShapeDtypeStruct((ro...  10.1 us
    ppermute x3, starting transfers between devices, on_device(): got = lax.ppermute(scaled, 'tp', perm)  3.71 us
    unnamed x13, local copies, waits for them, and re-layouts  3.65 us
    ppermute x3, starting transfers between devices, on_device(): squares = squares + lax.ppermute(part_sq, 'tp', perm)  2.65 us
    convert_element_type x2, other arithmetic, on_device(): scaled = (wide * norm_gain.astype(jnp.float32)).astype(jnp.bfloat16)  2.05 us
  transfers between devices with their start and end apart: 7, of which 3 were waited for; matrix products, arithmetic and copies ran while one was open for 30% of the time, Pallas kernels for 0%

profile of v11, /device:TPU:9, one launch (start us, length us, event | category | flops | bytes accessed | tf_op | source)
XLA Modules:
  0.0 97.6 jit_solution(9467089452937503347)
XLA Ops:
  7.9 1.4 %fusion.18 = (bf16[256,1280]{1,0:T(8,128)(2,1)S(1)}, f32[256]{0:T(256)S(1)}) fusion(bf16[256,1280]{1,0:T(8,128)(2,1)} %param.10, f32[1280]{0:T(1024)S(1)} %convert_element_type.43), kind=kLoop, calls=%fused_computation.14 | loop fusion | flops 1638144 | bytes 1316864 | tf_op jit(solution)/shard_map/convert_element_type | solution.py:133
  9.3 2.2 %collective-permute-start.5 = (bf16[256,1280]{1,0:T(8,128)(2,1)S(1)}, bf16[256,1280]{1,0:T(8,128)(2,1)}, u32[]{:S(2)}, u32[]{:S(2)}) collective-permute-start(bf16[256,1280]{1,0:T(8,128)(2,1)S(1)} %get-tuple-element.12), channel_id=1, source_target_pairs={{0,3},{1,2},{2,1},{3,0},{4,7},{5,6},{6,5},{7,4},{8,11},{9,10},{10,... | collective-permute-start | bytes 1966088 | tf_op jit(solution)/shard_map/ppermute | solution.py:155
  12.0 1.2 %collective-permute-start.1 = (f32[256]{0:T(256)S(1)}, f32[256]{0:T(256)S(1)}, u32[]{:S(2)}, u32[]{:S(2)}) collective-permute-start(f32[256]{0:T(256)S(1)} %get-tuple-element.13), channel_id=1, source_target_pairs={{0,2},{1,3},{2,0},{3,1},{4,6},{5,7},{6,4},{7,5},{8,10},{9,11},{10,... | collective-permute-start | bytes 3080 | tf_op jit(solution)/shard_map/ppermute | solution.py:138
  13.2 1.2 %collective-permute-start.2 = (f32[256]{0:T(256)S(1)}, f32[256]{0:T(256)S(1)}, u32[]{:S(2)}, u32[]{:S(2)}) collective-permute-start(f32[256]{0:T(256)S(1)} %get-tuple-element.13), channel_id=1, source_target_pairs={{0,3},{1,2},{2,1},{3,0},{4,7},{5,6},{6,5},{7,4},{8,11},{9,10},{10,... | collective-permute-start | bytes 3080 | tf_op jit(solution)/shard_map/ppermute | solution.py:138
  14.4 3.6 %constant_dynamic-update-slice_fusion.1 = bf16[5120,512]{1,0:T(8,128)(2,1)} fusion(bf16[5120,256]{1,0:T(8,128)(2,1)} %param.13), kind=kLoop, calls=%fused_computation.59 | loop fusion | bytes 5242880
  18.3 1.7 %constant_dynamic-update-slice_fusion = bf16[5120,512]{1,0:T(8,128)(2,1)} fusion(bf16[5120,512]{1,0:T(8,128)(2,1)} %constant_dynamic-update-slice_fusion.1, bf16[5120,256]{1,0:T(8,128)(2,1)S(1)} %copy-done), kind=kLoop, calls=%fused_computation.58 | loop fusion | bytes 5242880 | tf_op jit(solution)/shard_map/concatenate | solution.py:139
  20.0 1.8 %fusion.25 = f32[256,512]{1,0:T(8,128)S(1)} fusion(bf16[256,1280]{1,0:T(8,128)(2,1)S(1)} %get-tuple-element.12, bf16[5120,512]{1,0:T(8,128)(2,1)} %constant_dynamic-update-slice_fusion, s32[]{:T(128)S(6)} %select_n.38), kind=kOutput, calls=%fused_computation.21 | convolution fusion | flops 335544320 | bytes 2490372 | tf_op jit(solution)/shard_map/dot_general | solution.py:145
  22.4 3.6 %collective-permute-done = f32[256]{0:T(256)S(1)} collective-permute-done((f32[256]{0:T(256)S(1)}, f32[256]{0:T(256)S(1)}, u32[]{:S(2)}, u32[]{:S(2)}) %collective-permute-start) | collective-permute-done | bytes 1056 | tf_op jit(solution)/shard_map/ppermute | solution.py:138
  26.0 1.3 %collective-permute-start.3 = (bf16[256,1280]{1,0:T(8,128)(2,1)S(1)}, bf16[256,1280]{1,0:T(8,128)(2,1)S(1)}, u32[]{:S(2)}, u32[]{:S(2)}) collective-permute-start(bf16[256,1280]{1,0:T(8,128)(2,1)S(1)} %get-tuple-element.12), channel_id=1, source_target_pairs={{0,1},{1,0},{2,3},{3,2},{4,5},{5,4},{6,7},{7,6},{8,9},{9,8},{10,11... | collective-permute-start | bytes 1966088 | tf_op jit(solution)/shard_map/ppermute | solution.py:155
  27.3 13.8 %collective-permute-done.1 = f32[256]{0:T(256)S(1)} collective-permute-done((f32[256]{0:T(256)S(1)}, f32[256]{0:T(256)S(1)}, u32[]{:S(2)}, u32[]{:S(2)}) %collective-permute-start.1) | collective-permute-done | bytes 1056 | tf_op jit(solution)/shard_map/ppermute | solution.py:138
  41.1 2.0 %fusion.19 = f32[256,512]{1,0:T(8,128)S(1)} fusion(bf16[256,1280]{1,0:T(8,128)(2,1)} %collective-permute-done.5, bf16[5120,512]{1,0:T(8,128)(2,1)} %constant_dynamic-update-slice_fusion, s32[]{:T(128)S(6)} %select_n.41), kind=kOutput, calls=%fused_computation.15 | convolution fusion | flops 335544320 | bytes 2490372 | tf_op jit(solution)/shard_map/dot_general | solution.py:145
  43.1 2.0 %fusion.21 = f32[256,512]{1,0:T(8,128)S(1)} fusion(bf16[256,1280]{1,0:T(8,128)(2,1)} %collective-permute-done.4, bf16[5120,512]{1,0:T(8,128)(2,1)} %constant_dynamic-update-slice_fusion, s32[]{:T(128)S(6)} %select_n.40), kind=kOutput, calls=%fused_computation.17 | convolution fusion | flops 335544320 | bytes 2490372 | tf_op jit(solution)/shard_map/dot_general | solution.py:145
  45.2 1.8 %fusion.33 = f32[256,512]{1,0:T(8,128)S(1)} fusion(f32[256,512]{1,0:T(8,128)S(1)} %fusion.19, f32[256,512]{1,0:T(8,128)S(1)} %fusion.21, f32[256,512]{1,0:T(8,128)S(1)} %fusion.25, bf16[256,1280]{1,0:T(8,128)(2,1)S(1)} %collective-permute-done.3, bf16[5120,512]{1,0:T(8,128)(2,1)} %constant_dynamic-update-slice_fusion, s32[]{:T(128)S(6)} %select_n.39), kind=kOutput, calls=%fused_computation.26 | convolution fusion | flops 335937536 | bytes 4063236 | tf_op jit(solution)/shard_map/dot_general | solution.py:145
  48.3 0.7 pad_maximum_fusion.2
  51.0 0.8 copy.21.qs_ref
  53.8 2.9 %fusion.6 = f32[256,1280]{1,0:T(8,128)S(1)} fusion(bf16[256,1280]{1,0:T(8,128)(2,1)S(1)} %get-tuple-element.12, bf16[5120,1280]{1,0:T(8,128)(2,1)} %param.12, s32[]{:T(128)S(6)} %select_n.38), kind=kOutput, calls=%fused_computation.6 | convolution fusion | flops 838860800 | bytes 5242884 | tf_op jit(solution)/shard_map/dot_general | solution.py:145
  56.7 3.4 %fusion = f32[256,1280]{1,0:T(8,128)S(1)} fusion(bf16[256,1280]{1,0:T(8,128)(2,1)} %collective-permute-done.5, bf16[5120,1280]{1,0:T(8,128)(2,1)} %param.12, s32[]{:T(128)S(6)} %select_n.41), kind=kOutput, calls=%fused_computation | convolution fusion | flops 838860800 | bytes 5242884 | tf_op jit(solution)/shard_map/dot_general | solution.py:145
  60.1 3.2 %fusion.2 = f32[256,1280]{1,0:T(8,128)S(1)} fusion(bf16[256,1280]{1,0:T(8,128)(2,1)} %collective-permute-done.4, bf16[5120,1280]{1,0:T(8,128)(2,1)} %param.12, s32[]{:T(128)S(6)} %select_n.40), kind=kOutput, calls=%fused_computation.2 | convolution fusion | flops 838860800 | bytes 5242884 | tf_op jit(solution)/shard_map/dot_general | solution.py:145
  63.3 3.1 %multiply_add_fusion = f32[256,1280]{1,0:T(8,128)S(1)} fusion(f32[1280]{0:T(1024)S(1)} %convert_element_type.45, f32[256]{0:T(256)S(1)} %add_rsqrt_fusion, f32[256,1280]{1,0:T(8,128)S(1)} %fusion, f32[256,1280]{1,0:T(8,128)S(1)} %fusion.2, f32[256,1280]{1,0:T(8,128)S(1)} %fusion.6, bf16[256,1280]{1,0:T(8,128)(2,1)S(1)} %collective-permute-done.3, ...), kind=kOutput, calls=%fused_computation.23 | convolution fusion | flops 840499200 | bytes 9181188 | tf_op jit(solution)/shard_map/dot_general | solution.py:145
  67.0 1.1 %copy.20.q_ref = bf16[256,1280]{1,0:T(8,128)(2,1)} copy(bf16[256,1280]{0,1:T(8,128)(2,1)S(1)} %bitcast.32) | data formatting | bytes 1310720 | tf_op jit(solution)/shard_map/convert_element_type | solution.py:171
  68.1 10.8 %all-gather.2.cloned.1.call-done.k_ref.v_ref = bf16[2048,512]{1,0:T(8,128)(2,1)} async-done(((bf16[256,512]{1,0:T(8,128)(2,1)}), bf16[2048,512]{1,0:T(8,128)(2,1)}) %all-gather.2.cloned.1.call-update) | async-done | bytes 2097168 | tf_op jit(solution)/shard_map/all_gather | solution.py:183
  79.0 1.0 dynamic-slice_bitcast_fusion.3
  79.9 0.7 pad_maximum_fusion.3
  80.7 10.1 %shard_map.113 = bf16[256,1280]{1,0:T(8,128)(2,1)} custom-call(s32[1]{0:T(128)} %bitcast.first_ref, bf16[256,1280]{1,0:T(8,128)(2,1)} %copy.20.q_ref, bf16[2048,512]{1,0:T(8,128)(2,1)} %all-gather.2.cloned.1.call-done.k_ref.v_ref, bf16[2048,512]{1,0:T(8,128)(2,1)} %all-gather.2.cloned.1.call-done.k_ref.v_ref, s32[256,1]{1,0:T(8,128)} %copy.21.qs_ref, ...), custom_call_target="tpu_custom_call" | custom-call | tf_op jit(solution)/shard_map/pallas_call | solution.py:94
  (49 shorter events, 6.6 us)
Async XLA Ops:
  7.2 71.8 %all-gather.2.cloned.1.call-start = ((), (), s32[]{:S(2)}) async-start(), calls=%async_computation | async-start | bytes 2359296 | tf_op jit(solution)/shard_map/all_gather | solution.py:183
  9.3 31.8 %collective-permute-start.5 = (bf16[256,1280]{1,0:T(8,128)(2,1)S(1)}, bf16[256,1280]{1,0:T(8,128)(2,1)}, u32[]{:S(2)}, u32[]{:S(2)}) collective-permute-start(bf16[256,1280]{1,0:T(8,128)(2,1)S(1)} %get-tuple-element.12), channel_id=1, source_target_pairs={{0,3},{1,2},{2,1},{3,0},{4,7},{5,6},{6,5},{7,4},{8,11},{9,10},{10,... | collective-permute-start | bytes 1966088 | tf_op jit(solution)/shard_map/ppermute | solution.py:155
  11.5 31.6 %collective-permute-start.4 = (bf16[256,1280]{1,0:T(8,128)(2,1)S(1)}, bf16[256,1280]{1,0:T(8,128)(2,1)}, u32[]{:S(2)}, u32[]{:S(2)}) collective-permute-start(bf16[256,1280]{1,0:T(8,128)(2,1)S(1)} %get-tuple-element.12), channel_id=1, source_target_pairs={{0,2},{1,3},{2,0},{3,1},{4,6},{5,7},{6,4},{7,5},{8,10},{9,11},{10,... | collective-permute-start | bytes 1966088 | tf_op jit(solution)/shard_map/ppermute | solution.py:155
  11.7 14.3 %collective-permute-start = (f32[256]{0:T(256)S(1)}, f32[256]{0:T(256)S(1)}, u32[]{:S(2)}, u32[]{:S(2)}) collective-permute-start(f32[256]{0:T(256)S(1)} %get-tuple-element.13), channel_id=1, source_target_pairs={{0,1},{1,0},{2,3},{3,2},{4,5},{5,4},{6,7},{7,6},{8,9},{9,8},{10,11... | collective-permute-start | bytes 3080 | tf_op jit(solution)/shard_map/ppermute | solution.py:138
  12.0 29.1 %collective-permute-start.1 = (f32[256]{0:T(256)S(1)}, f32[256]{0:T(256)S(1)}, u32[]{:S(2)}, u32[]{:S(2)}) collective-permute-start(f32[256]{0:T(256)S(1)} %get-tuple-element.13), channel_id=1, source_target_pairs={{0,2},{1,3},{2,0},{3,1},{4,6},{5,7},{6,4},{7,5},{8,10},{9,11},{10,... | collective-permute-start | bytes 3080 | tf_op jit(solution)/shard_map/ppermute | solution.py:138
  13.2 27.9 %collective-permute-start.2 = (f32[256]{0:T(256)S(1)}, f32[256]{0:T(256)S(1)}, u32[]{:S(2)}, u32[]{:S(2)}) collective-permute-start(f32[256]{0:T(256)S(1)} %get-tuple-element.13), channel_id=1, source_target_pairs={{0,3},{1,2},{2,1},{3,0},{4,7},{5,6},{6,5},{7,4},{8,11},{9,10},{10,... | collective-permute-start | bytes 3080 | tf_op jit(solution)/shard_map/ppermute | solution.py:138
  14.4 3.6 %copy-start.3 = (s32[8]{0:T(128)S(1)}, s32[8]{0:T(128)}, u32[]{:S(2)}) copy-start(s32[8]{0:T(128)} %param.18) | copy-start | bytes 100
  14.4 3.9 %copy-start = (bf16[5120,256]{1,0:T(8,128)(2,1)S(1)}, bf16[5120,256]{1,0:T(8,128)(2,1)}, u32[]{:S(2)}) copy-start(bf16[5120,256]{1,0:T(8,128)(2,1)} %param.14) | copy-start | bytes 7864324
  20.0 2.2 %copy-start.4 = (bf16[256]{0:T(256)(128)(2,1)S(1)}, bf16[256]{0:T(256)(128)(2,1)}, u32[]{:S(2)}) copy-start(bf16[256]{0:T(256)(128)(2,1)} %param.16) | copy-start | bytes 1540
  20.0 2.2 %copy-start.5 = (bf16[256]{0:T(256)(128)(2,1)S(1)}, bf16[256]{0:T(256)(128)(2,1)}, u32[]{:S(2)}) copy-start(bf16[256]{0:T(256)(128)(2,1)} %param.17) | copy-start | bytes 1540
  26.0 19.1 %collective-permute-start.3 = (bf16[256,1280]{1,0:T(8,128)(2,1)S(1)}, bf16[256,1280]{1,0:T(8,128)(2,1)S(1)}, u32[]{:S(2)}, u32[]{:S(2)}) collective-permute-start(bf16[256,1280]{1,0:T(8,128)(2,1)S(1)} %get-tuple-element.12), channel_id=1, source_target_pairs={{0,1},{1,0},{2,3},{3,2},{4,5},{5,4},{6,7},{7,6},{8,9},{9,8},{10,11... | collective-permute-start | bytes 1966088 | tf_op jit(solution)/shard_map/ppermute | solution.py:155
  47.0 2.0 %copy-start.2 = (s32[16]{0:T(128)S(1)}, s32[16]{0:T(128)}, u32[]{:S(2)}) copy-start(s32[16]{0:T(128)} %param.19) | copy-start | bytes 196
  47.0 4.0 %copy-start.1 = (bf16[1280]{0:T(1024)(128)(2,1)S(1)}, bf16[1280]{0:T(1024)(128)(2,1)}, u32[]{:S(2)}) copy-start(bf16[1280]{0:T(1024)(128)(2,1)} %param.15) | copy-start | bytes 7684
Sparse Core Ops, SparseCore 0:
  49.1 29.7 all-gather.1

commit v12 on v6

--- a/solution.py
+++ b/solution.py
@@ -49,7 +49,7 @@
         for s in range(1, size)
     ]
 
-def window_attention(first, query, both, q_seg, q_pos, k_seg, k_pos, docs, interpret=False):
+def window_attention(first, query, both, q_seg, q_pos, k_seg, k_pos, docs, pages, interpret=False):
     rows, q_width = query.shape
     count, both_width = both.shape
     span = k_seg.shape[0]
@@ -57,7 +57,13 @@
     group = q_width // (kv_dev * HEAD)
     scale = 1.0 / float(HEAD) ** 0.5
 
-    def kernel(first_ref, q_ref, k_ref, v_ref, qs_ref, qp_ref, ks_ref, kp_ref, o_ref):
+    slots = pages.shape[0]
+
+    def kernel(first_ref, page_ref, q_ref, k_ref, v_ref, qs_ref, qp_ref, ks_ref, kp_ref, o_ref, c_ref):
+        for j in range(slots):
+            row = pl.multiple_of(page_ref[j] * PAGE, PAGE)
+            c_ref[j, 0] = k_ref[pl.ds(row, PAGE), :]
+            c_ref[j, 1] = v_ref[pl.ds(row, PAGE), :]
         start = pl.multiple_of(first_ref[0], PAGE)
         keys = k_ref[pl.ds(start, span), :]
         values = v_ref[pl.ds(start, span), :]
@@ -78,26 +84,33 @@
             o_ref[:, g * HEAD:(g + 1) * HEAD] = out.astype(o_ref.dtype)
 
     spec = pltpu.PrefetchScalarGridSpec(
-        num_scalar_prefetch=1,
+        num_scalar_prefetch=2,
         grid=(kv_dev,),
         in_specs=[
-            pl.BlockSpec((rows, group * HEAD), lambda c, f: (0, c)),
-            pl.BlockSpec((count, HEAD), lambda c, f: (0, c)),
-            pl.BlockSpec((count, HEAD), lambda c, f: (0, kv_dev + c)),
-            pl.BlockSpec((rows, 1), lambda c, f: (0, 0)),
-            pl.BlockSpec((rows, 1), lambda c, f: (0, 0)),
-            pl.BlockSpec((1, span), lambda c, f: (0, 0)),
-            pl.BlockSpec((1, span), lambda c, f: (0, 0)),
+            pl.BlockSpec((rows, group * HEAD), lambda c, f, p: (0, c)),
+            pl.BlockSpec((count, HEAD), lambda c, f, p: (0, c)),
+            pl.BlockSpec((count, HEAD), lambda c, f, p: (0, kv_dev + c)),
+            pl.BlockSpec((rows, 1), lambda c, f, p: (0, 0)),
+            pl.BlockSpec((rows, 1), lambda c, f, p: (0, 0)),
+            pl.BlockSpec((1, span), lambda c, f, p: (0, 0)),
+            pl.BlockSpec((1, span), lambda c, f, p: (0, 0)),
         ],
-        out_specs=pl.BlockSpec((rows, group * HEAD), lambda c, f: (0, c)),
+        out_specs=[
+            pl.BlockSpec((rows, group * HEAD), lambda c, f, p: (0, c)),
+            pl.BlockSpec((slots, 2, PAGE, HEAD), lambda c, f, p: (0, 0, 0, c)),
+        ],
     )
     return pl.pallas_call(
         kernel,
         grid_spec=spec,
-        out_shape=jax.ShapeDtypeStruct((rows, q_width), jnp.bfloat16),
+        out_shape=[
+            jax.ShapeDtypeStruct((rows, q_width), jnp.bfloat16),
+            jax.ShapeDtypeStruct((slots, 2, PAGE, kv_dev * HEAD), both.dtype),
+        ],
         interpret=interpret,
     )(
         first.reshape(1).astype(jnp.int32),
+        pages.astype(jnp.int32),
         query,
         both,
         both,
@@ -187,14 +200,14 @@
     first = jnp.clip(me * rows - longest, 0, count - span)
     k_pos = first + jnp.arange(span, dtype=jnp.int32)
     k_seg, k_off = token_meta(k_pos, lengths)
-    mixed = window_attention(first, query, both, q_seg, own_pos, k_seg, k_pos, docs)
     numbers = jnp.arange(page_table.shape[0], dtype=jnp.int32)
-    cache = []
-    for j in range(slots):
-        page = jnp.sum(jnp.where(page_table == me * slots + j, numbers, 0))
-        held = lax.dynamic_slice_in_dim(both, page * PAGE, PAGE, 0)
-        cache.append(jnp.stack([held[:, :kv_width], held[:, kv_width:]], axis=0))
-    kv_cache = jnp.stack(cache, axis=0)
+    pages = jnp.stack(
+        [jnp.sum(jnp.where(page_table == me * slots + j, numbers, 0)) for j in range(slots)]
+    )
+    pages = jnp.clip(pages, 0, count // PAGE - 1)
+    mixed, kv_cache = window_attention(
+        first, query, both, q_seg, own_pos, k_seg, k_pos, docs, pages
+    )
     return (mixed, kv_cache)
 
 

time: 98.9 us -> 97.9 us (0.990)
  between operations: 15.6 us -> 14.3 us
  other arithmetic: 7.49 us -> 8.76 us
    min x0 -> x1, other arithmetic: none -> 1.99 us  [on_device(): pages = jnp.clip(pages, 0, count // PAGE - 1)]
  transfers between devices with their start and end apart: 7 -> 7, of which waited for: 3 -> 3; matrix products, arithmetic and copies ran while one was open for 31% -> 33% of each run, Pallas kernels for 0% -> 0%
where the time goes in v12:
time: 97.9 us; the launch traced here: 96.3 us
  waiting for transfers between devices  27.5 us (28%)
  matrix products  20.3 us (21%)
  between operations  14.3 us (15%)
  Pallas kernels  10.5 us (11%)
  other arithmetic  8.76 us (9%)
  local copies, waits for them, and re-layouts  8.54 us (9%)
  starting transfers between devices  6.4 us (7%)
    dot_general x8, matrix products, project(): jnp.dot(chunk, lax.dynamic_slice_in_dim(weight, source * width, width, 0)...  20.3 us
    ppermute x3, waiting for transfers between devices, on_device(): squares = squares + lax.ppermute(part_sq, 'tp', perm)  17.4 us
    pallas_call x1, Pallas kernels, window_attention(): pl.pallas_call(kernel, grid_spec=spec, out_shape=[jax.ShapeDtypeStruct((r...  10.5 us
    all_gather x1, waiting for transfers between devices, on_device(): lax.all_gather(jnp.concatenate([key, value], axis=1), 'blk', axis=0, tile...  10.1 us
    ppermute x3, starting transfers between devices, on_device(): got = lax.ppermute(scaled, 'tp', perm)  3.71 us
    unnamed x13, local copies, waits for them, and re-layouts  3.64 us
    ppermute x3, starting transfers between devices, on_device(): squares = squares + lax.ppermute(part_sq, 'tp', perm)  2.65 us
    convert_element_type x2, other arithmetic, on_device(): scaled = (wide * norm_gain.astype(jnp.float32)).astype(jnp.bfloat16)  2.05 us
  transfers between devices with their start and end apart: 7, of which 3 were waited for; matrix products, arithmetic and copies ran while one was open for 33% of the time, Pallas kernels for 0%

profile of v12, /device:TPU:9, one launch (start us, length us, event | category | flops | bytes accessed | tf_op | source)
XLA Modules:
  0.0 96.3 jit_solution(14466912461389569277)
XLA Ops:
  7.9 1.4 %fusion.18 = (bf16[256,1280]{1,0:T(8,128)(2,1)S(1)}, f32[256]{0:T(256)S(1)}) fusion(bf16[256,1280]{1,0:T(8,128)(2,1)} %param.10, f32[1280]{0:T(1024)S(1)} %convert_element_type.43), kind=kLoop, calls=%fused_computation.14 | loop fusion | flops 1638144 | bytes 1316864 | tf_op jit(solution)/shard_map/convert_element_type | solution.py:146
  9.3 2.2 %collective-permute-start.5 = (bf16[256,1280]{1,0:T(8,128)(2,1)S(1)}, bf16[256,1280]{1,0:T(8,128)(2,1)}, u32[]{:S(2)}, u32[]{:S(2)}) collective-permute-start(bf16[256,1280]{1,0:T(8,128)(2,1)S(1)} %get-tuple-element.8), channel_id=1, source_target_pairs={{0,3},{1,2},{2,1},{3,0},{4,7},{5,6},{6,5},{7,4},{8,11},{9,10},{10,... | collective-permute-start | bytes 1966088 | tf_op jit(solution)/shard_map/ppermute | solution.py:168
  12.0 1.2 %collective-permute-start.1 = (f32[256]{0:T(256)S(1)}, f32[256]{0:T(256)S(1)}, u32[]{:S(2)}, u32[]{:S(2)}) collective-permute-start(f32[256]{0:T(256)S(1)} %get-tuple-element.9), channel_id=1, source_target_pairs={{0,2},{1,3},{2,0},{3,1},{4,6},{5,7},{6,4},{7,5},{8,10},{9,11},{10,... | collective-permute-start | bytes 3080 | tf_op jit(solution)/shard_map/ppermute | solution.py:151
  13.2 1.2 %collective-permute-start.2 = (f32[256]{0:T(256)S(1)}, f32[256]{0:T(256)S(1)}, u32[]{:S(2)}, u32[]{:S(2)}) collective-permute-start(f32[256]{0:T(256)S(1)} %get-tuple-element.9), channel_id=1, source_target_pairs={{0,3},{1,2},{2,1},{3,0},{4,7},{5,6},{6,5},{7,4},{8,11},{9,10},{10,... | collective-permute-start | bytes 3080 | tf_op jit(solution)/shard_map/ppermute | solution.py:151
  14.4 3.6 %constant_dynamic-update-slice_fusion.1 = bf16[5120,512]{1,0:T(8,128)(2,1)} fusion(bf16[5120,256]{1,0:T(8,128)(2,1)} %param.13), kind=kLoop, calls=%fused_computation.52 | loop fusion | bytes 5242880
  18.3 1.7 %constant_dynamic-update-slice_fusion = bf16[5120,512]{1,0:T(8,128)(2,1)} fusion(bf16[5120,512]{1,0:T(8,128)(2,1)} %constant_dynamic-update-slice_fusion.1, bf16[5120,256]{1,0:T(8,128)(2,1)S(1)} %copy-done), kind=kLoop, calls=%fused_computation.51 | loop fusion | bytes 5242880 | tf_op jit(solution)/shard_map/concatenate | solution.py:152
  20.0 1.8 %fusion.25 = f32[256,512]{1,0:T(8,128)S(1)} fusion(bf16[256,1280]{1,0:T(8,128)(2,1)S(1)} %get-tuple-element.8, bf16[5120,512]{1,0:T(8,128)(2,1)} %constant_dynamic-update-slice_fusion, s32[]{:T(128)S(6)} %select_n.34), kind=kOutput, calls=%fused_computation.21 | convolution fusion | flops 335544320 | bytes 2490372 | tf_op jit(solution)/shard_map/dot_general | solution.py:158
  22.4 3.6 %collective-permute-done = f32[256]{0:T(256)S(1)} collective-permute-done((f32[256]{0:T(256)S(1)}, f32[256]{0:T(256)S(1)}, u32[]{:S(2)}, u32[]{:S(2)}) %collective-permute-start) | collective-permute-done | bytes 1056 | tf_op jit(solution)/shard_map/ppermute | solution.py:151
  26.0 1.3 %collective-permute-start.3 = (bf16[256,1280]{1,0:T(8,128)(2,1)S(1)}, bf16[256,1280]{1,0:T(8,128)(2,1)S(1)}, u32[]{:S(2)}, u32[]{:S(2)}) collective-permute-start(bf16[256,1280]{1,0:T(8,128)(2,1)S(1)} %get-tuple-element.8), channel_id=1, source_target_pairs={{0,1},{1,0},{2,3},{3,2},{4,5},{5,4},{6,7},{7,6},{8,9},{9,8},{10,11... | collective-permute-start | bytes 1966088 | tf_op jit(solution)/shard_map/ppermute | solution.py:168
  27.3 13.8 %collective-permute-done.1 = f32[256]{0:T(256)S(1)} collective-permute-done((f32[256]{0:T(256)S(1)}, f32[256]{0:T(256)S(1)}, u32[]{:S(2)}, u32[]{:S(2)}) %collective-permute-start.1) | collective-permute-done | bytes 1056 | tf_op jit(solution)/shard_map/ppermute | solution.py:151
  41.1 2.0 %fusion.19 = f32[256,512]{1,0:T(8,128)S(1)} fusion(bf16[256,1280]{1,0:T(8,128)(2,1)} %collective-permute-done.5, bf16[5120,512]{1,0:T(8,128)(2,1)} %constant_dynamic-update-slice_fusion, s32[]{:T(128)S(6)} %select_n.37), kind=kOutput, calls=%fused_computation.15 | convolution fusion | flops 335544320 | bytes 2490372 | tf_op jit(solution)/shard_map/dot_general | solution.py:158
  43.1 2.0 %fusion.21 = f32[256,512]{1,0:T(8,128)S(1)} fusion(bf16[256,1280]{1,0:T(8,128)(2,1)} %collective-permute-done.4, bf16[5120,512]{1,0:T(8,128)(2,1)} %constant_dynamic-update-slice_fusion, s32[]{:T(128)S(6)} %select_n.36), kind=kOutput, calls=%fused_computation.17 | convolution fusion | flops 335544320 | bytes 2490372 | tf_op jit(solution)/shard_map/dot_general | solution.py:158
  45.2 1.8 %fusion.33 = f32[256,512]{1,0:T(8,128)S(1)} fusion(f32[256,512]{1,0:T(8,128)S(1)} %fusion.19, f32[256,512]{1,0:T(8,128)S(1)} %fusion.21, f32[256,512]{1,0:T(8,128)S(1)} %fusion.25, bf16[256,1280]{1,0:T(8,128)(2,1)S(1)} %collective-permute-done.3, bf16[5120,512]{1,0:T(8,128)(2,1)} %constant_dynamic-update-slice_fusion, s32[]{:T(128)S(6)} %select_n.35), kind=kOutput, calls=%fused_computation.26 | convolution fusion | flops 335937536 | bytes 4063236 | tf_op jit(solution)/shard_map/dot_general | solution.py:158
  48.3 0.7 pad_maximum_fusion.2
  49.0 0.8 copy.21.qs_ref
  50.5 0.7 fusion.53
  51.3 2.0 %add_clamp_fusion.page_ref = s32[2]{0:T(128)} fusion(s32[1]{0:T(128)} %bitcast.2, s32[1]{0:T(128)} %bitcast.1), kind=kLoop, calls=%fused_computation.69 | loop fusion | flops 4 | bytes 16 | tf_op jit(solution)/shard_map/jit(clip)/min | solution.py:207
  54.5 2.9 %fusion.6 = f32[256,1280]{1,0:T(8,128)S(1)} fusion(bf16[256,1280]{1,0:T(8,128)(2,1)S(1)} %get-tuple-element.8, bf16[5120,1280]{1,0:T(8,128)(2,1)} %param.12, s32[]{:T(128)S(6)} %select_n.34), kind=kOutput, calls=%fused_computation.6 | convolution fusion | flops 838860800 | bytes 5242884 | tf_op jit(solution)/shard_map/dot_general | solution.py:158
  57.5 3.3 %fusion = f32[256,1280]{1,0:T(8,128)S(1)} fusion(bf16[256,1280]{1,0:T(8,128)(2,1)} %collective-permute-done.5, bf16[5120,1280]{1,0:T(8,128)(2,1)} %param.12, s32[]{:T(128)S(6)} %select_n.37), kind=kOutput, calls=%fused_computation | convolution fusion | flops 838860800 | bytes 5242884 | tf_op jit(solution)/shard_map/dot_general | solution.py:158
  60.8 3.2 %fusion.2 = f32[256,1280]{1,0:T(8,128)S(1)} fusion(bf16[256,1280]{1,0:T(8,128)(2,1)} %collective-permute-done.4, bf16[5120,1280]{1,0:T(8,128)(2,1)} %param.12, s32[]{:T(128)S(6)} %select_n.36), kind=kOutput, calls=%fused_computation.2 | convolution fusion | flops 838860800 | bytes 5242884 | tf_op jit(solution)/shard_map/dot_general | solution.py:158
  64.0 3.1 %multiply_add_fusion = f32[256,1280]{1,0:T(8,128)S(1)} fusion(f32[1280]{0:T(1024)S(1)} %convert_element_type.45, f32[256]{0:T(256)S(1)} %add_rsqrt_fusion, f32[256,1280]{1,0:T(8,128)S(1)} %fusion, f32[256,1280]{1,0:T(8,128)S(1)} %fusion.2, f32[256,1280]{1,0:T(8,128)S(1)} %fusion.6, bf16[256,1280]{1,0:T(8,128)(2,1)S(1)} %collective-permute-done.3, ...), kind=kOutput, calls=%fused_computation.23 | convolution fusion | flops 840499200 | bytes 9181188 | tf_op jit(solution)/shard_map/dot_general | solution.py:158
  67.8 1.1 %copy.20.q_ref = bf16[256,1280]{1,0:T(8,128)(2,1)} copy(bf16[256,1280]{0,1:T(8,128)(2,1)S(1)} %bitcast.22) | data formatting | bytes 1310720 | tf_op jit(solution)/shard_map/convert_element_type | solution.py:184
  68.9 10.1 %all-gather.2.cloned.1.call-done.k_ref.v_ref = bf16[2048,512]{1,0:T(8,128)(2,1)} async-done(((bf16[256,512]{1,0:T(8,128)(2,1)}), bf16[2048,512]{1,0:T(8,128)(2,1)}) %all-gather.2.cloned.1.call-update) | async-done | bytes 2097168 | tf_op jit(solution)/shard_map/all_gather | solution.py:196
  79.0 10.5 %shard_map.113 = (bf16[256,1280]{1,0:T(8,128)(2,1)}, bf16[2,2,128,256]{3,2,1,0:T(8,128)(2,1)}) custom-call(s32[1]{0:T(128)} %bitcast.first_ref, s32[2]{0:T(128)} %add_clamp_fusion.page_ref, bf16[256,1280]{1,0:T(8,128)(2,1)} %copy.20.q_ref, bf16[2048,512]{1,0:T(8,128)(2,1)} %all-gather.2.cloned.1.call-done.k_ref.v_ref, ...), custom_call_target="tpu_custom_call" | custom-call | tf_op jit(solution)/shard_map/pallas_call | solution.py:103
  (47 shorter events, 5.9 us)
Async XLA Ops:
  7.2 71.8 %all-gather.2.cloned.1.call-start = ((), (), s32[]{:S(2)}) async-start(), calls=%async_computation | async-start | bytes 2359296 | tf_op jit(solution)/shard_map/all_gather | solution.py:196
  9.3 31.8 %collective-permute-start.5 = (bf16[256,1280]{1,0:T(8,128)(2,1)S(1)}, bf16[256,1280]{1,0:T(8,128)(2,1)}, u32[]{:S(2)}, u32[]{:S(2)}) collective-permute-start(bf16[256,1280]{1,0:T(8,128)(2,1)S(1)} %get-tuple-element.8), channel_id=1, source_target_pairs={{0,3},{1,2},{2,1},{3,0},{4,7},{5,6},{6,5},{7,4},{8,11},{9,10},{10,... | collective-permute-start | bytes 1966088 | tf_op jit(solution)/shard_map/ppermute | solution.py:168
  11.5 31.6 %collective-permute-start.4 = (bf16[256,1280]{1,0:T(8,128)(2,1)S(1)}, bf16[256,1280]{1,0:T(8,128)(2,1)}, u32[]{:S(2)}, u32[]{:S(2)}) collective-permute-start(bf16[256,1280]{1,0:T(8,128)(2,1)S(1)} %get-tuple-element.8), channel_id=1, source_target_pairs={{0,2},{1,3},{2,0},{3,1},{4,6},{5,7},{6,4},{7,5},{8,10},{9,11},{10,... | collective-permute-start | bytes 1966088 | tf_op jit(solution)/shard_map/ppermute | solution.py:168
  11.7 14.3 %collective-permute-start = (f32[256]{0:T(256)S(1)}, f32[256]{0:T(256)S(1)}, u32[]{:S(2)}, u32[]{:S(2)}) collective-permute-start(f32[256]{0:T(256)S(1)} %get-tuple-element.9), channel_id=1, source_target_pairs={{0,1},{1,0},{2,3},{3,2},{4,5},{5,4},{6,7},{7,6},{8,9},{9,8},{10,11... | collective-permute-start | bytes 3080 | tf_op jit(solution)/shard_map/ppermute | solution.py:151
  12.0 29.1 %collective-permute-start.1 = (f32[256]{0:T(256)S(1)}, f32[256]{0:T(256)S(1)}, u32[]{:S(2)}, u32[]{:S(2)}) collective-permute-start(f32[256]{0:T(256)S(1)} %get-tuple-element.9), channel_id=1, source_target_pairs={{0,2},{1,3},{2,0},{3,1},{4,6},{5,7},{6,4},{7,5},{8,10},{9,11},{10,... | collective-permute-start | bytes 3080 | tf_op jit(solution)/shard_map/ppermute | solution.py:151
  13.2 27.9 %collective-permute-start.2 = (f32[256]{0:T(256)S(1)}, f32[256]{0:T(256)S(1)}, u32[]{:S(2)}, u32[]{:S(2)}) collective-permute-start(f32[256]{0:T(256)S(1)} %get-tuple-element.9), channel_id=1, source_target_pairs={{0,3},{1,2},{2,1},{3,0},{4,7},{5,6},{6,5},{7,4},{8,11},{9,10},{10,... | collective-permute-start | bytes 3080 | tf_op jit(solution)/shard_map/ppermute | solution.py:151
  14.4 3.6 %copy-start.3 = (s32[8]{0:T(128)S(1)}, s32[8]{0:T(128)}, u32[]{:S(2)}) copy-start(s32[8]{0:T(128)} %param.18) | copy-start | bytes 100
  14.4 3.9 %copy-start = (bf16[5120,256]{1,0:T(8,128)(2,1)S(1)}, bf16[5120,256]{1,0:T(8,128)(2,1)}, u32[]{:S(2)}) copy-start(bf16[5120,256]{1,0:T(8,128)(2,1)} %param.14) | copy-start | bytes 7864324
  20.0 2.2 %copy-start.4 = (bf16[256]{0:T(256)(128)(2,1)S(1)}, bf16[256]{0:T(256)(128)(2,1)}, u32[]{:S(2)}) copy-start(bf16[256]{0:T(256)(128)(2,1)} %param.16) | copy-start | bytes 1540
  20.0 2.2 %copy-start.5 = (bf16[256]{0:T(256)(128)(2,1)S(1)}, bf16[256]{0:T(256)(128)(2,1)}, u32[]{:S(2)}) copy-start(bf16[256]{0:T(256)(128)(2,1)} %param.17) | copy-start | bytes 1540
  26.0 19.1 %collective-permute-start.3 = (bf16[256,1280]{1,0:T(8,128)(2,1)S(1)}, bf16[256,1280]{1,0:T(8,128)(2,1)S(1)}, u32[]{:S(2)}, u32[]{:S(2)}) collective-permute-start(bf16[256,1280]{1,0:T(8,128)(2,1)S(1)} %get-tuple-element.8), channel_id=1, source_target_pairs={{0,1},{1,0},{2,3},{3,2},{4,5},{5,4},{6,7},{7,6},{8,9},{9,8},{10,11... | collective-permute-start | bytes 1966088 | tf_op jit(solution)/shard_map/ppermute | solution.py:168
  47.0 2.0 %copy-start.1 = (bf16[1280]{0:T(1024)(128)(2,1)S(1)}, bf16[1280]{0:T(1024)(128)(2,1)}, u32[]{:S(2)}) copy-start(bf16[1280]{0:T(1024)(128)(2,1)} %param.15) | copy-start | bytes 7684
  47.0 3.5 %copy-start.2 = (s32[16]{0:T(128)S(1)}, s32[16]{0:T(128)}, u32[]{:S(2)}) copy-start(s32[16]{0:T(128)} %param.19) | copy-start | bytes 196
Sparse Core Ops, SparseCore 0:
  49.1 29.7 all-gather.1

commit v13 on v12

--- a/solution.py
+++ b/solution.py
@@ -164,11 +164,22 @@
         ]
 
     proj_kv, proj_query = project(scaled, mine)
+    received = []
+    w_far = []
     for flip, perm in partners(parts):
         got = lax.ppermute(scaled, "tp", perm)
-        more = project(got, flip(mine))
-        proj_kv = proj_kv + more[0]
-        proj_query = proj_query + more[1]
+        received.append(got)
+        w_far.append(lax.dynamic_slice_in_dim(w_kv, flip(mine) * width, width, 0))
+        proj_query = proj_query + jnp.dot(
+            got,
+            lax.dynamic_slice_in_dim(w_query, flip(mine) * width, width, 0),
+            preferred_element_type=jnp.float32,
+        )
+    proj_kv = proj_kv + jnp.dot(
+        jnp.concatenate(received, axis=1),
+        jnp.concatenate(w_far, axis=0),
+        preferred_element_type=jnp.float32,
+    )
     proj_key = proj_kv[:, :kv_width]
     proj_value = proj_kv[:, kv_width:]
     rstd = lax.rsqrt(squares / D + norm_eps)

time: 97.9 us -> 101 us (1.032)
  local copies, waits for them, and re-layouts: 8.54 us -> 13.3 us
  waiting for transfers between devices: 27.5 us -> 24.1 us
  other arithmetic: 8.76 us -> 11.4 us
  matrix products: 20.3 us -> 18.6 us
    dot_general x8 -> x2, matrix products: 20.3 us -> 5.55 us  [project(): jnp.dot(chunk, lax.dynamic_slice_in_dim(weight, source * width, width, 0)...]
    dot_general x0 -> x4, matrix products: none -> 13 us  [the longest x3 9.82 us: on_device(): jnp.dot(got, lax.dynamic_slice_in_dim(w_query, flip(mine) * width, width,...]
    ppermute x3, waiting for transfers between devices: 17.4 us -> 12.6 us  [on_device(): squares = squares + lax.ppermute(part_sq, 'tp', perm)]
    dynamic_slice x0 -> x1, local copies, waits for them, and re-layouts: none -> 3.56 us  [on_device(): w_far.append(lax.dynamic_slice_in_dim(w_kv, flip(mine) * width, width, 0))]
    ppermute x3, starting transfers between devices: 2.65 us -> 4.57 us  [on_device(): squares = squares + lax.ppermute(part_sq, 'tp', perm)]
    all_gather x1, waiting for transfers between devices: 10.1 us -> 11.5 us  [on_device(): lax.all_gather(jnp.concatenate([key, value], axis=1), 'blk', axis=0, tile...]
    unnamed x13 -> x25, local copies, waits for them, and re-layouts: 3.64 us -> 4.19 us
  transfers between devices with their start and end apart: 7 -> 7, of which waited for: 3 -> 2; matrix products, arithmetic and copies ran while one was open for 33% -> 35% of each run, Pallas kernels for 0% -> 0%
where the time goes in v13:
time: 101 us; the launch traced here: 99.6 us
  waiting for transfers between devices  24.1 us (24%)
  matrix products  18.6 us (18%)
  between operations  14.3 us (14%)
  local copies, waits for them, and re-layouts  13.3 us (13%)
  other arithmetic  11.4 us (11%)
  Pallas kernels  10.7 us (11%)
  starting transfers between devices  7.32 us (7%)
    ppermute x3, waiting for transfers between devices, on_device(): squares = squares + lax.ppermute(part_sq, 'tp', perm)  12.6 us
    all_gather x1, waiting for transfers between devices, on_device(): lax.all_gather(jnp.concatenate([key, value], axis=1), 'blk', axis=0, tile...  11.5 us
    pallas_call x1, Pallas kernels, window_attention(): pl.pallas_call(kernel, grid_spec=spec, out_shape=[jax.ShapeDtypeStruct((r...  10.7 us
    dot_general x3, matrix products, on_device(): jnp.dot(got, lax.dynamic_slice_in_dim(w_query, flip(mine) * width, width,...  9.82 us
    dot_general x2, matrix products, project(): jnp.dot(chunk, lax.dynamic_slice_in_dim(weight, source * width, width, 0)...  5.55 us
    ppermute x3, starting transfers between devices, on_device(): squares = squares + lax.ppermute(part_sq, 'tp', perm)  4.57 us
    unnamed x25, local copies, waits for them, and re-layouts  4.19 us
    dynamic_slice x1, local copies, waits for them, and re-layouts, on_device(): w_far.append(lax.dynamic_slice_in_dim(w_kv, flip(mine) * width, width, 0))  3.56 us
  transfers between devices with their start and end apart: 7, of which 2 were waited for; matrix products, arithmetic and copies ran while one was open for 35% of the time, Pallas kernels for 0%

profile of v13, /device:TPU:9, one launch (start us, length us, event | category | flops | bytes accessed | tf_op | source)
XLA Modules:
  0.0 99.6 jit_solution(4593462224784330541)
XLA Ops:
  7.9 1.4 %fusion.29 = (bf16[256,1280]{1,0:T(8,128)(2,1)S(1)}, f32[256]{0:T(256)S(1)}) fusion(bf16[256,1280]{1,0:T(8,128)(2,1)} %param.10, f32[1280]{0:T(1024)S(1)} %convert_element_type.43), kind=kLoop, calls=%fused_computation.25 | loop fusion | flops 1638144 | bytes 1316864 | tf_op jit(solution)/shard_map/convert_element_type | solution.py:146
  9.3 1.3 %collective-permute-start.3 = (bf16[256,1280]{1,0:T(8,128)(2,1)S(1)}, bf16[256,1280]{1,0:T(8,128)(2,1)}, u32[]{:S(2)}, u32[]{:S(2)}) collective-permute-start(bf16[256,1280]{1,0:T(8,128)(2,1)S(1)} %get-tuple-element.11), channel_id=1, source_target_pairs={{0,1},{1,0},{2,3},{3,2},{4,5},{5,4},{6,7},{7,6},{8,9},{9,8},{10,11... | collective-permute-start | bytes 1966088 | tf_op jit(solution)/shard_map/ppermute | solution.py:170
  10.5 1.2 %collective-permute-start.4 = (bf16[256,1280]{1,0:T(8,128)(2,1)S(1)}, bf16[256,1280]{1,0:T(8,128)(2,1)}, u32[]{:S(2)}, u32[]{:S(2)}) collective-permute-start(bf16[256,1280]{1,0:T(8,128)(2,1)S(1)} %get-tuple-element.11), channel_id=1, source_target_pairs={{0,2},{1,3},{2,0},{3,1},{4,6},{5,7},{6,4},{7,5},{8,10},{9,11},{10,... | collective-permute-start | bytes 1966088 | tf_op jit(solution)/shard_map/ppermute | solution.py:170
  12.0 1.2 %collective-permute-start = (f32[256]{0:T(256)S(1)}, f32[256]{0:T(256)S(1)}, u32[]{:S(2)}, u32[]{:S(2)}) collective-permute-start(f32[256]{0:T(256)S(1)} %get-tuple-element.12), channel_id=1, source_target_pairs={{0,1},{1,0},{2,3},{3,2},{4,5},{5,4},{6,7},{7,6},{8,9},{9,8},{10,11... | collective-permute-start | bytes 3080 | tf_op jit(solution)/shard_map/ppermute | solution.py:151
  13.2 1.2 %collective-permute-start.1 = (f32[256]{0:T(256)S(1)}, f32[256]{0:T(256)S(1)}, u32[]{:S(2)}, u32[]{:S(2)}) collective-permute-start(f32[256]{0:T(256)S(1)} %get-tuple-element.12), channel_id=1, source_target_pairs={{0,2},{1,3},{2,0},{3,1},{4,6},{5,7},{6,4},{7,5},{8,10},{9,11},{10,... | collective-permute-start | bytes 3080 | tf_op jit(solution)/shard_map/ppermute | solution.py:151
  14.4 3.6 %constant_dynamic-update-slice_fusion.1 = bf16[5120,512]{1,0:T(8,128)(2,1)} fusion(bf16[5120,256]{1,0:T(8,128)(2,1)} %param.13), kind=kLoop, calls=%fused_computation.55 | loop fusion | bytes 5242880
  18.4 1.7 %constant_dynamic-update-slice_fusion = bf16[5120,512]{1,0:T(8,128)(2,1)} fusion(bf16[5120,512]{1,0:T(8,128)(2,1)} %constant_dynamic-update-slice_fusion.1, bf16[5120,256]{1,0:T(8,128)(2,1)S(1)} %copy-done), kind=kLoop, calls=%fused_computation.54 | loop fusion | bytes 5242880 | tf_op jit(solution)/shard_map/concatenate | solution.py:152
  20.1 2.6 %fusion.30 = f32[256,512]{1,0:T(8,128)} fusion(bf16[256,1280]{1,0:T(8,128)(2,1)S(1)} %get-tuple-element.11, bf16[5120,512]{1,0:T(8,128)(2,1)} %constant_dynamic-update-slice_fusion, s32[]{:T(128)S(6)} %select_n.34), kind=kOutput, calls=%fused_computation.26 | convolution fusion | flops 335544320 | bytes 2490372 | tf_op jit(solution)/shard_map/dot_general | solution.py:158
  22.7 3.6 %constant_dynamic-slice_fusion.2 = (bf16[1280,512]{1,0:T(8,128)(2,1)S(1)}, bf16[1280,512]{1,0:T(8,128)(2,1)S(1)}, bf16[1280,512]{1,0:T(8,128)(2,1)}) fusion(bf16[5120,512]{1,0:T(8,128)(2,1)} %constant_dynamic-update-slice_fusion, s32[]{:T(128)S(6)} %select_n.35, s32[]{:T(128)S(6)} %select_n.37, s32[]{:T(128)S(6)} %select_n.36), kind=kLoop, calls=%fused_computation.59 | loop fusion | bytes 7864332 | tf_op jit(solution)/shard_map/dynamic_slice | solution.py:172
  26.5 12.6 %collective-permute-done = f32[256]{0:T(256)S(1)} collective-permute-done((f32[256]{0:T(256)S(1)}, f32[256]{0:T(256)S(1)}, u32[]{:S(2)}, u32[]{:S(2)}) %collective-permute-start) | collective-permute-done | bytes 1056 | tf_op jit(solution)/shard_map/ppermute | solution.py:151
  39.1 2.1 %collective-permute-start.2 = (f32[256]{0:T(256)S(1)}, f32[256]{0:T(256)}, u32[]{:S(2)}, u32[]{:S(2)}) collective-permute-start(f32[256]{0:T(256)S(1)} %get-tuple-element.12), channel_id=1, source_target_pairs={{0,3},{1,2},{2,1},{3,0},{4,7},{5,6},{6,5},{7,4},{8,11},{9,10},{10,... | collective-permute-start | bytes 3080 | tf_op jit(solution)/shard_map/ppermute | solution.py:151
  42.5 0.8 copy.19
  44.5 3.2 %fusion.32 = f32[256,512]{1,0:T(8,128)S(1)} fusion(f32[256,512]{1,0:T(8,128)} %fusion.30, bf16[1280,512]{1,0:T(8,128)(2,1)S(1)} %get-tuple-element.7, bf16[1280,512]{1,0:T(8,128)(2,1)} %get-tuple-element.8, bf16[1280,512]{1,0:T(8,128)(2,1)S(1)} %get-tuple-element.6, bf16[256,1280]{1,0:T(8,128)(2,1)} %collective-permute-done.5, ...), kind=kOutput, calls=%fused_computation.29 | convolution fusion | flops 1024458752 | bytes 6946816 | tf_op jit(solution)/shard_map/dot_general | solution.py:178
  48.1 1.4 %multiply_subtract_fusion = (bf16[256,2,64]{2,1,0:T(2,128)(2,1)S(1)}, bf16[256,2,64]{2,1,0:T(2,128)(2,1)S(1)}) fusion(f32[256,2,128]{2,1,0:T(2,128)S(1)} %reshape.140, f32[256,64]{1,0:T(8,128)} %copy.19, f32[256,64]{1,0:T(8,128)S(1)} %copy.18), kind=kLoop, calls=%fused_computation.44 | loop fusion | flops 262144 | bytes 524288 | tf_op jit(solution)/shard_map/sub | solution.py:37
  50.0 0.7 pad_maximum_fusion.2
  50.7 0.8 copy.21.qs_ref
  52.9 1.9 %add_clamp_fusion.page_ref = s32[2]{0:T(128)} fusion(s32[1]{0:T(128)} %bitcast.2, s32[1]{0:T(128)} %bitcast.1), kind=kLoop, calls=%fused_computation.72 | loop fusion | flops 4 | bytes 16 | tf_op jit(solution)/shard_map/jit(clip)/min | solution.py:218
  56.1 2.9 %fusion.12 = f32[256,1280]{1,0:T(8,128)S(1)} fusion(bf16[256,1280]{1,0:T(8,128)(2,1)S(1)} %get-tuple-element.11, bf16[5120,1280]{1,0:T(8,128)(2,1)} %param.12, s32[]{:T(128)S(6)} %select_n.34), kind=kOutput, calls=%fused_computation.12 | convolution fusion | flops 838860800 | bytes 5242884 | tf_op jit(solution)/shard_map/dot_general | solution.py:158
  59.0 3.3 %fusion.6 = f32[256,1280]{1,0:T(8,128)S(1)} fusion(bf16[256,1280]{1,0:T(8,128)(2,1)} %collective-permute-done.5, bf16[5120,1280]{1,0:T(8,128)(2,1)} %param.12, s32[]{:T(128)S(6)} %select_n.37), kind=kOutput, calls=%fused_computation.6 | convolution fusion | flops 838860800 | bytes 5242884 | tf_op jit(solution)/shard_map/dot_general | solution.py:173
  62.4 3.2 %fusion.8 = f32[256,1280]{1,0:T(8,128)S(1)} fusion(bf16[256,1280]{1,0:T(8,128)(2,1)} %collective-permute-done.4, bf16[5120,1280]{1,0:T(8,128)(2,1)} %param.12, s32[]{:T(128)S(6)} %select_n.36), kind=kOutput, calls=%fused_computation.8 | convolution fusion | flops 838860800 | bytes 5242884 | tf_op jit(solution)/shard_map/dot_general | solution.py:173
  65.5 3.4 %multiply_add_fusion = f32[256,1280]{1,0:T(8,128)S(1)} fusion(f32[1280]{0:T(1024)S(1)} %convert_element_type.45, f32[256]{0:T(256)S(1)} %add_rsqrt_fusion, f32[256,1280]{1,0:T(8,128)S(1)} %fusion.6, f32[256,1280]{1,0:T(8,128)S(1)} %fusion.8, f32[256,1280]{1,0:T(8,128)S(1)} %fusion.12, bf16[256,1280]{1,0:T(8,128)(2,1)} %collective-permute-done.3, ...), kind=kOutput, calls=%fused_computation.28 | convolution fusion | flops 840499200 | bytes 9181188 | tf_op jit(solution)/shard_map/dot_general | solution.py:173
  69.5 1.1 %copy.20.q_ref = bf16[256,1280]{1,0:T(8,128)(2,1)} copy(bf16[256,1280]{0,1:T(8,128)(2,1)S(1)} %bitcast.19) | data formatting | bytes 1310720 | tf_op jit(solution)/shard_map/convert_element_type | solution.py:195
  70.6 11.5 %all-gather.2.cloned.1.call-done.k_ref.v_ref = bf16[2048,512]{1,0:T(8,128)(2,1)} async-done(((bf16[256,512]{1,0:T(8,128)(2,1)}), bf16[2048,512]{1,0:T(8,128)(2,1)}) %all-gather.2.cloned.1.call-update) | async-done | bytes 2097168 | tf_op jit(solution)/shard_map/all_gather | solution.py:207
  82.1 10.7 %shard_map.113 = (bf16[256,1280]{1,0:T(8,128)(2,1)}, bf16[2,2,128,256]{3,2,1,0:T(8,128)(2,1)}) custom-call(s32[1]{0:T(128)} %bitcast.first_ref, s32[2]{0:T(128)} %add_clamp_fusion.page_ref, bf16[256,1280]{1,0:T(8,128)(2,1)} %copy.20.q_ref, bf16[2048,512]{1,0:T(8,128)(2,1)} %all-gather.2.cloned.1.call-done.k_ref.v_ref, ...), custom_call_target="tpu_custom_call" | custom-call | tf_op jit(solution)/shard_map/pallas_call | solution.py:103
  (58 shorter events, 8.1 us)
Async XLA Ops:
  7.2 75.0 %all-gather.2.cloned.1.call-start = ((), (), s32[]{:S(2)}) async-start(), calls=%async_computation | async-start | bytes 2359296 | tf_op jit(solution)/shard_map/all_gather | solution.py:207
  9.3 35.2 %collective-permute-start.3 = (bf16[256,1280]{1,0:T(8,128)(2,1)S(1)}, bf16[256,1280]{1,0:T(8,128)(2,1)}, u32[]{:S(2)}, u32[]{:S(2)}) collective-permute-start(bf16[256,1280]{1,0:T(8,128)(2,1)S(1)} %get-tuple-element.11), channel_id=1, source_target_pairs={{0,1},{1,0},{2,3},{3,2},{4,5},{5,4},{6,7},{7,6},{8,9},{9,8},{10,11... | collective-permute-start | bytes 1966088 | tf_op jit(solution)/shard_map/ppermute | solution.py:170
  10.5 34.0 %collective-permute-start.4 = (bf16[256,1280]{1,0:T(8,128)(2,1)S(1)}, bf16[256,1280]{1,0:T(8,128)(2,1)}, u32[]{:S(2)}, u32[]{:S(2)}) collective-permute-start(bf16[256,1280]{1,0:T(8,128)(2,1)S(1)} %get-tuple-element.11), channel_id=1, source_target_pairs={{0,2},{1,3},{2,0},{3,1},{4,6},{5,7},{6,4},{7,5},{8,10},{9,11},{10,... | collective-permute-start | bytes 1966088 | tf_op jit(solution)/shard_map/ppermute | solution.py:170
  11.8 32.7 %collective-permute-start.5 = (bf16[256,1280]{1,0:T(8,128)(2,1)S(1)}, bf16[256,1280]{1,0:T(8,128)(2,1)}, u32[]{:S(2)}, u32[]{:S(2)}) collective-permute-start(bf16[256,1280]{1,0:T(8,128)(2,1)S(1)} %get-tuple-element.11), channel_id=1, source_target_pairs={{0,3},{1,2},{2,1},{3,0},{4,7},{5,6},{6,5},{7,4},{8,11},{9,10},{10,... | collective-permute-start | bytes 1966088 | tf_op jit(solution)/shard_map/ppermute | solution.py:170
  12.0 27.2 %collective-permute-start = (f32[256]{0:T(256)S(1)}, f32[256]{0:T(256)S(1)}, u32[]{:S(2)}, u32[]{:S(2)}) collective-permute-start(f32[256]{0:T(256)S(1)} %get-tuple-element.12), channel_id=1, source_target_pairs={{0,1},{1,0},{2,3},{3,2},{4,5},{5,4},{6,7},{7,6},{8,9},{9,8},{10,11... | collective-permute-start | bytes 3080 | tf_op jit(solution)/shard_map/ppermute | solution.py:151
  13.2 30.1 %collective-permute-start.1 = (f32[256]{0:T(256)S(1)}, f32[256]{0:T(256)S(1)}, u32[]{:S(2)}, u32[]{:S(2)}) collective-permute-start(f32[256]{0:T(256)S(1)} %get-tuple-element.12), channel_id=1, source_target_pairs={{0,2},{1,3},{2,0},{3,1},{4,6},{5,7},{6,4},{7,5},{8,10},{9,11},{10,... | collective-permute-start | bytes 3080 | tf_op jit(solution)/shard_map/ppermute | solution.py:151
  14.4 3.6 %copy-start.9 = (s32[8]{0:T(128)S(1)}, s32[8]{0:T(128)}, u32[]{:S(2)}) copy-start(s32[8]{0:T(128)} %param.18) | copy-start | bytes 100
  14.4 3.9 %copy-start = (bf16[5120,256]{1,0:T(8,128)(2,1)S(1)}, bf16[5120,256]{1,0:T(8,128)(2,1)}, u32[]{:S(2)}) copy-start(bf16[5120,256]{1,0:T(8,128)(2,1)} %param.14) | copy-start | bytes 7864324
  18.2 1.8 %copy-start.2 = (s32[8,1]{0,1:T(1,128)}, s32[8,1]{0,1:T(1,128)S(1)}, u32[]{:S(2)}) copy-start(s32[8,1]{0,1:T(1,128)S(1)} %reduce-window.8) | copy-start | bytes 100
  22.7 18.6 %copy-start.10 = (bf16[256]{0:T(256)(128)(2,1)S(1)}, bf16[256]{0:T(256)(128)(2,1)}, u32[]{:S(2)}) copy-start(bf16[256]{0:T(256)(128)(2,1)} %param.16) | copy-start | bytes 1540
  22.7 19.2 %copy-start.11 = (bf16[256]{0:T(256)(128)(2,1)S(1)}, bf16[256]{0:T(256)(128)(2,1)}, u32[]{:S(2)}) copy-start(bf16[256]{0:T(256)(128)(2,1)} %param.17) | copy-start | bytes 1540
  39.1 3.3 %copy-start.4 = (f32[256]{0:T(256)}, f32[256]{0:T(256)S(1)}, u32[]{:S(2)}) copy-start(f32[256]{0:T(256)S(1)} %collective-permute-done) | copy-start | bytes 3076
  39.1 4.7 %collective-permute-start.2 = (f32[256]{0:T(256)S(1)}, f32[256]{0:T(256)}, u32[]{:S(2)}, u32[]{:S(2)}) collective-permute-start(f32[256]{0:T(256)S(1)} %get-tuple-element.12), channel_id=1, source_target_pairs={{0,3},{1,2},{2,1},{3,0},{4,7},{5,6},{6,5},{7,4},{8,11},{9,10},{10,... | collective-permute-start | bytes 3080 | tf_op jit(solution)/shard_map/ppermute | solution.py:151
  43.3 0.5 copy-start.5
  44.5 3.2 %copy-start.6 = (f32[256]{0:T(256)S(1)}, f32[256]{0:T(256)}, u32[]{:S(2)}) copy-start(f32[256]{0:T(256)} %convert_element_type.49) | copy-start | bytes 3076
  44.5 3.2 %copy-start.7 = (f32[256]{0:T(256)S(1)}, f32[256]{0:T(256)}, u32[]{:S(2)}) copy-start(f32[256]{0:T(256)} %convert_element_type.51) | copy-start | bytes 3076
  47.8 2.9 %copy-start.1 = (bf16[1280]{0:T(1024)(128)(2,1)S(1)}, bf16[1280]{0:T(1024)(128)(2,1)}, u32[]{:S(2)}) copy-start(bf16[1280]{0:T(1024)(128)(2,1)} %param.15) | copy-start | bytes 7684
  47.8 3.7 %copy-start.3 = (s32[8,1]{0,1:T(1,128)S(1)}, s32[8,1]{0,1:T(1,128)}, u32[]{:S(2)}) copy-start(s32[8,1]{0,1:T(1,128)} %copy-done.2) | copy-start | bytes 100
  47.8 4.4 %copy-start.8 = (s32[16]{0:T(128)S(1)}, s32[16]{0:T(128)}, u32[]{:S(2)}) copy-start(s32[16]{0:T(128)} %param.19) | copy-start | bytes 196
Sparse Core Ops, SparseCore 0:
  50.8 31.2 all-gather.1

commit v14 on v12

--- a/solution.py
+++ b/solution.py
@@ -166,9 +166,15 @@
     proj_kv, proj_query = project(scaled, mine)
     for flip, perm in partners(parts):
         got = lax.ppermute(scaled, "tp", perm)
-        more = project(got, flip(mine))
-        proj_kv = proj_kv + more[0]
-        proj_query = proj_query + more[1]
+        w_far = lax.optimization_barrier(
+            lax.dynamic_slice_in_dim(w_kv, flip(mine) * width, width, 0)
+        )
+        proj_kv = proj_kv + jnp.dot(got, w_far, preferred_element_type=jnp.float32)
+        proj_query = proj_query + jnp.dot(
+            got,
+            lax.dynamic_slice_in_dim(w_query, flip(mine) * width, width, 0),
+            preferred_element_type=jnp.float32,
+        )
     proj_key = proj_kv[:, :kv_width]
     proj_value = proj_kv[:, kv_width:]
     rstd = lax.rsqrt(squares / D + norm_eps)

time: 97.9 us -> 110 us (1.12)
  waiting for transfers between devices: 27.5 us -> 34 us
  local copies, waits for them, and re-layouts: 8.54 us -> 13.6 us
  other arithmetic: 8.76 us -> 11.2 us
  matrix products: 20.3 us -> 18.3 us
    dot_general x8 -> x2, matrix products: 20.3 us -> 5.96 us  [project(): jnp.dot(chunk, lax.dynamic_slice_in_dim(weight, source * width, width, 0)...]
    dot_general x0 -> x6, matrix products: none -> 12.3 us  [the longest x3 9.32 us: on_device(): jnp.dot(got, lax.dynamic_slice_in_dim(w_query, flip(mine) * width, width,...]
    ppermute x3, waiting for transfers between devices: 0.01 us -> 10.4 us  [on_device(): got = lax.ppermute(scaled, 'tp', perm)]
    ppermute x3, waiting for transfers between devices: 17.4 us -> 10.7 us  [on_device(): squares = squares + lax.ppermute(part_sq, 'tp', perm)]
    dynamic_slice x0 -> x1, local copies, waits for them, and re-layouts: none -> 3.49 us  [on_device(): lax.dynamic_slice_in_dim(w_kv, flip(mine) * width, width, 0)]
    all_gather x1, waiting for transfers between devices: 10.1 us -> 13 us  [on_device(): lax.all_gather(jnp.concatenate([key, value], axis=1), 'blk', axis=0, tile...]
    unnamed x13 -> x29, local copies, waits for them, and re-layouts: 3.64 us -> 4.61 us
  transfers between devices with their start and end apart: 7 -> 7, of which waited for: 3 -> 3; matrix products, arithmetic and copies ran while one was open for 33% -> 34% of each run, Pallas kernels for 0% -> 0%
where the time goes in v14:
time: 110 us; the launch traced here: 108 us
  waiting for transfers between devices  34 us (31%)
  matrix products  18.3 us (17%)
  between operations  14.3 us (13%)
  local copies, waits for them, and re-layouts  13.6 us (12%)
  other arithmetic  11.2 us (10%)
  Pallas kernels  10.6 us (10%)
  starting transfers between devices  6.35 us (6%)
    all_gather x1, waiting for transfers between devices, on_device(): lax.all_gather(jnp.concatenate([key, value], axis=1), 'blk', axis=0, tile...  13 us
    ppermute x3, waiting for transfers between devices, on_device(): squares = squares + lax.ppermute(part_sq, 'tp', perm)  10.7 us
    pallas_call x1, Pallas kernels, window_attention(): pl.pallas_call(kernel, grid_spec=spec, out_shape=[jax.ShapeDtypeStruct((r...  10.6 us
    ppermute x3, waiting for transfers between devices, on_device(): got = lax.ppermute(scaled, 'tp', perm)  10.4 us
    dot_general x3, matrix products, on_device(): jnp.dot(got, lax.dynamic_slice_in_dim(w_query, flip(mine) * width, width,...  9.32 us
    dot_general x2, matrix products, project(): jnp.dot(chunk, lax.dynamic_slice_in_dim(weight, source * width, width, 0)...  5.96 us
    unnamed x29, local copies, waits for them, and re-layouts  4.61 us
    ppermute x3, starting transfers between devices, on_device(): got = lax.ppermute(scaled, 'tp', perm)  3.66 us
  transfers between devices with their start and end apart: 7, of which 3 were waited for; matrix products, arithmetic and copies ran while one was open for 34% of the time, Pallas kernels for 0%

profile of v14, /device:TPU:9, one launch (start us, length us, event | category | flops | bytes accessed | tf_op | source)
XLA Modules:
  0.0 108.5 jit_solution(3448951705421588605)
XLA Ops:
  7.9 2.1 %fusion.18 = (bf16[256,1280]{1,0:T(8,128)(2,1)}, f32[256]{0:T(256)S(1)}) fusion(bf16[256,1280]{1,0:T(8,128)(2,1)} %param.10, f32[1280]{0:T(1024)S(1)} %convert_element_type.43), kind=kLoop, calls=%fused_computation.14 | loop fusion | flops 1638144 | bytes 1316864 | tf_op jit(solution)/shard_map/convert_element_type | solution.py:146
  10.0 1.2 %collective-permute-start.3 = (bf16[256,1280]{1,0:T(8,128)(2,1)}, bf16[256,1280]{1,0:T(8,128)(2,1)S(1)}, u32[]{:S(2)}, u32[]{:S(2)}) collective-permute-start(bf16[256,1280]{1,0:T(8,128)(2,1)} %get-tuple-element.11), channel_id=1, source_target_pairs={{0,1},{1,0},{2,3},{3,2},{4,5},{5,4},{6,7},{7,6},{8,9},{9,8},{10,11... | collective-permute-start | bytes 1966088 | tf_op jit(solution)/shard_map/ppermute | solution.py:168
  11.2 1.2 %collective-permute-start.5 = (bf16[256,1280]{1,0:T(8,128)(2,1)}, bf16[256,1280]{1,0:T(8,128)(2,1)}, u32[]{:S(2)}, u32[]{:S(2)}) collective-permute-start(bf16[256,1280]{1,0:T(8,128)(2,1)} %get-tuple-element.11), channel_id=1, source_target_pairs={{0,3},{1,2},{2,1},{3,0},{4,7},{5,6},{6,5},{7,4},{8,11},{9,10},{10,... | collective-permute-start | bytes 1966088 | tf_op jit(solution)/shard_map/ppermute | solution.py:168
  12.4 1.2 %collective-permute-start = (f32[256]{0:T(256)S(1)}, f32[256]{0:T(256)}, u32[]{:S(2)}, u32[]{:S(2)}) collective-permute-start(f32[256]{0:T(256)S(1)} %get-tuple-element.12), channel_id=1, source_target_pairs={{0,1},{1,0},{2,3},{3,2},{4,5},{5,4},{6,7},{7,6},{8,9},{9,8},{10,11... | collective-permute-start | bytes 3080 | tf_op jit(solution)/shard_map/ppermute | solution.py:151
  13.9 1.2 %collective-permute-start.2 = (f32[256]{0:T(256)S(1)}, f32[256]{0:T(256)}, u32[]{:S(2)}, u32[]{:S(2)}) collective-permute-start(f32[256]{0:T(256)S(1)} %get-tuple-element.12), channel_id=1, source_target_pairs={{0,3},{1,2},{2,1},{3,0},{4,7},{5,6},{6,5},{7,4},{8,11},{9,10},{10,... | collective-permute-start | bytes 3080 | tf_op jit(solution)/shard_map/ppermute | solution.py:151
  15.1 3.6 %constant_dynamic-update-slice_fusion.1 = bf16[5120,512]{1,0:T(8,128)(2,1)} fusion(bf16[5120,256]{1,0:T(8,128)(2,1)} %param.13), kind=kLoop, calls=%fused_computation.46 | loop fusion | bytes 5242880
  19.0 1.7 %constant_dynamic-update-slice_fusion = bf16[5120,512]{1,0:T(8,128)(2,1)} fusion(bf16[5120,512]{1,0:T(8,128)(2,1)} %constant_dynamic-update-slice_fusion.1, bf16[5120,256]{1,0:T(8,128)(2,1)S(1)} %copy-done), kind=kLoop, calls=%fused_computation.45 | loop fusion | bytes 5242880 | tf_op jit(solution)/shard_map/concatenate | solution.py:152
  20.7 2.8 %fusion.19 = f32[256,512]{1,0:T(8,128)} fusion(bf16[256,1280]{1,0:T(8,128)(2,1)} %get-tuple-element.11, bf16[5120,512]{1,0:T(8,128)(2,1)} %constant_dynamic-update-slice_fusion, s32[]{:T(128)S(6)} %select_n.34), kind=kOutput, calls=%fused_computation.15 | convolution fusion | flops 335544320 | bytes 2490372 | tf_op jit(solution)/shard_map/dot_general | solution.py:158
  23.5 3.5 %constant_dynamic-slice_fusion.1 = (bf16[1280,512]{1,0:T(8,128)(2,1)S(1)}, bf16[1280,512]{1,0:T(8,128)(2,1)}, bf16[1280,512]{1,0:T(8,128)(2,1)S(1)}) fusion(bf16[5120,512]{1,0:T(8,128)(2,1)} %constant_dynamic-update-slice_fusion, s32[]{:T(128)S(6)} %select_n.36, s32[]{:T(128)S(6)} %select_n.37, s32[]{:T(128)S(6)} %select_n.35), kind=kLoop, calls=%fused_computation.49 | loop fusion | bytes 7864332 | tf_op jit(solution)/shard_map/dynamic_slice | solution.py:170
  28.6 0.8 copy.19
  29.3 10.7 %collective-permute-done = f32[256]{0:T(256)} collective-permute-done((f32[256]{0:T(256)S(1)}, f32[256]{0:T(256)}, u32[]{:S(2)}, u32[]{:S(2)}) %collective-permute-start) | collective-permute-done | bytes 1056 | tf_op jit(solution)/shard_map/ppermute | solution.py:151
  40.0 1.2 %collective-permute-start.4 = (bf16[256,1280]{1,0:T(8,128)(2,1)}, bf16[256,1280]{1,0:T(8,128)(2,1)S(1)}, u32[]{:S(2)}, u32[]{:S(2)}) collective-permute-start(bf16[256,1280]{1,0:T(8,128)(2,1)} %get-tuple-element.11), channel_id=1, source_target_pairs={{0,2},{1,3},{2,0},{3,1},{4,6},{5,7},{6,4},{7,5},{8,10},{9,11},{10,... | collective-permute-start | bytes 1966088 | tf_op jit(solution)/shard_map/ppermute | solution.py:168
  41.9 2.0 %fusion.38 = f32[256,512]{1,0:T(8,128)S(1)} fusion(bf16[256,1280]{1,0:T(8,128)(2,1)} %collective-permute-done.5, bf16[1280,512]{1,0:T(8,128)(2,1)} %get-tuple-element.7), kind=kOutput, calls=%fused_computation.66 | convolution fusion | flops 335544320 | bytes 2490368 | tf_op jit(solution)/shard_map/dot_general | solution.py:172
  44.5 10.4 %collective-permute-done.4 = bf16[256,1280]{1,0:T(8,128)(2,1)S(1)} collective-permute-done((bf16[256,1280]{1,0:T(8,128)(2,1)}, bf16[256,1280]{1,0:T(8,128)(2,1)S(1)}, u32[]{:S(2)}, u32[]{:S(2)}) %collective-permute-start.4) | collective-permute-done | bytes 655392 | tf_op jit(solution)/shard_map/ppermute | solution.py:168
  57.6 0.7 pad_maximum_fusion.2
  58.4 0.8 copy.21.qs_ref
  60.6 1.9 %add_clamp_fusion.page_ref = s32[2]{0:T(128)} fusion(s32[1]{0:T(128)} %bitcast.2, s32[1]{0:T(128)} %bitcast.1), kind=kLoop, calls=%fused_computation.63 | loop fusion | flops 4 | bytes 16 | tf_op jit(solution)/shard_map/jit(clip)/min | solution.py:213
  63.8 3.1 %fusion.6 = f32[256,1280]{1,0:T(8,128)S(1)} fusion(bf16[256,1280]{1,0:T(8,128)(2,1)} %get-tuple-element.11, bf16[5120,1280]{1,0:T(8,128)(2,1)} %param.12, s32[]{:T(128)S(6)} %select_n.34), kind=kOutput, calls=%fused_computation.6 | convolution fusion | flops 838860800 | bytes 5242884 | tf_op jit(solution)/shard_map/dot_general | solution.py:158
  66.9 3.3 %fusion = f32[256,1280]{1,0:T(8,128)S(1)} fusion(bf16[256,1280]{1,0:T(8,128)(2,1)} %collective-permute-done.5, bf16[5120,1280]{1,0:T(8,128)(2,1)} %param.12, s32[]{:T(128)S(6)} %select_n.37), kind=kOutput, calls=%fused_computation | convolution fusion | flops 838860800 | bytes 5242884 | tf_op jit(solution)/shard_map/dot_general | solution.py:173
  70.2 2.9 %fusion.2 = f32[256,1280]{1,0:T(8,128)S(1)} fusion(bf16[256,1280]{1,0:T(8,128)(2,1)S(1)} %copy-done.3, bf16[5120,1280]{1,0:T(8,128)(2,1)} %param.12, s32[]{:T(128)S(6)} %select_n.36), kind=kOutput, calls=%fused_computation.2 | convolution fusion | flops 838860800 | bytes 5242884 | tf_op jit(solution)/shard_map/dot_general | solution.py:173
  73.2 3.1 %multiply_add_fusion = f32[256,1280]{1,0:T(8,128)S(1)} fusion(f32[1280]{0:T(1024)S(1)} %convert_element_type.45, f32[256]{0:T(256)S(1)} %add_rsqrt_fusion, f32[256,1280]{1,0:T(8,128)S(1)} %fusion, f32[256,1280]{1,0:T(8,128)S(1)} %fusion.2, f32[256,1280]{1,0:T(8,128)S(1)} %fusion.6, bf16[256,1280]{1,0:T(8,128)(2,1)S(1)} %collective-permute-done.3, ...), kind=kOutput, calls=%fused_computation.17 | convolution fusion | flops 840499200 | bytes 9181188 | tf_op jit(solution)/shard_map/dot_general | solution.py:173
  76.9 1.1 %copy.20.q_ref = bf16[256,1280]{1,0:T(8,128)(2,1)} copy(bf16[256,1280]{0,1:T(8,128)(2,1)S(1)} %bitcast.25) | data formatting | bytes 1310720 | tf_op jit(solution)/shard_map/convert_element_type | solution.py:190
  78.0 13.0 %all-gather.2.cloned.1.call-done.k_ref.v_ref = bf16[2048,512]{1,0:T(8,128)(2,1)} async-done(((bf16[256,512]{1,0:T(8,128)(2,1)}), bf16[2048,512]{1,0:T(8,128)(2,1)}) %all-gather.2.cloned.1.call-update) | async-done | bytes 2097168 | tf_op jit(solution)/shard_map/all_gather | solution.py:202
  91.0 10.6 %shard_map.113 = (bf16[256,1280]{1,0:T(8,128)(2,1)}, bf16[2,2,128,256]{3,2,1,0:T(8,128)(2,1)}) custom-call(s32[1]{0:T(128)} %bitcast.first_ref, s32[2]{0:T(128)} %add_clamp_fusion.page_ref, bf16[256,1280]{1,0:T(8,128)(2,1)} %copy.20.q_ref, bf16[2048,512]{1,0:T(8,128)(2,1)} %all-gather.2.cloned.1.call-done.k_ref.v_ref, ...), custom_call_target="tpu_custom_call" | custom-call | tf_op jit(solution)/shard_map/pallas_call | solution.py:103
  (64 shorter events, 10.0 us)
Async XLA Ops:
  7.2 83.8 %all-gather.2.cloned.1.call-start = ((), (), s32[]{:S(2)}) async-start(), calls=%async_computation | async-start | bytes 2359296 | tf_op jit(solution)/shard_map/all_gather | solution.py:202
  10.0 33.9 %collective-permute-start.3 = (bf16[256,1280]{1,0:T(8,128)(2,1)}, bf16[256,1280]{1,0:T(8,128)(2,1)S(1)}, u32[]{:S(2)}, u32[]{:S(2)}) collective-permute-start(bf16[256,1280]{1,0:T(8,128)(2,1)} %get-tuple-element.11), channel_id=1, source_target_pairs={{0,1},{1,0},{2,3},{3,2},{4,5},{5,4},{6,7},{7,6},{8,9},{9,8},{10,11... | collective-permute-start | bytes 1966088 | tf_op jit(solution)/shard_map/ppermute | solution.py:168
  11.2 30.7 %collective-permute-start.5 = (bf16[256,1280]{1,0:T(8,128)(2,1)}, bf16[256,1280]{1,0:T(8,128)(2,1)}, u32[]{:S(2)}, u32[]{:S(2)}) collective-permute-start(bf16[256,1280]{1,0:T(8,128)(2,1)} %get-tuple-element.11), channel_id=1, source_target_pairs={{0,3},{1,2},{2,1},{3,0},{4,7},{5,6},{6,5},{7,4},{8,11},{9,10},{10,... | collective-permute-start | bytes 1966088 | tf_op jit(solution)/shard_map/ppermute | solution.py:168
  12.4 27.6 %collective-permute-start = (f32[256]{0:T(256)S(1)}, f32[256]{0:T(256)}, u32[]{:S(2)}, u32[]{:S(2)}) collective-permute-start(f32[256]{0:T(256)S(1)} %get-tuple-element.12), channel_id=1, source_target_pairs={{0,1},{1,0},{2,3},{3,2},{4,5},{5,4},{6,7},{7,6},{8,9},{9,8},{10,11... | collective-permute-start | bytes 3080 | tf_op jit(solution)/shard_map/ppermute | solution.py:151
  13.6 27.6 %collective-permute-start.1 = (f32[256]{0:T(256)S(1)}, f32[256]{0:T(256)}, u32[]{:S(2)}, u32[]{:S(2)}) collective-permute-start(f32[256]{0:T(256)S(1)} %get-tuple-element.12), channel_id=1, source_target_pairs={{0,2},{1,3},{2,0},{3,1},{4,6},{5,7},{6,4},{7,5},{8,10},{9,11},{10,... | collective-permute-start | bytes 3080 | tf_op jit(solution)/shard_map/ppermute | solution.py:151
  13.9 27.4 %collective-permute-start.2 = (f32[256]{0:T(256)S(1)}, f32[256]{0:T(256)}, u32[]{:S(2)}, u32[]{:S(2)}) collective-permute-start(f32[256]{0:T(256)S(1)} %get-tuple-element.12), channel_id=1, source_target_pairs={{0,3},{1,2},{2,1},{3,0},{4,7},{5,6},{6,5},{7,4},{8,11},{9,10},{10,... | collective-permute-start | bytes 3080 | tf_op jit(solution)/shard_map/ppermute | solution.py:151
  15.1 3.6 %copy-start.11 = (s32[8]{0:T(128)S(1)}, s32[8]{0:T(128)}, u32[]{:S(2)}) copy-start(s32[8]{0:T(128)} %param.18) | copy-start | bytes 100
  15.1 3.9 %copy-start = (bf16[5120,256]{1,0:T(8,128)(2,1)S(1)}, bf16[5120,256]{1,0:T(8,128)(2,1)}, u32[]{:S(2)}) copy-start(bf16[5120,256]{1,0:T(8,128)(2,1)} %param.14) | copy-start | bytes 7864324
  18.9 1.8 %copy-start.6 = (s32[8,1]{0,1:T(1,128)}, s32[8,1]{0,1:T(1,128)S(1)}, u32[]{:S(2)}) copy-start(s32[8,1]{0,1:T(1,128)S(1)} %reduce-window.8) | copy-start | bytes 100
  23.5 3.8 %copy-start.12 = (bf16[256]{0:T(256)(128)(2,1)S(1)}, bf16[256]{0:T(256)(128)(2,1)}, u32[]{:S(2)}) copy-start(bf16[256]{0:T(256)(128)(2,1)} %param.16) | copy-start | bytes 1540
  23.5 4.4 %copy-start.13 = (bf16[256]{0:T(256)(128)(2,1)S(1)}, bf16[256]{0:T(256)(128)(2,1)}, u32[]{:S(2)}) copy-start(bf16[256]{0:T(256)(128)(2,1)} %param.17) | copy-start | bytes 1540
  29.3 14.6 %copy-start.1 = (f32[256,512]{1,0:T(8,128)S(1)}, f32[256,512]{1,0:T(8,128)}, u32[]{:S(2)}) copy-start(f32[256,512]{1,0:T(8,128)} %fusion.19) | copy-start | bytes 1572868
  40.0 14.9 %collective-permute-start.4 = (bf16[256,1280]{1,0:T(8,128)(2,1)}, bf16[256,1280]{1,0:T(8,128)(2,1)S(1)}, u32[]{:S(2)}, u32[]{:S(2)}) collective-permute-start(bf16[256,1280]{1,0:T(8,128)(2,1)} %get-tuple-element.11), channel_id=1, source_target_pairs={{0,2},{1,3},{2,0},{3,1},{4,6},{5,7},{6,4},{7,5},{8,10},{9,11},{10,... | collective-permute-start | bytes 1966088 | tf_op jit(solution)/shard_map/ppermute | solution.py:168
  44.5 11.2 %copy-start.8 = (f32[256]{0:T(256)S(1)}, f32[256]{0:T(256)}, u32[]{:S(2)}) copy-start(f32[256]{0:T(256)} %convert_element_type.49) | copy-start | bytes 3076
  44.5 11.2 %copy-start.9 = (f32[256]{0:T(256)S(1)}, f32[256]{0:T(256)}, u32[]{:S(2)}) copy-start(f32[256]{0:T(256)} %convert_element_type.51) | copy-start | bytes 3076
  54.9 0.9 copy-start.2
  55.7 0.9 copy-start.4
  56.6 1.7 %copy-start.5 = (bf16[1280]{0:T(1024)(128)(2,1)S(1)}, bf16[1280]{0:T(1024)(128)(2,1)}, u32[]{:S(2)}) copy-start(bf16[1280]{0:T(1024)(128)(2,1)} %param.15) | copy-start | bytes 7684
  56.6 2.6 %copy-start.7 = (s32[8,1]{0,1:T(1,128)S(1)}, s32[8,1]{0,1:T(1,128)}, u32[]{:S(2)}) copy-start(s32[8,1]{0,1:T(1,128)} %copy-done.6) | copy-start | bytes 100
  56.6 3.2 %copy-start.10 = (s32[16]{0:T(128)S(1)}, s32[16]{0:T(128)}, u32[]{:S(2)}) copy-start(s32[16]{0:T(128)} %param.19) | copy-start | bytes 196
  66.9 3.3 %copy-start.3 = (bf16[256,1280]{1,0:T(8,128)(2,1)S(1)}, bf16[256,1280]{1,0:T(8,128)(2,1)}, u32[]{:S(2)}) copy-start(bf16[256,1280]{1,0:T(8,128)(2,1)} %copy-done.2) | copy-start | bytes 1966084
Sparse Core Ops, SparseCore 0:
  58.5 32.4 all-gather.1

commit v15 on v12

--- a/solution.py
+++ b/solution.py
@@ -163,12 +163,14 @@
             for weight in (w_kv, w_query)
         ]
 
-    proj_kv, proj_query = project(scaled, mine)
+    piece = jnp.zeros((parts,) + scaled.shape, scaled.dtype)
+    piece = lax.dynamic_update_slice_in_dim(piece, scaled[None], mine, 0)
     for flip, perm in partners(parts):
         got = lax.ppermute(scaled, "tp", perm)
-        more = project(got, flip(mine))
-        proj_kv = proj_kv + more[0]
-        proj_query = proj_query + more[1]
+        piece = lax.dynamic_update_slice_in_dim(piece, got[None], flip(mine), 0)
+    piece = jnp.transpose(piece, (1, 0, 2)).reshape(rows, parts * width)
+    proj_kv = jnp.dot(piece, w_kv, preferred_element_type=jnp.float32)
+    proj_query = jnp.dot(piece, w_query, preferred_element_type=jnp.float32)
     proj_key = proj_kv[:, :kv_width]
     proj_value = proj_kv[:, kv_width:]
     rstd = lax.rsqrt(squares / D + norm_eps)

time: 97.9 us -> 101 us (1.032)
  matrix products: 20.3 us -> 11.3 us
  waiting for transfers between devices: 27.5 us -> 36.4 us
  other arithmetic: 8.76 us -> 12.8 us
  starting transfers between devices: 6.4 us -> 5.39 us
    ppermute x3, waiting for transfers between devices: 0.01 us -> 22.2 us  [on_device(): got = lax.ppermute(scaled, 'tp', perm)]
    ppermute x3, waiting for transfers between devices: 17.4 us -> 0.01 us  [on_device(): squares = squares + lax.ppermute(part_sq, 'tp', perm)]
    dot_general x8 -> x2, matrix products: 20.3 us -> 11.3 us  [the longest x1 8.06 us: on_device(): proj_query = jnp.dot(piece, w_query, preferred_element_type=jnp.float32)]
    all_gather x1, waiting for transfers between devices: 10.1 us -> 14.1 us  [on_device(): lax.all_gather(jnp.concatenate([key, value], axis=1), 'blk', axis=0, tile...]
    unnamed x13 -> x17, local copies, waits for them, and re-layouts: 3.64 us -> 1.8 us
    concatenate x1 -> x0, local copies, waits for them, and re-layouts: 1.7 us -> none  [on_device(): w_kv = jnp.concatenate([w_key, w_value], axis=1)]
    convert_element_type x2 -> x1, other arithmetic: 2.05 us -> 0.69 us  [on_device(): scaled = (wide * norm_gain.astype(jnp.float32)).astype(jnp.bfloat16)]
    add x1, local copies, waits for them, and re-layouts: 0.4 us -> 1.71 us  [on_device(): query = rstd[:, None] * proj_query + query_bias.astype(jnp.float32)]
  transfers between devices with their start and end apart: 7 -> 7, of which waited for: 3 -> 3; matrix products, arithmetic and copies ran while one was open for 33% -> 25% of each run, Pallas kernels for 0% -> 0%
where the time goes in v15:
time: 101 us; the launch traced here: 98.9 us
  waiting for transfers between devices  36.4 us (36%)
  between operations  14.3 us (14%)
  other arithmetic  12.8 us (13%)
  matrix products  11.3 us (11%)
  Pallas kernels  10.5 us (10%)
  local copies, waits for them, and re-layouts  8.38 us (8%)
  starting transfers between devices  5.39 us (5%)
    ppermute x3, waiting for transfers between devices, on_device(): got = lax.ppermute(scaled, 'tp', perm)  22.2 us
    all_gather x1, waiting for transfers between devices, on_device(): lax.all_gather(jnp.concatenate([key, value], axis=1), 'blk', axis=0, tile...  14.1 us
    pallas_call x1, Pallas kernels, window_attention(): pl.pallas_call(kernel, grid_spec=spec, out_shape=[jax.ShapeDtypeStruct((r...  10.5 us
    dot_general x1, matrix products, on_device(): proj_query = jnp.dot(piece, w_query, preferred_element_type=jnp.float32)  8.06 us
    dot_general x1, matrix products, on_device(): proj_kv = jnp.dot(piece, w_kv, preferred_element_type=jnp.float32)  3.27 us
    ppermute x3, starting transfers between devices, on_device(): squares = squares + lax.ppermute(part_sq, 'tp', perm)  2.7 us
    ppermute x3, starting transfers between devices, on_device(): got = lax.ppermute(scaled, 'tp', perm)  2.65 us
  transfers between devices with their start and end apart: 7, of which 3 were waited for; matrix products, arithmetic and copies ran while one was open for 25% of the time, Pallas kernels for 0%

profile of v15, /device:TPU:9, one launch (start us, length us, event | category | flops | bytes accessed | tf_op | source)
XLA Modules:
  0.0 98.9 jit_solution(9589923884522742643)
XLA Ops:
  7.2 1.3 %copy.18 = bf16[256,1280]{0,1:T(8,128)(2,1)S(1)} copy(bf16[256,1280]{1,0:T(8,128)(2,1)} %param.10) | data formatting | bytes 1310720 | tf_op args[0]
  8.8 2.2 %collective-permute-start.2 = (f32[256]{0:T(256)S(1)}, f32[256]{0:T(256)}, u32[]{:S(2)}, u32[]{:S(2)}) collective-permute-start(f32[256]{0:T(256)S(1)} %fusion.4), channel_id=1, source_target_pairs={{0,3},{1,2},{2,1},{3,0},{4,7},{5,6},{6,5},{7,4},{8,11},{9,10},{10,... | collective-permute-start | bytes 3080 | tf_op jit(solution)/shard_map/ppermute | solution.py:151
  11.5 0.7 convert_element_type.43
  12.3 1.1 %bitcast_dynamic-update-slice_fusion.3 = (bf16[4,256,1280]{1,2,0:T(8,128)(2,1)S(1)}, bf16[256,1280]{0,1:T(8,128)(2,1)}) fusion(bf16[4,256,1280]{1,2,0:T(8,128)(2,1)S(1)} %broadcast_in_dim.27, s32[]{:T(128)S(6)} %select_n.30, f32[1280]{0:T(1024)S(1)} %convert_element_type.43, bf16[256,1280]{0,1:T(8,128)(2,1)S(1)} %copy.18), kind=kLoop, calls=%fused_computation.13 | loop fusion | flops 983040 | bytes 1974276 | tf_op jit(solution)/shard_map/dynamic_update_slice | solution.py:167
  13.4 1.2 %collective-permute-start.3 = (bf16[256,1280]{0,1:T(8,128)(2,1)}, bf16[256,1280]{0,1:T(8,128)(2,1)}, u32[]{:S(2)}, u32[]{:S(2)}) collective-permute-start(bf16[256,1280]{0,1:T(8,128)(2,1)} %get-tuple-element.7), channel_id=1, source_target_pairs={{0,1},{1,0},{2,3},{3,2},{4,5},{5,4},{6,7},{7,6},{8,9},{9,8},{10,11... | collective-permute-start | bytes 1966088 | tf_op jit(solution)/shard_map/ppermute | solution.py:169
  14.6 1.2 %collective-permute-start.4 = (bf16[256,1280]{0,1:T(8,128)(2,1)}, bf16[256,1280]{0,1:T(8,128)(2,1)S(1)}, u32[]{:S(2)}, u32[]{:S(2)}) collective-permute-start(bf16[256,1280]{0,1:T(8,128)(2,1)} %get-tuple-element.7), channel_id=1, source_target_pairs={{0,2},{1,3},{2,0},{3,1},{4,6},{5,7},{6,4},{7,5},{8,10},{9,11},{10,... | collective-permute-start | bytes 1966088 | tf_op jit(solution)/shard_map/ppermute | solution.py:169
  18.2 0.8 copy.20
  19.2 0.8 add_rsqrt_fusion
  20.0 8.4 %collective-permute-done.3 = bf16[256,1280]{0,1:T(8,128)(2,1)} collective-permute-done((bf16[256,1280]{0,1:T(8,128)(2,1)}, bf16[256,1280]{0,1:T(8,128)(2,1)}, u32[]{:S(2)}, u32[]{:S(2)}) %collective-permute-start.3) | collective-permute-done | bytes 655392 | tf_op jit(solution)/shard_map/ppermute | solution.py:169
  28.5 1.1 %bitcast_dynamic-update-slice_fusion.2 = bf16[4,256,1280]{1,2,0:T(8,128)(2,1)S(1)} fusion(bf16[4,256,1280]{1,2,0:T(8,128)(2,1)S(1)} %get-tuple-element.6, s32[]{:T(128)S(6)} %select_n.31, bf16[256,1280]{0,1:T(8,128)(2,1)} %collective-permute-done.3), kind=kLoop, calls=%fused_computation.12 | loop fusion | bytes 1310724 | tf_op jit(solution)/shard_map/dynamic_update_slice | solution.py:170
  29.7 13.7 %collective-permute-done.5 = bf16[256,1280]{0,1:T(8,128)(2,1)S(1)} collective-permute-done((bf16[256,1280]{0,1:T(8,128)(2,1)}, bf16[256,1280]{0,1:T(8,128)(2,1)S(1)}, u32[]{:S(2)}, u32[]{:S(2)}) %collective-permute-start.5) | collective-permute-done | bytes 655392 | tf_op jit(solution)/shard_map/ppermute | solution.py:169
  43.5 3.3 %fusion = f32[256,512]{1,0:T(8,128)S(1)} fusion(bf16[256,5120]{0,1:T(8,128)(2,1)S(1)} %bitcast.27, bf16[5120,256]{1,0:T(8,128)(2,1)S(1)} %copy-done.5, bf16[5120,256]{1,0:T(8,128)(2,1)} %param.13), kind=kOutput, calls=%fused_computation | convolution fusion | flops 1352663040 | bytes 8388608 | tf_op jit(solution)/shard_map/dot_general | solution.py:172
  47.1 1.4 %multiply_subtract_fusion = (bf16[256,2,64]{2,1,0:T(2,128)(2,1)S(1)}, bf16[256,2,64]{2,1,0:T(2,128)(2,1)S(1)}) fusion(f32[256,2,128]{2,1,0:T(2,128)S(1)} %reshape.144, f32[256,64]{1,0:T(8,128)S(1)} %copy.21, f32[256,64]{1,0:T(8,128)} %copy.20), kind=kLoop, calls=%fused_computation.27 | loop fusion | flops 262144 | bytes 524288 | tf_op jit(solution)/shard_map/sub | solution.py:37
  49.0 0.7 pad_maximum_fusion.2
  49.7 0.8 copy.23.qs_ref
  50.5 0.7 convert_reduce_fusion
  51.8 1.4 %fusion.13 = (s32[]{:T(128)}, s32[]{:T(128)}) fusion(s32[16]{0:T(128)} %param.19, s32[]{:T(128)S(6)} %mul.63, s32[]{:T(128)S(6)} %add.103), kind=kLoop, calls=%fused_computation.43 | loop fusion | flops 94 | bytes 80 | tf_op jit(solution)/shard_map/reduce_sum | solution.py:207
  53.2 1.9 %add_clamp_fusion.page_ref = s32[2]{0:T(128)} fusion(s32[1]{0:T(128)} %bitcast.2, s32[1]{0:T(128)} %bitcast.1), kind=kLoop, calls=%fused_computation.45 | loop fusion | flops 4 | bytes 16 | tf_op jit(solution)/shard_map/jit(clip)/min | solution.py:209
  55.1 0.7 iota_add_fusion.qp_ref
  56.4 8.1 %multiply_add_fusion = f32[256,1280]{1,0:T(8,128)} fusion(f32[1280]{0:T(1024)S(1)} %convert_element_type.45, f32[256]{0:T(256)S(1)} %add_rsqrt_fusion, bf16[256,5120]{0,1:T(8,128)(2,1)S(1)} %bitcast.28, bf16[5120,1280]{1,0:T(8,128)(2,1)} %param.12), kind=kOutput, calls=%fused_computation.8 | convolution fusion | flops 3356098560 | bytes 17045504 | tf_op jit(solution)/shard_map/dot_general | solution.py:173
  64.4 1.7 %copy.19 = f32[256,1280]{0,1:T(8,128)S(1)} copy(f32[256,1280]{1,0:T(8,128)} %multiply_add_fusion) | data formatting | bytes 2621440 | tf_op jit(solution)/shard_map/add | solution.py:180
  66.4 1.1 %copy.22.q_ref = bf16[256,1280]{1,0:T(8,128)(2,1)} copy(bf16[256,1280]{0,1:T(8,128)(2,1)S(1)} %bitcast.30) | data formatting | bytes 1310720 | tf_op jit(solution)/shard_map/convert_element_type | solution.py:186
  67.5 14.1 %all-gather.2.cloned.1.call-done.k_ref.v_ref = bf16[2048,512]{1,0:T(8,128)(2,1)} async-done(((bf16[256,512]{1,0:T(8,128)(2,1)}), bf16[2048,512]{1,0:T(8,128)(2,1)}) %all-gather.2.cloned.1.call-update) | async-done | bytes 2097168 | tf_op jit(solution)/shard_map/all_gather | solution.py:198
  81.6 10.5 %shard_map.113 = (bf16[256,1280]{1,0:T(8,128)(2,1)}, bf16[2,2,128,256]{3,2,1,0:T(8,128)(2,1)}) custom-call(s32[1]{0:T(128)} %bitcast.first_ref, s32[2]{0:T(128)} %add_clamp_fusion.page_ref, bf16[256,1280]{1,0:T(8,128)(2,1)} %copy.22.q_ref, bf16[2048,512]{1,0:T(8,128)(2,1)} %all-gather.2.cloned.1.call-done.k_ref.v_ref, ...), custom_call_target="tpu_custom_call" | custom-call | tf_op jit(solution)/shard_map/pallas_call | solution.py:103
  (49 shorter events, 5.7 us)
Async XLA Ops:
  7.2 74.5 %all-gather.2.cloned.1.call-start = ((), (), s32[]{:S(2)}) async-start(), calls=%async_computation | async-start | bytes 2359296 | tf_op jit(solution)/shard_map/all_gather | solution.py:198
  8.5 7.4 %copy-start.4 = (s32[8]{0:T(128)S(1)}, s32[8]{0:T(128)}, u32[]{:S(2)}) copy-start(s32[8]{0:T(128)} %param.18) | copy-start | bytes 100
  8.5 8.4 %copy-start.6 = (bf16[256]{0:T(256)(128)(2,1)S(1)}, bf16[256]{0:T(256)(128)(2,1)}, u32[]{:S(2)}) copy-start(bf16[256]{0:T(256)(128)(2,1)} %param.16) | copy-start | bytes 1540
  8.6 9.0 %copy-start.7 = (bf16[256]{0:T(256)(128)(2,1)S(1)}, bf16[256]{0:T(256)(128)(2,1)}, u32[]{:S(2)}) copy-start(bf16[256]{0:T(256)(128)(2,1)} %param.17) | copy-start | bytes 1540
  8.8 10.2 %collective-permute-start.2 = (f32[256]{0:T(256)S(1)}, f32[256]{0:T(256)}, u32[]{:S(2)}, u32[]{:S(2)}) collective-permute-start(f32[256]{0:T(256)S(1)} %fusion.4), channel_id=1, source_target_pairs={{0,3},{1,2},{2,1},{3,0},{4,7},{5,6},{6,5},{7,4},{8,11},{9,10},{10,... | collective-permute-start | bytes 3080 | tf_op jit(solution)/shard_map/ppermute | solution.py:151
  11.0 8.2 %collective-permute-start.1 = (f32[256]{0:T(256)S(1)}, f32[256]{0:T(256)}, u32[]{:S(2)}, u32[]{:S(2)}) collective-permute-start(f32[256]{0:T(256)S(1)} %fusion.4), channel_id=1, source_target_pairs={{0,2},{1,3},{2,0},{3,1},{4,6},{5,7},{6,4},{7,5},{8,10},{9,11},{10,... | collective-permute-start | bytes 3080 | tf_op jit(solution)/shard_map/ppermute | solution.py:151
  11.2 8.0 %collective-permute-start = (f32[256]{0:T(256)S(1)}, f32[256]{0:T(256)}, u32[]{:S(2)}, u32[]{:S(2)}) collective-permute-start(f32[256]{0:T(256)S(1)} %fusion.4), channel_id=1, source_target_pairs={{0,1},{1,0},{2,3},{3,2},{4,5},{5,4},{6,7},{7,6},{8,9},{9,8},{10,11... | collective-permute-start | bytes 3080 | tf_op jit(solution)/shard_map/ppermute | solution.py:151
  13.4 15.0 %collective-permute-start.3 = (bf16[256,1280]{0,1:T(8,128)(2,1)}, bf16[256,1280]{0,1:T(8,128)(2,1)}, u32[]{:S(2)}, u32[]{:S(2)}) collective-permute-start(bf16[256,1280]{0,1:T(8,128)(2,1)} %get-tuple-element.7), channel_id=1, source_target_pairs={{0,1},{1,0},{2,3},{3,2},{4,5},{5,4},{6,7},{7,6},{8,9},{9,8},{10,11... | collective-permute-start | bytes 1966088 | tf_op jit(solution)/shard_map/ppermute | solution.py:169
  14.6 14.9 %collective-permute-start.4 = (bf16[256,1280]{0,1:T(8,128)(2,1)}, bf16[256,1280]{0,1:T(8,128)(2,1)S(1)}, u32[]{:S(2)}, u32[]{:S(2)}) collective-permute-start(bf16[256,1280]{0,1:T(8,128)(2,1)} %get-tuple-element.7), channel_id=1, source_target_pairs={{0,2},{1,3},{2,0},{3,1},{4,6},{5,7},{6,4},{7,5},{8,10},{9,11},{10,... | collective-permute-start | bytes 1966088 | tf_op jit(solution)/shard_map/ppermute | solution.py:169
  16.1 0.5 copy-start.1
  19.0 24.5 %copy-start.5 = (bf16[5120,256]{1,0:T(8,128)(2,1)S(1)}, bf16[5120,256]{1,0:T(8,128)(2,1)}, u32[]{:S(2)}) copy-start(bf16[5120,256]{1,0:T(8,128)(2,1)} %param.14) | copy-start | bytes 7864324
  19.0 24.4 %collective-permute-start.5 = (bf16[256,1280]{0,1:T(8,128)(2,1)}, bf16[256,1280]{0,1:T(8,128)(2,1)S(1)}, u32[]{:S(2)}, u32[]{:S(2)}) collective-permute-start(bf16[256,1280]{0,1:T(8,128)(2,1)} %get-tuple-element.7), channel_id=1, source_target_pairs={{0,3},{1,2},{2,1},{3,0},{4,7},{5,6},{6,5},{7,4},{8,11},{9,10},{10,... | collective-permute-start | bytes 1966088 | tf_op jit(solution)/shard_map/ppermute | solution.py:169
  43.5 3.3 %copy-start.2 = (f32[256]{0:T(256)S(1)}, f32[256]{0:T(256)}, u32[]{:S(2)}) copy-start(f32[256]{0:T(256)} %convert_element_type.49) | copy-start | bytes 3076
  43.5 3.3 %copy-start.3 = (f32[256]{0:T(256)S(1)}, f32[256]{0:T(256)}, u32[]{:S(2)}) copy-start(f32[256]{0:T(256)} %convert_element_type.51) | copy-start | bytes 3076
  46.8 2.9 %copy-start = (bf16[1280]{0:T(1024)(128)(2,1)S(1)}, bf16[1280]{0:T(1024)(128)(2,1)}, u32[]{:S(2)}) copy-start(bf16[1280]{0:T(1024)(128)(2,1)} %param.15) | copy-start | bytes 7684
Sparse Core Ops, SparseCore 0:
  49.8 31.7 all-gather.1

commit v16 on v12

--- a/solution.py
+++ b/solution.py
@@ -59,7 +59,7 @@
 
     slots = pages.shape[0]
 
-    def kernel(first_ref, page_ref, q_ref, k_ref, v_ref, qs_ref, qp_ref, ks_ref, kp_ref, o_ref, c_ref):
+    def kernel(first_ref, page_ref, q_ref, k_ref, v_ref, qs_ref, ks_ref, o_ref, c_ref):
         for j in range(slots):
             row = pl.multiple_of(page_ref[j] * PAGE, PAGE)
             c_ref[j, 0] = k_ref[pl.ds(row, PAGE), :]
@@ -67,15 +67,14 @@
         start = pl.multiple_of(first_ref[0], PAGE)
         keys = k_ref[pl.ds(start, span), :]
         values = v_ref[pl.ds(start, span), :]
-        qs = qs_ref[...]
-        live = qs < docs - 1
-        allowed = (ks_ref[...] == qs) & (kp_ref[...] <= qp_ref[...]) & live
+        live = qs_ref[...] < docs - 1
+        bias = ks_ref[...].astype(jnp.float32)
         for g in range(group):
             q = q_ref[:, g * HEAD:(g + 1) * HEAD]
             scores = lax.dot_general(
                 q, keys, (((1,), (1,)), ((), ())), preferred_element_type=jnp.float32
             ) * scale
-            scores = jnp.where(allowed, scores, neg_large)
+            scores = scores + bias
             top = jnp.max(scores, axis=1, keepdims=True)
             expo = jnp.exp(scores - top)
             denom = jnp.sum(expo, axis=1, keepdims=True)
@@ -91,9 +90,7 @@
             pl.BlockSpec((count, HEAD), lambda c, f, p: (0, c)),
             pl.BlockSpec((count, HEAD), lambda c, f, p: (0, kv_dev + c)),
             pl.BlockSpec((rows, 1), lambda c, f, p: (0, 0)),
-            pl.BlockSpec((rows, 1), lambda c, f, p: (0, 0)),
-            pl.BlockSpec((1, span), lambda c, f, p: (0, 0)),
-            pl.BlockSpec((1, span), lambda c, f, p: (0, 0)),
+            pl.BlockSpec((rows, span), lambda c, f, p: (0, 0)),
         ],
         out_specs=[
             pl.BlockSpec((rows, group * HEAD), lambda c, f, p: (0, c)),
@@ -115,9 +112,13 @@
         both,
         both,
         q_seg.reshape(rows, 1),
-        q_pos.reshape(rows, 1),
-        k_seg.reshape(1, span),
-        k_pos.reshape(1, span),
+        jnp.where(
+            (k_seg[None, :] == q_seg[:, None])
+            & (k_pos[None, :] <= q_pos[:, None])
+            & (q_seg[:, None] < docs - 1),
+            0.0,
+            neg_large,
+        ).astype(jnp.bfloat16),
     )
 
 def on_device(

time: 97.9 us -> 97.2 us (level)
    convert_element_type x0 -> x1, other arithmetic: none -> 1.25 us  [window_attention(): return pl.pallas_call(kernel, grid_spec=spec, out_shape=[jax.ShapeDtypeSt...]
  transfers between devices with their start and end apart: 7 -> 7, of which waited for: 3 -> 3; matrix products, arithmetic and copies ran while one was open for 33% -> 32% of each run, Pallas kernels for 0% -> 0%
where the time goes in v16:
time: 97.2 us; the launch traced here: 95.6 us
  waiting for transfers between devices  28.3 us (29%)
  matrix products  20.3 us (21%)
  between operations  14.3 us (15%)
  Pallas kernels  9.84 us (10%)
  other arithmetic  8.54 us (9%)
  local copies, waits for them, and re-layouts  7.95 us (8%)
  starting transfers between devices  6.4 us (7%)
    dot_general x8, matrix products, project(): jnp.dot(chunk, lax.dynamic_slice_in_dim(weight, source * width, width, 0)...  20.3 us
    ppermute x3, waiting for transfers between devices, on_device(): squares = squares + lax.ppermute(part_sq, 'tp', perm)  17.4 us
    all_gather x1, waiting for transfers between devices, on_device(): lax.all_gather(jnp.concatenate([key, value], axis=1), 'blk', axis=0, tile...  10.9 us
    pallas_call x1, Pallas kernels, window_attention(): pl.pallas_call(kernel, grid_spec=spec, out_shape=[jax.ShapeDtypeStruct((r...  9.84 us
    ppermute x3, starting transfers between devices, on_device(): got = lax.ppermute(scaled, 'tp', perm)  3.71 us
    unnamed x13, local copies, waits for them, and re-layouts  3.64 us
    ppermute x3, starting transfers between devices, on_device(): squares = squares + lax.ppermute(part_sq, 'tp', perm)  2.65 us
    convert_element_type x2, other arithmetic, on_device(): scaled = (wide * norm_gain.astype(jnp.float32)).astype(jnp.bfloat16)  2.05 us
  transfers between devices with their start and end apart: 7, of which 3 were waited for; matrix products, arithmetic and copies ran while one was open for 32% of the time, Pallas kernels for 0%

profile of v16, /device:TPU:9, one launch (start us, length us, event | category | flops | bytes accessed | tf_op | source)
XLA Modules:
  0.0 95.6 jit_solution(6961922011877007878)
XLA Ops:
  7.9 1.4 %fusion.18 = (bf16[256,1280]{1,0:T(8,128)(2,1)S(1)}, f32[256]{0:T(256)S(1)}) fusion(bf16[256,1280]{1,0:T(8,128)(2,1)} %param.10, f32[1280]{0:T(1024)S(1)} %convert_element_type.46), kind=kLoop, calls=%fused_computation.14 | loop fusion | flops 1638144 | bytes 1316864 | tf_op jit(solution)/shard_map/convert_element_type | solution.py:147
  9.3 2.2 %collective-permute-start.5 = (bf16[256,1280]{1,0:T(8,128)(2,1)S(1)}, bf16[256,1280]{1,0:T(8,128)(2,1)}, u32[]{:S(2)}, u32[]{:S(2)}) collective-permute-start(bf16[256,1280]{1,0:T(8,128)(2,1)S(1)} %get-tuple-element.8), channel_id=1, source_target_pairs={{0,3},{1,2},{2,1},{3,0},{4,7},{5,6},{6,5},{7,4},{8,11},{9,10},{10,... | collective-permute-start | bytes 1966088 | tf_op jit(solution)/shard_map/ppermute | solution.py:169
  12.0 1.2 %collective-permute-start.1 = (f32[256]{0:T(256)S(1)}, f32[256]{0:T(256)S(1)}, u32[]{:S(2)}, u32[]{:S(2)}) collective-permute-start(f32[256]{0:T(256)S(1)} %get-tuple-element.9), channel_id=1, source_target_pairs={{0,2},{1,3},{2,0},{3,1},{4,6},{5,7},{6,4},{7,5},{8,10},{9,11},{10,... | collective-permute-start | bytes 3080 | tf_op jit(solution)/shard_map/ppermute | solution.py:152
  13.2 1.2 %collective-permute-start.2 = (f32[256]{0:T(256)S(1)}, f32[256]{0:T(256)S(1)}, u32[]{:S(2)}, u32[]{:S(2)}) collective-permute-start(f32[256]{0:T(256)S(1)} %get-tuple-element.9), channel_id=1, source_target_pairs={{0,3},{1,2},{2,1},{3,0},{4,7},{5,6},{6,5},{7,4},{8,11},{9,10},{10,... | collective-permute-start | bytes 3080 | tf_op jit(solution)/shard_map/ppermute | solution.py:152
  14.4 3.6 %constant_dynamic-update-slice_fusion.1 = bf16[5120,512]{1,0:T(8,128)(2,1)} fusion(bf16[5120,256]{1,0:T(8,128)(2,1)} %param.13), kind=kLoop, calls=%fused_computation.52 | loop fusion | bytes 5242880
  18.3 1.7 %constant_dynamic-update-slice_fusion = bf16[5120,512]{1,0:T(8,128)(2,1)} fusion(bf16[5120,512]{1,0:T(8,128)(2,1)} %constant_dynamic-update-slice_fusion.1, bf16[5120,256]{1,0:T(8,128)(2,1)S(1)} %copy-done), kind=kLoop, calls=%fused_computation.51 | loop fusion | bytes 5242880 | tf_op jit(solution)/shard_map/concatenate | solution.py:153
  20.0 1.8 %fusion.25 = f32[256,512]{1,0:T(8,128)S(1)} fusion(bf16[256,1280]{1,0:T(8,128)(2,1)S(1)} %get-tuple-element.8, bf16[5120,512]{1,0:T(8,128)(2,1)} %constant_dynamic-update-slice_fusion, s32[]{:T(128)S(6)} %select_n.38), kind=kOutput, calls=%fused_computation.22 | convolution fusion | flops 335544320 | bytes 2490372 | tf_op jit(solution)/shard_map/dot_general | solution.py:159
  22.4 3.6 %collective-permute-done = f32[256]{0:T(256)S(1)} collective-permute-done((f32[256]{0:T(256)S(1)}, f32[256]{0:T(256)S(1)}, u32[]{:S(2)}, u32[]{:S(2)}) %collective-permute-start) | collective-permute-done | bytes 1056 | tf_op jit(solution)/shard_map/ppermute | solution.py:152
  26.0 1.3 %collective-permute-start.3 = (bf16[256,1280]{1,0:T(8,128)(2,1)S(1)}, bf16[256,1280]{1,0:T(8,128)(2,1)S(1)}, u32[]{:S(2)}, u32[]{:S(2)}) collective-permute-start(bf16[256,1280]{1,0:T(8,128)(2,1)S(1)} %get-tuple-element.8), channel_id=1, source_target_pairs={{0,1},{1,0},{2,3},{3,2},{4,5},{5,4},{6,7},{7,6},{8,9},{9,8},{10,11... | collective-permute-start | bytes 1966088 | tf_op jit(solution)/shard_map/ppermute | solution.py:169
  27.3 13.8 %collective-permute-done.1 = f32[256]{0:T(256)S(1)} collective-permute-done((f32[256]{0:T(256)S(1)}, f32[256]{0:T(256)S(1)}, u32[]{:S(2)}, u32[]{:S(2)}) %collective-permute-start.1) | collective-permute-done | bytes 1056 | tf_op jit(solution)/shard_map/ppermute | solution.py:152
  41.1 2.0 %fusion.19 = f32[256,512]{1,0:T(8,128)S(1)} fusion(bf16[256,1280]{1,0:T(8,128)(2,1)} %collective-permute-done.5, bf16[5120,512]{1,0:T(8,128)(2,1)} %constant_dynamic-update-slice_fusion, s32[]{:T(128)S(6)} %select_n.41), kind=kOutput, calls=%fused_computation.16 | convolution fusion | flops 335544320 | bytes 2490372 | tf_op jit(solution)/shard_map/dot_general | solution.py:159
  43.1 2.0 %fusion.21 = f32[256,512]{1,0:T(8,128)S(1)} fusion(bf16[256,1280]{1,0:T(8,128)(2,1)} %collective-permute-done.4, bf16[5120,512]{1,0:T(8,128)(2,1)} %constant_dynamic-update-slice_fusion, s32[]{:T(128)S(6)} %select_n.40), kind=kOutput, calls=%fused_computation.18 | convolution fusion | flops 335544320 | bytes 2490372 | tf_op jit(solution)/shard_map/dot_general | solution.py:159
  45.2 1.8 %fusion.33 = f32[256,512]{1,0:T(8,128)S(1)} fusion(f32[256,512]{1,0:T(8,128)S(1)} %fusion.19, f32[256,512]{1,0:T(8,128)S(1)} %fusion.21, f32[256,512]{1,0:T(8,128)S(1)} %fusion.25, bf16[256,1280]{1,0:T(8,128)(2,1)S(1)} %collective-permute-done.3, bf16[5120,512]{1,0:T(8,128)(2,1)} %constant_dynamic-update-slice_fusion, s32[]{:T(128)S(6)} %select_n.39), kind=kOutput, calls=%fused_computation.27 | convolution fusion | flops 335937536 | bytes 4063236 | tf_op jit(solution)/shard_map/dot_general | solution.py:159
  48.3 0.7 pad_maximum_fusion.2
  49.1 0.8 copy.21.qs_ref
  50.5 1.9 %add_clamp_fusion.page_ref = s32[2]{0:T(128)} fusion(s32[1]{0:T(128)} %bitcast.2, s32[1]{0:T(128)} %bitcast.1), kind=kLoop, calls=%fused_computation.68 | loop fusion | flops 4 | bytes 16 | tf_op jit(solution)/shard_map/jit(clip)/min | solution.py:208
  52.5 2.9 %fusion.6 = f32[256,1280]{1,0:T(8,128)S(1)} fusion(bf16[256,1280]{1,0:T(8,128)(2,1)S(1)} %get-tuple-element.8, bf16[5120,1280]{1,0:T(8,128)(2,1)} %param.12, s32[]{:T(128)S(6)} %select_n.38), kind=kOutput, calls=%fused_computation.6 | convolution fusion | flops 838860800 | bytes 5242884 | tf_op jit(solution)/shard_map/dot_general | solution.py:159
  55.4 1.3 %select_convert_fusion.ks_ref = bf16[256,1280]{1,0:T(8,128)(2,1)} fusion(s32[1280]{0:T(1024)S(1)} %iota_add_fusion, s32[1280]{0:T(1024)S(1)} %convert_reduce_fusion, s32[256]{0:T(256)S(1)} %iota_add_fusion.1, s32[256]{0:T(256)S(1)} %get-tuple-element.2, pred[256]{0:T(512)(128)(4,1)S(1)} %broadcast_compare_fusion), kind=kLoop, calls=%fused_computation.15 | loop fusion | flops 1966080 | bytes 667904 | tf_op jit(solution)/shard_map/convert_element_type | solution.py:121
  56.7 3.4 %fusion = f32[256,1280]{1,0:T(8,128)S(1)} fusion(bf16[256,1280]{1,0:T(8,128)(2,1)} %collective-permute-done.5, bf16[5120,1280]{1,0:T(8,128)(2,1)} %param.12, s32[]{:T(128)S(6)} %select_n.41), kind=kOutput, calls=%fused_computation | convolution fusion | flops 838860800 | bytes 5242884 | tf_op jit(solution)/shard_map/dot_general | solution.py:159
  60.1 3.2 %fusion.2 = f32[256,1280]{1,0:T(8,128)S(1)} fusion(bf16[256,1280]{1,0:T(8,128)(2,1)} %collective-permute-done.4, bf16[5120,1280]{1,0:T(8,128)(2,1)} %param.12, s32[]{:T(128)S(6)} %select_n.40), kind=kOutput, calls=%fused_computation.2 | convolution fusion | flops 838860800 | bytes 5242884 | tf_op jit(solution)/shard_map/dot_general | solution.py:159
  63.2 3.1 %multiply_add_fusion = f32[256,1280]{1,0:T(8,128)S(1)} fusion(f32[1280]{0:T(1024)S(1)} %convert_element_type.48, f32[256]{0:T(256)S(1)} %add_rsqrt_fusion, f32[256,1280]{1,0:T(8,128)S(1)} %fusion, f32[256,1280]{1,0:T(8,128)S(1)} %fusion.2, f32[256,1280]{1,0:T(8,128)S(1)} %fusion.6, bf16[256,1280]{1,0:T(8,128)(2,1)S(1)} %collective-permute-done.3, ...), kind=kOutput, calls=%fused_computation.24 | convolution fusion | flops 840499200 | bytes 9181188 | tf_op jit(solution)/shard_map/dot_general | solution.py:159
  67.0 1.1 %copy.20.q_ref = bf16[256,1280]{1,0:T(8,128)(2,1)} copy(bf16[256,1280]{0,1:T(8,128)(2,1)S(1)} %bitcast.22) | data formatting | bytes 1310720 | tf_op jit(solution)/shard_map/convert_element_type | solution.py:185
  68.1 10.9 %all-gather.2.cloned.1.call-done.k_ref.v_ref = bf16[2048,512]{1,0:T(8,128)(2,1)} async-done(((bf16[256,512]{1,0:T(8,128)(2,1)}), bf16[2048,512]{1,0:T(8,128)(2,1)}) %all-gather.2.cloned.1.call-update) | async-done | bytes 2097168 | tf_op jit(solution)/shard_map/all_gather | solution.py:197
  79.0 9.8 %shard_map.113 = (bf16[256,1280]{1,0:T(8,128)(2,1)}, bf16[2,2,128,256]{3,2,1,0:T(8,128)(2,1)}) custom-call(s32[1]{0:T(128)} %bitcast.first_ref, s32[2]{0:T(128)} %add_clamp_fusion.page_ref, bf16[256,1280]{1,0:T(8,128)(2,1)} %copy.20.q_ref, bf16[2048,512]{1,0:T(8,128)(2,1)} %all-gather.2.cloned.1.call-done.k_ref.v_ref, ...), custom_call_target="tpu_custom_call" | custom-call | tf_op jit(solution)/shard_map/pallas_call | solution.py:100
  (45 shorter events, 4.6 us)
Async XLA Ops:
  7.2 71.8 %all-gather.2.cloned.1.call-start = ((), (), s32[]{:S(2)}) async-start(), calls=%async_computation | async-start | bytes 2359296 | tf_op jit(solution)/shard_map/all_gather | solution.py:197
  9.3 31.8 %collective-permute-start.5 = (bf16[256,1280]{1,0:T(8,128)(2,1)S(1)}, bf16[256,1280]{1,0:T(8,128)(2,1)}, u32[]{:S(2)}, u32[]{:S(2)}) collective-permute-start(bf16[256,1280]{1,0:T(8,128)(2,1)S(1)} %get-tuple-element.8), channel_id=1, source_target_pairs={{0,3},{1,2},{2,1},{3,0},{4,7},{5,6},{6,5},{7,4},{8,11},{9,10},{10,... | collective-permute-start | bytes 1966088 | tf_op jit(solution)/shard_map/ppermute | solution.py:169
  11.5 31.6 %collective-permute-start.4 = (bf16[256,1280]{1,0:T(8,128)(2,1)S(1)}, bf16[256,1280]{1,0:T(8,128)(2,1)}, u32[]{:S(2)}, u32[]{:S(2)}) collective-permute-start(bf16[256,1280]{1,0:T(8,128)(2,1)S(1)} %get-tuple-element.8), channel_id=1, source_target_pairs={{0,2},{1,3},{2,0},{3,1},{4,6},{5,7},{6,4},{7,5},{8,10},{9,11},{10,... | collective-permute-start | bytes 1966088 | tf_op jit(solution)/shard_map/ppermute | solution.py:169
  11.7 14.3 %collective-permute-start = (f32[256]{0:T(256)S(1)}, f32[256]{0:T(256)S(1)}, u32[]{:S(2)}, u32[]{:S(2)}) collective-permute-start(f32[256]{0:T(256)S(1)} %get-tuple-element.9), channel_id=1, source_target_pairs={{0,1},{1,0},{2,3},{3,2},{4,5},{5,4},{6,7},{7,6},{8,9},{9,8},{10,11... | collective-permute-start | bytes 3080 | tf_op jit(solution)/shard_map/ppermute | solution.py:152
  12.0 29.1 %collective-permute-start.1 = (f32[256]{0:T(256)S(1)}, f32[256]{0:T(256)S(1)}, u32[]{:S(2)}, u32[]{:S(2)}) collective-permute-start(f32[256]{0:T(256)S(1)} %get-tuple-element.9), channel_id=1, source_target_pairs={{0,2},{1,3},{2,0},{3,1},{4,6},{5,7},{6,4},{7,5},{8,10},{9,11},{10,... | collective-permute-start | bytes 3080 | tf_op jit(solution)/shard_map/ppermute | solution.py:152
  13.2 27.9 %collective-permute-start.2 = (f32[256]{0:T(256)S(1)}, f32[256]{0:T(256)S(1)}, u32[]{:S(2)}, u32[]{:S(2)}) collective-permute-start(f32[256]{0:T(256)S(1)} %get-tuple-element.9), channel_id=1, source_target_pairs={{0,3},{1,2},{2,1},{3,0},{4,7},{5,6},{6,5},{7,4},{8,11},{9,10},{10,... | collective-permute-start | bytes 3080 | tf_op jit(solution)/shard_map/ppermute | solution.py:152
  14.4 3.6 %copy-start.3 = (s32[8]{0:T(128)S(1)}, s32[8]{0:T(128)}, u32[]{:S(2)}) copy-start(s32[8]{0:T(128)} %param.18) | copy-start | bytes 100
  14.4 3.9 %copy-start = (bf16[5120,256]{1,0:T(8,128)(2,1)S(1)}, bf16[5120,256]{1,0:T(8,128)(2,1)}, u32[]{:S(2)}) copy-start(bf16[5120,256]{1,0:T(8,128)(2,1)} %param.14) | copy-start | bytes 7864324
  20.0 2.2 %copy-start.4 = (bf16[256]{0:T(256)(128)(2,1)S(1)}, bf16[256]{0:T(256)(128)(2,1)}, u32[]{:S(2)}) copy-start(bf16[256]{0:T(256)(128)(2,1)} %param.16) | copy-start | bytes 1540
  20.0 2.2 %copy-start.5 = (bf16[256]{0:T(256)(128)(2,1)S(1)}, bf16[256]{0:T(256)(128)(2,1)}, u32[]{:S(2)}) copy-start(bf16[256]{0:T(256)(128)(2,1)} %param.17) | copy-start | bytes 1540
  26.0 19.1 %collective-permute-start.3 = (bf16[256,1280]{1,0:T(8,128)(2,1)S(1)}, bf16[256,1280]{1,0:T(8,128)(2,1)S(1)}, u32[]{:S(2)}, u32[]{:S(2)}) collective-permute-start(bf16[256,1280]{1,0:T(8,128)(2,1)S(1)} %get-tuple-element.8), channel_id=1, source_target_pairs={{0,1},{1,0},{2,3},{3,2},{4,5},{5,4},{6,7},{7,6},{8,9},{9,8},{10,11... | collective-permute-start | bytes 1966088 | tf_op jit(solution)/shard_map/ppermute | solution.py:169
  47.3 1.7 %copy-start.1 = (bf16[1280]{0:T(1024)(128)(2,1)S(1)}, bf16[1280]{0:T(1024)(128)(2,1)}, u32[]{:S(2)}) copy-start(bf16[1280]{0:T(1024)(128)(2,1)} %param.15) | copy-start | bytes 7684
  47.3 2.6 %copy-start.2 = (s32[16]{0:T(128)S(1)}, s32[16]{0:T(128)}, u32[]{:S(2)}) copy-start(s32[16]{0:T(128)} %param.19) | copy-start | bytes 196
Sparse Core Ops, SparseCore 0:
  49.1 29.7 all-gather.1

commit v17 on v16

--- a/solution.py
+++ b/solution.py
@@ -73,10 +73,10 @@
             q = q_ref[:, g * HEAD:(g + 1) * HEAD]
             scores = lax.dot_general(
                 q, keys, (((1,), (1,)), ((), ())), preferred_element_type=jnp.float32
-            ) * scale
+            )
             scores = scores + bias
             top = jnp.max(scores, axis=1, keepdims=True)
-            expo = jnp.exp(scores - top)
+            expo = jnp.exp((scores - top) * scale)
             denom = jnp.sum(expo, axis=1, keepdims=True)
             acc = jnp.dot(expo.astype(jnp.bfloat16), values, preferred_element_type=jnp.float32)
             out = jnp.where(live, acc / jnp.where(live, denom, 1.0), 0.0)

time: 97.2 us -> 97.3 us (level)
  no operation moved by 1% of the time
where the time goes in v17:
time: 97.3 us; the launch traced here: 95.7 us
  waiting for transfers between devices  28.3 us (29%)
  matrix products  20.3 us (21%)
  between operations  14.3 us (15%)
  Pallas kernels  9.93 us (10%)
  other arithmetic  8.54 us (9%)
  local copies, waits for them, and re-layouts  7.95 us (8%)
  starting transfers between devices  6.4 us (7%)
    dot_general x8, matrix products, project(): jnp.dot(chunk, lax.dynamic_slice_in_dim(weight, source * width, width, 0)...  20.3 us
    ppermute x3, waiting for transfers between devices, on_device(): squares = squares + lax.ppermute(part_sq, 'tp', perm)  17.4 us
    all_gather x1, waiting for transfers between devices, on_device(): lax.all_gather(jnp.concatenate([key, value], axis=1), 'blk', axis=0, tile...  10.9 us
    pallas_call x1, Pallas kernels, window_attention(): pl.pallas_call(kernel, grid_spec=spec, out_shape=[jax.ShapeDtypeStruct((r...  9.93 us
    ppermute x3, starting transfers between devices, on_device(): got = lax.ppermute(scaled, 'tp', perm)  3.71 us
    unnamed x13, local copies, waits for them, and re-layouts  3.64 us
    ppermute x3, starting transfers between devices, on_device(): squares = squares + lax.ppermute(part_sq, 'tp', perm)  2.65 us
    convert_element_type x2, other arithmetic, on_device(): scaled = (wide * norm_gain.astype(jnp.float32)).astype(jnp.bfloat16)  2.05 us
  transfers between devices with their start and end apart: 7, of which 3 were waited for; matrix products, arithmetic and copies ran while one was open for 32% of the time, Pallas kernels for 0%

profile of v17, /device:TPU:9, one launch (start us, length us, event | category | flops | bytes accessed | tf_op | source)
XLA Modules:
  0.0 95.7 jit_solution(6683420293580260216)
XLA Ops:
  7.9 1.4 %fusion.18 = (bf16[256,1280]{1,0:T(8,128)(2,1)S(1)}, f32[256]{0:T(256)S(1)}) fusion(bf16[256,1280]{1,0:T(8,128)(2,1)} %param.10, f32[1280]{0:T(1024)S(1)} %convert_element_type.46), kind=kLoop, calls=%fused_computation.14 | loop fusion | flops 1638144 | bytes 1316864 | tf_op jit(solution)/shard_map/convert_element_type | solution.py:147
  9.3 2.2 %collective-permute-start.5 = (bf16[256,1280]{1,0:T(8,128)(2,1)S(1)}, bf16[256,1280]{1,0:T(8,128)(2,1)}, u32[]{:S(2)}, u32[]{:S(2)}) collective-permute-start(bf16[256,1280]{1,0:T(8,128)(2,1)S(1)} %get-tuple-element.8), channel_id=1, source_target_pairs={{0,3},{1,2},{2,1},{3,0},{4,7},{5,6},{6,5},{7,4},{8,11},{9,10},{10,... | collective-permute-start | bytes 1966088 | tf_op jit(solution)/shard_map/ppermute | solution.py:169
  12.0 1.2 %collective-permute-start.1 = (f32[256]{0:T(256)S(1)}, f32[256]{0:T(256)S(1)}, u32[]{:S(2)}, u32[]{:S(2)}) collective-permute-start(f32[256]{0:T(256)S(1)} %get-tuple-element.9), channel_id=1, source_target_pairs={{0,2},{1,3},{2,0},{3,1},{4,6},{5,7},{6,4},{7,5},{8,10},{9,11},{10,... | collective-permute-start | bytes 3080 | tf_op jit(solution)/shard_map/ppermute | solution.py:152
  13.2 1.2 %collective-permute-start.2 = (f32[256]{0:T(256)S(1)}, f32[256]{0:T(256)S(1)}, u32[]{:S(2)}, u32[]{:S(2)}) collective-permute-start(f32[256]{0:T(256)S(1)} %get-tuple-element.9), channel_id=1, source_target_pairs={{0,3},{1,2},{2,1},{3,0},{4,7},{5,6},{6,5},{7,4},{8,11},{9,10},{10,... | collective-permute-start | bytes 3080 | tf_op jit(solution)/shard_map/ppermute | solution.py:152
  14.4 3.6 %constant_dynamic-update-slice_fusion.1 = bf16[5120,512]{1,0:T(8,128)(2,1)} fusion(bf16[5120,256]{1,0:T(8,128)(2,1)} %param.13), kind=kLoop, calls=%fused_computation.52 | loop fusion | bytes 5242880
  18.3 1.7 %constant_dynamic-update-slice_fusion = bf16[5120,512]{1,0:T(8,128)(2,1)} fusion(bf16[5120,512]{1,0:T(8,128)(2,1)} %constant_dynamic-update-slice_fusion.1, bf16[5120,256]{1,0:T(8,128)(2,1)S(1)} %copy-done), kind=kLoop, calls=%fused_computation.51 | loop fusion | bytes 5242880 | tf_op jit(solution)/shard_map/concatenate | solution.py:153
  20.0 1.8 %fusion.25 = f32[256,512]{1,0:T(8,128)S(1)} fusion(bf16[256,1280]{1,0:T(8,128)(2,1)S(1)} %get-tuple-element.8, bf16[5120,512]{1,0:T(8,128)(2,1)} %constant_dynamic-update-slice_fusion, s32[]{:T(128)S(6)} %select_n.38), kind=kOutput, calls=%fused_computation.22 | convolution fusion | flops 335544320 | bytes 2490372 | tf_op jit(solution)/shard_map/dot_general | solution.py:159
  22.4 3.6 %collective-permute-done = f32[256]{0:T(256)S(1)} collective-permute-done((f32[256]{0:T(256)S(1)}, f32[256]{0:T(256)S(1)}, u32[]{:S(2)}, u32[]{:S(2)}) %collective-permute-start) | collective-permute-done | bytes 1056 | tf_op jit(solution)/shard_map/ppermute | solution.py:152
  26.0 1.3 %collective-permute-start.3 = (bf16[256,1280]{1,0:T(8,128)(2,1)S(1)}, bf16[256,1280]{1,0:T(8,128)(2,1)S(1)}, u32[]{:S(2)}, u32[]{:S(2)}) collective-permute-start(bf16[256,1280]{1,0:T(8,128)(2,1)S(1)} %get-tuple-element.8), channel_id=1, source_target_pairs={{0,1},{1,0},{2,3},{3,2},{4,5},{5,4},{6,7},{7,6},{8,9},{9,8},{10,11... | collective-permute-start | bytes 1966088 | tf_op jit(solution)/shard_map/ppermute | solution.py:169
  27.3 13.8 %collective-permute-done.1 = f32[256]{0:T(256)S(1)} collective-permute-done((f32[256]{0:T(256)S(1)}, f32[256]{0:T(256)S(1)}, u32[]{:S(2)}, u32[]{:S(2)}) %collective-permute-start.1) | collective-permute-done | bytes 1056 | tf_op jit(solution)/shard_map/ppermute | solution.py:152
  41.1 2.0 %fusion.19 = f32[256,512]{1,0:T(8,128)S(1)} fusion(bf16[256,1280]{1,0:T(8,128)(2,1)} %collective-permute-done.5, bf16[5120,512]{1,0:T(8,128)(2,1)} %constant_dynamic-update-slice_fusion, s32[]{:T(128)S(6)} %select_n.41), kind=kOutput, calls=%fused_computation.16 | convolution fusion | flops 335544320 | bytes 2490372 | tf_op jit(solution)/shard_map/dot_general | solution.py:159
  43.1 2.0 %fusion.21 = f32[256,512]{1,0:T(8,128)S(1)} fusion(bf16[256,1280]{1,0:T(8,128)(2,1)} %collective-permute-done.4, bf16[5120,512]{1,0:T(8,128)(2,1)} %constant_dynamic-update-slice_fusion, s32[]{:T(128)S(6)} %select_n.40), kind=kOutput, calls=%fused_computation.18 | convolution fusion | flops 335544320 | bytes 2490372 | tf_op jit(solution)/shard_map/dot_general | solution.py:159
  45.2 1.8 %fusion.33 = f32[256,512]{1,0:T(8,128)S(1)} fusion(f32[256,512]{1,0:T(8,128)S(1)} %fusion.19, f32[256,512]{1,0:T(8,128)S(1)} %fusion.21, f32[256,512]{1,0:T(8,128)S(1)} %fusion.25, bf16[256,1280]{1,0:T(8,128)(2,1)S(1)} %collective-permute-done.3, bf16[5120,512]{1,0:T(8,128)(2,1)} %constant_dynamic-update-slice_fusion, s32[]{:T(128)S(6)} %select_n.39), kind=kOutput, calls=%fused_computation.27 | convolution fusion | flops 335937536 | bytes 4063236 | tf_op jit(solution)/shard_map/dot_general | solution.py:159
  48.3 0.7 pad_maximum_fusion.2
  49.1 0.8 copy.21.qs_ref
  50.5 1.9 %add_clamp_fusion.page_ref = s32[2]{0:T(128)} fusion(s32[1]{0:T(128)} %bitcast.2, s32[1]{0:T(128)} %bitcast.1), kind=kLoop, calls=%fused_computation.68 | loop fusion | flops 4 | bytes 16 | tf_op jit(solution)/shard_map/jit(clip)/min | solution.py:208
  52.5 2.9 %fusion.6 = f32[256,1280]{1,0:T(8,128)S(1)} fusion(bf16[256,1280]{1,0:T(8,128)(2,1)S(1)} %get-tuple-element.8, bf16[5120,1280]{1,0:T(8,128)(2,1)} %param.12, s32[]{:T(128)S(6)} %select_n.38), kind=kOutput, calls=%fused_computation.6 | convolution fusion | flops 838860800 | bytes 5242884 | tf_op jit(solution)/shard_map/dot_general | solution.py:159
  55.4 1.3 %select_convert_fusion.ks_ref = bf16[256,1280]{1,0:T(8,128)(2,1)} fusion(s32[1280]{0:T(1024)S(1)} %iota_add_fusion, s32[1280]{0:T(1024)S(1)} %convert_reduce_fusion, s32[256]{0:T(256)S(1)} %iota_add_fusion.1, s32[256]{0:T(256)S(1)} %get-tuple-element.2, pred[256]{0:T(512)(128)(4,1)S(1)} %broadcast_compare_fusion), kind=kLoop, calls=%fused_computation.15 | loop fusion | flops 1966080 | bytes 667904 | tf_op jit(solution)/shard_map/convert_element_type | solution.py:121
  56.7 3.4 %fusion = f32[256,1280]{1,0:T(8,128)S(1)} fusion(bf16[256,1280]{1,0:T(8,128)(2,1)} %collective-permute-done.5, bf16[5120,1280]{1,0:T(8,128)(2,1)} %param.12, s32[]{:T(128)S(6)} %select_n.41), kind=kOutput, calls=%fused_computation | convolution fusion | flops 838860800 | bytes 5242884 | tf_op jit(solution)/shard_map/dot_general | solution.py:159
  60.1 3.2 %fusion.2 = f32[256,1280]{1,0:T(8,128)S(1)} fusion(bf16[256,1280]{1,0:T(8,128)(2,1)} %collective-permute-done.4, bf16[5120,1280]{1,0:T(8,128)(2,1)} %param.12, s32[]{:T(128)S(6)} %select_n.40), kind=kOutput, calls=%fused_computation.2 | convolution fusion | flops 838860800 | bytes 5242884 | tf_op jit(solution)/shard_map/dot_general | solution.py:159
  63.2 3.1 %multiply_add_fusion = f32[256,1280]{1,0:T(8,128)S(1)} fusion(f32[1280]{0:T(1024)S(1)} %convert_element_type.48, f32[256]{0:T(256)S(1)} %add_rsqrt_fusion, f32[256,1280]{1,0:T(8,128)S(1)} %fusion, f32[256,1280]{1,0:T(8,128)S(1)} %fusion.2, f32[256,1280]{1,0:T(8,128)S(1)} %fusion.6, bf16[256,1280]{1,0:T(8,128)(2,1)S(1)} %collective-permute-done.3, ...), kind=kOutput, calls=%fused_computation.24 | convolution fusion | flops 840499200 | bytes 9181188 | tf_op jit(solution)/shard_map/dot_general | solution.py:159
  67.0 1.1 %copy.20.q_ref = bf16[256,1280]{1,0:T(8,128)(2,1)} copy(bf16[256,1280]{0,1:T(8,128)(2,1)S(1)} %bitcast.22) | data formatting | bytes 1310720 | tf_op jit(solution)/shard_map/convert_element_type | solution.py:185
  68.1 10.9 %all-gather.2.cloned.1.call-done.k_ref.v_ref = bf16[2048,512]{1,0:T(8,128)(2,1)} async-done(((bf16[256,512]{1,0:T(8,128)(2,1)}), bf16[2048,512]{1,0:T(8,128)(2,1)}) %all-gather.2.cloned.1.call-update) | async-done | bytes 2097168 | tf_op jit(solution)/shard_map/all_gather | solution.py:197
  79.0 9.9 %shard_map.113 = (bf16[256,1280]{1,0:T(8,128)(2,1)}, bf16[2,2,128,256]{3,2,1,0:T(8,128)(2,1)}) custom-call(s32[1]{0:T(128)} %bitcast.first_ref, s32[2]{0:T(128)} %add_clamp_fusion.page_ref, bf16[256,1280]{1,0:T(8,128)(2,1)} %copy.20.q_ref, bf16[2048,512]{1,0:T(8,128)(2,1)} %all-gather.2.cloned.1.call-done.k_ref.v_ref, ...), custom_call_target="tpu_custom_call" | custom-call | tf_op jit(solution)/shard_map/pallas_call | solution.py:100
  (45 shorter events, 4.6 us)
Async XLA Ops:
  7.2 71.8 %all-gather.2.cloned.1.call-start = ((), (), s32[]{:S(2)}) async-start(), calls=%async_computation | async-start | bytes 2359296 | tf_op jit(solution)/shard_map/all_gather | solution.py:197
  9.3 31.8 %collective-permute-start.5 = (bf16[256,1280]{1,0:T(8,128)(2,1)S(1)}, bf16[256,1280]{1,0:T(8,128)(2,1)}, u32[]{:S(2)}, u32[]{:S(2)}) collective-permute-start(bf16[256,1280]{1,0:T(8,128)(2,1)S(1)} %get-tuple-element.8), channel_id=1, source_target_pairs={{0,3},{1,2},{2,1},{3,0},{4,7},{5,6},{6,5},{7,4},{8,11},{9,10},{10,... | collective-permute-start | bytes 1966088 | tf_op jit(solution)/shard_map/ppermute | solution.py:169
  11.5 31.6 %collective-permute-start.4 = (bf16[256,1280]{1,0:T(8,128)(2,1)S(1)}, bf16[256,1280]{1,0:T(8,128)(2,1)}, u32[]{:S(2)}, u32[]{:S(2)}) collective-permute-start(bf16[256,1280]{1,0:T(8,128)(2,1)S(1)} %get-tuple-element.8), channel_id=1, source_target_pairs={{0,2},{1,3},{2,0},{3,1},{4,6},{5,7},{6,4},{7,5},{8,10},{9,11},{10,... | collective-permute-start | bytes 1966088 | tf_op jit(solution)/shard_map/ppermute | solution.py:169
  11.7 14.3 %collective-permute-start = (f32[256]{0:T(256)S(1)}, f32[256]{0:T(256)S(1)}, u32[]{:S(2)}, u32[]{:S(2)}) collective-permute-start(f32[256]{0:T(256)S(1)} %get-tuple-element.9), channel_id=1, source_target_pairs={{0,1},{1,0},{2,3},{3,2},{4,5},{5,4},{6,7},{7,6},{8,9},{9,8},{10,11... | collective-permute-start | bytes 3080 | tf_op jit(solution)/shard_map/ppermute | solution.py:152
  12.0 29.1 %collective-permute-start.1 = (f32[256]{0:T(256)S(1)}, f32[256]{0:T(256)S(1)}, u32[]{:S(2)}, u32[]{:S(2)}) collective-permute-start(f32[256]{0:T(256)S(1)} %get-tuple-element.9), channel_id=1, source_target_pairs={{0,2},{1,3},{2,0},{3,1},{4,6},{5,7},{6,4},{7,5},{8,10},{9,11},{10,... | collective-permute-start | bytes 3080 | tf_op jit(solution)/shard_map/ppermute | solution.py:152
  13.2 27.9 %collective-permute-start.2 = (f32[256]{0:T(256)S(1)}, f32[256]{0:T(256)S(1)}, u32[]{:S(2)}, u32[]{:S(2)}) collective-permute-start(f32[256]{0:T(256)S(1)} %get-tuple-element.9), channel_id=1, source_target_pairs={{0,3},{1,2},{2,1},{3,0},{4,7},{5,6},{6,5},{7,4},{8,11},{9,10},{10,... | collective-permute-start | bytes 3080 | tf_op jit(solution)/shard_map/ppermute | solution.py:152
  14.4 3.6 %copy-start.3 = (s32[8]{0:T(128)S(1)}, s32[8]{0:T(128)}, u32[]{:S(2)}) copy-start(s32[8]{0:T(128)} %param.18) | copy-start | bytes 100
  14.4 3.9 %copy-start = (bf16[5120,256]{1,0:T(8,128)(2,1)S(1)}, bf16[5120,256]{1,0:T(8,128)(2,1)}, u32[]{:S(2)}) copy-start(bf16[5120,256]{1,0:T(8,128)(2,1)} %param.14) | copy-start | bytes 7864324
  20.0 2.2 %copy-start.4 = (bf16[256]{0:T(256)(128)(2,1)S(1)}, bf16[256]{0:T(256)(128)(2,1)}, u32[]{:S(2)}) copy-start(bf16[256]{0:T(256)(128)(2,1)} %param.16) | copy-start | bytes 1540
  20.0 2.2 %copy-start.5 = (bf16[256]{0:T(256)(128)(2,1)S(1)}, bf16[256]{0:T(256)(128)(2,1)}, u32[]{:S(2)}) copy-start(bf16[256]{0:T(256)(128)(2,1)} %param.17) | copy-start | bytes 1540
  26.0 19.1 %collective-permute-start.3 = (bf16[256,1280]{1,0:T(8,128)(2,1)S(1)}, bf16[256,1280]{1,0:T(8,128)(2,1)S(1)}, u32[]{:S(2)}, u32[]{:S(2)}) collective-permute-start(bf16[256,1280]{1,0:T(8,128)(2,1)S(1)} %get-tuple-element.8), channel_id=1, source_target_pairs={{0,1},{1,0},{2,3},{3,2},{4,5},{5,4},{6,7},{7,6},{8,9},{9,8},{10,11... | collective-permute-start | bytes 1966088 | tf_op jit(solution)/shard_map/ppermute | solution.py:169
  47.3 1.7 %copy-start.1 = (bf16[1280]{0:T(1024)(128)(2,1)S(1)}, bf16[1280]{0:T(1024)(128)(2,1)}, u32[]{:S(2)}) copy-start(bf16[1280]{0:T(1024)(128)(2,1)} %param.15) | copy-start | bytes 7684
  47.3 2.6 %copy-start.2 = (s32[16]{0:T(128)S(1)}, s32[16]{0:T(128)}, u32[]{:S(2)}) copy-start(s32[16]{0:T(128)} %param.19) | copy-start | bytes 196
Sparse Core Ops, SparseCore 0:
  49.1 29.7 all-gather.1
